TPU v7x, 32 devices: a whole 2x2x4 slice. The times are simulated.
32 devices in a mesh: tm: 16 (over z, y, x), sec: 2 (over core).
Axes of the slice: x: 2, y: 2, z: 4, core: 2. Of those that a mesh axis runs over, the one named last changes fastest.
Arguments:
- signal: bfloat16 [2048, 16384], P('sec', 'tm')
- round_shard: int32 [2], replicated, may hold values from 0 to 15
- offsets: int32 [2, 16], replicated, may hold values from 0 to 896
- chan_range: int32 [2, 16, 2], replicated, may hold values from 0 to 2048, as said below
Outputs:
- detection: float32 [2, 16, 16384], P(None, None, 'tm')
Inputs may be any that keep to these rules, and one draw needn't show every extreme that they name: chan_range[r, k] = (lo, hi) with lo < hi and hi - lo >= 512.
All inputs are finite; a program needn't handle non-finite values.
Results may differ from a plain program's by a relative error of at most 0.0003.
Values may be sent and summed in bfloat16 or wider, within the bound.
No kernel may reach another device: no remote copies, remote signals or barrier semaphores. Data moves between devices by JAX's collectives and lax.ppermute only.
A program may use at most 64 MiB of HBM per device.

v0:
```python
import jax
import jax.numpy as jnp
from jax import lax
from jax.sharding import PartitionSpec as P

L = 128
TPL_BLOCK = 4
ROUNDS = 2


EPS = 1e-06


def from_behind(value, axis, by):
    length = lax.axis_size(axis)
    pairs = [(i, i + by) for i in range(length) if 0 <= i + by < length]
    return lax.ppermute(value, axis, pairs)


def spread(value, axis, source):
    kept = jnp.where(lax.axis_index(axis) == source, value, 0).astype(value.dtype)
    return lax.psum(kept, axis)


def skew_sum(product, lag_count):
    group_count, tap_count, span_width = product.shape
    flipped = product[:, :, ::-1]
    widened = jnp.pad(flipped, ((0, 0), (0, 0), (0, 1)))
    sheared = widened.reshape(group_count, tap_count * (span_width + 1))[
        :, : tap_count * span_width
    ]
    sheared = sheared.reshape(group_count, tap_count, span_width)
    summed = jnp.sum(sheared, axis=1)
    return summed[:, span_width - lag_count :][:, ::-1]


def correlate(templates, extended, lag_count):
    template_count = templates.shape[0]
    grouped = templates.reshape(
        template_count // TPL_BLOCK, TPL_BLOCK, templates.shape[1], templates.shape[2]
    )

    def one_block(block):
        product = jnp.einsum("kcl,cw->klw", block, extended, preferred_element_type=jnp.float32)
        return skew_sum(product, lag_count)

    return lax.map(one_block, grouped).reshape(template_count, lag_count)


def sliding_energy(masks, extended, lag_count, tap_count):
    squares = jnp.square(extended.astype(jnp.float32))
    summed = jnp.dot(
        masks, squares, precision=lax.Precision.HIGHEST, preferred_element_type=jnp.float32
    )
    running = jnp.pad(jnp.cumsum(summed, axis=1), ((0, 0), (1, 0)))
    return running[:, tap_count : tap_count + lag_count] - running[:, :lag_count]


def cut_windows(records, starts, inside):
    windows = jax.vmap(lambda first: lax.dynamic_slice_in_dim(records, first, L, axis=1))(starts)
    return jnp.where(inside[:, :, None], windows, jnp.zeros_like(windows))


def shards(signal, round_shard, offsets, chan_range):
    chan_local = signal.shape[0]
    lag_count = signal.shape[1]
    section = lax.axis_index("sec")
    total_lags = lag_count * lax.axis_size("tm")
    right_rim = from_behind(signal[:, :L], "tm", -1)
    extended = jnp.concatenate([signal, right_rim], axis=1)
    channel = section * chan_local + jnp.arange(chan_local, dtype=jnp.int32)

    def make_template(level):
        lower = chan_range[level, :, 0]
        upper = chan_range[level, :, 1]
        inside = (channel[None, :] >= lower[:, None]) & (channel[None, :] < upper[:, None])
        local_tmpl = cut_windows(signal, offsets[level], inside)
        templates = spread(local_tmpl, "tm", round_shard[level])
        local_power = jnp.sum(jnp.square(templates.astype(jnp.float32)), axis=(1, 2))
        tmpl_power = lax.psum(local_power, "sec")
        return (templates, inside.astype(jnp.float32), tmpl_power)

    def finish(templates, masks, tmpl_power):
        corr_local = correlate(templates, extended, lag_count)
        energy_local = sliding_energy(masks, extended, lag_count, L)
        corr, energy = lax.psum((corr_local, energy_local), "sec")
        normed = corr / jnp.sqrt(energy * tmpl_power[:, None] + EPS)
        power_sum = lax.psum(jnp.sum(normed * normed, axis=1), "tm")
        meansq = power_sum / total_lags
        scored = normed / jnp.sqrt(meansq[:, None] + EPS)
        return scored

    results = [finish(*make_template(level)) for level in range(ROUNDS)]
    return jnp.stack(results, axis=0)


def solution(mesh):
    placed = (P("sec", "tm"), P(), P(), P())
    return jax.shard_map(
        shards, mesh=mesh, in_specs=placed, out_specs=P(None, None, "tm"), check_vma=False
    )
```

profile of v0, /device:TPU:0, one launch (start us, length us, event | category | flops | bytes accessed | tf_op | source)
XLA Modules:
  0.0 749.8 jit_solution(7222854212829165390)
XLA Ops:
  13.5 50.0 %while.28 = (s32[]{:T(128)}, bf16[1024,1024]{1,0:T(8,128)(2,1)}, s32[16,2]{0,1:T(2,128)S(1)}, bf16[16,1024,128]{2,1,0:T(8,128)(2,1)}, s32[]{:T(128)}) while((s32[]{:T(128)}, bf16[1024,1024]{1,0:T(8,128)(2,1)}, s32[16,2]{0,1:T(2,128)S(1)}, bf16[16,1024,128]{2,1,0:T(8,128)(2,1)}, s32[]{:T(128)}) %tuple.84), condition=%wide.while_cond, body=%wide.while_body.sunk | while | flops 2 | bytes 525401 | solution.py:60
  66.3 49.9 %while.29 = (s32[]{:T(128)}, bf16[1024,1024]{1,0:T(8,128)(2,1)}, s32[16,2]{0,1:T(2,128)S(1)}, bf16[16,1024,128]{2,1,0:T(8,128)(2,1)}, s32[]{:T(128)}) while((s32[]{:T(128)}, bf16[1024,1024]{1,0:T(8,128)(2,1)}, s32[16,2]{0,1:T(2,128)S(1)}, bf16[16,1024,128]{2,1,0:T(8,128)(2,1)}, s32[]{:T(128)}) %tuple.102), condition=%wide.while_cond.1, body=%wide.while_body.1.sunk | while | flops 2 | bytes 525401 | solution.py:60
  116.2 8.0 %select_select_fusion = (bf16[16,1024,128]{2,1,0:T(8,128)(2,1)}, bf16[16,1024,128]{2,1,0:T(8,128)(2,1)}) fusion(bf16[16,1024,128]{2,1,0:T(8,128)(2,1)} %get-tuple-element.128, pred[16,1024]{1,0:T(8,128)(4,1)S(1)} %get-tuple-element.188, pred[]{:T(512)S(6)} %eq.7, bf16[16,1024,128]{2,1,0:T(8,128)(2,1)} %get-tuple-element.120, ...), kind=kLoop, calls=%fused_computation.23 | loop fusion | flops 8388608 | bytes 16809986 | tf_op jit(solution)/shard_map/jit(_where)/select_n | solution.py:21
  128.3 10.6 %collective-permute-done = bf16[1024,128]{1,0:T(8,128)(2,1)S(1)} collective-permute-done((bf16[1024,128]{1,0:T(8,128)(2,1)S(1)}, bf16[1024,128]{1,0:T(8,128)(2,1)S(1)}, u32[]{:S(2)}, u32[]{:S(2)}) %collective-permute-start) | collective-permute-done | bytes 262176 | tf_op jit(solution)/shard_map/ppermute | solution.py:17
  141.0 4.7 reduce-window.16
  148.1 4.5 reduce-window.14
  153.9 233.3 %all-reduce.15.cloned.1.call-done = (bf16[16,1024,128]{2,1,0:T(8,128)(2,1)}, bf16[16,1024,128]{2,1,0:T(8,128)(2,1)}) async-done(((bf16[16,1024,128]{2,1,0:T(8,128)(2,1)}, bf16[16,1024,128]{2,1,0:T(8,128)(2,1)}), (bf16[16,1024,128]{2,1,0:T(8,128)(2,1)}, bf16[16,1024,128]{2,1,0:T(8,128)(2,1)})) %all-reduce.15.cloned.1.call-update) | async-done | bytes 8388624 | tf_op jit(solution)/shard_map/psum | solution.py:22
  390.4 143.4 %while.26 = (s32[]{:T(128)}, f32[4,4,1024]{2,1,0:T(4,128)S(1)}, bf16[4,4,1024,128]{3,2,1,0:T(8,128)(2,1)}, bf16[1024,1152]{1,0:T(8,128)(2,1)S(1)}, s32[]{:T(128)}, /*index=5*/f32[]{:T(128)}) while((s32[]{:T(128)}, f32[4,4,1024]{2,1,0:T(4,128)S(1)}, bf16[4,4,1024,128]{3,2,1,0:T(8,128)(2,1)}, bf16[1024,1152]{1,0:T(8,128)(2,1)S(1)}, s32[]{:T(128)}, ...), condition=%wide.region_3.4_spmd, body=%wide.region_1.3_spmd.sunk | while | flops 1208544768 | bytes 29483620 | solution.py:47
  390.5 4.3 fusion.23
  394.7 19.8 %rev.28 = f32[4,128,1152]{2,1,0:T(8,128)} reverse(f32[4,128,1152]{2,1,0:T(8,128)} %fusion.23), dimensions={2} | reverse | bytes 4718592 | tf_op jit(solution)/shard_map/while/body/eval_jaxpr/rev | solution.py:27
  418.0 5.8 reshape.302
  426.3 4.3 fusion.23
  430.6 19.8 %rev.28 = f32[4,128,1152]{2,1,0:T(8,128)} reverse(f32[4,128,1152]{2,1,0:T(8,128)} %fusion.23), dimensions={2} | reverse | bytes 4718592 | tf_op jit(solution)/shard_map/while/body/eval_jaxpr/rev | solution.py:27
  453.8 5.8 reshape.302
  462.2 4.3 fusion.23
  466.4 19.8 %rev.28 = f32[4,128,1152]{2,1,0:T(8,128)} reverse(f32[4,128,1152]{2,1,0:T(8,128)} %fusion.23), dimensions={2} | reverse | bytes 4718592 | tf_op jit(solution)/shard_map/while/body/eval_jaxpr/rev | solution.py:27
  489.6 5.8 reshape.302
  502.3 19.8 %rev.28 = f32[4,128,1152]{2,1,0:T(8,128)} reverse(f32[4,128,1152]{2,1,0:T(8,128)} %fusion.23), dimensions={2} | reverse | bytes 4718592 | tf_op jit(solution)/shard_map/while/body/eval_jaxpr/rev | solution.py:27
  525.5 5.8 reshape.302
  534.5 143.4 %while.27 = (s32[]{:T(128)}, f32[4,4,1024]{2,1,0:T(4,128)S(1)}, bf16[4,4,1024,128]{3,2,1,0:T(8,128)(2,1)}, bf16[1024,1152]{1,0:T(8,128)(2,1)S(1)}, s32[]{:T(128)}, /*index=5*/f32[]{:T(128)}) while((s32[]{:T(128)}, f32[4,4,1024]{2,1,0:T(4,128)S(1)}, bf16[4,4,1024,128]{3,2,1,0:T(8,128)(2,1)}, bf16[1024,1152]{1,0:T(8,128)(2,1)S(1)}, ...), condition=%wide.region_15.16_spmd, body=%wide.region_13.15_spmd.sunk | while | flops 1208544768 | bytes 29483620 | solution.py:47
  534.5 4.3 fusion.26
  538.8 19.8 %rev.30 = f32[4,128,1152]{2,1,0:T(8,128)} reverse(f32[4,128,1152]{2,1,0:T(8,128)} %fusion.26), dimensions={2} | reverse | bytes 4718592 | tf_op jit(solution)/shard_map/while/body/eval_jaxpr/rev | solution.py:27
  562.0 5.8 reshape.303
  574.6 19.8 %rev.30 = f32[4,128,1152]{2,1,0:T(8,128)} reverse(f32[4,128,1152]{2,1,0:T(8,128)} %fusion.26), dimensions={2} | reverse | bytes 4718592 | tf_op jit(solution)/shard_map/while/body/eval_jaxpr/rev | solution.py:27
  597.9 5.8 reshape.303
  606.2 4.3 fusion.26
  610.5 19.8 %rev.30 = f32[4,128,1152]{2,1,0:T(8,128)} reverse(f32[4,128,1152]{2,1,0:T(8,128)} %fusion.26), dimensions={2} | reverse | bytes 4718592 | tf_op jit(solution)/shard_map/while/body/eval_jaxpr/rev | solution.py:27
  633.7 5.8 reshape.303
  646.3 19.8 %rev.30 = f32[4,128,1152]{2,1,0:T(8,128)} reverse(f32[4,128,1152]{2,1,0:T(8,128)} %fusion.26), dimensions={2} | reverse | bytes 4718592 | tf_op jit(solution)/shard_map/while/body/eval_jaxpr/rev | solution.py:27
  669.6 5.8 reshape.303
  684.2 11.9 %all-reduce.13.cloned.1.call-done = (f32[16,1024]{1,0:T(8,128)}, f32[16,1024]{1,0:T(8,128)}, f32[16,1024]{1,0:T(8,128)}, f32[16,1024]{1,0:T(8,128)}) async-done(((f32[16,1024]{1,0:T(8,128)}, f32[16,1024]{1,0:T(8,128)}, f32[16,1024]{1,0:T(8,128)}, f32[16,1024]{1,0:T(8,128)}), (f32[16,1024]{1,0:T(8,128)}, f32[16,1024]{1,0:T(8,128)}, f32[16,1024]{1,0:T(8,128)}, ...) | async-done | bytes 262160 | tf_op jit(solution)/shard_map/psum | solution.py:86
  698.3 42.0 %all-reduce.6 = (f32[16]{0:T(128)S(1)}, f32[16]{0:T(128)S(1)}) all-reduce(f32[16]{0:T(128)S(1)} %multiply_reduce_fusion.2, f32[16]{0:T(128)S(1)} %multiply_reduce_fusion.3), channel_id=1, replica_groups=mesh['tm'=16,'sec'=2] {'tm'}, use_global_device_ids=true, to_apply=%region_23.24 | all-reduce | flops 32 | bytes 256 | tf_op jit(solution)/shard_map/psum | solution.py:88
  (199 shorter events, 193.9 us)
Async XLA Ops:
  6.5 380.7 %all-reduce.15.cloned.1.call-start = ((), (), s32[]{:S(2)}) async-start(), calls=%async_computation.1 | async-start | bytes 16777216 | tf_op jit(solution)/shard_map/psum | solution.py:22
  124.2 571.9 %all-reduce.13.cloned.1.call-start = ((), (), s32[]{:S(2)}) async-start(), calls=%async_computation | async-start | bytes 524288 | tf_op jit(solution)/shard_map/psum | solution.py:86
  125.3 13.7 %collective-permute-start = (bf16[1024,128]{1,0:T(8,128)(2,1)S(1)}, bf16[1024,128]{1,0:T(8,128)(2,1)S(1)}, u32[]{:S(2)}, u32[]{:S(2)}) collective-permute-start(bf16[1024,128]{1,0:T(8,128)(2,1)S(1)} %slice.81), channel_id=1, source_target_pairs={{2,0},{4,2},{6,4},{8,6},{10,8},{12,10},{14,12},{16,14},{18,16},{20... | collective-permute-start | bytes 786440 | tf_op jit(solution)/shard_map/ppermute | solution.py:17
  423.8 1.7 slice-start
  459.6 1.7 slice-start
  495.4 1.7 slice-start
  531.3 1.7 slice-start
  567.8 1.7 slice-start.1
  603.7 1.7 slice-start.1
  639.5 1.7 slice-start.1
  675.4 1.7 slice-start.1
Sparse Core Ops, SparseCore 0:
  124.4 262.8 all-reduce.14
  678.7 17.4 all-reduce.12
where the time goes:
time: 764 us; the launch traced here: 750 us
  local copies, waits for them, and re-layouts  364 us (48%)
  waiting for transfers between devices  256 us (34%)
  blocking collectives  44.4 us (6%)
  matrix products  37.8 us (5%)
  other arithmetic  31.7 us (4%)
  between operations  14.8 us (2%)
    psum x1, waiting for transfers between devices, spread(): return lax.psum(kept, axis)  233 us
    rev x8, local copies, waits for them, and re-layouts, skew_sum(): flipped = product[:, :, ::-1]  158 us
    gather x96, local copies, waits for them, and re-layouts  99.8 us
    reshape x8, local copies, waits for them, and re-layouts, skew_sum(): widened.reshape(group_count, tap_count * (span_width + 1))  46.4 us
    psum x1, blocking collectives, finish(): power_sum = lax.psum(jnp.sum(normed * normed, axis=1), 'tm')  42 us
    dot_general x8, matrix products, one_block(): jnp.einsum('kcl,cw->klw', block, extended, preferred_element_type=jnp.flo...  34 us
    pad x8, local copies, waits for them, and re-layouts, skew_sum(): widened = jnp.pad(flipped, ((0, 0), (0, 0), (0, 1)))  27.8 us
  transfers between devices with their start and end apart: 3, of which 3 were waited for; matrix products, arithmetic and copies ran while one was open for 3% of the time, Pallas kernels for 0%

commit v1 on v0

v1 whole, which is shorter than its diff:
```python
import jax
import jax.numpy as jnp
from jax import lax
from jax.experimental import pallas as pl
from jax.experimental.pallas import tpu as pltpu
from jax.sharding import PartitionSpec as P

L = 128
GROUP = 4

EPS = 1e-06


def from_behind(value, axis, by):
    length = lax.axis_size(axis)
    pairs = [(i, i + by) for i in range(length) if 0 <= i + by < length]
    return lax.ppermute(value, axis, pairs)


def butterfly_sum(value, axis):
    size = lax.axis_size(axis)
    if size & (size - 1):
        return lax.psum(value, axis)
    step = 1
    while step < size:
        value = value + lax.ppermute(value, axis, [(i, i ^ step) for i in range(size)])
        step *= 2
    return value


def correlate_kernel(tmpl_ref, ext_ref, out_ref):
    width = ext_ref.shape[1]
    lags = out_ref.shape[2]
    group, taps, chans = tmpl_ref.shape
    product = jnp.dot(
        tmpl_ref[...].reshape(group * taps, chans), ext_ref[...], preferred_element_type=jnp.float32
    )
    for g in range(group):
        rows = product[g * taps : (g + 1) * taps]
        sheared = pltpu.roll(rows, width - (taps - 1), 1, stride=1, stride_axis=0)
        out_ref[0, g : g + 1, :] = jnp.sum(sheared, axis=0, keepdims=True)[:, :lags]


def correlate(templates, extended, lag_count):
    count, taps, chans = templates.shape
    width = extended.shape[1]
    steps = count // GROUP
    cost = pl.CostEstimate(
        flops=2 * count * taps * chans * width,
        transcendentals=0,
        bytes_accessed=templates.size * 2 + extended.size * 2 + count * lag_count * 4,
    )
    out = pl.pallas_call(
        correlate_kernel,
        grid=(steps,),
        in_specs=[
            pl.BlockSpec((GROUP, taps, chans), lambda i: (i, 0, 0)),
            pl.BlockSpec((chans, width), lambda i: (0, 0)),
        ],
        out_specs=pl.BlockSpec((1, GROUP, lag_count), lambda i: (i, 0, 0)),
        out_shape=jax.ShapeDtypeStruct((steps, GROUP, lag_count), jnp.float32),
        cost_estimate=cost,
    )(templates, extended)
    return out.reshape(count, lag_count)


def window_sum(values, taps, lag_count):
    span = 1
    while span < taps:
        values = values[:, :-span] + values[:, span:]
        span *= 2
    return values[:, :lag_count]


def shards(signal, round_shard, offsets, chan_range):
    chan_local, lag_count = signal.shape
    rounds, count = offsets.shape
    section = lax.axis_index("sec")
    place = lax.axis_index("tm")
    total_lags = lag_count * lax.axis_size("tm")

    right_rim = from_behind(signal[:, :L], "tm", -1)
    extended = jnp.concatenate([signal, right_rim], axis=1)
    channel = section * chan_local + jnp.arange(chan_local, dtype=jnp.int32)
    lower = chan_range[:, :, 0]
    upper = chan_range[:, :, 1]
    inside = (channel >= lower[:, :, None]) & (channel < upper[:, :, None])

    flipped = jnp.transpose(signal)[::-1]
    own = place == round_shard
    blocks = jnp.where(own[:, None, None], flipped[None], jnp.zeros_like(flipped)[None])
    blocks = lax.psum(blocks, "tm")
    starts = (lag_count - L) - offsets
    rows = [
        lax.dynamic_slice_in_dim(blocks[r], starts[r, k], L, axis=0)
        for r in range(rounds)
        for k in range(count)
    ]
    templates = jnp.stack(rows).reshape(rounds, count, L, chan_local)
    templates = jnp.where(inside[:, :, None, :], templates, jnp.zeros_like(templates))
    templates = templates.reshape(rounds * count, L, chan_local)
    local_power = jnp.sum(jnp.square(templates.astype(jnp.float32)), axis=(1, 2))
    tmpl_power = butterfly_sum(local_power, "sec")

    squares = jnp.square(extended.astype(jnp.float32))
    high = lax.reduce_precision(squares, exponent_bits=8, mantissa_bits=7)
    low = (squares - high).astype(jnp.bfloat16)
    masks = inside.reshape(rounds * count, chan_local).astype(jnp.bfloat16)
    summed = jnp.dot(masks, high.astype(jnp.bfloat16), preferred_element_type=jnp.float32)
    summed = summed + jnp.dot(masks, low, preferred_element_type=jnp.float32)
    energy_local = window_sum(summed, L, lag_count)

    corr_local = correlate(templates, extended, lag_count)
    both = butterfly_sum(jnp.stack([corr_local, energy_local]), "sec")
    corr, energy = both[0], both[1]
    normed = corr / jnp.sqrt(energy * tmpl_power[:, None] + EPS)
    power_sum = butterfly_sum(jnp.sum(normed * normed, axis=1), "tm")
    meansq = power_sum / total_lags
    scored = normed / jnp.sqrt(meansq[:, None] + EPS)
    return scored.reshape(rounds, count, lag_count)


def solution(mesh):
    placed = (P("sec", "tm"), P(), P(), P())
    return jax.shard_map(
        shards, mesh=mesh, in_specs=placed, out_specs=P(None, None, "tm"), check_vma=False
    )
```

time: 764 us -> 304 us (0.40); the launches traced: 750 us -> 299 us
  local copies, waits for them, and re-layouts: 364 us -> 68.7 us
  waiting for transfers between devices: 256 us -> 114 us
  between operations: 14.8 us -> 73.1 us
  blocking collectives: 44.4 us -> 0 us
  matrix products: 37.8 us -> 4.84 us
  Pallas kernels: 0 us -> 16.1 us
  other arithmetic: 31.7 us -> 16 us
    psum x2 -> x1, waiting for transfers between devices: 245 us -> 102 us  [shards(): blocks = lax.psum(blocks, 'tm')]
    rev x16 -> x2, local copies, waits for them, and re-layouts: 164 us -> 36 us  [shards(): flipped = jnp.transpose(signal)[::-1]]
    gather x96 -> x0, local copies, waits for them, and re-layouts: 99.8 us -> none
    reshape x11 -> x0, local copies, waits for them, and re-layouts: 47.7 us -> none  [the longest x8 46.4 us: skew_sum(): widened.reshape(group_count, tap_count * (span_width + 1))]
    psum x2 -> x0, blocking collectives: 44.4 us -> none  [the longest x1 42 us: finish(): power_sum = lax.psum(jnp.sum(normed * normed, axis=1), 'tm')]
    dot_general x10 -> x2, matrix products: 37.8 us -> 4.84 us  [the longest x1 2.55 us: shards(): summed = summed + jnp.dot(masks, low, preferred_element_type=jnp.float32)]
    pad x8 -> x0, local copies, waits for them, and re-layouts: 27.8 us -> none  [skew_sum(): widened = jnp.pad(flipped, ((0, 0), (0, 0), (0, 1)))]
    unnamed x5 -> x40, local copies, waits for them, and re-layouts: 7.33 us -> 25.6 us
  transfers between devices with their start and end apart: 3 -> 8, of which waited for: 3 -> 6; matrix products, arithmetic and copies ran while one was open for 3% -> 3% of each run, Pallas kernels for 0% -> 0%
where the time goes in v1:
time: 304 us; the launch traced here: 299 us
  waiting for transfers between devices  114 us (38%)
  between operations  73.1 us (24%)
  local copies, waits for them, and re-layouts  68.7 us (23%)
  Pallas kernels  16.1 us (5%)
  other arithmetic  16 us (5%)
  starting transfers between devices  6.21 us (2%)
  matrix products  4.84 us (2%)
    psum x1, waiting for transfers between devices, shards(): blocks = lax.psum(blocks, 'tm')  102 us
    rev x2, local copies, waits for them, and re-layouts, shards(): flipped = jnp.transpose(signal)[::-1]  36 us
    unnamed x40, local copies, waits for them, and re-layouts  25.6 us
    pallas_call x1, Pallas kernels, correlate(): pl.pallas_call(correlate_kernel, grid=(steps,), in_specs=[pl.BlockSpec((G...  16.1 us
    ppermute x6, waiting for transfers between devices, butterfly_sum(): lax.ppermute(value, axis, [(i, i ^ step) for i in range(size)])  11.7 us
    reduce_sum x1, other arithmetic, shards(): jnp.sum(jnp.square(templates.astype(jnp.float32)), axis=(1, 2))  10.3 us
  transfers between devices with their start and end apart: 8, of which 6 were waited for; matrix products, arithmetic and copies ran while one was open for 3% of the time, Pallas kernels for 0%

profile of v1, /device:TPU:0, one launch (start us, length us, event | category | flops | bytes accessed | tf_op | source)
XLA Modules:
  0.0 298.8 jit_solution(13131438235637473996)
XLA Ops:
  6.5 31.9 %rev.3 = bf16[1024,1024]{0,1:T(8,128)(2,1)} reverse(bf16[1024,1024]{0,1:T(8,128)(2,1)} %bitcast.51), dimensions={0} | reverse | bytes 4194304 | tf_op jit(solution)/shard_map/rev | solution.py:89
  38.5 4.1 %copy.6 = bf16[1024,1024]{1,0:T(8,128)(2,1)} copy(bf16[1024,1024]{0,1:T(8,128)(2,1)} %rev.3) | data formatting | bytes 4194304 | tf_op jit(solution)/shard_map/rev | solution.py:89
  42.6 3.9 %broadcast_select_fusion.1 = bf16[2,1024,1024]{2,1,0:T(8,128)(2,1)} fusion(pred[2]{0:T(512)(128)(4,1)S(1)} %broadcast_compare_fusion, bf16[1024,1024]{1,0:T(8,128)(2,1)} %copy.6), kind=kLoop, calls=%fused_computation.6 | loop fusion | flops 2097152 | bytes 6291458 | tf_op jit(solution)/shard_map/jit(_where)/select_n | solution.py:91
  46.6 1.3 collective-permute-start
  48.9 1.5 constant_dynamic-update-slice_fusion.1
  111.4 2.6 fusion.2
  113.9 2.3 fusion.4
  117.0 102.1 %all-reduce.2.cloned.1.call-done = bf16[2,1024,1024]{2,1,0:T(8,128)(2,1)} async-done(((bf16[2,1024,1024]{2,1,0:T(8,128)(2,1)}), bf16[2,1024,1024]{2,1,0:T(8,128)(2,1)}) %all-reduce.2.cloned.1.call-update) | async-done | bytes 4194320 | tf_op jit(solution)/shard_map/psum | solution.py:92
  219.2 2.7 fusion.12
  221.8 0.8 dynamic-slice_dynamic-update-slice_fusion.31
  222.6 0.8 dynamic-slice_dynamic-update-slice_fusion.30
  223.4 0.8 dynamic-slice_dynamic-update-slice_fusion.29
  224.2 0.8 dynamic-slice_dynamic-update-slice_fusion.28
  228.8 0.8 dynamic-slice_dynamic-update-slice_fusion.22
  229.6 0.8 dynamic-slice_dynamic-update-slice_fusion.21
  231.2 0.8 dynamic-slice_dynamic-update-slice_fusion.19
  235.0 0.8 dynamic-slice_dynamic-update-slice_fusion.14
  235.8 0.8 dynamic-slice_dynamic-update-slice_fusion.13
  240.5 0.8 dynamic-slice_dynamic-update-slice_fusion.7
  242.8 0.8 dynamic-slice_dynamic-update-slice_fusion.4
  245.9 0.8 dynamic-slice_dynamic-update-slice_fusion
  246.7 10.3 %multiply_reduce_fusion = (f32[32]{0:T(128)S(1)}, bf16[32,128,1024]{2,1,0:T(8,128)(2,1)}) fusion(bf16[32,128,1024]{2,1,0:T(8,128)(2,1)} %dynamic-slice_dynamic-update-slice_fusion, pred[32,1024]{1,0:T(8,128)(4,1)S(1)} %compare_and_fusion), kind=kLoop, calls=%fused_computation | loop fusion | flops 16777184 | bytes 16810112 | tf_op jit(solution)/shard_map/reduce_sum | solution.py:102
  257.0 16.1 %shard_map.46 = f32[8,4,1024]{2,1,0:T(4,128)} custom-call(bf16[32,128,1024]{2,1,0:T(8,128)(2,1)} %get-tuple-element.8.tmpl_ref, bf16[1024,1152]{1,0:T(8,128)(2,1)} %constant_dynamic-update-slice_fusion.ext_ref), custom_call_target="tpu_custom_call" | custom-call | flops 9663676416 | bytes 10878976 | tf_op jit(solution)/shard_map/pallas_call | solution.py:53
  273.1 0.9 stack_reshape.3
  274.6 1.0 collective-permute-done.2
  275.9 1.5 collective-permute-start.3
  277.4 2.1 collective-permute-done.3
  279.5 1.5 collective-permute-start.4
  281.0 2.0 collective-permute-done.4
  283.2 3.4 %collective-permute-done.5 = f32[32]{0:T(128)S(1)} collective-permute-done((f32[32]{0:T(128)S(1)}, f32[32]{0:T(128)S(1)}, u32[]{:S(2)}, u32[]{:S(2)}) %collective-permute-start.5) | collective-permute-done | bytes 160 | tf_op jit(solution)/shard_map/ppermute | solution.py:26
  286.6 1.2 collective-permute-start.6
  287.9 3.2 %collective-permute-done.6 = f32[32]{0:T(128)S(1)} collective-permute-done((f32[32]{0:T(128)S(1)}, f32[32]{0:T(128)S(1)}, u32[]{:S(2)}, u32[]{:S(2)}) %collective-permute-start.6) | collective-permute-done | bytes 160 | tf_op jit(solution)/shard_map/ppermute | solution.py:26
  (66 shorter events, 20.5 us)
Async XLA Ops:
  6.5 36.0 %copy-start.3 = (s32[2]{0:T(128)S(1)}, s32[2]{0:T(128)}, u32[]{:S(2)}) copy-start(s32[2]{0:T(128)} %param.5) | copy-start | bytes 28
  6.5 212.6 %all-reduce.2.cloned.1.call-start = ((), (), s32[]{:S(2)}) async-start(), calls=%async_computation | async-start | bytes 8388608 | tf_op jit(solution)/shard_map/psum | solution.py:92
  38.5 8.0 %copy-start = (bf16[1024,1024]{1,0:T(8,128)(2,1)S(1)}, bf16[1024,1024]{1,0:T(8,128)(2,1)}, u32[]{:S(2)}) copy-start(bf16[1024,1024]{1,0:T(8,128)(2,1)} %param.4) | copy-start | bytes 6291460
  38.5 9.4 %copy-start.2 = (s32[2,16]{1,0:T(2,128)S(1)}, s32[2,16]{1,0:T(2,128)}, u32[]{:S(2)}) copy-start(s32[2,16]{1,0:T(2,128)} %param.6) | copy-start | bytes 388
  38.5 10.2 %copy-start.1 = (s32[2,16,2]{1,2,0:T(2,128)S(1)}, s32[2,16,2]{1,2,0:T(2,128)}, u32[]{:S(2)}) copy-start(s32[2,16,2]{1,2,0:T(2,128)} %param.7) | copy-start | bytes 772
  46.6 64.1 %collective-permute-start = (bf16[1024,128]{1,0:T(8,128)(2,1)S(1)}, bf16[1024,128]{1,0:T(8,128)(2,1)S(1)}, u32[]{:S(2)}, u32[]{:S(2)}) collective-permute-start(bf16[1024,128]{1,0:T(8,128)(2,1)S(1)} %slice.228), channel_id=1, source_target_pairs={{2,0},{4,2},{6,4},{8,6},{10,8},{12,10},{14,12},{16,14},{18,16},{20... | collective-permute-start | bytes 786440 | tf_op jit(solution)/shard_map/ppermute | solution.py:17
  274.1 1.6 collective-permute-start.1
  274.1 1.5 collective-permute-start.2
  275.9 3.6 %collective-permute-start.3 = (f32[32]{0:T(128)S(1)}, f32[32]{0:T(128)S(1)}, u32[]{:S(2)}, u32[]{:S(2)}) collective-permute-start(f32[32]{0:T(128)S(1)} %fusion.10), channel_id=1, source_target_pairs={{0,2},{2,0},{4,6},{6,4},{8,10},{10,8},{12,14},{14,12},{16,18},{18,... | collective-permute-start | bytes 392 | tf_op jit(solution)/shard_map/ppermute | solution.py:26
  279.5 3.5 %collective-permute-start.4 = (f32[32]{0:T(128)S(1)}, f32[32]{0:T(128)S(1)}, u32[]{:S(2)}, u32[]{:S(2)}) collective-permute-start(f32[32]{0:T(128)S(1)} %add.216), channel_id=1, source_target_pairs={{0,4},{2,6},{4,0},{6,2},{8,12},{10,14},{12,8},{14,10},{16,20},{18,... | collective-permute-start | bytes 392 | tf_op jit(solution)/shard_map/ppermute | solution.py:26
  283.1 3.5 %collective-permute-start.5 = (f32[32]{0:T(128)S(1)}, f32[32]{0:T(128)S(1)}, u32[]{:S(2)}, u32[]{:S(2)}) collective-permute-start(f32[32]{0:T(128)S(1)} %add.217), channel_id=1, source_target_pairs={{0,8},{2,10},{4,12},{6,14},{8,0},{10,2},{12,4},{14,6},{16,24},{18,... | collective-permute-start | bytes 392 | tf_op jit(solution)/shard_map/ppermute | solution.py:26
  286.6 4.4 %collective-permute-start.6 = (f32[32]{0:T(128)S(1)}, f32[32]{0:T(128)S(1)}, u32[]{:S(2)}, u32[]{:S(2)}) collective-permute-start(f32[32]{0:T(128)S(1)} %add.218), channel_id=1, source_target_pairs={{0,16},{2,18},{4,20},{6,22},{8,24},{10,26},{12,28},{14,30},{16,0},... | collective-permute-start | bytes 392 | tf_op jit(solution)/shard_map/ppermute | solution.py:26
Sparse Core Ops, SparseCore 0:
  46.6 172.5 all-reduce.1

commit v2 on v1

v2 whole, which is shorter than its diff:
```python
import jax
import jax.numpy as jnp
from jax import lax
from jax.experimental import pallas as pl
from jax.experimental.pallas import tpu as pltpu
from jax.sharding import PartitionSpec as P

L = 128
GROUP = 4
REACH = L + 16

EPS = 1e-06


def from_behind(value, axis, by):
    length = lax.axis_size(axis)
    pairs = [(i, i + by) for i in range(length) if 0 <= i + by < length]
    return lax.ppermute(value, axis, pairs)


def group_sum(value, axis):
    size = lax.axis_size(axis)
    place = lax.axis_index(axis)
    stride = 1
    while stride < size:
        fan = 4 if size % (stride * 4) == 0 else 2 if size % (stride * 2) == 0 else 0
        if fan == 0:
            return lax.psum(value, axis)
        member = (place // stride) % fan
        got = {0: value}
        for d in range(1, fan):
            pairs = [(i, i ^ (d * stride)) for i in range(size)]
            got[d] = lax.ppermute(value, axis, pairs)
        total = None
        for m in range(fan):
            part = got[0]
            for d in range(1, fan):
                part = jnp.where((member ^ d) == m, got[d], part)
            total = part if total is None else total + part
        value = total
        stride *= fan
    return value


def correlate_kernel(meta_ref, blk_ref, ext_ref, corr_ref, power_ref):
    step = pl.program_id(0)
    chans = blk_ref.shape[2]
    width = ext_ref.shape[1]
    group = corr_ref.shape[1]
    lags = corr_ref.shape[2]
    tap = lax.broadcasted_iota(jnp.int32, (L, REACH), 0)
    col = lax.broadcasted_iota(jnp.int32, (L, REACH), 1)
    lane = lax.broadcasted_iota(jnp.int32, (L, chans), 1)
    pieces = []
    for g in range(group):
        idx = step * group + g
        first = meta_ref[4 * idx]
        shift = meta_ref[4 * idx + 1]
        lower = meta_ref[4 * idx + 2]
        upper = meta_ref[4 * idx + 3]
        rows = blk_ref[0, pl.ds(pl.multiple_of(first, 16), REACH), :]
        pick = (col == shift + (L - 1) - tap).astype(jnp.bfloat16)
        chosen = jnp.dot(pick, rows, preferred_element_type=jnp.float32)
        chosen = jnp.where((lane >= lower) & (lane < upper), chosen, 0.0)
        power_ref[0, g : g + 1, :] = jnp.full((1, 128), jnp.sum(chosen * chosen), jnp.float32)
        pieces.append(chosen.astype(jnp.bfloat16))
    product = jnp.dot(
        jnp.concatenate(pieces, axis=0), ext_ref[...], preferred_element_type=jnp.float32
    )
    for g in range(group):
        rows = product[g * L : (g + 1) * L]
        sheared = pltpu.roll(rows, width - (L - 1), 1, stride=1, stride_axis=0)
        corr_ref[0, g : g + 1, :] = jnp.sum(sheared, axis=0, keepdims=True)[:, :lags]


def correlate(meta, blocks, extended, count):
    rounds, span, chans = blocks.shape
    width = extended.shape[1]
    lag_count = span
    steps = rounds * count // GROUP
    per_round = count // GROUP
    cost = pl.CostEstimate(
        flops=2 * rounds * count * L * (chans * width + REACH * chans),
        transcendentals=0,
        bytes_accessed=blocks.size * 2 + extended.size * 2 + rounds * count * lag_count * 4,
    )
    grid_spec = pltpu.PrefetchScalarGridSpec(
        num_scalar_prefetch=1,
        grid=(steps,),
        in_specs=[
            pl.BlockSpec((1, span, chans), lambda i, m: (i // per_round, 0, 0)),
            pl.BlockSpec((chans, width), lambda i, m: (0, 0)),
        ],
        out_specs=[
            pl.BlockSpec((1, GROUP, lag_count), lambda i, m: (i, 0, 0)),
            pl.BlockSpec((1, GROUP, 128), lambda i, m: (i, 0, 0)),
        ],
    )
    corr, power = pl.pallas_call(
        correlate_kernel,
        grid_spec=grid_spec,
        out_shape=[
            jax.ShapeDtypeStruct((steps, GROUP, lag_count), jnp.float32),
            jax.ShapeDtypeStruct((steps, GROUP, 128), jnp.float32),
        ],
        cost_estimate=cost,
    )(meta, blocks, extended)
    return corr.reshape(rounds * count, lag_count), power[:, :, 0].reshape(rounds * count)


def window_sum(values, taps, lag_count):
    span = 1
    while span < taps:
        values = values[:, :-span] + values[:, span:]
        span *= 2
    return values[:, :lag_count]


def shards(signal, round_shard, offsets, chan_range):
    chan_local, lag_count = signal.shape
    rounds, count = offsets.shape
    section = lax.axis_index("sec")
    place = lax.axis_index("tm")
    total_lags = lag_count * lax.axis_size("tm")

    right_rim = from_behind(signal[:, :L], "tm", -1)
    extended = jnp.concatenate([signal, right_rim], axis=1)
    channel = section * chan_local + jnp.arange(chan_local, dtype=jnp.int32)
    lower = chan_range[:, :, 0]
    upper = chan_range[:, :, 1]
    inside = (channel >= lower[:, :, None]) & (channel < upper[:, :, None])

    flipped = jnp.transpose(signal)
    own = place == round_shard
    blocks = jnp.where(own[:, None, None], flipped[None], jnp.zeros_like(flipped)[None])
    blocks = lax.psum(blocks, "tm")
    offs = jnp.clip(offsets, 0, lag_count - L)
    first = jnp.minimum((offs // 16) * 16, lag_count - REACH)
    base = section * chan_local
    meta = jnp.stack([first, offs - first, lower - base, upper - base], axis=-1).reshape(-1)

    squares = jnp.square(extended.astype(jnp.float32))
    high = lax.reduce_precision(squares, exponent_bits=8, mantissa_bits=7)
    low = (squares - high).astype(jnp.bfloat16)
    masks = inside.reshape(rounds * count, chan_local).astype(jnp.bfloat16)
    summed = jnp.dot(masks, high.astype(jnp.bfloat16), preferred_element_type=jnp.float32)
    summed = summed + jnp.dot(masks, low, preferred_element_type=jnp.float32)
    energy_local = window_sum(summed, L, lag_count)

    corr_local, local_power = correlate(meta.astype(jnp.int32), blocks, extended, count)
    tmpl_power = group_sum(local_power, "sec")
    both = group_sum(jnp.stack([corr_local, energy_local]), "sec")
    corr, energy = both[0], both[1]
    normed = corr / jnp.sqrt(energy * tmpl_power[:, None] + EPS)
    power_sum = group_sum(jnp.sum(normed * normed, axis=1), "tm")
    meansq = power_sum / total_lags
    scored = normed / jnp.sqrt(meansq[:, None] + EPS)
    return scored.reshape(rounds, count, lag_count)


def solution(mesh):
    placed = (P("sec", "tm"), P(), P(), P())
    return jax.shard_map(
        shards, mesh=mesh, in_specs=placed, out_specs=P(None, None, "tm"), check_vma=False
    )
```

time: 304 us -> 230 us (0.76); the launches traced: 299 us -> 230 us
  between operations: 73.1 us -> 13.6 us
  local copies, waits for them, and re-layouts: 68.7 us -> 9.76 us
  waiting for transfers between devices: 114 us -> 169 us
  other arithmetic: 16 us -> 4.03 us
  Pallas kernels: 16.1 us -> 19.9 us
  starting transfers between devices: 6.21 us -> 9.87 us
    psum x1, waiting for transfers between devices: 102 us -> 154 us  [shards(): blocks = lax.psum(blocks, 'tm')]
    rev x2 -> x0, local copies, waits for them, and re-layouts: 36 us -> none  [shards(): flipped = jnp.transpose(signal)[::-1]]
    unnamed x40 -> x11, local copies, waits for them, and re-layouts: 25.6 us -> 3.08 us
    reduce_sum x2 -> x1, other arithmetic: 10.5 us -> 0.2 us  [shards(): power_sum = group_sum(jnp.sum(normed * normed, axis=1), 'tm')]
    ppermute x1, waiting for transfers between devices: 0.01 us -> 9.48 us  [from_behind(): return lax.ppermute(value, axis, pairs)]
    ppermute x6 -> x8, waiting for transfers between devices: 11.7 us -> 5.3 us  [group_sum(): got[d] = lax.ppermute(value, axis, pairs)]
    pallas_call x1, Pallas kernels: 16.1 us -> 19.9 us  [correlate(): pl.pallas_call(correlate_kernel, grid_spec=grid_spec, out_shape=[jax.Shap...]
    ppermute x6 -> x8, starting transfers between devices: 4.91 us -> 8.58 us  [group_sum(): got[d] = lax.ppermute(value, axis, pairs)]
  transfers between devices with their start and end apart: 8 -> 10, of which waited for: 6 -> 9; matrix products, arithmetic and copies ran while one was open for 3% -> 4% of each run, Pallas kernels for 0% -> 0%
where the time goes in v2:
time: 230 us
  waiting for transfers between devices  169 us (73%)
  Pallas kernels  19.9 us (9%)
  between operations  13.6 us (6%)
  starting transfers between devices  9.87 us (4%)
  local copies, waits for them, and re-layouts  9.76 us (4%)
  other arithmetic  4.03 us (2%)
  matrix products  3.29 us (1%)
    psum x1, waiting for transfers between devices, shards(): blocks = lax.psum(blocks, 'tm')  154 us
    pallas_call x1, Pallas kernels, correlate(): pl.pallas_call(correlate_kernel, grid_spec=grid_spec, out_shape=[jax.Shap...  19.9 us
    ppermute x1, waiting for transfers between devices, from_behind(): return lax.ppermute(value, axis, pairs)  9.48 us
    ppermute x8, starting transfers between devices, group_sum(): got[d] = lax.ppermute(value, axis, pairs)  8.58 us
    ppermute x8, waiting for transfers between devices, group_sum(): got[d] = lax.ppermute(value, axis, pairs)  5.3 us
  transfers between devices with their start and end apart: 10, of which 9 were waited for; matrix products, arithmetic and copies ran while one was open for 4% of the time, Pallas kernels for 0%

profile of v2, /device:TPU:0, one launch (start us, length us, event | category | flops | bytes accessed | tf_op | source)
XLA Modules:
  0.0 229.7 jit_solution(16840110183470927899)
XLA Ops:
  6.5 2.9 %copy.12 = bf16[1024,1024]{1,0:T(8,128)(2,1)S(1)} copy(bf16[1024,1024]{0,1:T(8,128)(2,1)} %bitcast.28) | data formatting | bytes 4194304 | tf_op jit(solution)/shard_map/transpose | solution.py:133
  9.4 2.3 %broadcast_select_fusion = bf16[2,1024,1024]{2,1,0:T(8,128)(2,1)} fusion(pred[2]{0:T(512)(128)(4,1)S(1)} %broadcast_compare_fusion, bf16[1024,1024]{1,0:T(8,128)(2,1)S(1)} %copy.12), kind=kLoop, calls=%fused_computation.4 | loop fusion | flops 2097152 | bytes 6291458 | tf_op jit(solution)/shard_map/jit(_where)/select_n | solution.py:135
  11.8 1.6 copy-done
  13.4 1.3 collective-permute-start
  14.8 1.5 constant_dynamic-update-slice_fusion.1
  16.6 0.6 reshape.31.meta_ref
  17.2 9.5 %collective-permute-done = bf16[1024,128]{1,0:T(8,128)(2,1)S(1)} collective-permute-done((bf16[1024,128]{1,0:T(8,128)(2,1)S(1)}, bf16[1024,128]{1,0:T(8,128)(2,1)S(1)}, u32[]{:S(2)}, u32[]{:S(2)}) %collective-permute-start) | collective-permute-done | bytes 262176 | tf_op jit(solution)/shard_map/ppermute | solution.py:18
  26.7 0.8 constant_dynamic-update-slice_fusion.ext_ref
  27.4 2.7 %fusion.2 = f32[32,1152]{1,0:T(8,128)S(1)} fusion(bf16[1024,1152]{1,0:T(8,128)(2,1)} %constant_dynamic-update-slice_fusion.ext_ref, s32[1024]{0:T(1024)S(1)} %iota_add_fusion, s32[32]{0:T(128)S(1)} %lt.31, s32[32]{0:T(128)S(1)} %ge.17), kind=kOutput, calls=%fused_computation.6 | convolution fusion | flops 81494016 | bytes 2511104 | tf_op jit(solution)/shard_map/dot_general | solution.py:147
  30.1 0.6 fusion.4
  30.7 0.1 slice_add_fusion.5
  30.8 0.1 slice_add_fusion.4
  31.0 0.1 slice_add_fusion.3
  31.5 154.5 %all-reduce.2.cloned.1.call-done.blk_ref = bf16[2,1024,1024]{2,1,0:T(8,128)(2,1)} async-done(((bf16[2,1024,1024]{2,1,0:T(8,128)(2,1)}), bf16[2,1024,1024]{2,1,0:T(8,128)(2,1)}) %all-reduce.2.cloned.1.call-update) | async-done | bytes 4194320 | tf_op jit(solution)/shard_map/psum | solution.py:136
  186.0 19.9 %shard_map.46 = (f32[8,4,1024]{2,1,0:T(4,128)}, f32[8,4,128]{2,1,0:T(4,128)}) custom-call(s32[128]{0:T(128)} %reshape.31.meta_ref, bf16[2,1024,1024]{2,1,0:T(8,128)(2,1)} %all-reduce.2.cloned.1.call-done.blk_ref, bf16[1024,1152]{1,0:T(8,128)(2,1)} %constant_dynamic-update-slice_fusion.ext_ref), custom_call_target="tpu_custom_call" | custom-call | flops 10871635968 | bytes 6684672 | tf_op jit(solution)/shard_map/pallas_call | solution.py:99
  205.9 0.9 stack_reshape.3
  206.9 0.8 slice_reduce_fusion
  207.8 0.5 collective-permute-start.2
  208.3 0.8 collective-permute-done.2
  209.3 0.2 fusion.10
  209.5 2.5 %collective-permute-start.3 = (f32[32]{0:T(128)S(1)}, f32[32]{0:T(128)S(1)}, u32[]{:S(2)}, u32[]{:S(2)}) collective-permute-start(f32[32]{0:T(128)S(1)} %fusion.10), channel_id=1, source_target_pairs={{0,6},{2,4},{4,2},{6,0},{8,14},{10,12},{12,10},{14,8},{16,22},{18,... | collective-permute-start | bytes 392 | tf_op jit(solution)/shard_map/ppermute | solution.py:33
  212.0 0.5 collective-permute-start.4
  212.5 0.6 collective-permute-start.5
  213.1 0.9 collective-permute-done.3
  214.0 1.5 collective-permute-done.4
  215.5 0.5 collective-permute-done.5
  216.0 1.4 collective-permute-start.6
  217.5 0.2 collective-permute-start.7
  217.6 2.8 %collective-permute-start.8 = (f32[32]{0:T(128)S(1)}, f32[32]{0:T(128)S(1)}, u32[]{:S(2)}, u32[]{:S(2)}) collective-permute-start(f32[32]{0:T(128)S(1)} %fusion.23), channel_id=1, source_target_pairs={{0,8},{2,10},{4,12},{6,14},{8,0},{10,2},{12,4},{14,6},{16,24},{18,... | collective-permute-start | bytes 392 | tf_op jit(solution)/shard_map/ppermute | solution.py:33
  220.5 0.9 collective-permute-done.6
  221.4 0.5 collective-permute-done.7
  222.1 0.8 multiply_divide_fusion
  (38 shorter events, 1.3 us)
Async XLA Ops:
  6.5 2.9 %copy-start.4 = (s32[2]{0:T(128)S(1)}, s32[2]{0:T(128)}, u32[]{:S(2)}) copy-start(s32[2]{0:T(128)} %param.5) | copy-start | bytes 28
  6.5 179.5 %all-reduce.2.cloned.1.call-start = ((), (), s32[]{:S(2)}) async-start(), calls=%async_computation | async-start | bytes 8388608 | tf_op jit(solution)/shard_map/psum | solution.py:136
  11.7 1.6 copy-start
  11.7 3.0 %copy-start.2 = (s32[2,16,2]{1,2,0:T(2,128)S(1)}, s32[2,16,2]{1,2,0:T(2,128)}, u32[]{:S(2)}) copy-start(s32[2,16,2]{1,2,0:T(2,128)} %param.7) | copy-start | bytes 772
  11.8 3.0 %copy-start.3 = (s32[2,16]{1,0:T(2,128)S(1)}, s32[2,16]{1,0:T(2,128)}, u32[]{:S(2)}) copy-start(s32[2,16]{1,0:T(2,128)} %param.6) | copy-start | bytes 388
  13.4 13.2 %collective-permute-start = (bf16[1024,128]{1,0:T(8,128)(2,1)S(1)}, bf16[1024,128]{1,0:T(8,128)(2,1)S(1)}, u32[]{:S(2)}, u32[]{:S(2)}) collective-permute-start(bf16[1024,128]{1,0:T(8,128)(2,1)S(1)} %slice.65), channel_id=1, source_target_pairs={{2,0},{4,2},{6,4},{8,6},{10,8},{12,10},{14,12},{16,14},{18,16},{20... | collective-permute-start | bytes 786440 | tf_op jit(solution)/shard_map/ppermute | solution.py:18
  27.4 2.7 %copy-start.1 = (bf16[1024,1152]{1,0:T(8,128)(2,1)S(1)}, bf16[1024,1152]{1,0:T(8,128)(2,1)}, u32[]{:S(2)}) copy-start(bf16[1024,1152]{1,0:T(8,128)(2,1)} %constant_dynamic-update-slice_fusion.ext_ref) | copy-start | bytes 7077892
  206.9 2.4 %collective-permute-start.1 = (f32[2,32,1024]{2,1,0:T(8,128)S(1)}, f32[2,32,1024]{2,1,0:T(8,128)S(1)}, u32[]{:S(2)}, u32[]{:S(2)}) collective-permute-start(f32[2,32,1024]{2,1,0:T(8,128)S(1)} %pad_maximum_fusion), channel_id=1, source_target_pairs={{0,1},{1,0},{2,3},{3,2},{4,5},{5,4},{6,7},{7,6},{8,9},{9,8},{10,11... | collective-permute-start | bytes 786440 | tf_op jit(solution)/shard_map/ppermute | solution.py:33
  207.8 1.3 collective-permute-start.2
  209.5 4.5 %collective-permute-start.3 = (f32[32]{0:T(128)S(1)}, f32[32]{0:T(128)S(1)}, u32[]{:S(2)}, u32[]{:S(2)}) collective-permute-start(f32[32]{0:T(128)S(1)} %fusion.10), channel_id=1, source_target_pairs={{0,6},{2,4},{4,2},{6,0},{8,14},{10,12},{12,10},{14,8},{16,22},{18,... | collective-permute-start | bytes 392 | tf_op jit(solution)/shard_map/ppermute | solution.py:33
  212.0 3.5 %collective-permute-start.4 = (f32[32]{0:T(128)S(1)}, f32[32]{0:T(128)S(1)}, u32[]{:S(2)}, u32[]{:S(2)}) collective-permute-start(f32[32]{0:T(128)S(1)} %fusion.10), channel_id=1, source_target_pairs={{0,4},{2,6},{4,0},{6,2},{8,12},{10,14},{12,8},{14,10},{16,20},{18,... | collective-permute-start | bytes 392 | tf_op jit(solution)/shard_map/ppermute | solution.py:33
  212.5 3.5 %collective-permute-start.5 = (f32[32]{0:T(128)S(1)}, f32[32]{0:T(128)S(1)}, u32[]{:S(2)}, u32[]{:S(2)}) collective-permute-start(f32[32]{0:T(128)S(1)} %fusion.10), channel_id=1, source_target_pairs={{0,2},{2,0},{4,6},{6,4},{8,10},{10,8},{12,14},{14,12},{16,18},{18,... | collective-permute-start | bytes 392 | tf_op jit(solution)/shard_map/ppermute | solution.py:33
  216.0 5.4 %collective-permute-start.6 = (f32[32]{0:T(128)S(1)}, f32[32]{0:T(128)S(1)}, u32[]{:S(2)}, u32[]{:S(2)}) collective-permute-start(f32[32]{0:T(128)S(1)} %fusion.23), channel_id=1, source_target_pairs={{0,24},{2,26},{4,28},{6,30},{8,16},{10,18},{12,20},{14,22},{16,8},... | collective-permute-start | bytes 392 | tf_op jit(solution)/shard_map/ppermute | solution.py:33
  217.5 4.4 %collective-permute-start.7 = (f32[32]{0:T(128)S(1)}, f32[32]{0:T(128)S(1)}, u32[]{:S(2)}, u32[]{:S(2)}) collective-permute-start(f32[32]{0:T(128)S(1)} %fusion.23), channel_id=1, source_target_pairs={{0,16},{2,18},{4,20},{6,22},{8,24},{10,26},{12,28},{14,30},{16,0},... | collective-permute-start | bytes 392 | tf_op jit(solution)/shard_map/ppermute | solution.py:33
  217.6 4.4 %collective-permute-start.8 = (f32[32]{0:T(128)S(1)}, f32[32]{0:T(128)S(1)}, u32[]{:S(2)}, u32[]{:S(2)}) collective-permute-start(f32[32]{0:T(128)S(1)} %fusion.23), channel_id=1, source_target_pairs={{0,8},{2,10},{4,12},{6,14},{8,0},{10,2},{12,4},{14,6},{16,24},{18,... | collective-permute-start | bytes 392 | tf_op jit(solution)/shard_map/ppermute | solution.py:33
Sparse Core Ops, SparseCore 0:
  13.0 172.9 all-reduce.1

commit v3 on v2

--- a/solution.py
+++ b/solution.py
@@ -40,6 +40,61 @@
         value = total
         stride *= fan
     return value
+
+
+def spread_blocks(block, roots, axis):
+    size = lax.axis_size(axis)
+    place = lax.axis_index(axis)
+    nbits = size.bit_length() - 1
+    rounds = roots.shape[0]
+    rows, chans = block.shape
+    parts = next(p for p in (4, 2, 1) if rows % (p * size) == 0)
+    if size & (size - 1) or rows % (parts * size) or nbits == 0:
+        own = place == roots
+        masked = jnp.where(own[:, None, None], block[None], jnp.zeros_like(block)[None])
+        return lax.psum(masked, axis)
+    piece = rows // (parts * size)
+    orders = [[1 << ((p + s) % nbits) for s in range(nbits)] for p in range(parts)]
+    bufs = {}
+    for p in range(parts):
+        seg = block[p * piece * size : (p + 1) * piece * size].reshape([2] * nbits + [piece, chans])
+        perm = [nbits - 1 - (m.bit_length() - 1) for m in orders[p]] + [nbits, nbits + 1]
+        seg = jnp.transpose(seg, perm)
+        for r in range(rounds):
+            bufs[p, r] = seg
+    for s in range(nbits):
+        sends, keeps = {}, {}
+        for (p, r), buf in bufs.items():
+            mask = orders[p][s]
+            bit = (place // mask) % 2
+            keeps[p, r] = jnp.where(bit == 1, buf[1], buf[0])
+            sends.setdefault(mask, []).append(((p, r), jnp.where(bit == 1, buf[0], buf[1])))
+        for mask, items in sends.items():
+            got = lax.ppermute(jnp.stack([v for _, v in items]), axis, [(i, i ^ mask) for i in range(size)])
+            for n, (key, _) in enumerate(items):
+                held = sum(orders[key[0]][:s])
+                holder = ((place ^ roots[key[1]]) & (size - 1 - held)) == 0
+                bufs[key] = jnp.where(holder, keeps[key], got[n])
+    for s in reversed(range(nbits)):
+        sends = {}
+        for (p, r), buf in bufs.items():
+            sends.setdefault(orders[p][s], []).append(((p, r), buf))
+        for mask, items in sends.items():
+            got = lax.ppermute(jnp.stack([v for _, v in items]), axis, [(i, i ^ mask) for i in range(size)])
+            bit = (place // mask) % 2
+            for n, (key, buf) in enumerate(items):
+                low = jnp.where(bit == 1, got[n], buf)
+                high = jnp.where(bit == 1, buf, got[n])
+                bufs[key] = jnp.stack([low, high])
+    out = []
+    for r in range(rounds):
+        segs = []
+        for p in range(parts):
+            perm = [nbits - 1 - (m.bit_length() - 1) for m in orders[p]]
+            inverse = [perm.index(k) for k in range(nbits)] + [nbits, nbits + 1]
+            segs.append(jnp.transpose(bufs[p, r], inverse).reshape(piece * size, chans))
+        out.append(jnp.concatenate(segs, axis=0))
+    return jnp.stack(out)
 
 
 def correlate_kernel(meta_ref, blk_ref, ext_ref, corr_ref, power_ref):
@@ -130,10 +185,7 @@
     upper = chan_range[:, :, 1]
     inside = (channel >= lower[:, :, None]) & (channel < upper[:, :, None])
 
-    flipped = jnp.transpose(signal)
-    own = place == round_shard
-    blocks = jnp.where(own[:, None, None], flipped[None], jnp.zeros_like(flipped)[None])
-    blocks = lax.psum(blocks, "tm")
+    blocks = spread_blocks(jnp.transpose(signal), round_shard, "tm")
     offs = jnp.clip(offsets, 0, lag_count - L)
     first = jnp.minimum((offs // 16) * 16, lag_count - REACH)
     base = section * chan_local

time: 230 us -> 174 us (0.76)
  waiting for transfers between devices: 169 us -> 51.1 us
  starting transfers between devices: 9.87 us -> 69.5 us
  other arithmetic: 4.03 us -> 16.8 us
  between operations: 13.6 us -> 2.7 us
  local copies, waits for them, and re-layouts: 9.76 us -> 12.4 us
    psum x1 -> x0, waiting for transfers between devices: 154 us -> none  [shards(): blocks = lax.psum(blocks, 'tm')]
    ppermute x0 -> x32, starting transfers between devices: none -> 59.7 us  [spread_blocks(): lax.ppermute(jnp.stack([v for _, v in items]), axis, [(i, i ^ mask) for i...]
    ppermute x0 -> x32, waiting for transfers between devices: none -> 41.1 us  [spread_blocks(): lax.ppermute(jnp.stack([v for _, v in items]), axis, [(i, i ^ mask) for i...]
    another operation x0 -> x59, other arithmetic: none -> 7.16 us  [the longest x56 4.42 us: spread_blocks(): jnp.stack([v for _, v in items])]
    ppermute x1, waiting for transfers between devices: 9.48 us -> 4.74 us  [from_behind(): return lax.ppermute(value, axis, pairs)]
    select_n x1 -> x57, other arithmetic: 2.31 us -> 6.7 us  [the longest x18 5.7 us: spread_blocks(): bufs[key] = jnp.where(holder, keeps[key], got[n])]
    transpose x1 -> x8, local copies, waits for them, and re-layouts: 2.86 us -> 0.29 us  [spread_blocks(): segs.append(jnp.transpose(bufs[p, r], inverse).reshape(piece * size, chans))]
  transfers between devices with their start and end apart: 10 -> 41, of which waited for: 9 -> 17; matrix products, arithmetic and copies ran while one was open for 4% -> 11% of each run, Pallas kernels for 0% -> 0%
where the time goes in v3:
time: 174 us
  starting transfers between devices  69.5 us (40%)
  waiting for transfers between devices  51.1 us (29%)
  Pallas kernels  19.9 us (11%)
  other arithmetic  16.8 us (10%)
  local copies, waits for them, and re-layouts  12.4 us (7%)
  between operations  2.7 us (2%)
    ppermute x32, starting transfers between devices, spread_blocks(): lax.ppermute(jnp.stack([v for _, v in items]), axis, [(i, i ^ mask) for i...  59.7 us
    ppermute x32, waiting for transfers between devices, spread_blocks(): lax.ppermute(jnp.stack([v for _, v in items]), axis, [(i, i ^ mask) for i...  41.1 us
    pallas_call x1, Pallas kernels, correlate(): pl.pallas_call(correlate_kernel, grid_spec=grid_spec, out_shape=[jax.Shap...  19.9 us
    ppermute x8, starting transfers between devices, group_sum(): got[d] = lax.ppermute(value, axis, pairs)  8.58 us
    select_n x18, other arithmetic, spread_blocks(): bufs[key] = jnp.where(holder, keeps[key], got[n])  5.7 us
    ppermute x8, waiting for transfers between devices, group_sum(): got[d] = lax.ppermute(value, axis, pairs)  5.21 us
    ppermute x1, waiting for transfers between devices, from_behind(): return lax.ppermute(value, axis, pairs)  4.74 us
    unnamed x18, local copies, waits for them, and re-layouts  4.51 us
  transfers between devices with their start and end apart: 41, of which 17 were waited for; matrix products, arithmetic and copies ran while one was open for 11% of the time, Pallas kernels for 0%

profile of v3, /device:TPU:0, one launch (start us, length us, event | category | flops | bytes accessed | tf_op | source)
XLA Modules:
  0.0 173.8 jit_solution(8385770415915288004)
XLA Ops:
  0.0 2.9 %copy.37 = bf16[1024,1024]{0,1:T(8,128)(2,1)S(1)} copy(bf16[1024,1024]{1,0:T(8,128)(2,1)} %param.4) | data formatting | bytes 4194304 | tf_op args[0]
  5.5 2.9 %collective-permute-start = (bf16[2,2,2,2,16,1024]{5,4,0,1,2,3:T(8,128)(2,1)}, bf16[2,2,2,2,16,1024]{5,4,0,1,2,3:T(8,128)(2,1)}, u32[]{:S(2)}, u32[]{:S(2)}) collective-permute-start(bf16[2,2,2,2,16,1024]{5,4,0,1,2,3:T(8,128)(2,1)} %pad_maximum_fusion.1), channel_id=1, source_target_pairs={{0,2},{2,0},{4,6},{6,4},{8,10},{10,8},{12,14},{14,12},{16,18},{18,... | collective-permute-start | bytes 1572872 | tf_op jit(solution)/shard_map/ppermute | solution.py:73
  9.3 1.5 collective-permute-start.8
  11.8 1.6 collective-permute-start.16
  16.2 2.6 %collective-permute-start.24 = (bf16[2,2,2,2,16,1024]{5,4,3,2,1,0:T(8,128)(2,1)}, bf16[2,2,2,2,16,1024]{5,4,3,2,1,0:T(8,128)(2,1)}, u32[]{:S(2)}, u32[]{:S(2)}) collective-permute-start(bf16[2,2,2,2,16,1024]{5,4,3,2,1,0:T(8,128)(2,1)} %pad_maximum_fusion.7), channel_id=1, source_target_pairs={{0,16},{2,18},{4,20},{6,22},{8,24},{10,26},{12,28},{14,30},{16,0},... | collective-permute-start | bytes 1572872 | tf_op jit(solution)/shard_map/ppermute | solution.py:73
  19.6 1.3 collective-permute-start.32
  23.9 4.7 %collective-permute-done.32 = bf16[1024,128]{1,0:T(8,128)(2,1)} collective-permute-done((bf16[1024,128]{1,0:T(8,128)(2,1)}, bf16[1024,128]{1,0:T(8,128)(2,1)}, u32[]{:S(2)}, u32[]{:S(2)}) %collective-permute-start.32) | collective-permute-done | bytes 262176 | tf_op jit(solution)/shard_map/ppermute | solution.py:18
  32.7 1.1 copy_select_fusion
  36.6 11.0 %collective-permute-start.9 = (bf16[2,2,2,16,1024]{4,3,2,1,0:T(8,128)(2,1)S(1)}, bf16[2,2,2,16,1024]{4,3,2,1,0:T(8,128)(2,1)S(1)}, u32[]{:S(2)}, u32[]{:S(2)}) collective-permute-start(bf16[2,2,2,16,1024]{4,3,2,1,0:T(8,128)(2,1)S(1)} %pad_maximum_fusion.12), channel_id=1, source_target_pairs={{0,8},{2,10},{4,12},{6,14},{8,0},{10,2},{12,4},{14,6},{16,24},{18,... | collective-permute-start | bytes 786440 | tf_op jit(solution)/shard_map/ppermute | solution.py:73
  48.8 6.7 %collective-permute-start.17 = (bf16[2,2,2,16,1024]{4,3,2,1,0:T(8,128)(2,1)S(1)}, bf16[2,2,2,16,1024]{4,3,2,1,0:T(8,128)(2,1)S(1)}, u32[]{:S(2)}, u32[]{:S(2)}) collective-permute-start(bf16[2,2,2,16,1024]{4,3,2,1,0:T(8,128)(2,1)S(1)} %pad_maximum_fusion.15), channel_id=1, source_target_pairs={{0,16},{2,18},{4,20},{6,22},{8,24},{10,26},{12,28},{14,30},{16,0},... | collective-permute-start | bytes 786440 | tf_op jit(solution)/shard_map/ppermute | solution.py:73
  56.6 4.0 %collective-permute-start.25 = (bf16[2,2,2,16,1024]{4,3,2,1,0:T(8,128)(2,1)S(1)}, bf16[2,2,2,16,1024]{4,3,2,1,0:T(8,128)(2,1)S(1)}, u32[]{:S(2)}, u32[]{:S(2)}) collective-permute-start(bf16[2,2,2,16,1024]{4,3,2,1,0:T(8,128)(2,1)S(1)} %pad_maximum_fusion.18), channel_id=1, source_target_pairs={{0,2},{2,0},{4,6},{6,4},{8,10},{10,8},{12,14},{14,12},{16,18},{18,... | collective-permute-start | bytes 786440 | tf_op jit(solution)/shard_map/ppermute | solution.py:73
  60.9 3.0 %collective-permute-start.10 = (bf16[2,2,16,1024]{3,2,1,0:T(8,128)(2,1)S(1)}, bf16[2,2,16,1024]{3,2,1,0:T(8,128)(2,1)S(1)}, u32[]{:S(2)}, u32[]{:S(2)}) collective-permute-start(bf16[2,2,16,1024]{3,2,1,0:T(8,128)(2,1)S(1)} %pad_maximum_fusion.30), channel_id=1, source_target_pairs={{0,16},{2,18},{4,20},{6,22},{8,24},{10,26},{12,28},{14,30},{16,0},... | collective-permute-start | bytes 393224 | tf_op jit(solution)/shard_map/ppermute | solution.py:73
  64.2 11.1 %collective-permute-start.18 = (bf16[2,2,16,1024]{3,2,1,0:T(8,128)(2,1)S(1)}, bf16[2,2,16,1024]{3,2,1,0:T(8,128)(2,1)S(1)}, u32[]{:S(2)}, u32[]{:S(2)}) collective-permute-start(bf16[2,2,16,1024]{3,2,1,0:T(8,128)(2,1)S(1)} %pad_maximum_fusion.34), channel_id=1, source_target_pairs={{0,2},{2,0},{4,6},{6,4},{8,10},{10,8},{12,14},{14,12},{16,18},{18,... | collective-permute-start | bytes 393224 | tf_op jit(solution)/shard_map/ppermute | solution.py:73
  76.0 2.0 %collective-permute-start.11 = (bf16[2,16,1024]{2,1,0:T(8,128)(2,1)S(1)}, bf16[2,16,1024]{2,1,0:T(8,128)(2,1)S(1)}, u32[]{:S(2)}, u32[]{:S(2)}) collective-permute-start(bf16[2,16,1024]{2,1,0:T(8,128)(2,1)S(1)} %pad_maximum_fusion.46), channel_id=1, source_target_pairs={{0,2},{2,0},{4,6},{6,4},{8,10},{10,8},{12,14},{14,12},{16,18},{18,... | collective-permute-start | bytes 196616 | tf_op jit(solution)/shard_map/ppermute | solution.py:73
  78.8 2.3 %collective-permute-done.26 = bf16[2,2,16,1024]{3,2,1,0:T(8,128)(2,1)S(1)} collective-permute-done((bf16[2,2,16,1024]{3,2,1,0:T(8,128)(2,1)S(1)}, bf16[2,2,16,1024]{3,2,1,0:T(8,128)(2,1)S(1)}, u32[]{:S(2)}, u32[]{:S(2)}) %collective-permute-start.26) | collective-permute-done | bytes 131104 | tf_op jit(solution)/shard_map/ppermute | solution.py:73
  81.5 1.8 %collective-permute-start.12 = (bf16[2,16,1024]{2,1,0:T(8,128)(2,1)S(1)}, bf16[2,16,1024]{2,1,0:T(8,128)(2,1)S(1)}, u32[]{:S(2)}, u32[]{:S(2)}) collective-permute-start(bf16[2,16,1024]{2,1,0:T(8,128)(2,1)S(1)} %pad_maximum_fusion.47), channel_id=1, source_target_pairs={{0,2},{2,0},{4,6},{6,4},{8,10},{10,8},{12,14},{14,12},{16,18},{18,... | collective-permute-start | bytes 196616 | tf_op jit(solution)/shard_map/ppermute | solution.py:83
  83.6 3.3 %collective-permute-done.27 = bf16[2,16,1024]{2,1,0:T(8,128)(2,1)S(1)} collective-permute-done((bf16[2,16,1024]{2,1,0:T(8,128)(2,1)S(1)}, bf16[2,16,1024]{2,1,0:T(8,128)(2,1)S(1)}, u32[]{:S(2)}, u32[]{:S(2)}) %collective-permute-start.27) | collective-permute-done | bytes 65568 | tf_op jit(solution)/shard_map/ppermute | solution.py:73
  87.1 2.5 %collective-permute-start.5 = (bf16[2,2,16,1024]{3,2,1,0:T(8,128)(2,1)S(1)}, bf16[2,2,16,1024]{3,2,1,0:T(8,128)(2,1)S(1)}, u32[]{:S(2)}, u32[]{:S(2)}) collective-permute-start(bf16[2,2,16,1024]{3,2,1,0:T(8,128)(2,1)S(1)} %pad_maximum_fusion.27), channel_id=1, source_target_pairs={{0,8},{2,10},{4,12},{6,14},{8,0},{10,2},{12,4},{14,6},{16,24},{18,... | collective-permute-start | bytes 393224 | tf_op jit(solution)/shard_map/ppermute | solution.py:83
  89.8 1.5 collective-permute-start.21
  93.1 2.8 %collective-permute-start.6 = (bf16[2,2,2,16,1024]{4,3,2,1,0:T(8,128)(2,1)S(1)}, bf16[2,2,2,16,1024]{4,3,2,1,0:T(8,128)(2,1)S(1)}, u32[]{:S(2)}, u32[]{:S(2)}) collective-permute-start(bf16[2,2,2,16,1024]{4,3,2,1,0:T(8,128)(2,1)S(1)} %pad_maximum_fusion.10), channel_id=1, source_target_pairs={{0,4},{2,6},{4,0},{6,2},{8,12},{10,14},{12,8},{14,10},{16,20},{18,... | collective-permute-start | bytes 786440 | tf_op jit(solution)/shard_map/ppermute | solution.py:83
  95.8 4.8 %collective-permute-done.13 = bf16[2,2,16,1024]{3,2,1,0:T(8,128)(2,1)S(1)} collective-permute-done((bf16[2,2,16,1024]{3,2,1,0:T(8,128)(2,1)S(1)}, bf16[2,2,16,1024]{3,2,1,0:T(8,128)(2,1)S(1)}, u32[]{:S(2)}, u32[]{:S(2)}) %collective-permute-start.13) | collective-permute-done | bytes 131104 | tf_op jit(solution)/shard_map/ppermute | solution.py:83
  101.4 2.1 %collective-permute-start.7 = (bf16[2,2,2,2,16,1024]{5,4,3,2,1,0:T(8,128)(2,1)S(1)}, bf16[2,2,2,2,16,1024]{5,4,3,2,1,0:T(8,128)(2,1)S(1)}, u32[]{:S(2)}, u32[]{:S(2)}) collective-permute-start(bf16[2,2,2,2,16,1024]{5,4,3,2,1,0:T(8,128)(2,1)S(1)} %pad_maximum_fusion.2), channel_id=1, source_target_pairs={{0,2},{2,0},{4,6},{6,4},{8,10},{10,8},{12,14},{14,12},{16,18},{18,... | collective-permute-start | bytes 1572872 | tf_op jit(solution)/shard_map/ppermute | solution.py:83
  103.5 12.1 %collective-permute-done.14 = bf16[2,2,2,16,1024]{4,3,2,1,0:T(8,128)(2,1)S(1)} collective-permute-done((bf16[2,2,2,16,1024]{4,3,2,1,0:T(8,128)(2,1)S(1)}, bf16[2,2,2,16,1024]{4,3,2,1,0:T(8,128)(2,1)S(1)}, u32[]{:S(2)}, u32[]{:S(2)}) %collective-permute-start.14) | collective-permute-done | bytes 262176 | tf_op jit(solution)/shard_map/ppermute | solution.py:83
  116.5 8.5 %collective-permute-done.15 = bf16[2,2,2,2,16,1024]{5,4,3,2,1,0:T(8,128)(2,1)S(1)} collective-permute-done((bf16[2,2,2,2,16,1024]{5,4,3,2,1,0:T(8,128)(2,1)S(1)}, bf16[2,2,2,2,16,1024]{5,4,3,2,1,0:T(8,128)(2,1)S(1)}, u32[]{:S(2)}, u32[]{:S(2)}) %collective-permute-start.15) | collective-permute-done | bytes 524320 | tf_op jit(solution)/shard_map/ppermute | solution.py:83
  125.3 5.3 %collective-permute-done.23 = bf16[2,2,2,2,16,1024]{5,4,3,2,1,0:T(8,128)(2,1)S(1)} collective-permute-done((bf16[2,2,2,2,16,1024]{5,4,3,2,1,0:T(8,128)(2,1)S(1)}, bf16[2,2,2,2,16,1024]{5,4,3,2,1,0:T(8,128)(2,1)S(1)}, u32[]{:S(2)}, u32[]{:S(2)}) %collective-permute-start.23) | collective-permute-done | bytes 524320 | tf_op jit(solution)/shard_map/ppermute | solution.py:83
  130.8 2.9 %collective-permute-done.31 = bf16[2,2,2,2,16,1024]{5,4,3,2,1,0:T(8,128)(2,1)S(1)} collective-permute-done((bf16[2,2,2,2,16,1024]{5,4,3,2,1,0:T(8,128)(2,1)S(1)}, bf16[2,2,2,2,16,1024]{5,4,3,2,1,0:T(8,128)(2,1)S(1)}, u32[]{:S(2)}, u32[]{:S(2)}) %collective-permute-start.31) | collective-permute-done | bytes 524320 | tf_op jit(solution)/shard_map/ppermute | solution.py:83
  134.6 2.4 %pad_maximum_fusion.blk_ref = bf16[2,1024,1024]{2,1,0:T(8,128)(2,1)} fusion(bf16[1,1024,1024]{2,1,0:T(8,128)(2,1)S(1)} %maximum_bitcast_fusion.1, bf16[1,1024,1024]{2,1,0:T(8,128)(2,1)S(1)} %maximum_bitcast_fusion), kind=kLoop, calls=%fused_computation.4 | loop fusion | flops 2097152 | bytes 8388608 | tf_op jit(solution)/shard_map/stack | solution.py:97
  137.0 19.9 %shard_map.46 = (f32[8,4,1024]{2,1,0:T(4,128)}, f32[8,4,128]{2,1,0:T(4,128)}) custom-call(s32[128]{0:T(128)} %reshape.393.meta_ref, bf16[2,1024,1024]{2,1,0:T(8,128)(2,1)} %pad_maximum_fusion.blk_ref, bf16[1024,1152]{1,0:T(8,128)(2,1)} %copy-done.3), custom_call_target="tpu_custom_call" | custom-call | flops 10871635968 | bytes 6684672 | tf_op jit(solution)/shard_map/pallas_call | solution.py:154
  160.5 2.9 %collective-permute-start.35 = (f32[32]{0:T(128)S(1)}, f32[32]{0:T(128)S(1)}, u32[]{:S(2)}, u32[]{:S(2)}) collective-permute-start(f32[32]{0:T(128)S(1)} %fusion.11), channel_id=1, source_target_pairs={{0,6},{2,4},{4,2},{6,0},{8,14},{10,12},{12,10},{14,8},{16,22},{18,... | collective-permute-start | bytes 392 | tf_op jit(solution)/shard_map/ppermute | solution.py:33
  165.0 1.9 %collective-permute-done.36 = f32[32]{0:T(128)S(1)} collective-permute-done((f32[32]{0:T(128)S(1)}, f32[32]{0:T(128)S(1)}, u32[]{:S(2)}, u32[]{:S(2)}) %collective-permute-start.36) | collective-permute-done | bytes 160 | tf_op jit(solution)/shard_map/ppermute | solution.py:33
  166.9 1.5 collective-permute-start.38
  168.5 2.9 %collective-permute-start.40 = (f32[32]{0:T(128)S(1)}, f32[32]{0:T(128)S(1)}, u32[]{:S(2)}, u32[]{:S(2)}) collective-permute-start(f32[32]{0:T(128)S(1)} %fusion.27), channel_id=1, source_target_pairs={{0,8},{2,10},{4,12},{6,14},{8,0},{10,2},{12,4},{14,6},{16,24},{18,... | collective-permute-start | bytes 392 | tf_op jit(solution)/shard_map/ppermute | solution.py:33
  (242 shorter events, 33.3 us)
Async XLA Ops:
  5.5 27.0 %collective-permute-start = (bf16[2,2,2,2,16,1024]{5,4,0,1,2,3:T(8,128)(2,1)}, bf16[2,2,2,2,16,1024]{5,4,0,1,2,3:T(8,128)(2,1)}, u32[]{:S(2)}, u32[]{:S(2)}) collective-permute-start(bf16[2,2,2,2,16,1024]{5,4,0,1,2,3:T(8,128)(2,1)} %pad_maximum_fusion.1), channel_id=1, source_target_pairs={{0,2},{2,0},{4,6},{6,4},{8,10},{10,8},{12,14},{14,12},{16,18},{18,... | collective-permute-start | bytes 1572872 | tf_op jit(solution)/shard_map/ppermute | solution.py:73
  9.3 26.1 %collective-permute-start.8 = (bf16[2,2,2,2,16,1024]{5,4,3,2,1,0:T(8,128)(2,1)}, bf16[2,2,2,2,16,1024]{5,4,3,2,1,0:T(8,128)(2,1)}, u32[]{:S(2)}, u32[]{:S(2)}) collective-permute-start(bf16[2,2,2,2,16,1024]{5,4,3,2,1,0:T(8,128)(2,1)} %pad_maximum_fusion.3), channel_id=1, source_target_pairs={{0,4},{2,6},{4,0},{6,2},{8,12},{10,14},{12,8},{14,10},{16,20},{18,... | collective-permute-start | bytes 1572872 | tf_op jit(solution)/shard_map/ppermute | solution.py:73
  11.8 35.8 %collective-permute-start.16 = (bf16[2,2,2,2,16,1024]{5,4,3,2,1,0:T(8,128)(2,1)}, bf16[2,2,2,2,16,1024]{5,4,3,2,1,0:T(8,128)(2,1)}, u32[]{:S(2)}, u32[]{:S(2)}) collective-permute-start(bf16[2,2,2,2,16,1024]{5,4,3,2,1,0:T(8,128)(2,1)} %pad_maximum_fusion.5), channel_id=1, source_target_pairs={{0,8},{2,10},{4,12},{6,14},{8,0},{10,2},{12,4},{14,6},{16,24},{18,... | collective-permute-start | bytes 1572872 | tf_op jit(solution)/shard_map/ppermute | solution.py:73
  16.2 39.2 %collective-permute-start.24 = (bf16[2,2,2,2,16,1024]{5,4,3,2,1,0:T(8,128)(2,1)}, bf16[2,2,2,2,16,1024]{5,4,3,2,1,0:T(8,128)(2,1)}, u32[]{:S(2)}, u32[]{:S(2)}) collective-permute-start(bf16[2,2,2,2,16,1024]{5,4,3,2,1,0:T(8,128)(2,1)} %pad_maximum_fusion.7), channel_id=1, source_target_pairs={{0,16},{2,18},{4,20},{6,22},{8,24},{10,26},{12,28},{14,30},{16,0},... | collective-permute-start | bytes 1572872 | tf_op jit(solution)/shard_map/ppermute | solution.py:73
  19.6 9.1 %collective-permute-start.32 = (bf16[1024,128]{1,0:T(8,128)(2,1)}, bf16[1024,128]{1,0:T(8,128)(2,1)}, u32[]{:S(2)}, u32[]{:S(2)}) collective-permute-start(bf16[1024,128]{1,0:T(8,128)(2,1)} %slice.751), channel_id=1, source_target_pairs={{2,0},{4,2},{6,4},{8,6},{10,8},{12,10},{14,12},{16,14},{18,16},{20... | collective-permute-start | bytes 786440 | tf_op jit(solution)/shard_map/ppermute | solution.py:18
  34.9 25.8 %collective-permute-start.1 = (bf16[2,2,2,16,1024]{4,3,2,1,0:T(8,128)(2,1)S(1)}, bf16[2,2,2,16,1024]{4,3,2,1,0:T(8,128)(2,1)S(1)}, u32[]{:S(2)}, u32[]{:S(2)}) collective-permute-start(bf16[2,2,2,16,1024]{4,3,2,1,0:T(8,128)(2,1)S(1)} %pad_maximum_fusion.9), channel_id=1, source_target_pairs={{0,4},{2,6},{4,0},{6,2},{8,12},{10,14},{12,8},{14,10},{16,20},{18,... | collective-permute-start | bytes 786440 | tf_op jit(solution)/shard_map/ppermute | solution.py:73
  36.6 24.2 %collective-permute-start.9 = (bf16[2,2,2,16,1024]{4,3,2,1,0:T(8,128)(2,1)S(1)}, bf16[2,2,2,16,1024]{4,3,2,1,0:T(8,128)(2,1)S(1)}, u32[]{:S(2)}, u32[]{:S(2)}) collective-permute-start(bf16[2,2,2,16,1024]{4,3,2,1,0:T(8,128)(2,1)S(1)} %pad_maximum_fusion.12), channel_id=1, source_target_pairs={{0,8},{2,10},{4,12},{6,14},{8,0},{10,2},{12,4},{14,6},{16,24},{18,... | collective-permute-start | bytes 786440 | tf_op jit(solution)/shard_map/ppermute | solution.py:73
  48.8 15.3 %collective-permute-start.17 = (bf16[2,2,2,16,1024]{4,3,2,1,0:T(8,128)(2,1)S(1)}, bf16[2,2,2,16,1024]{4,3,2,1,0:T(8,128)(2,1)S(1)}, u32[]{:S(2)}, u32[]{:S(2)}) collective-permute-start(bf16[2,2,2,16,1024]{4,3,2,1,0:T(8,128)(2,1)S(1)} %pad_maximum_fusion.15), channel_id=1, source_target_pairs={{0,16},{2,18},{4,20},{6,22},{8,24},{10,26},{12,28},{14,30},{16,0},... | collective-permute-start | bytes 786440 | tf_op jit(solution)/shard_map/ppermute | solution.py:73
  56.6 18.7 %collective-permute-start.25 = (bf16[2,2,2,16,1024]{4,3,2,1,0:T(8,128)(2,1)S(1)}, bf16[2,2,2,16,1024]{4,3,2,1,0:T(8,128)(2,1)S(1)}, u32[]{:S(2)}, u32[]{:S(2)}) collective-permute-start(bf16[2,2,2,16,1024]{4,3,2,1,0:T(8,128)(2,1)S(1)} %pad_maximum_fusion.18), channel_id=1, source_target_pairs={{0,2},{2,0},{4,6},{6,4},{8,10},{10,8},{12,14},{14,12},{16,18},{18,... | collective-permute-start | bytes 786440 | tf_op jit(solution)/shard_map/ppermute | solution.py:73
  60.7 15.0 %collective-permute-start.2 = (bf16[2,2,16,1024]{3,2,1,0:T(8,128)(2,1)S(1)}, bf16[2,2,16,1024]{3,2,1,0:T(8,128)(2,1)S(1)}, u32[]{:S(2)}, u32[]{:S(2)}) collective-permute-start(bf16[2,2,16,1024]{3,2,1,0:T(8,128)(2,1)S(1)} %pad_maximum_fusion.26), channel_id=1, source_target_pairs={{0,8},{2,10},{4,12},{6,14},{8,0},{10,2},{12,4},{14,6},{16,24},{18,... | collective-permute-start | bytes 393224 | tf_op jit(solution)/shard_map/ppermute | solution.py:73
  60.9 14.9 %collective-permute-start.10 = (bf16[2,2,16,1024]{3,2,1,0:T(8,128)(2,1)S(1)}, bf16[2,2,16,1024]{3,2,1,0:T(8,128)(2,1)S(1)}, u32[]{:S(2)}, u32[]{:S(2)}) collective-permute-start(bf16[2,2,16,1024]{3,2,1,0:T(8,128)(2,1)S(1)} %pad_maximum_fusion.30), channel_id=1, source_target_pairs={{0,16},{2,18},{4,20},{6,22},{8,24},{10,26},{12,28},{14,30},{16,0},... | collective-permute-start | bytes 393224 | tf_op jit(solution)/shard_map/ppermute | solution.py:73
  64.2 14.2 %collective-permute-start.18 = (bf16[2,2,16,1024]{3,2,1,0:T(8,128)(2,1)S(1)}, bf16[2,2,16,1024]{3,2,1,0:T(8,128)(2,1)S(1)}, u32[]{:S(2)}, u32[]{:S(2)}) collective-permute-start(bf16[2,2,16,1024]{3,2,1,0:T(8,128)(2,1)S(1)} %pad_maximum_fusion.34), channel_id=1, source_target_pairs={{0,2},{2,0},{4,6},{6,4},{8,10},{10,8},{12,14},{14,12},{16,18},{18,... | collective-permute-start | bytes 393224 | tf_op jit(solution)/shard_map/ppermute | solution.py:73
  75.4 5.7 %collective-permute-start.26 = (bf16[2,2,16,1024]{3,2,1,0:T(8,128)(2,1)S(1)}, bf16[2,2,16,1024]{3,2,1,0:T(8,128)(2,1)S(1)}, u32[]{:S(2)}, u32[]{:S(2)}) collective-permute-start(bf16[2,2,16,1024]{3,2,1,0:T(8,128)(2,1)S(1)} %pad_maximum_fusion.38), channel_id=1, source_target_pairs={{0,4},{2,6},{4,0},{6,2},{8,12},{10,14},{12,8},{14,10},{16,20},{18,... | collective-permute-start | bytes 393224 | tf_op jit(solution)/shard_map/ppermute | solution.py:73
  75.8 5.5 %collective-permute-start.3 = (bf16[2,16,1024]{2,1,0:T(8,128)(2,1)S(1)}, bf16[2,16,1024]{2,1,0:T(8,128)(2,1)S(1)}, u32[]{:S(2)}, u32[]{:S(2)}) collective-permute-start(bf16[2,16,1024]{2,1,0:T(8,128)(2,1)S(1)} %pad_maximum_fusion.42), channel_id=1, source_target_pairs={{0,16},{2,18},{4,20},{6,22},{8,24},{10,26},{12,28},{14,30},{16,0},... | collective-permute-start | bytes 196616 | tf_op jit(solution)/shard_map/ppermute | solution.py:73
  76.0 5.5 %collective-permute-start.11 = (bf16[2,16,1024]{2,1,0:T(8,128)(2,1)S(1)}, bf16[2,16,1024]{2,1,0:T(8,128)(2,1)S(1)}, u32[]{:S(2)}, u32[]{:S(2)}) collective-permute-start(bf16[2,16,1024]{2,1,0:T(8,128)(2,1)S(1)} %pad_maximum_fusion.46), channel_id=1, source_target_pairs={{0,2},{2,0},{4,6},{6,4},{8,10},{10,8},{12,14},{14,12},{16,18},{18,... | collective-permute-start | bytes 196616 | tf_op jit(solution)/shard_map/ppermute | solution.py:73
  81.2 5.7 %collective-permute-start.27 = (bf16[2,16,1024]{2,1,0:T(8,128)(2,1)S(1)}, bf16[2,16,1024]{2,1,0:T(8,128)(2,1)S(1)}, u32[]{:S(2)}, u32[]{:S(2)}) collective-permute-start(bf16[2,16,1024]{2,1,0:T(8,128)(2,1)S(1)} %pad_maximum_fusion.54), channel_id=1, source_target_pairs={{0,8},{2,10},{4,12},{6,14},{8,0},{10,2},{12,4},{14,6},{16,24},{18,... | collective-permute-start | bytes 196616 | tf_op jit(solution)/shard_map/ppermute | solution.py:73
  81.4 5.7 %collective-permute-start.4 = (bf16[2,16,1024]{2,1,0:T(8,128)(2,1)S(1)}, bf16[2,16,1024]{2,1,0:T(8,128)(2,1)S(1)}, u32[]{:S(2)}, u32[]{:S(2)}) collective-permute-start(bf16[2,16,1024]{2,1,0:T(8,128)(2,1)S(1)} %pad_maximum_fusion.43), channel_id=1, source_target_pairs={{0,16},{2,18},{4,20},{6,22},{8,24},{10,26},{12,28},{14,30},{16,0},... | collective-permute-start | bytes 196616 | tf_op jit(solution)/shard_map/ppermute | solution.py:83
  81.5 8.1 %collective-permute-start.12 = (bf16[2,16,1024]{2,1,0:T(8,128)(2,1)S(1)}, bf16[2,16,1024]{2,1,0:T(8,128)(2,1)S(1)}, u32[]{:S(2)}, u32[]{:S(2)}) collective-permute-start(bf16[2,16,1024]{2,1,0:T(8,128)(2,1)S(1)} %pad_maximum_fusion.47), channel_id=1, source_target_pairs={{0,2},{2,0},{4,6},{6,4},{8,10},{10,8},{12,14},{14,12},{16,18},{18,... | collective-permute-start | bytes 196616 | tf_op jit(solution)/shard_map/ppermute | solution.py:83
  83.3 6.4 %collective-permute-start.20 = (bf16[2,16,1024]{2,1,0:T(8,128)(2,1)S(1)}, bf16[2,16,1024]{2,1,0:T(8,128)(2,1)S(1)}, u32[]{:S(2)}, u32[]{:S(2)}) collective-permute-start(bf16[2,16,1024]{2,1,0:T(8,128)(2,1)S(1)} %pad_maximum_fusion.51), channel_id=1, source_target_pairs={{0,4},{2,6},{4,0},{6,2},{8,12},{10,14},{12,8},{14,10},{16,20},{18,... | collective-permute-start | bytes 196616 | tf_op jit(solution)/shard_map/ppermute | solution.py:83
  87.1 5.8 %collective-permute-start.5 = (bf16[2,2,16,1024]{3,2,1,0:T(8,128)(2,1)S(1)}, bf16[2,2,16,1024]{3,2,1,0:T(8,128)(2,1)S(1)}, u32[]{:S(2)}, u32[]{:S(2)}) collective-permute-start(bf16[2,2,16,1024]{3,2,1,0:T(8,128)(2,1)S(1)} %pad_maximum_fusion.27), channel_id=1, source_target_pairs={{0,8},{2,10},{4,12},{6,14},{8,0},{10,2},{12,4},{14,6},{16,24},{18,... | collective-permute-start | bytes 393224 | tf_op jit(solution)/shard_map/ppermute | solution.py:83
  89.7 11.0 %collective-permute-start.13 = (bf16[2,2,16,1024]{3,2,1,0:T(8,128)(2,1)S(1)}, bf16[2,2,16,1024]{3,2,1,0:T(8,128)(2,1)S(1)}, u32[]{:S(2)}, u32[]{:S(2)}) collective-permute-start(bf16[2,2,16,1024]{3,2,1,0:T(8,128)(2,1)S(1)} %pad_maximum_fusion.31), channel_id=1, source_target_pairs={{0,16},{2,18},{4,20},{6,22},{8,24},{10,26},{12,28},{14,30},{16,0},... | collective-permute-start | bytes 393224 | tf_op jit(solution)/shard_map/ppermute | solution.py:83
  89.8 11.0 %collective-permute-start.21 = (bf16[2,2,16,1024]{3,2,1,0:T(8,128)(2,1)S(1)}, bf16[2,2,16,1024]{3,2,1,0:T(8,128)(2,1)S(1)}, u32[]{:S(2)}, u32[]{:S(2)}) collective-permute-start(bf16[2,2,16,1024]{3,2,1,0:T(8,128)(2,1)S(1)} %pad_maximum_fusion.35), channel_id=1, source_target_pairs={{0,2},{2,0},{4,6},{6,4},{8,10},{10,8},{12,14},{14,12},{16,18},{18,... | collective-permute-start | bytes 393224 | tf_op jit(solution)/shard_map/ppermute | solution.py:83
  91.6 9.4 %collective-permute-start.29 = (bf16[2,2,16,1024]{3,2,1,0:T(8,128)(2,1)S(1)}, bf16[2,2,16,1024]{3,2,1,0:T(8,128)(2,1)S(1)}, u32[]{:S(2)}, u32[]{:S(2)}) collective-permute-start(bf16[2,2,16,1024]{3,2,1,0:T(8,128)(2,1)S(1)} %pad_maximum_fusion.39), channel_id=1, source_target_pairs={{0,4},{2,6},{4,0},{6,2},{8,12},{10,14},{12,8},{14,10},{16,20},{18,... | collective-permute-start | bytes 393224 | tf_op jit(solution)/shard_map/ppermute | solution.py:83
  93.1 8.2 %collective-permute-start.6 = (bf16[2,2,2,16,1024]{4,3,2,1,0:T(8,128)(2,1)S(1)}, bf16[2,2,2,16,1024]{4,3,2,1,0:T(8,128)(2,1)S(1)}, u32[]{:S(2)}, u32[]{:S(2)}) collective-permute-start(bf16[2,2,2,16,1024]{4,3,2,1,0:T(8,128)(2,1)S(1)} %pad_maximum_fusion.10), channel_id=1, source_target_pairs={{0,4},{2,6},{4,0},{6,2},{8,12},{10,14},{12,8},{14,10},{16,20},{18,... | collective-permute-start | bytes 786440 | tf_op jit(solution)/shard_map/ppermute | solution.py:83
  100.7 14.9 %collective-permute-start.14 = (bf16[2,2,2,16,1024]{4,3,2,1,0:T(8,128)(2,1)S(1)}, bf16[2,2,2,16,1024]{4,3,2,1,0:T(8,128)(2,1)S(1)}, u32[]{:S(2)}, u32[]{:S(2)}) collective-permute-start(bf16[2,2,2,16,1024]{4,3,2,1,0:T(8,128)(2,1)S(1)} %pad_maximum_fusion.13), channel_id=1, source_target_pairs={{0,8},{2,10},{4,12},{6,14},{8,0},{10,2},{12,4},{14,6},{16,24},{18,... | collective-permute-start | bytes 786440 | tf_op jit(solution)/shard_map/ppermute | solution.py:83
  100.9 14.9 %collective-permute-start.22 = (bf16[2,2,2,16,1024]{4,3,2,1,0:T(8,128)(2,1)S(1)}, bf16[2,2,2,16,1024]{4,3,2,1,0:T(8,128)(2,1)S(1)}, u32[]{:S(2)}, u32[]{:S(2)}) collective-permute-start(bf16[2,2,2,16,1024]{4,3,2,1,0:T(8,128)(2,1)S(1)} %pad_maximum_fusion.16), channel_id=1, source_target_pairs={{0,16},{2,18},{4,20},{6,22},{8,24},{10,26},{12,28},{14,30},{16,0},... | collective-permute-start | bytes 786440 | tf_op jit(solution)/shard_map/ppermute | solution.py:83
  101.1 15.0 %collective-permute-start.30 = (bf16[2,2,2,16,1024]{4,3,2,1,0:T(8,128)(2,1)S(1)}, bf16[2,2,2,16,1024]{4,3,2,1,0:T(8,128)(2,1)S(1)}, u32[]{:S(2)}, u32[]{:S(2)}) collective-permute-start(bf16[2,2,2,16,1024]{4,3,2,1,0:T(8,128)(2,1)S(1)} %pad_maximum_fusion.19), channel_id=1, source_target_pairs={{0,2},{2,0},{4,6},{6,4},{8,10},{10,8},{12,14},{14,12},{16,18},{18,... | collective-permute-start | bytes 786440 | tf_op jit(solution)/shard_map/ppermute | solution.py:83
  101.4 15.0 %collective-permute-start.7 = (bf16[2,2,2,2,16,1024]{5,4,3,2,1,0:T(8,128)(2,1)S(1)}, bf16[2,2,2,2,16,1024]{5,4,3,2,1,0:T(8,128)(2,1)S(1)}, u32[]{:S(2)}, u32[]{:S(2)}) collective-permute-start(bf16[2,2,2,2,16,1024]{5,4,3,2,1,0:T(8,128)(2,1)S(1)} %pad_maximum_fusion.2), channel_id=1, source_target_pairs={{0,2},{2,0},{4,6},{6,4},{8,10},{10,8},{12,14},{14,12},{16,18},{18,... | collective-permute-start | bytes 1572872 | tf_op jit(solution)/shard_map/ppermute | solution.py:83
  115.8 9.2 %collective-permute-start.15 = (bf16[2,2,2,2,16,1024]{5,4,3,2,1,0:T(8,128)(2,1)S(1)}, bf16[2,2,2,2,16,1024]{5,4,3,2,1,0:T(8,128)(2,1)S(1)}, u32[]{:S(2)}, u32[]{:S(2)}) collective-permute-start(bf16[2,2,2,2,16,1024]{5,4,3,2,1,0:T(8,128)(2,1)S(1)} %pad_maximum_fusion.4), channel_id=1, source_target_pairs={{0,4},{2,6},{4,0},{6,2},{8,12},{10,14},{12,8},{14,10},{16,20},{18,... | collective-permute-start | bytes 1572872 | tf_op jit(solution)/shard_map/ppermute | solution.py:83
  116.1 14.5 %collective-permute-start.23 = (bf16[2,2,2,2,16,1024]{5,4,3,2,1,0:T(8,128)(2,1)S(1)}, bf16[2,2,2,2,16,1024]{5,4,3,2,1,0:T(8,128)(2,1)S(1)}, u32[]{:S(2)}, u32[]{:S(2)}) collective-permute-start(bf16[2,2,2,2,16,1024]{5,4,3,2,1,0:T(8,128)(2,1)S(1)} %pad_maximum_fusion.6), channel_id=1, source_target_pairs={{0,8},{2,10},{4,12},{6,14},{8,0},{10,2},{12,4},{14,6},{16,24},{18,... | collective-permute-start | bytes 1572872 | tf_op jit(solution)/shard_map/ppermute | solution.py:83
  116.3 17.3 %collective-permute-start.31 = (bf16[2,2,2,2,16,1024]{5,4,3,2,1,0:T(8,128)(2,1)S(1)}, bf16[2,2,2,2,16,1024]{5,4,3,2,1,0:T(8,128)(2,1)S(1)}, u32[]{:S(2)}, u32[]{:S(2)}) collective-permute-start(bf16[2,2,2,2,16,1024]{5,4,3,2,1,0:T(8,128)(2,1)S(1)} %pad_maximum_fusion.8), channel_id=1, source_target_pairs={{0,16},{2,18},{4,20},{6,22},{8,24},{10,26},{12,28},{14,30},{16,0},... | collective-permute-start | bytes 1572872 | tf_op jit(solution)/shard_map/ppermute | solution.py:83
  166.9 5.4 %collective-permute-start.38 = (f32[32]{0:T(128)S(1)}, f32[32]{0:T(128)S(1)}, u32[]{:S(2)}, u32[]{:S(2)}) collective-permute-start(f32[32]{0:T(128)S(1)} %fusion.27), channel_id=1, source_target_pairs={{0,24},{2,26},{4,28},{6,30},{8,16},{10,18},{12,20},{14,22},{16,8},... | collective-permute-start | bytes 392 | tf_op jit(solution)/shard_map/ppermute | solution.py:33
  (17 other events, 97.4 us)

commit v4 on v3

--- a/solution.py
+++ b/solution.py
@@ -6,7 +6,7 @@
 from jax.sharding import PartitionSpec as P
 
 L = 128
-GROUP = 4
+GROUP = 8
 REACH = L + 16
 
 EPS = 1e-06
@@ -48,37 +48,41 @@
     nbits = size.bit_length() - 1
     rounds = roots.shape[0]
     rows, chans = block.shape
-    parts = next(p for p in (4, 2, 1) if rows % (p * size) == 0)
+    parts = next(p for p in (2, 1) if rows % (p * size) == 0)
     if size & (size - 1) or rows % (parts * size) or nbits == 0:
         own = place == roots
         masked = jnp.where(own[:, None, None], block[None], jnp.zeros_like(block)[None])
         return lax.psum(masked, axis)
     piece = rows // (parts * size)
-    orders = [[1 << ((p + s) % nbits) for s in range(nbits)] for p in range(parts)]
+    orders = {}
+    for r in range(rounds):
+        for p in range(parts):
+            order = [1 << ((p * nbits // parts + s) % nbits) for s in range(nbits)]
+            if r % 2:
+                order = [order[s ^ 1] if (s ^ 1) < nbits else order[s] for s in range(nbits)]
+            orders[p, r] = order
     bufs = {}
-    for p in range(parts):
+    for (p, r), order in orders.items():
         seg = block[p * piece * size : (p + 1) * piece * size].reshape([2] * nbits + [piece, chans])
-        perm = [nbits - 1 - (m.bit_length() - 1) for m in orders[p]] + [nbits, nbits + 1]
-        seg = jnp.transpose(seg, perm)
-        for r in range(rounds):
-            bufs[p, r] = seg
+        perm = [nbits - 1 - (m.bit_length() - 1) for m in order] + [nbits, nbits + 1]
+        bufs[p, r] = jnp.transpose(seg, perm)
     for s in range(nbits):
         sends, keeps = {}, {}
         for (p, r), buf in bufs.items():
-            mask = orders[p][s]
+            mask = orders[p, r][s]
             bit = (place // mask) % 2
             keeps[p, r] = jnp.where(bit == 1, buf[1], buf[0])
             sends.setdefault(mask, []).append(((p, r), jnp.where(bit == 1, buf[0], buf[1])))
         for mask, items in sends.items():
             got = lax.ppermute(jnp.stack([v for _, v in items]), axis, [(i, i ^ mask) for i in range(size)])
             for n, (key, _) in enumerate(items):
-                held = sum(orders[key[0]][:s])
+                held = sum(orders[key][:s])
                 holder = ((place ^ roots[key[1]]) & (size - 1 - held)) == 0
                 bufs[key] = jnp.where(holder, keeps[key], got[n])
     for s in reversed(range(nbits)):
         sends = {}
         for (p, r), buf in bufs.items():
-            sends.setdefault(orders[p][s], []).append(((p, r), buf))
+            sends.setdefault(orders[p, r][s], []).append(((p, r), buf))
         for mask, items in sends.items():
             got = lax.ppermute(jnp.stack([v for _, v in items]), axis, [(i, i ^ mask) for i in range(size)])
             bit = (place // mask) % 2
@@ -90,7 +94,7 @@
     for r in range(rounds):
         segs = []
         for p in range(parts):
-            perm = [nbits - 1 - (m.bit_length() - 1) for m in orders[p]]
+            perm = [nbits - 1 - (m.bit_length() - 1) for m in orders[p, r]]
             inverse = [perm.index(k) for k in range(nbits)] + [nbits, nbits + 1]
             segs.append(jnp.transpose(bufs[p, r], inverse).reshape(piece * size, chans))
         out.append(jnp.concatenate(segs, axis=0))

time: 174 us -> 180 us (1.034)
  waiting for transfers between devices: 51.1 us -> 70.9 us
  starting transfers between devices: 69.5 us -> 61.3 us
  local copies, waits for them, and re-layouts: 12.4 us -> 8.86 us
    ppermute x32, waiting for transfers between devices: 41.1 us -> 56.4 us  [spread_blocks(): lax.ppermute(jnp.stack([v for _, v in items]), axis, [(i, i ^ mask) for i...]
    ppermute x32, starting transfers between devices: 59.7 us -> 51.5 us  [spread_blocks(): lax.ppermute(jnp.stack([v for _, v in items]), axis, [(i, i ^ mask) for i...]
    ppermute x1, waiting for transfers between devices: 4.74 us -> 10.6 us  [from_behind(): return lax.ppermute(value, axis, pairs)]
    another operation x56 -> x12, other arithmetic: 4.42 us -> 0.38 us  [spread_blocks(): jnp.stack([v for _, v in items])]
    select_n x18 -> x16, other arithmetic: 5.7 us -> 4.16 us  [spread_blocks(): bufs[key] = jnp.where(holder, keeps[key], got[n])]
    unnamed x18 -> x24, local copies, waits for them, and re-layouts: 4.51 us -> 4.03 us
  transfers between devices with their start and end apart: 41 -> 41, of which waited for: 17 -> 20; matrix products, arithmetic and copies ran while one was open for 11% -> 8% of each run, Pallas kernels for 0% -> 0%
where the time goes in v4:
time: 180 us
  waiting for transfers between devices  70.9 us (39%)
  starting transfers between devices  61.3 us (34%)
  Pallas kernels  19.6 us (11%)
  other arithmetic  15.6 us (9%)
  local copies, waits for them, and re-layouts  8.86 us (5%)
  between operations  2.08 us (1%)
    ppermute x32, waiting for transfers between devices, spread_blocks(): lax.ppermute(jnp.stack([v for _, v in items]), axis, [(i, i ^ mask) for i...  56.4 us
    ppermute x32, starting transfers between devices, spread_blocks(): lax.ppermute(jnp.stack([v for _, v in items]), axis, [(i, i ^ mask) for i...  51.5 us
    pallas_call x1, Pallas kernels, correlate(): pl.pallas_call(correlate_kernel, grid_spec=grid_spec, out_shape=[jax.Shap...  19.6 us
    ppermute x1, waiting for transfers between devices, from_behind(): return lax.ppermute(value, axis, pairs)  10.6 us
    ppermute x8, starting transfers between devices, group_sum(): got[d] = lax.ppermute(value, axis, pairs)  8.58 us
    select_n x16, other arithmetic, spread_blocks(): bufs[key] = jnp.where(holder, keeps[key], got[n])  4.16 us
    unnamed x24, local copies, waits for them, and re-layouts  4.03 us
    ppermute x8, waiting for transfers between devices, group_sum(): got[d] = lax.ppermute(value, axis, pairs)  3.91 us
  transfers between devices with their start and end apart: 41, of which 20 were waited for; matrix products, arithmetic and copies ran while one was open for 8% of the time, Pallas kernels for 0%

profile of v4, /device:TPU:0, one launch (start us, length us, event | category | flops | bytes accessed | tf_op | source)
XLA Modules:
  0.0 179.9 jit_solution(11898866985625011177)
XLA Ops:
  0.0 2.9 %copy.28 = bf16[1024,1024]{0,1:T(8,128)(2,1)S(1)} copy(bf16[1024,1024]{1,0:T(8,128)(2,1)} %param.4) | data formatting | bytes 4194304 | tf_op args[0]
  5.2 3.0 %collective-permute-start.16 = (bf16[1,2,2,2,32,1024]{5,4,1,0,3,2:T(8,128)(2,1)}, bf16[1,2,2,2,32,1024]{5,4,1,0,3,2:T(8,128)(2,1)}, u32[]{:S(2)}, u32[]{:S(2)}) collective-permute-start(bf16[1,2,2,2,32,1024]{5,4,1,0,3,2:T(8,128)(2,1)} %get-tuple-element.27), channel_id=1, source_target_pairs={{0,4},{2,6},{4,0},{6,2},{8,12},{10,14},{12,8},{14,10},{16,20},{18,... | collective-permute-start | bytes 1572872 | tf_op jit(solution)/shard_map/ppermute | solution.py:77
  9.3 2.6 %collective-permute-start.24 = (bf16[1,2,2,2,32,1024]{5,4,3,2,1,0:T(8,128)(2,1)}, bf16[1,2,2,2,32,1024]{5,4,3,2,1,0:T(8,128)(2,1)}, u32[]{:S(2)}, u32[]{:S(2)}) collective-permute-start(bf16[1,2,2,2,32,1024]{5,4,3,2,1,0:T(8,128)(2,1)} %bitcast.80), channel_id=1, source_target_pairs={{0,16},{2,18},{4,20},{6,22},{8,24},{10,26},{12,28},{14,30},{16,0},... | collective-permute-start | bytes 1572872 | tf_op jit(solution)/shard_map/ppermute | solution.py:77
  13.1 1.5 collective-permute-start
  14.8 1.6 collective-permute-start.8
  21.4 10.6 %collective-permute-done.32 = bf16[1024,128]{1,0:T(8,128)(2,1)S(1)} collective-permute-done((bf16[1024,128]{1,0:T(8,128)(2,1)}, bf16[1024,128]{1,0:T(8,128)(2,1)S(1)}, u32[]{:S(2)}, u32[]{:S(2)}) %collective-permute-start.32) | collective-permute-done | bytes 262176 | tf_op jit(solution)/shard_map/ppermute | solution.py:18
  36.8 1.5 collective-permute-start.17
  39.5 9.7 %collective-permute-start.25 = (bf16[1,2,2,32,1024]{4,3,2,1,0:T(8,128)(2,1)S(1)}, bf16[1,2,2,32,1024]{4,3,2,1,0:T(8,128)(2,1)S(1)}, u32[]{:S(2)}, u32[]{:S(2)}) collective-permute-start(bf16[1,2,2,32,1024]{4,3,2,1,0:T(8,128)(2,1)S(1)} %broadcast_select_fusion.16), channel_id=1, source_target_pairs={{0,8},{2,10},{4,12},{6,14},{8,0},{10,2},{12,4},{14,6},{16,24},{18,... | collective-permute-start | bytes 786440 | tf_op jit(solution)/shard_map/ppermute | solution.py:77
  49.5 4.4 %collective-permute-start.1 = (bf16[1,2,2,32,1024]{4,3,1,2,0:T(8,128)(2,1)S(1)}, bf16[1,2,2,32,1024]{4,3,1,2,0:T(8,128)(2,1)S(1)}, u32[]{:S(2)}, u32[]{:S(2)}) collective-permute-start(bf16[1,2,2,32,1024]{4,3,1,2,0:T(8,128)(2,1)S(1)} %fusion.5), channel_id=1, source_target_pairs={{0,4},{2,6},{4,0},{6,2},{8,12},{10,14},{12,8},{14,10},{16,20},{18,... | collective-permute-start | bytes 786440 | tf_op jit(solution)/shard_map/ppermute | solution.py:77
  55.3 3.0 %collective-permute-start.18 = (bf16[1,2,32,1024]{3,2,1,0:T(8,128)(2,1)S(1)}, bf16[1,2,32,1024]{3,2,1,0:T(8,128)(2,1)S(1)}, u32[]{:S(2)}, u32[]{:S(2)}) collective-permute-start(bf16[1,2,32,1024]{3,2,1,0:T(8,128)(2,1)S(1)} %select_bitcast_fusion.1), channel_id=1, source_target_pairs={{0,16},{2,18},{4,20},{6,22},{8,24},{10,26},{12,28},{14,30},{16,0},... | collective-permute-start | bytes 393224 | tf_op jit(solution)/shard_map/ppermute | solution.py:77
  58.3 2.0 %collective-permute-start.26 = (bf16[1,2,32,1024]{3,2,1,0:T(8,128)(2,1)S(1)}, bf16[1,2,32,1024]{3,2,1,0:T(8,128)(2,1)S(1)}, u32[]{:S(2)}, u32[]{:S(2)}) collective-permute-start(bf16[1,2,32,1024]{3,2,1,0:T(8,128)(2,1)S(1)} %select_bitcast_fusion), channel_id=1, source_target_pairs={{0,4},{2,6},{4,0},{6,2},{8,12},{10,14},{12,8},{14,10},{16,20},{18,... | collective-permute-start | bytes 393224 | tf_op jit(solution)/shard_map/ppermute | solution.py:77
  60.4 1.7 collective-permute-start.2
  62.0 9.5 %collective-permute-done.9 = bf16[1,2,2,32,1024]{4,3,1,2,0:T(8,128)(2,1)S(1)} collective-permute-done((bf16[1,2,2,32,1024]{4,3,1,2,0:T(8,128)(2,1)S(1)}, bf16[1,2,2,32,1024]{4,3,1,2,0:T(8,128)(2,1)S(1)}, u32[]{:S(2)}, u32[]{:S(2)}) %collective-permute-start.9) | collective-permute-done | bytes 262176 | tf_op jit(solution)/shard_map/ppermute | solution.py:77
  74.0 1.6 collective-permute-start.3
  77.5 1.4 collective-permute-start.28
  79.3 1.7 collective-permute-start.4
  81.2 1.6 collective-permute-start.12
  83.0 1.7 collective-permute-start.29
  84.6 1.6 collective-permute-done.4
  88.3 1.6 collective-permute-done.21
  91.4 1.7 collective-permute-start.6
  93.7 1.5 collective-permute-start.14
  95.3 2.2 %collective-permute-done.22 = bf16[1,2,2,32,1024]{4,3,2,1,0:T(8,128)(2,1)S(1)} collective-permute-done((bf16[1,2,2,32,1024]{4,3,2,1,0:T(8,128)(2,1)S(1)}, bf16[1,2,2,32,1024]{4,3,2,1,0:T(8,128)(2,1)S(1)}, u32[]{:S(2)}, u32[]{:S(2)}) %collective-permute-start.22) | collective-permute-done | bytes 262176 | tf_op jit(solution)/shard_map/ppermute | solution.py:87
  98.8 1.6 collective-permute-done.30
  101.2 2.4 %collective-permute-start.7 = (bf16[1,2,2,2,32,1024]{5,4,3,2,1,0:T(8,128)(2,1)S(1)}, bf16[1,2,2,2,32,1024]{5,4,3,2,1,0:T(8,128)(2,1)S(1)}, u32[]{:S(2)}, u32[]{:S(2)}) collective-permute-start(bf16[1,2,2,2,32,1024]{5,4,3,2,1,0:T(8,128)(2,1)S(1)} %maximum_bitcast_fusion.5), channel_id=1, source_target_pairs={{0,2},{2,0},{4,6},{6,4},{8,10},{10,8},{12,14},{14,12},{16,18},{18,... | collective-permute-start | bytes 1572872 | tf_op jit(solution)/shard_map/ppermute | solution.py:87
  103.6 16.6 %collective-permute-done.14 = bf16[1,2,2,32,1024]{4,3,2,1,0:T(8,128)(2,1)S(1)} collective-permute-done((bf16[1,2,2,32,1024]{4,3,2,1,0:T(8,128)(2,1)S(1)}, bf16[1,2,2,32,1024]{4,3,2,1,0:T(8,128)(2,1)S(1)}, u32[]{:S(2)}, u32[]{:S(2)}) %collective-permute-start.14) | collective-permute-done | bytes 262176 | tf_op jit(solution)/shard_map/ppermute | solution.py:87
  120.9 19.7 %collective-permute-done.15 = bf16[1,2,2,2,32,1024]{5,4,3,2,1,0:T(8,128)(2,1)S(1)} collective-permute-done((bf16[1,2,2,2,32,1024]{5,4,3,2,1,0:T(8,128)(2,1)S(1)}, bf16[1,2,2,2,32,1024]{5,4,3,2,1,0:T(8,128)(2,1)S(1)}, u32[]{:S(2)}, u32[]{:S(2)}) %collective-permute-start.15) | collective-permute-done | bytes 524320 | tf_op jit(solution)/shard_map/ppermute | solution.py:87
  141.5 2.3 %pad_maximum_fusion.blk_ref = bf16[2,1024,1024]{2,1,0:T(8,128)(2,1)} fusion(bf16[1,1024,1024]{2,1,0:T(8,128)(2,1)S(1)} %get-tuple-element.66, bf16[1,1024,1024]{2,1,0:T(8,128)(2,1)S(1)} %get-tuple-element.65), kind=kLoop, calls=%fused_computation.4 | loop fusion | flops 2097152 | bytes 8388608 | tf_op jit(solution)/shard_map/stack | solution.py:101
  143.8 19.6 %shard_map.46 = (f32[4,8,1024]{2,1,0:T(8,128)}, f32[4,8,128]{2,1,0:T(8,128)}) custom-call(s32[128]{0:T(128)} %reshape.232.meta_ref, bf16[2,1024,1024]{2,1,0:T(8,128)(2,1)} %pad_maximum_fusion.blk_ref, bf16[1024,1152]{1,0:T(8,128)(2,1)} %copy-done.7), custom_call_target="tpu_custom_call" | custom-call | flops 10871635968 | bytes 6684672 | tf_op jit(solution)/shard_map/pallas_call | solution.py:158
  168.5 2.9 %collective-permute-start.37 = (f32[32]{0:T(128)S(1)}, f32[32]{0:T(128)S(1)}, u32[]{:S(2)}, u32[]{:S(2)}) collective-permute-start(f32[32]{0:T(128)S(1)} %fusion.25), channel_id=1, source_target_pairs={{0,2},{2,0},{4,6},{6,4},{8,10},{10,8},{12,14},{14,12},{16,18},{18,... | collective-permute-start | bytes 392 | tf_op jit(solution)/shard_map/ppermute | solution.py:33
  173.0 1.6 collective-permute-start.38
  174.6 2.8 %collective-permute-start.40 = (f32[32]{0:T(128)S(1)}, f32[32]{0:T(128)S(1)}, u32[]{:S(2)}, u32[]{:S(2)}) collective-permute-start(f32[32]{0:T(128)S(1)} %fusion.38), channel_id=1, source_target_pairs={{0,8},{2,10},{4,12},{6,14},{8,0},{10,2},{12,4},{14,6},{16,24},{18,... | collective-permute-start | bytes 392 | tf_op jit(solution)/shard_map/ppermute | solution.py:33
  (180 shorter events, 37.8 us)
Async XLA Ops:
  5.2 29.8 %collective-permute-start.16 = (bf16[1,2,2,2,32,1024]{5,4,1,0,3,2:T(8,128)(2,1)}, bf16[1,2,2,2,32,1024]{5,4,1,0,3,2:T(8,128)(2,1)}, u32[]{:S(2)}, u32[]{:S(2)}) collective-permute-start(bf16[1,2,2,2,32,1024]{5,4,1,0,3,2:T(8,128)(2,1)} %get-tuple-element.27), channel_id=1, source_target_pairs={{0,4},{2,6},{4,0},{6,2},{8,12},{10,14},{12,8},{14,10},{16,20},{18,... | collective-permute-start | bytes 1572872 | tf_op jit(solution)/shard_map/ppermute | solution.py:77
  9.3 29.1 %collective-permute-start.24 = (bf16[1,2,2,2,32,1024]{5,4,3,2,1,0:T(8,128)(2,1)}, bf16[1,2,2,2,32,1024]{5,4,3,2,1,0:T(8,128)(2,1)}, u32[]{:S(2)}, u32[]{:S(2)}) collective-permute-start(bf16[1,2,2,2,32,1024]{5,4,3,2,1,0:T(8,128)(2,1)} %bitcast.80), channel_id=1, source_target_pairs={{0,16},{2,18},{4,20},{6,22},{8,24},{10,26},{12,28},{14,30},{16,0},... | collective-permute-start | bytes 1572872 | tf_op jit(solution)/shard_map/ppermute | solution.py:77
  13.1 36.1 %collective-permute-start = (bf16[1,2,2,2,32,1024]{5,4,0,1,2,3:T(8,128)(2,1)}, bf16[1,2,2,2,32,1024]{5,4,0,1,2,3:T(8,128)(2,1)}, u32[]{:S(2)}, u32[]{:S(2)}) collective-permute-start(bf16[1,2,2,2,32,1024]{5,4,0,1,2,3:T(8,128)(2,1)} %get-tuple-element.18), channel_id=1, source_target_pairs={{0,2},{2,0},{4,6},{6,4},{8,10},{10,8},{12,14},{14,12},{16,18},{18,... | collective-permute-start | bytes 1572872 | tf_op jit(solution)/shard_map/ppermute | solution.py:77
  14.8 39.2 %collective-permute-start.8 = (bf16[1,2,2,2,32,1024]{5,4,3,2,1,0:T(8,128)(2,1)S(1)}, bf16[1,2,2,2,32,1024]{5,4,3,2,1,0:T(8,128)(2,1)}, u32[]{:S(2)}, u32[]{:S(2)}) collective-permute-start(bf16[1,2,2,2,32,1024]{5,4,3,2,1,0:T(8,128)(2,1)S(1)} %get-tuple-element.23), channel_id=1, source_target_pairs={{0,8},{2,10},{4,12},{6,14},{8,0},{10,2},{12,4},{14,6},{16,24},{18,... | collective-permute-start | bytes 1572872 | tf_op jit(solution)/shard_map/ppermute | solution.py:77
  17.2 14.9 %collective-permute-start.32 = (bf16[1024,128]{1,0:T(8,128)(2,1)}, bf16[1024,128]{1,0:T(8,128)(2,1)S(1)}, u32[]{:S(2)}, u32[]{:S(2)}) collective-permute-start(bf16[1024,128]{1,0:T(8,128)(2,1)} %slice.283), channel_id=1, source_target_pairs={{2,0},{4,2},{6,4},{8,6},{10,8},{12,10},{14,12},{16,14},{18,16},{20... | collective-permute-start | bytes 786440 | tf_op jit(solution)/shard_map/ppermute | solution.py:18
  36.8 18.4 %collective-permute-start.17 = (bf16[1,2,2,32,1024]{4,3,2,1,0:T(8,128)(2,1)S(1)}, bf16[1,2,2,32,1024]{4,3,2,1,0:T(8,128)(2,1)S(1)}, u32[]{:S(2)}, u32[]{:S(2)}) collective-permute-start(bf16[1,2,2,32,1024]{4,3,2,1,0:T(8,128)(2,1)S(1)} %fusion.7), channel_id=1, source_target_pairs={{0,2},{2,0},{4,6},{6,4},{8,10},{10,8},{12,14},{14,12},{16,18},{18,... | collective-permute-start | bytes 786440 | tf_op jit(solution)/shard_map/ppermute | solution.py:77
  39.5 18.8 %collective-permute-start.25 = (bf16[1,2,2,32,1024]{4,3,2,1,0:T(8,128)(2,1)S(1)}, bf16[1,2,2,32,1024]{4,3,2,1,0:T(8,128)(2,1)S(1)}, u32[]{:S(2)}, u32[]{:S(2)}) collective-permute-start(bf16[1,2,2,32,1024]{4,3,2,1,0:T(8,128)(2,1)S(1)} %broadcast_select_fusion.16), channel_id=1, source_target_pairs={{0,8},{2,10},{4,12},{6,14},{8,0},{10,2},{12,4},{14,6},{16,24},{18,... | collective-permute-start | bytes 786440 | tf_op jit(solution)/shard_map/ppermute | solution.py:77
  49.5 10.8 %collective-permute-start.1 = (bf16[1,2,2,32,1024]{4,3,1,2,0:T(8,128)(2,1)S(1)}, bf16[1,2,2,32,1024]{4,3,1,2,0:T(8,128)(2,1)S(1)}, u32[]{:S(2)}, u32[]{:S(2)}) collective-permute-start(bf16[1,2,2,32,1024]{4,3,1,2,0:T(8,128)(2,1)S(1)} %fusion.5), channel_id=1, source_target_pairs={{0,4},{2,6},{4,0},{6,2},{8,12},{10,14},{12,8},{14,10},{16,20},{18,... | collective-permute-start | bytes 786440 | tf_op jit(solution)/shard_map/ppermute | solution.py:77
  55.1 16.4 %collective-permute-start.9 = (bf16[1,2,2,32,1024]{4,3,1,2,0:T(8,128)(2,1)S(1)}, bf16[1,2,2,32,1024]{4,3,1,2,0:T(8,128)(2,1)S(1)}, u32[]{:S(2)}, u32[]{:S(2)}) collective-permute-start(bf16[1,2,2,32,1024]{4,3,1,2,0:T(8,128)(2,1)S(1)} %fusion.6), channel_id=1, source_target_pairs={{0,16},{2,18},{4,20},{6,22},{8,24},{10,26},{12,28},{14,30},{16,0},... | collective-permute-start | bytes 786440 | tf_op jit(solution)/shard_map/ppermute | solution.py:77
  55.3 17.7 %collective-permute-start.18 = (bf16[1,2,32,1024]{3,2,1,0:T(8,128)(2,1)S(1)}, bf16[1,2,32,1024]{3,2,1,0:T(8,128)(2,1)S(1)}, u32[]{:S(2)}, u32[]{:S(2)}) collective-permute-start(bf16[1,2,32,1024]{3,2,1,0:T(8,128)(2,1)S(1)} %select_bitcast_fusion.1), channel_id=1, source_target_pairs={{0,16},{2,18},{4,20},{6,22},{8,24},{10,26},{12,28},{14,30},{16,0},... | collective-permute-start | bytes 393224 | tf_op jit(solution)/shard_map/ppermute | solution.py:77
  58.3 14.8 %collective-permute-start.26 = (bf16[1,2,32,1024]{3,2,1,0:T(8,128)(2,1)S(1)}, bf16[1,2,32,1024]{3,2,1,0:T(8,128)(2,1)S(1)}, u32[]{:S(2)}, u32[]{:S(2)}) collective-permute-start(bf16[1,2,32,1024]{3,2,1,0:T(8,128)(2,1)S(1)} %select_bitcast_fusion), channel_id=1, source_target_pairs={{0,4},{2,6},{4,0},{6,2},{8,12},{10,14},{12,8},{14,10},{16,20},{18,... | collective-permute-start | bytes 393224 | tf_op jit(solution)/shard_map/ppermute | solution.py:77
  60.4 13.5 %collective-permute-start.2 = (bf16[1,2,32,1024]{3,2,1,0:T(8,128)(2,1)S(1)}, bf16[1,2,32,1024]{3,2,1,0:T(8,128)(2,1)S(1)}, u32[]{:S(2)}, u32[]{:S(2)}) collective-permute-start(bf16[1,2,32,1024]{3,2,1,0:T(8,128)(2,1)S(1)} %fusion.14), channel_id=1, source_target_pairs={{0,8},{2,10},{4,12},{6,14},{8,0},{10,2},{12,4},{14,6},{16,24},{18,... | collective-permute-start | bytes 393224 | tf_op jit(solution)/shard_map/ppermute | solution.py:77
  71.6 5.2 %collective-permute-start.10 = (bf16[1,2,32,1024]{3,2,1,0:T(8,128)(2,1)S(1)}, bf16[1,2,32,1024]{3,2,1,0:T(8,128)(2,1)S(1)}, u32[]{:S(2)}, u32[]{:S(2)}) collective-permute-start(bf16[1,2,32,1024]{3,2,1,0:T(8,128)(2,1)S(1)} %fusion.15), channel_id=1, source_target_pairs={{0,2},{2,0},{4,6},{6,4},{8,10},{10,8},{12,14},{14,12},{16,18},{18,... | collective-permute-start | bytes 393224 | tf_op jit(solution)/shard_map/ppermute | solution.py:77
  74.0 5.3 %collective-permute-start.3 = (bf16[1,32,1024]{2,1,0:T(8,128)(2,1)S(1)}, bf16[1,32,1024]{2,1,0:T(8,128)(2,1)S(1)}, u32[]{:S(2)}, u32[]{:S(2)}) collective-permute-start(bf16[1,32,1024]{2,1,0:T(8,128)(2,1)S(1)} %select_bitcast_fusion.5), channel_id=1, source_target_pairs={{0,16},{2,18},{4,20},{6,22},{8,24},{10,26},{12,28},{14,30},{16,0},... | collective-permute-start | bytes 196616 | tf_op jit(solution)/shard_map/ppermute | solution.py:77
  77.4 5.4 %collective-permute-start.20 = (bf16[1,32,1024]{2,1,0:T(8,128)(2,1)S(1)}, bf16[1,32,1024]{2,1,0:T(8,128)(2,1)S(1)}, u32[]{:S(2)}, u32[]{:S(2)}) collective-permute-start(bf16[1,32,1024]{2,1,0:T(8,128)(2,1)S(1)} %bitcast_select_fusion.14), channel_id=1, source_target_pairs={{0,8},{2,10},{4,12},{6,14},{8,0},{10,2},{12,4},{14,6},{16,24},{18,... | collective-permute-start | bytes 196616 | tf_op jit(solution)/shard_map/ppermute | solution.py:87
  77.5 5.4 %collective-permute-start.28 = (bf16[1,32,1024]{2,1,0:T(8,128)(2,1)S(1)}, bf16[1,32,1024]{2,1,0:T(8,128)(2,1)S(1)}, u32[]{:S(2)}, u32[]{:S(2)}) collective-permute-start(bf16[1,32,1024]{2,1,0:T(8,128)(2,1)S(1)} %bitcast_select_fusion.13), channel_id=1, source_target_pairs={{0,2},{2,0},{4,6},{6,4},{8,10},{10,8},{12,14},{14,12},{16,18},{18,... | collective-permute-start | bytes 196616 | tf_op jit(solution)/shard_map/ppermute | solution.py:87
  79.3 6.9 %collective-permute-start.4 = (bf16[1,32,1024]{2,1,0:T(8,128)(2,1)S(1)}, bf16[1,32,1024]{2,1,0:T(8,128)(2,1)S(1)}, u32[]{:S(2)}, u32[]{:S(2)}) collective-permute-start(bf16[1,32,1024]{2,1,0:T(8,128)(2,1)S(1)} %bitcast_select_fusion.16), channel_id=1, source_target_pairs={{0,16},{2,18},{4,20},{6,22},{8,24},{10,26},{12,28},{14,30},{16,0},... | collective-permute-start | bytes 196616 | tf_op jit(solution)/shard_map/ppermute | solution.py:87
  81.2 6.1 %collective-permute-start.12 = (bf16[1,32,1024]{2,1,0:T(8,128)(2,1)S(1)}, bf16[1,32,1024]{2,1,0:T(8,128)(2,1)S(1)}, u32[]{:S(2)}, u32[]{:S(2)}) collective-permute-start(bf16[1,32,1024]{2,1,0:T(8,128)(2,1)S(1)} %bitcast_select_fusion.15), channel_id=1, source_target_pairs={{0,4},{2,6},{4,0},{6,2},{8,12},{10,14},{12,8},{14,10},{16,20},{18,... | collective-permute-start | bytes 196616 | tf_op jit(solution)/shard_map/ppermute | solution.py:87
  82.8 7.1 %collective-permute-start.21 = (bf16[1,2,32,1024]{3,2,1,0:T(8,128)(2,1)S(1)}, bf16[1,2,32,1024]{3,2,1,0:T(8,128)(2,1)S(1)}, u32[]{:S(2)}, u32[]{:S(2)}) collective-permute-start(bf16[1,2,32,1024]{3,2,1,0:T(8,128)(2,1)S(1)} %maximum_bitcast_fusion.15), channel_id=1, source_target_pairs={{0,16},{2,18},{4,20},{6,22},{8,24},{10,26},{12,28},{14,30},{16,0},... | collective-permute-start | bytes 393224 | tf_op jit(solution)/shard_map/ppermute | solution.py:87
  83.0 8.1 %collective-permute-start.29 = (bf16[1,2,32,1024]{3,2,1,0:T(8,128)(2,1)S(1)}, bf16[1,2,32,1024]{3,2,1,0:T(8,128)(2,1)S(1)}, u32[]{:S(2)}, u32[]{:S(2)}) collective-permute-start(bf16[1,2,32,1024]{3,2,1,0:T(8,128)(2,1)S(1)} %maximum_bitcast_fusion.16), channel_id=1, source_target_pairs={{0,4},{2,6},{4,0},{6,2},{8,12},{10,14},{12,8},{14,10},{16,20},{18,... | collective-permute-start | bytes 393224 | tf_op jit(solution)/shard_map/ppermute | solution.py:87
  86.2 5.1 %collective-permute-start.5 = (bf16[1,2,32,1024]{3,2,1,0:T(8,128)(2,1)S(1)}, bf16[1,2,32,1024]{3,2,1,0:T(8,128)(2,1)S(1)}, u32[]{:S(2)}, u32[]{:S(2)}) collective-permute-start(bf16[1,2,32,1024]{3,2,1,0:T(8,128)(2,1)S(1)} %maximum_bitcast_fusion.13), channel_id=1, source_target_pairs={{0,8},{2,10},{4,12},{6,14},{8,0},{10,2},{12,4},{14,6},{16,24},{18,... | collective-permute-start | bytes 393224 | tf_op jit(solution)/shard_map/ppermute | solution.py:87
  87.3 6.4 %collective-permute-start.13 = (bf16[1,2,32,1024]{3,2,1,0:T(8,128)(2,1)S(1)}, bf16[1,2,32,1024]{3,2,1,0:T(8,128)(2,1)S(1)}, u32[]{:S(2)}, u32[]{:S(2)}) collective-permute-start(bf16[1,2,32,1024]{3,2,1,0:T(8,128)(2,1)S(1)} %maximum_bitcast_fusion.14), channel_id=1, source_target_pairs={{0,2},{2,0},{4,6},{6,4},{8,10},{10,8},{12,14},{14,12},{16,18},{18,... | collective-permute-start | bytes 393224 | tf_op jit(solution)/shard_map/ppermute | solution.py:87
  90.0 7.5 %collective-permute-start.22 = (bf16[1,2,2,32,1024]{4,3,2,1,0:T(8,128)(2,1)S(1)}, bf16[1,2,2,32,1024]{4,3,2,1,0:T(8,128)(2,1)S(1)}, u32[]{:S(2)}, u32[]{:S(2)}) collective-permute-start(bf16[1,2,2,32,1024]{4,3,2,1,0:T(8,128)(2,1)S(1)} %maximum_bitcast_fusion.11), channel_id=1, source_target_pairs={{0,2},{2,0},{4,6},{6,4},{8,10},{10,8},{12,14},{14,12},{16,18},{18,... | collective-permute-start | bytes 786440 | tf_op jit(solution)/shard_map/ppermute | solution.py:87
  91.2 9.3 %collective-permute-start.30 = (bf16[1,2,2,32,1024]{4,3,2,1,0:T(8,128)(2,1)S(1)}, bf16[1,2,2,32,1024]{4,3,2,1,0:T(8,128)(2,1)S(1)}, u32[]{:S(2)}, u32[]{:S(2)}) collective-permute-start(bf16[1,2,2,32,1024]{4,3,2,1,0:T(8,128)(2,1)S(1)} %maximum_bitcast_fusion.12), channel_id=1, source_target_pairs={{0,8},{2,10},{4,12},{6,14},{8,0},{10,2},{12,4},{14,6},{16,24},{18,... | collective-permute-start | bytes 786440 | tf_op jit(solution)/shard_map/ppermute | solution.py:87
  91.4 9.7 %collective-permute-start.6 = (bf16[1,2,2,32,1024]{4,3,2,1,0:T(8,128)(2,1)S(1)}, bf16[1,2,2,32,1024]{4,3,2,1,0:T(8,128)(2,1)S(1)}, u32[]{:S(2)}, u32[]{:S(2)}) collective-permute-start(bf16[1,2,2,32,1024]{4,3,2,1,0:T(8,128)(2,1)S(1)} %maximum_bitcast_fusion.9), channel_id=1, source_target_pairs={{0,4},{2,6},{4,0},{6,2},{8,12},{10,14},{12,8},{14,10},{16,20},{18,... | collective-permute-start | bytes 786440 | tf_op jit(solution)/shard_map/ppermute | solution.py:87
  93.7 26.4 %collective-permute-start.14 = (bf16[1,2,2,32,1024]{4,3,2,1,0:T(8,128)(2,1)S(1)}, bf16[1,2,2,32,1024]{4,3,2,1,0:T(8,128)(2,1)S(1)}, u32[]{:S(2)}, u32[]{:S(2)}) collective-permute-start(bf16[1,2,2,32,1024]{4,3,2,1,0:T(8,128)(2,1)S(1)} %maximum_bitcast_fusion.10), channel_id=1, source_target_pairs={{0,16},{2,18},{4,20},{6,22},{8,24},{10,26},{12,28},{14,30},{16,0},... | collective-permute-start | bytes 786440 | tf_op jit(solution)/shard_map/ppermute | solution.py:87
  97.6 22.8 %collective-permute-start.23 = (bf16[1,2,2,2,32,1024]{5,4,3,2,1,0:T(8,128)(2,1)S(1)}, bf16[1,2,2,2,32,1024]{5,4,3,2,1,0:T(8,128)(2,1)S(1)}, u32[]{:S(2)}, u32[]{:S(2)}) collective-permute-start(bf16[1,2,2,2,32,1024]{5,4,3,2,1,0:T(8,128)(2,1)S(1)} %maximum_bitcast_fusion.7), channel_id=1, source_target_pairs={{0,4},{2,6},{4,0},{6,2},{8,12},{10,14},{12,8},{14,10},{16,20},{18,... | collective-permute-start | bytes 1572872 | tf_op jit(solution)/shard_map/ppermute | solution.py:87
  100.6 40.2 %collective-permute-start.31 = (bf16[1,2,2,2,32,1024]{5,4,3,2,1,0:T(8,128)(2,1)S(1)}, bf16[1,2,2,2,32,1024]{5,4,3,2,1,0:T(8,128)(2,1)S(1)}, u32[]{:S(2)}, u32[]{:S(2)}) collective-permute-start(bf16[1,2,2,2,32,1024]{5,4,3,2,1,0:T(8,128)(2,1)S(1)} %maximum_bitcast_fusion.8), channel_id=1, source_target_pairs={{0,16},{2,18},{4,20},{6,22},{8,24},{10,26},{12,28},{14,30},{16,0},... | collective-permute-start | bytes 1572872 | tf_op jit(solution)/shard_map/ppermute | solution.py:87
  101.2 19.4 %collective-permute-start.7 = (bf16[1,2,2,2,32,1024]{5,4,3,2,1,0:T(8,128)(2,1)S(1)}, bf16[1,2,2,2,32,1024]{5,4,3,2,1,0:T(8,128)(2,1)S(1)}, u32[]{:S(2)}, u32[]{:S(2)}) collective-permute-start(bf16[1,2,2,2,32,1024]{5,4,3,2,1,0:T(8,128)(2,1)S(1)} %maximum_bitcast_fusion.5), channel_id=1, source_target_pairs={{0,2},{2,0},{4,6},{6,4},{8,10},{10,8},{12,14},{14,12},{16,18},{18,... | collective-permute-start | bytes 1572872 | tf_op jit(solution)/shard_map/ppermute | solution.py:87
  120.2 20.3 %collective-permute-start.15 = (bf16[1,2,2,2,32,1024]{5,4,3,2,1,0:T(8,128)(2,1)S(1)}, bf16[1,2,2,2,32,1024]{5,4,3,2,1,0:T(8,128)(2,1)S(1)}, u32[]{:S(2)}, u32[]{:S(2)}) collective-permute-start(bf16[1,2,2,2,32,1024]{5,4,3,2,1,0:T(8,128)(2,1)S(1)} %maximum_bitcast_fusion.6), channel_id=1, source_target_pairs={{0,8},{2,10},{4,12},{6,14},{8,0},{10,2},{12,4},{14,6},{16,24},{18,... | collective-permute-start | bytes 1572872 | tf_op jit(solution)/shard_map/ppermute | solution.py:87
  167.9 4.5 %collective-permute-start.35 = (f32[32]{0:T(128)S(1)}, f32[32]{0:T(128)S(1)}, u32[]{:S(2)}, u32[]{:S(2)}) collective-permute-start(f32[32]{0:T(128)S(1)} %fusion.25), channel_id=1, source_target_pairs={{0,6},{2,4},{4,2},{6,0},{8,14},{10,12},{12,10},{14,8},{16,22},{18,... | collective-permute-start | bytes 392 | tf_op jit(solution)/shard_map/ppermute | solution.py:33
  173.0 5.4 %collective-permute-start.38 = (f32[32]{0:T(128)S(1)}, f32[32]{0:T(128)S(1)}, u32[]{:S(2)}, u32[]{:S(2)}) collective-permute-start(f32[32]{0:T(128)S(1)} %fusion.38), channel_id=1, source_target_pairs={{0,24},{2,26},{4,28},{6,30},{8,16},{10,18},{12,20},{14,22},{16,8},... | collective-permute-start | bytes 392 | tf_op jit(solution)/shard_map/ppermute | solution.py:33
  (20 other events, 93.2 us)

commit v5 on v4

--- a/solution.py
+++ b/solution.py
@@ -6,7 +6,8 @@
 from jax.sharding import PartitionSpec as P
 
 L = 128
-GROUP = 8
+GROUP = 4
+CHUNK = 256
 REACH = L + 16
 
 EPS = 1e-06
@@ -101,7 +102,7 @@
     return jnp.stack(out)
 
 
-def correlate_kernel(meta_ref, blk_ref, ext_ref, corr_ref, power_ref):
+def correlate_kernel(meta_ref, blk_ref, ext_ref, corr_ref, power_ref, tmpl_ref, acc_ref):
     step = pl.program_id(0)
     chans = blk_ref.shape[2]
     width = ext_ref.shape[1]
@@ -110,7 +111,6 @@
     tap = lax.broadcasted_iota(jnp.int32, (L, REACH), 0)
     col = lax.broadcasted_iota(jnp.int32, (L, REACH), 1)
     lane = lax.broadcasted_iota(jnp.int32, (L, chans), 1)
-    pieces = []
     for g in range(group):
         idx = step * group + g
         first = meta_ref[4 * idx]
@@ -122,13 +122,17 @@
         chosen = jnp.dot(pick, rows, preferred_element_type=jnp.float32)
         chosen = jnp.where((lane >= lower) & (lane < upper), chosen, 0.0)
         power_ref[0, g : g + 1, :] = jnp.full((1, 128), jnp.sum(chosen * chosen), jnp.float32)
-        pieces.append(chosen.astype(jnp.bfloat16))
-    product = jnp.dot(
-        jnp.concatenate(pieces, axis=0), ext_ref[...], preferred_element_type=jnp.float32
-    )
-    for g in range(group):
-        rows = product[g * L : (g + 1) * L]
-        sheared = pltpu.roll(rows, width - (L - 1), 1, stride=1, stride_axis=0)
+        tmpl_ref[...] = chosen.astype(jnp.bfloat16)
+        acc_ref[...] = jnp.zeros_like(acc_ref)
+        for q in range(chans // CHUNK):
+            @pl.when((q * CHUNK < upper) & ((q + 1) * CHUNK > lower))
+            def _():
+                acc_ref[...] += jnp.dot(
+                    tmpl_ref[:, q * CHUNK : (q + 1) * CHUNK],
+                    ext_ref[q * CHUNK : (q + 1) * CHUNK, :],
+                    preferred_element_type=jnp.float32,
+                )
+        sheared = pltpu.roll(acc_ref[...], width - (L - 1), 1, stride=1, stride_axis=0)
         corr_ref[0, g : g + 1, :] = jnp.sum(sheared, axis=0, keepdims=True)[:, :lags]
 
 
@@ -154,6 +158,7 @@
             pl.BlockSpec((1, GROUP, lag_count), lambda i, m: (i, 0, 0)),
             pl.BlockSpec((1, GROUP, 128), lambda i, m: (i, 0, 0)),
         ],
+        scratch_shapes=[pltpu.VMEM((L, chans), jnp.bfloat16), pltpu.VMEM((L, width), jnp.float32)],
     )
     corr, power = pl.pallas_call(
         correlate_kernel,

time: 180 us -> 204 us (1.13)
  Pallas kernels: 19.6 us -> 39.8 us
  starting transfers between devices: 61.3 us -> 64.7 us
    pallas_call x1, Pallas kernels: 19.6 us -> 39.8 us  [correlate(): pl.pallas_call(correlate_kernel, grid_spec=grid_spec, out_shape=[jax.Shap...]
    ppermute x8, starting transfers between devices: 8.58 us -> 13 us  [group_sum(): got[d] = lax.ppermute(value, axis, pairs)]
  transfers between devices with their start and end apart: 41 -> 41, of which waited for: 20 -> 20; matrix products, arithmetic and copies ran while one was open for 8% -> 7% of each run, Pallas kernels for 0% -> 0%
where the time goes in v5:
time: 204 us
  waiting for transfers between devices  71.1 us (35%)
  starting transfers between devices  64.7 us (32%)
  Pallas kernels  39.8 us (20%)
  other arithmetic  14.9 us (7%)
  local copies, waits for them, and re-layouts  9.8 us (5%)
  between operations  2.09 us (1%)
    ppermute x32, waiting for transfers between devices, spread_blocks(): lax.ppermute(jnp.stack([v for _, v in items]), axis, [(i, i ^ mask) for i...  56.4 us
    ppermute x32, starting transfers between devices, spread_blocks(): lax.ppermute(jnp.stack([v for _, v in items]), axis, [(i, i ^ mask) for i...  50.4 us
    pallas_call x1, Pallas kernels, correlate(): pl.pallas_call(correlate_kernel, grid_spec=grid_spec, out_shape=[jax.Shap...  39.8 us
    ppermute x8, starting transfers between devices, group_sum(): got[d] = lax.ppermute(value, axis, pairs)  13 us
    ppermute x1, waiting for transfers between devices, from_behind(): return lax.ppermute(value, axis, pairs)  10.6 us
    select_n x16, other arithmetic, spread_blocks(): bufs[key] = jnp.where(holder, keeps[key], got[n])  5.2 us
    ppermute x8, waiting for transfers between devices, group_sum(): got[d] = lax.ppermute(value, axis, pairs)  4.17 us
  transfers between devices with their start and end apart: 41, of which 20 were waited for; matrix products, arithmetic and copies ran while one was open for 7% of the time, Pallas kernels for 0%

profile of v5, /device:TPU:0, one launch (start us, length us, event | category | flops | bytes accessed | tf_op | source)
XLA Modules:
  0.0 203.9 jit_solution(11791965046619280433)
XLA Ops:
  0.0 2.9 %copy.28 = bf16[1024,1024]{0,1:T(8,128)(2,1)S(1)} copy(bf16[1024,1024]{1,0:T(8,128)(2,1)} %param.4) | data formatting | bytes 4194304 | tf_op args[0]
  5.2 3.0 %collective-permute-start.16 = (bf16[1,2,2,2,32,1024]{5,4,1,0,3,2:T(8,128)(2,1)}, bf16[1,2,2,2,32,1024]{5,4,1,0,3,2:T(8,128)(2,1)}, u32[]{:S(2)}, u32[]{:S(2)}) collective-permute-start(bf16[1,2,2,2,32,1024]{5,4,1,0,3,2:T(8,128)(2,1)} %get-tuple-element.27), channel_id=1, source_target_pairs={{0,4},{2,6},{4,0},{6,2},{8,12},{10,14},{12,8},{14,10},{16,20},{18,... | collective-permute-start | bytes 1572872 | tf_op jit(solution)/shard_map/ppermute | solution.py:78
  9.3 2.6 %collective-permute-start.24 = (bf16[1,2,2,2,32,1024]{5,4,3,2,1,0:T(8,128)(2,1)}, bf16[1,2,2,2,32,1024]{5,4,3,2,1,0:T(8,128)(2,1)}, u32[]{:S(2)}, u32[]{:S(2)}) collective-permute-start(bf16[1,2,2,2,32,1024]{5,4,3,2,1,0:T(8,128)(2,1)} %bitcast.80), channel_id=1, source_target_pairs={{0,16},{2,18},{4,20},{6,22},{8,24},{10,26},{12,28},{14,30},{16,0},... | collective-permute-start | bytes 1572872 | tf_op jit(solution)/shard_map/ppermute | solution.py:78
  13.1 1.5 collective-permute-start
  14.8 1.6 collective-permute-start.8
  21.4 10.6 %collective-permute-done.32 = bf16[1024,128]{1,0:T(8,128)(2,1)S(1)} collective-permute-done((bf16[1024,128]{1,0:T(8,128)(2,1)}, bf16[1024,128]{1,0:T(8,128)(2,1)S(1)}, u32[]{:S(2)}, u32[]{:S(2)}) %collective-permute-start.32) | collective-permute-done | bytes 262176 | tf_op jit(solution)/shard_map/ppermute | solution.py:19
  36.8 1.5 collective-permute-start.17
  39.5 9.7 %collective-permute-start.25 = (bf16[1,2,2,32,1024]{4,3,2,1,0:T(8,128)(2,1)S(1)}, bf16[1,2,2,32,1024]{4,3,2,1,0:T(8,128)(2,1)S(1)}, u32[]{:S(2)}, u32[]{:S(2)}) collective-permute-start(bf16[1,2,2,32,1024]{4,3,2,1,0:T(8,128)(2,1)S(1)} %broadcast_select_fusion.16), channel_id=1, source_target_pairs={{0,8},{2,10},{4,12},{6,14},{8,0},{10,2},{12,4},{14,6},{16,24},{18,... | collective-permute-start | bytes 786440 | tf_op jit(solution)/shard_map/ppermute | solution.py:78
  50.6 3.4 %collective-permute-start.1 = (bf16[1,2,2,32,1024]{4,3,1,2,0:T(8,128)(2,1)S(1)}, bf16[1,2,2,32,1024]{4,3,1,2,0:T(8,128)(2,1)S(1)}, u32[]{:S(2)}, u32[]{:S(2)}) collective-permute-start(bf16[1,2,2,32,1024]{4,3,1,2,0:T(8,128)(2,1)S(1)} %fusion.5), channel_id=1, source_target_pairs={{0,4},{2,6},{4,0},{6,2},{8,12},{10,14},{12,8},{14,10},{16,20},{18,... | collective-permute-start | bytes 786440 | tf_op jit(solution)/shard_map/ppermute | solution.py:78
  55.3 3.0 %collective-permute-start.18 = (bf16[1,2,32,1024]{3,2,1,0:T(8,128)(2,1)S(1)}, bf16[1,2,32,1024]{3,2,1,0:T(8,128)(2,1)S(1)}, u32[]{:S(2)}, u32[]{:S(2)}) collective-permute-start(bf16[1,2,32,1024]{3,2,1,0:T(8,128)(2,1)S(1)} %select_bitcast_fusion.1), channel_id=1, source_target_pairs={{0,16},{2,18},{4,20},{6,22},{8,24},{10,26},{12,28},{14,30},{16,0},... | collective-permute-start | bytes 393224 | tf_op jit(solution)/shard_map/ppermute | solution.py:78
  58.3 2.0 collective-permute-start.26
  60.4 1.7 collective-permute-start.2
  62.0 9.5 %collective-permute-done.9 = bf16[1,2,2,32,1024]{4,3,1,2,0:T(8,128)(2,1)S(1)} collective-permute-done((bf16[1,2,2,32,1024]{4,3,1,2,0:T(8,128)(2,1)S(1)}, bf16[1,2,2,32,1024]{4,3,1,2,0:T(8,128)(2,1)S(1)}, u32[]{:S(2)}, u32[]{:S(2)}) %collective-permute-start.9) | collective-permute-done | bytes 262176 | tf_op jit(solution)/shard_map/ppermute | solution.py:78
  74.0 1.6 collective-permute-start.3
  79.3 1.7 collective-permute-start.4
  81.2 1.6 collective-permute-start.12
  83.0 1.7 collective-permute-start.29
  84.6 1.6 collective-permute-done.4
  88.3 1.6 collective-permute-done.21
  91.4 1.7 collective-permute-start.6
  93.7 1.5 collective-permute-start.14
  95.3 2.2 %collective-permute-done.22 = bf16[1,2,2,32,1024]{4,3,2,1,0:T(8,128)(2,1)S(1)} collective-permute-done((bf16[1,2,2,32,1024]{4,3,2,1,0:T(8,128)(2,1)S(1)}, bf16[1,2,2,32,1024]{4,3,2,1,0:T(8,128)(2,1)S(1)}, u32[]{:S(2)}, u32[]{:S(2)}) %collective-permute-start.22) | collective-permute-done | bytes 262176 | tf_op jit(solution)/shard_map/ppermute | solution.py:88
  98.8 1.6 collective-permute-done.30
  101.2 2.4 %collective-permute-start.7 = (bf16[1,2,2,2,32,1024]{5,4,3,2,1,0:T(8,128)(2,1)S(1)}, bf16[1,2,2,2,32,1024]{5,4,3,2,1,0:T(8,128)(2,1)S(1)}, u32[]{:S(2)}, u32[]{:S(2)}) collective-permute-start(bf16[1,2,2,2,32,1024]{5,4,3,2,1,0:T(8,128)(2,1)S(1)} %maximum_bitcast_fusion.5), channel_id=1, source_target_pairs={{0,2},{2,0},{4,6},{6,4},{8,10},{10,8},{12,14},{14,12},{16,18},{18,... | collective-permute-start | bytes 1572872 | tf_op jit(solution)/shard_map/ppermute | solution.py:88
  103.6 16.6 %collective-permute-done.14 = bf16[1,2,2,32,1024]{4,3,2,1,0:T(8,128)(2,1)S(1)} collective-permute-done((bf16[1,2,2,32,1024]{4,3,2,1,0:T(8,128)(2,1)S(1)}, bf16[1,2,2,32,1024]{4,3,2,1,0:T(8,128)(2,1)S(1)}, u32[]{:S(2)}, u32[]{:S(2)}) %collective-permute-start.14) | collective-permute-done | bytes 262176 | tf_op jit(solution)/shard_map/ppermute | solution.py:88
  120.9 19.7 %collective-permute-done.15 = bf16[1,2,2,2,32,1024]{5,4,3,2,1,0:T(8,128)(2,1)S(1)} collective-permute-done((bf16[1,2,2,2,32,1024]{5,4,3,2,1,0:T(8,128)(2,1)S(1)}, bf16[1,2,2,2,32,1024]{5,4,3,2,1,0:T(8,128)(2,1)S(1)}, u32[]{:S(2)}, u32[]{:S(2)}) %collective-permute-start.15) | collective-permute-done | bytes 524320 | tf_op jit(solution)/shard_map/ppermute | solution.py:88
  141.5 2.3 %pad_maximum_fusion.blk_ref = bf16[2,1024,1024]{2,1,0:T(8,128)(2,1)} fusion(bf16[1,1024,1024]{2,1,0:T(8,128)(2,1)S(1)} %get-tuple-element.66, bf16[1,1024,1024]{2,1,0:T(8,128)(2,1)S(1)} %get-tuple-element.65), kind=kLoop, calls=%fused_computation.4 | loop fusion | flops 2097152 | bytes 8388608 | tf_op jit(solution)/shard_map/stack | solution.py:102
  143.8 39.8 %shard_map.46 = (f32[8,4,1024]{2,1,0:T(4,128)}, f32[8,4,128]{2,1,0:T(4,128)}) custom-call(s32[128]{0:T(128)} %reshape.232.meta_ref, bf16[2,1024,1024]{2,1,0:T(8,128)(2,1)} %pad_maximum_fusion.blk_ref, bf16[1024,1152]{1,0:T(8,128)(2,1)} %copy-done.7), custom_call_target="tpu_custom_call" | custom-call | flops 10871635968 | bytes 6684672 | tf_op jit(solution)/shard_map/pallas_call | solution.py:163
  184.5 5.0 %collective-permute-start.33 = (f32[2,32,1024]{2,1,0:T(8,128)S(1)}, f32[2,32,1024]{2,1,0:T(8,128)S(1)}, u32[]{:S(2)}, u32[]{:S(2)}) collective-permute-start(f32[2,32,1024]{2,1,0:T(8,128)S(1)} %pad_maximum_fusion.10), channel_id=1, source_target_pairs={{0,1},{1,0},{2,3},{3,2},{4,5},{5,4},{6,7},{7,6},{8,9},{9,8},{10,11... | collective-permute-start | bytes 786440 | tf_op jit(solution)/shard_map/ppermute | solution.py:34
  192.5 2.9 %collective-permute-start.37 = (f32[32]{0:T(128)S(1)}, f32[32]{0:T(128)S(1)}, u32[]{:S(2)}, u32[]{:S(2)}) collective-permute-start(f32[32]{0:T(128)S(1)} %fusion.25), channel_id=1, source_target_pairs={{0,2},{2,0},{4,6},{6,4},{8,10},{10,8},{12,14},{14,12},{16,18},{18,... | collective-permute-start | bytes 392 | tf_op jit(solution)/shard_map/ppermute | solution.py:34
  197.0 1.6 collective-permute-start.38
  198.5 2.9 %collective-permute-start.40 = (f32[32]{0:T(128)S(1)}, f32[32]{0:T(128)S(1)}, u32[]{:S(2)}, u32[]{:S(2)}) collective-permute-start(f32[32]{0:T(128)S(1)} %fusion.38), channel_id=1, source_target_pairs={{0,8},{2,10},{4,12},{6,14},{8,0},{10,2},{12,4},{14,6},{16,24},{18,... | collective-permute-start | bytes 392 | tf_op jit(solution)/shard_map/ppermute | solution.py:34
  (181 shorter events, 39.1 us)
Async XLA Ops:
  5.2 29.8 %collective-permute-start.16 = (bf16[1,2,2,2,32,1024]{5,4,1,0,3,2:T(8,128)(2,1)}, bf16[1,2,2,2,32,1024]{5,4,1,0,3,2:T(8,128)(2,1)}, u32[]{:S(2)}, u32[]{:S(2)}) collective-permute-start(bf16[1,2,2,2,32,1024]{5,4,1,0,3,2:T(8,128)(2,1)} %get-tuple-element.27), channel_id=1, source_target_pairs={{0,4},{2,6},{4,0},{6,2},{8,12},{10,14},{12,8},{14,10},{16,20},{18,... | collective-permute-start | bytes 1572872 | tf_op jit(solution)/shard_map/ppermute | solution.py:78
  9.3 29.1 %collective-permute-start.24 = (bf16[1,2,2,2,32,1024]{5,4,3,2,1,0:T(8,128)(2,1)}, bf16[1,2,2,2,32,1024]{5,4,3,2,1,0:T(8,128)(2,1)}, u32[]{:S(2)}, u32[]{:S(2)}) collective-permute-start(bf16[1,2,2,2,32,1024]{5,4,3,2,1,0:T(8,128)(2,1)} %bitcast.80), channel_id=1, source_target_pairs={{0,16},{2,18},{4,20},{6,22},{8,24},{10,26},{12,28},{14,30},{16,0},... | collective-permute-start | bytes 1572872 | tf_op jit(solution)/shard_map/ppermute | solution.py:78
  13.1 36.1 %collective-permute-start = (bf16[1,2,2,2,32,1024]{5,4,0,1,2,3:T(8,128)(2,1)}, bf16[1,2,2,2,32,1024]{5,4,0,1,2,3:T(8,128)(2,1)}, u32[]{:S(2)}, u32[]{:S(2)}) collective-permute-start(bf16[1,2,2,2,32,1024]{5,4,0,1,2,3:T(8,128)(2,1)} %get-tuple-element.18), channel_id=1, source_target_pairs={{0,2},{2,0},{4,6},{6,4},{8,10},{10,8},{12,14},{14,12},{16,18},{18,... | collective-permute-start | bytes 1572872 | tf_op jit(solution)/shard_map/ppermute | solution.py:78
  14.8 39.2 %collective-permute-start.8 = (bf16[1,2,2,2,32,1024]{5,4,3,2,1,0:T(8,128)(2,1)S(1)}, bf16[1,2,2,2,32,1024]{5,4,3,2,1,0:T(8,128)(2,1)}, u32[]{:S(2)}, u32[]{:S(2)}) collective-permute-start(bf16[1,2,2,2,32,1024]{5,4,3,2,1,0:T(8,128)(2,1)S(1)} %get-tuple-element.23), channel_id=1, source_target_pairs={{0,8},{2,10},{4,12},{6,14},{8,0},{10,2},{12,4},{14,6},{16,24},{18,... | collective-permute-start | bytes 1572872 | tf_op jit(solution)/shard_map/ppermute | solution.py:78
  17.2 14.9 %collective-permute-start.32 = (bf16[1024,128]{1,0:T(8,128)(2,1)}, bf16[1024,128]{1,0:T(8,128)(2,1)S(1)}, u32[]{:S(2)}, u32[]{:S(2)}) collective-permute-start(bf16[1024,128]{1,0:T(8,128)(2,1)} %slice.283), channel_id=1, source_target_pairs={{2,0},{4,2},{6,4},{8,6},{10,8},{12,10},{14,12},{16,14},{18,16},{20... | collective-permute-start | bytes 786440 | tf_op jit(solution)/shard_map/ppermute | solution.py:19
  36.8 18.4 %collective-permute-start.17 = (bf16[1,2,2,32,1024]{4,3,2,1,0:T(8,128)(2,1)S(1)}, bf16[1,2,2,32,1024]{4,3,2,1,0:T(8,128)(2,1)S(1)}, u32[]{:S(2)}, u32[]{:S(2)}) collective-permute-start(bf16[1,2,2,32,1024]{4,3,2,1,0:T(8,128)(2,1)S(1)} %fusion.7), channel_id=1, source_target_pairs={{0,2},{2,0},{4,6},{6,4},{8,10},{10,8},{12,14},{14,12},{16,18},{18,... | collective-permute-start | bytes 786440 | tf_op jit(solution)/shard_map/ppermute | solution.py:78
  39.5 18.8 %collective-permute-start.25 = (bf16[1,2,2,32,1024]{4,3,2,1,0:T(8,128)(2,1)S(1)}, bf16[1,2,2,32,1024]{4,3,2,1,0:T(8,128)(2,1)S(1)}, u32[]{:S(2)}, u32[]{:S(2)}) collective-permute-start(bf16[1,2,2,32,1024]{4,3,2,1,0:T(8,128)(2,1)S(1)} %broadcast_select_fusion.16), channel_id=1, source_target_pairs={{0,8},{2,10},{4,12},{6,14},{8,0},{10,2},{12,4},{14,6},{16,24},{18,... | collective-permute-start | bytes 786440 | tf_op jit(solution)/shard_map/ppermute | solution.py:78
  50.6 9.7 %collective-permute-start.1 = (bf16[1,2,2,32,1024]{4,3,1,2,0:T(8,128)(2,1)S(1)}, bf16[1,2,2,32,1024]{4,3,1,2,0:T(8,128)(2,1)S(1)}, u32[]{:S(2)}, u32[]{:S(2)}) collective-permute-start(bf16[1,2,2,32,1024]{4,3,1,2,0:T(8,128)(2,1)S(1)} %fusion.5), channel_id=1, source_target_pairs={{0,4},{2,6},{4,0},{6,2},{8,12},{10,14},{12,8},{14,10},{16,20},{18,... | collective-permute-start | bytes 786440 | tf_op jit(solution)/shard_map/ppermute | solution.py:78
  55.1 16.4 %collective-permute-start.9 = (bf16[1,2,2,32,1024]{4,3,1,2,0:T(8,128)(2,1)S(1)}, bf16[1,2,2,32,1024]{4,3,1,2,0:T(8,128)(2,1)S(1)}, u32[]{:S(2)}, u32[]{:S(2)}) collective-permute-start(bf16[1,2,2,32,1024]{4,3,1,2,0:T(8,128)(2,1)S(1)} %fusion.6), channel_id=1, source_target_pairs={{0,16},{2,18},{4,20},{6,22},{8,24},{10,26},{12,28},{14,30},{16,0},... | collective-permute-start | bytes 786440 | tf_op jit(solution)/shard_map/ppermute | solution.py:78
  55.3 17.7 %collective-permute-start.18 = (bf16[1,2,32,1024]{3,2,1,0:T(8,128)(2,1)S(1)}, bf16[1,2,32,1024]{3,2,1,0:T(8,128)(2,1)S(1)}, u32[]{:S(2)}, u32[]{:S(2)}) collective-permute-start(bf16[1,2,32,1024]{3,2,1,0:T(8,128)(2,1)S(1)} %select_bitcast_fusion.1), channel_id=1, source_target_pairs={{0,16},{2,18},{4,20},{6,22},{8,24},{10,26},{12,28},{14,30},{16,0},... | collective-permute-start | bytes 393224 | tf_op jit(solution)/shard_map/ppermute | solution.py:78
  58.3 14.8 %collective-permute-start.26 = (bf16[1,2,32,1024]{3,2,1,0:T(8,128)(2,1)S(1)}, bf16[1,2,32,1024]{3,2,1,0:T(8,128)(2,1)S(1)}, u32[]{:S(2)}, u32[]{:S(2)}) collective-permute-start(bf16[1,2,32,1024]{3,2,1,0:T(8,128)(2,1)S(1)} %select_bitcast_fusion), channel_id=1, source_target_pairs={{0,4},{2,6},{4,0},{6,2},{8,12},{10,14},{12,8},{14,10},{16,20},{18,... | collective-permute-start | bytes 393224 | tf_op jit(solution)/shard_map/ppermute | solution.py:78
  60.4 13.5 %collective-permute-start.2 = (bf16[1,2,32,1024]{3,2,1,0:T(8,128)(2,1)S(1)}, bf16[1,2,32,1024]{3,2,1,0:T(8,128)(2,1)S(1)}, u32[]{:S(2)}, u32[]{:S(2)}) collective-permute-start(bf16[1,2,32,1024]{3,2,1,0:T(8,128)(2,1)S(1)} %fusion.14), channel_id=1, source_target_pairs={{0,8},{2,10},{4,12},{6,14},{8,0},{10,2},{12,4},{14,6},{16,24},{18,... | collective-permute-start | bytes 393224 | tf_op jit(solution)/shard_map/ppermute | solution.py:78
  71.6 5.2 %collective-permute-start.10 = (bf16[1,2,32,1024]{3,2,1,0:T(8,128)(2,1)S(1)}, bf16[1,2,32,1024]{3,2,1,0:T(8,128)(2,1)S(1)}, u32[]{:S(2)}, u32[]{:S(2)}) collective-permute-start(bf16[1,2,32,1024]{3,2,1,0:T(8,128)(2,1)S(1)} %fusion.15), channel_id=1, source_target_pairs={{0,2},{2,0},{4,6},{6,4},{8,10},{10,8},{12,14},{14,12},{16,18},{18,... | collective-permute-start | bytes 393224 | tf_op jit(solution)/shard_map/ppermute | solution.py:78
  74.0 5.3 %collective-permute-start.3 = (bf16[1,32,1024]{2,1,0:T(8,128)(2,1)S(1)}, bf16[1,32,1024]{2,1,0:T(8,128)(2,1)S(1)}, u32[]{:S(2)}, u32[]{:S(2)}) collective-permute-start(bf16[1,32,1024]{2,1,0:T(8,128)(2,1)S(1)} %select_bitcast_fusion.5), channel_id=1, source_target_pairs={{0,16},{2,18},{4,20},{6,22},{8,24},{10,26},{12,28},{14,30},{16,0},... | collective-permute-start | bytes 196616 | tf_op jit(solution)/shard_map/ppermute | solution.py:78
  77.4 5.4 %collective-permute-start.20 = (bf16[1,32,1024]{2,1,0:T(8,128)(2,1)S(1)}, bf16[1,32,1024]{2,1,0:T(8,128)(2,1)S(1)}, u32[]{:S(2)}, u32[]{:S(2)}) collective-permute-start(bf16[1,32,1024]{2,1,0:T(8,128)(2,1)S(1)} %bitcast_select_fusion.14), channel_id=1, source_target_pairs={{0,8},{2,10},{4,12},{6,14},{8,0},{10,2},{12,4},{14,6},{16,24},{18,... | collective-permute-start | bytes 196616 | tf_op jit(solution)/shard_map/ppermute | solution.py:88
  77.5 5.4 %collective-permute-start.28 = (bf16[1,32,1024]{2,1,0:T(8,128)(2,1)S(1)}, bf16[1,32,1024]{2,1,0:T(8,128)(2,1)S(1)}, u32[]{:S(2)}, u32[]{:S(2)}) collective-permute-start(bf16[1,32,1024]{2,1,0:T(8,128)(2,1)S(1)} %bitcast_select_fusion.13), channel_id=1, source_target_pairs={{0,2},{2,0},{4,6},{6,4},{8,10},{10,8},{12,14},{14,12},{16,18},{18,... | collective-permute-start | bytes 196616 | tf_op jit(solution)/shard_map/ppermute | solution.py:88
  79.3 6.9 %collective-permute-start.4 = (bf16[1,32,1024]{2,1,0:T(8,128)(2,1)S(1)}, bf16[1,32,1024]{2,1,0:T(8,128)(2,1)S(1)}, u32[]{:S(2)}, u32[]{:S(2)}) collective-permute-start(bf16[1,32,1024]{2,1,0:T(8,128)(2,1)S(1)} %bitcast_select_fusion.16), channel_id=1, source_target_pairs={{0,16},{2,18},{4,20},{6,22},{8,24},{10,26},{12,28},{14,30},{16,0},... | collective-permute-start | bytes 196616 | tf_op jit(solution)/shard_map/ppermute | solution.py:88
  81.2 6.1 %collective-permute-start.12 = (bf16[1,32,1024]{2,1,0:T(8,128)(2,1)S(1)}, bf16[1,32,1024]{2,1,0:T(8,128)(2,1)S(1)}, u32[]{:S(2)}, u32[]{:S(2)}) collective-permute-start(bf16[1,32,1024]{2,1,0:T(8,128)(2,1)S(1)} %bitcast_select_fusion.15), channel_id=1, source_target_pairs={{0,4},{2,6},{4,0},{6,2},{8,12},{10,14},{12,8},{14,10},{16,20},{18,... | collective-permute-start | bytes 196616 | tf_op jit(solution)/shard_map/ppermute | solution.py:88
  82.8 7.1 %collective-permute-start.21 = (bf16[1,2,32,1024]{3,2,1,0:T(8,128)(2,1)S(1)}, bf16[1,2,32,1024]{3,2,1,0:T(8,128)(2,1)S(1)}, u32[]{:S(2)}, u32[]{:S(2)}) collective-permute-start(bf16[1,2,32,1024]{3,2,1,0:T(8,128)(2,1)S(1)} %maximum_bitcast_fusion.15), channel_id=1, source_target_pairs={{0,16},{2,18},{4,20},{6,22},{8,24},{10,26},{12,28},{14,30},{16,0},... | collective-permute-start | bytes 393224 | tf_op jit(solution)/shard_map/ppermute | solution.py:88
  83.0 8.1 %collective-permute-start.29 = (bf16[1,2,32,1024]{3,2,1,0:T(8,128)(2,1)S(1)}, bf16[1,2,32,1024]{3,2,1,0:T(8,128)(2,1)S(1)}, u32[]{:S(2)}, u32[]{:S(2)}) collective-permute-start(bf16[1,2,32,1024]{3,2,1,0:T(8,128)(2,1)S(1)} %maximum_bitcast_fusion.16), channel_id=1, source_target_pairs={{0,4},{2,6},{4,0},{6,2},{8,12},{10,14},{12,8},{14,10},{16,20},{18,... | collective-permute-start | bytes 393224 | tf_op jit(solution)/shard_map/ppermute | solution.py:88
  86.2 5.1 %collective-permute-start.5 = (bf16[1,2,32,1024]{3,2,1,0:T(8,128)(2,1)S(1)}, bf16[1,2,32,1024]{3,2,1,0:T(8,128)(2,1)S(1)}, u32[]{:S(2)}, u32[]{:S(2)}) collective-permute-start(bf16[1,2,32,1024]{3,2,1,0:T(8,128)(2,1)S(1)} %maximum_bitcast_fusion.13), channel_id=1, source_target_pairs={{0,8},{2,10},{4,12},{6,14},{8,0},{10,2},{12,4},{14,6},{16,24},{18,... | collective-permute-start | bytes 393224 | tf_op jit(solution)/shard_map/ppermute | solution.py:88
  87.3 6.4 %collective-permute-start.13 = (bf16[1,2,32,1024]{3,2,1,0:T(8,128)(2,1)S(1)}, bf16[1,2,32,1024]{3,2,1,0:T(8,128)(2,1)S(1)}, u32[]{:S(2)}, u32[]{:S(2)}) collective-permute-start(bf16[1,2,32,1024]{3,2,1,0:T(8,128)(2,1)S(1)} %maximum_bitcast_fusion.14), channel_id=1, source_target_pairs={{0,2},{2,0},{4,6},{6,4},{8,10},{10,8},{12,14},{14,12},{16,18},{18,... | collective-permute-start | bytes 393224 | tf_op jit(solution)/shard_map/ppermute | solution.py:88
  90.0 7.5 %collective-permute-start.22 = (bf16[1,2,2,32,1024]{4,3,2,1,0:T(8,128)(2,1)S(1)}, bf16[1,2,2,32,1024]{4,3,2,1,0:T(8,128)(2,1)S(1)}, u32[]{:S(2)}, u32[]{:S(2)}) collective-permute-start(bf16[1,2,2,32,1024]{4,3,2,1,0:T(8,128)(2,1)S(1)} %maximum_bitcast_fusion.11), channel_id=1, source_target_pairs={{0,2},{2,0},{4,6},{6,4},{8,10},{10,8},{12,14},{14,12},{16,18},{18,... | collective-permute-start | bytes 786440 | tf_op jit(solution)/shard_map/ppermute | solution.py:88
  91.2 9.3 %collective-permute-start.30 = (bf16[1,2,2,32,1024]{4,3,2,1,0:T(8,128)(2,1)S(1)}, bf16[1,2,2,32,1024]{4,3,2,1,0:T(8,128)(2,1)S(1)}, u32[]{:S(2)}, u32[]{:S(2)}) collective-permute-start(bf16[1,2,2,32,1024]{4,3,2,1,0:T(8,128)(2,1)S(1)} %maximum_bitcast_fusion.12), channel_id=1, source_target_pairs={{0,8},{2,10},{4,12},{6,14},{8,0},{10,2},{12,4},{14,6},{16,24},{18,... | collective-permute-start | bytes 786440 | tf_op jit(solution)/shard_map/ppermute | solution.py:88
  91.4 9.7 %collective-permute-start.6 = (bf16[1,2,2,32,1024]{4,3,2,1,0:T(8,128)(2,1)S(1)}, bf16[1,2,2,32,1024]{4,3,2,1,0:T(8,128)(2,1)S(1)}, u32[]{:S(2)}, u32[]{:S(2)}) collective-permute-start(bf16[1,2,2,32,1024]{4,3,2,1,0:T(8,128)(2,1)S(1)} %maximum_bitcast_fusion.9), channel_id=1, source_target_pairs={{0,4},{2,6},{4,0},{6,2},{8,12},{10,14},{12,8},{14,10},{16,20},{18,... | collective-permute-start | bytes 786440 | tf_op jit(solution)/shard_map/ppermute | solution.py:88
  93.7 26.4 %collective-permute-start.14 = (bf16[1,2,2,32,1024]{4,3,2,1,0:T(8,128)(2,1)S(1)}, bf16[1,2,2,32,1024]{4,3,2,1,0:T(8,128)(2,1)S(1)}, u32[]{:S(2)}, u32[]{:S(2)}) collective-permute-start(bf16[1,2,2,32,1024]{4,3,2,1,0:T(8,128)(2,1)S(1)} %maximum_bitcast_fusion.10), channel_id=1, source_target_pairs={{0,16},{2,18},{4,20},{6,22},{8,24},{10,26},{12,28},{14,30},{16,0},... | collective-permute-start | bytes 786440 | tf_op jit(solution)/shard_map/ppermute | solution.py:88
  97.6 22.8 %collective-permute-start.23 = (bf16[1,2,2,2,32,1024]{5,4,3,2,1,0:T(8,128)(2,1)S(1)}, bf16[1,2,2,2,32,1024]{5,4,3,2,1,0:T(8,128)(2,1)S(1)}, u32[]{:S(2)}, u32[]{:S(2)}) collective-permute-start(bf16[1,2,2,2,32,1024]{5,4,3,2,1,0:T(8,128)(2,1)S(1)} %maximum_bitcast_fusion.7), channel_id=1, source_target_pairs={{0,4},{2,6},{4,0},{6,2},{8,12},{10,14},{12,8},{14,10},{16,20},{18,... | collective-permute-start | bytes 1572872 | tf_op jit(solution)/shard_map/ppermute | solution.py:88
  100.6 40.2 %collective-permute-start.31 = (bf16[1,2,2,2,32,1024]{5,4,3,2,1,0:T(8,128)(2,1)S(1)}, bf16[1,2,2,2,32,1024]{5,4,3,2,1,0:T(8,128)(2,1)S(1)}, u32[]{:S(2)}, u32[]{:S(2)}) collective-permute-start(bf16[1,2,2,2,32,1024]{5,4,3,2,1,0:T(8,128)(2,1)S(1)} %maximum_bitcast_fusion.8), channel_id=1, source_target_pairs={{0,16},{2,18},{4,20},{6,22},{8,24},{10,26},{12,28},{14,30},{16,0},... | collective-permute-start | bytes 1572872 | tf_op jit(solution)/shard_map/ppermute | solution.py:88
  101.2 19.4 %collective-permute-start.7 = (bf16[1,2,2,2,32,1024]{5,4,3,2,1,0:T(8,128)(2,1)S(1)}, bf16[1,2,2,2,32,1024]{5,4,3,2,1,0:T(8,128)(2,1)S(1)}, u32[]{:S(2)}, u32[]{:S(2)}) collective-permute-start(bf16[1,2,2,2,32,1024]{5,4,3,2,1,0:T(8,128)(2,1)S(1)} %maximum_bitcast_fusion.5), channel_id=1, source_target_pairs={{0,2},{2,0},{4,6},{6,4},{8,10},{10,8},{12,14},{14,12},{16,18},{18,... | collective-permute-start | bytes 1572872 | tf_op jit(solution)/shard_map/ppermute | solution.py:88
  120.2 20.3 %collective-permute-start.15 = (bf16[1,2,2,2,32,1024]{5,4,3,2,1,0:T(8,128)(2,1)S(1)}, bf16[1,2,2,2,32,1024]{5,4,3,2,1,0:T(8,128)(2,1)S(1)}, u32[]{:S(2)}, u32[]{:S(2)}) collective-permute-start(bf16[1,2,2,2,32,1024]{5,4,3,2,1,0:T(8,128)(2,1)S(1)} %maximum_bitcast_fusion.6), channel_id=1, source_target_pairs={{0,8},{2,10},{4,12},{6,14},{8,0},{10,2},{12,4},{14,6},{16,24},{18,... | collective-permute-start | bytes 1572872 | tf_op jit(solution)/shard_map/ppermute | solution.py:88
  184.5 7.1 %collective-permute-start.33 = (f32[2,32,1024]{2,1,0:T(8,128)S(1)}, f32[2,32,1024]{2,1,0:T(8,128)S(1)}, u32[]{:S(2)}, u32[]{:S(2)}) collective-permute-start(f32[2,32,1024]{2,1,0:T(8,128)S(1)} %pad_maximum_fusion.10), channel_id=1, source_target_pairs={{0,1},{1,0},{2,3},{3,2},{4,5},{5,4},{6,7},{7,6},{8,9},{9,8},{10,11... | collective-permute-start | bytes 786440 | tf_op jit(solution)/shard_map/ppermute | solution.py:34
  197.0 5.4 %collective-permute-start.38 = (f32[32]{0:T(128)S(1)}, f32[32]{0:T(128)S(1)}, u32[]{:S(2)}, u32[]{:S(2)}) collective-permute-start(f32[32]{0:T(128)S(1)} %fusion.38), channel_id=1, source_target_pairs={{0,24},{2,26},{4,28},{6,30},{8,16},{10,18},{12,20},{14,22},{16,8},... | collective-permute-start | bytes 392 | tf_op jit(solution)/shard_map/ppermute | solution.py:34
  (20 other events, 95.1 us)

commit v6 on v3

--- a/solution.py
+++ b/solution.py
@@ -78,8 +78,8 @@
     for s in reversed(range(nbits)):
         sends = {}
         for (p, r), buf in bufs.items():
-            sends.setdefault(orders[p][s], []).append(((p, r), buf))
-        for mask, items in sends.items():
+            sends.setdefault((r if s == 0 else 0, orders[p][s]), []).append(((p, r), buf))
+        for (_, mask), items in sorted(sends.items()):
             got = lax.ppermute(jnp.stack([v for _, v in items]), axis, [(i, i ^ mask) for i in range(size)])
             bit = (place // mask) % 2
             for n, (key, buf) in enumerate(items):
@@ -199,7 +199,10 @@
     summed = summed + jnp.dot(masks, low, preferred_element_type=jnp.float32)
     energy_local = window_sum(summed, L, lag_count)
 
-    corr_local, local_power = correlate(meta.astype(jnp.int32), blocks, extended, count)
+    meta = meta.astype(jnp.int32).reshape(rounds, -1)
+    pieces = [correlate(meta[r], blocks[r : r + 1], extended, count) for r in range(rounds)]
+    corr_local = jnp.concatenate([c for c, _ in pieces])
+    local_power = jnp.concatenate([p for _, p in pieces])
     tmpl_power = group_sum(local_power, "sec")
     both = group_sum(jnp.stack([corr_local, energy_local]), "sec")
     corr, energy = both[0], both[1]

time: 174 us -> 158 us (0.908)
  starting transfers between devices: 69.5 us -> 52.3 us
  waiting for transfers between devices: 51.1 us -> 44 us
  Pallas kernels: 19.9 us -> 23.6 us
  local copies, waits for them, and re-layouts: 12.4 us -> 15.1 us
    ppermute x32 -> x36, starting transfers between devices: 59.7 us -> 42.5 us  [spread_blocks(): lax.ppermute(jnp.stack([v for _, v in items]), axis, [(i, i ^ mask) for i...]
    ppermute x1, waiting for transfers between devices: 4.74 us -> 0.01 us  [from_behind(): return lax.ppermute(value, axis, pairs)]
    pallas_call x1 -> x2, Pallas kernels: 19.9 us -> 23.6 us  [correlate(): pl.pallas_call(correlate_kernel, grid_spec=grid_spec, out_shape=[jax.Shap...]
    ppermute x32 -> x36, waiting for transfers between devices: 41.1 us -> 38.8 us  [spread_blocks(): lax.ppermute(jnp.stack([v for _, v in items]), axis, [(i, i ^ mask) for i...]
    another operation x56 -> x52, other arithmetic: 4.42 us -> 4.2 us  [spread_blocks(): jnp.stack([v for _, v in items])]
    unnamed x18 -> x20, local copies, waits for them, and re-layouts: 4.51 us -> 4.37 us
  transfers between devices with their start and end apart: 41 -> 45, of which waited for: 17 -> 21; matrix products, arithmetic and copies ran while one was open for 11% -> 18% of each run, Pallas kernels for 0% -> 7%
where the time goes in v6:
time: 158 us; the launch traced here: 157 us
  starting transfers between devices  52.3 us (33%)
  waiting for transfers between devices  44 us (28%)
  Pallas kernels  23.6 us (15%)
  other arithmetic  18 us (11%)
  local copies, waits for them, and re-layouts  15.1 us (10%)
  between operations  2.59 us (2%)
    ppermute x36, starting transfers between devices, spread_blocks(): lax.ppermute(jnp.stack([v for _, v in items]), axis, [(i, i ^ mask) for i...  42.5 us
    ppermute x36, waiting for transfers between devices, spread_blocks(): lax.ppermute(jnp.stack([v for _, v in items]), axis, [(i, i ^ mask) for i...  38.8 us
    pallas_call x2, Pallas kernels, correlate(): pl.pallas_call(correlate_kernel, grid_spec=grid_spec, out_shape=[jax.Shap...  23.6 us
    ppermute x8, starting transfers between devices, group_sum(): got[d] = lax.ppermute(value, axis, pairs)  8.57 us
    select_n x18, other arithmetic, spread_blocks(): bufs[key] = jnp.where(holder, keeps[key], got[n])  5.69 us
    ppermute x8, waiting for transfers between devices, group_sum(): got[d] = lax.ppermute(value, axis, pairs)  5.15 us
    unnamed x20, local copies, waits for them, and re-layouts  4.37 us
    another operation x52, other arithmetic, spread_blocks(): jnp.stack([v for _, v in items])  4.2 us
  transfers between devices with their start and end apart: 45, of which 21 were waited for; matrix products, arithmetic and copies ran while one was open for 18% of the time, Pallas kernels for 7%

profile of v6, /device:TPU:0, one launch (start us, length us, event | category | flops | bytes accessed | tf_op | source)
XLA Modules:
  0.0 157.0 jit_solution(17145707625160787396)
XLA Ops:
  0.0 1.7 %slice.719 = bf16[1024,128]{1,0:T(8,128)(2,1)} slice(bf16[1024,1024]{1,0:T(8,128)(2,1)} %param.4), slice={[0:1024], [0:128]} | slice | bytes 524288 | tf_op jit(solution)/shard_map/slice | solution.py:181
  3.0 2.9 %copy.32 = bf16[1024,1024]{0,1:T(8,128)(2,1)S(1)} copy(bf16[1024,1024]{1,0:T(8,128)(2,1)} %param.4) | data formatting | bytes 4194304 | tf_op args[0]
  8.0 7.0 %collective-permute-start.24 = (bf16[2,2,2,2,16,1024]{5,4,3,2,1,0:T(8,128)(2,1)}, bf16[2,2,2,2,16,1024]{5,4,3,2,1,0:T(8,128)(2,1)}, u32[]{:S(2)}, u32[]{:S(2)}) collective-permute-start(bf16[2,2,2,2,16,1024]{5,4,3,2,1,0:T(8,128)(2,1)} %pad_maximum_fusion.3), channel_id=1, source_target_pairs={{0,16},{2,18},{4,20},{6,22},{8,24},{10,26},{12,28},{14,30},{16,0},... | collective-permute-start | bytes 1572872 | tf_op jit(solution)/shard_map/ppermute | solution.py:73
  15.9 1.6 %collective-permute-start.16 = (bf16[2,2,2,2,16,1024]{5,4,3,2,1,0:T(8,128)(2,1)}, bf16[2,2,2,2,16,1024]{5,4,3,2,1,0:T(8,128)(2,1)}, u32[]{:S(2)}, u32[]{:S(2)}) collective-permute-start(bf16[2,2,2,2,16,1024]{5,4,3,2,1,0:T(8,128)(2,1)} %pad_maximum_fusion.2), channel_id=1, source_target_pairs={{0,8},{2,10},{4,12},{6,14},{8,0},{10,2},{12,4},{14,6},{16,24},{18,... | collective-permute-start | bytes 1572872 | tf_op jit(solution)/shard_map/ppermute | solution.py:73
  21.0 1.8 %fusion.29 = (bf16[1,2,2,2,16,1024]{5,4,0,1,2,3:T(8,128)(2,1)S(1)}, bf16[1,2,2,2,16,1024]{5,4,0,1,2,3:T(8,128)(2,1)S(1)}, bf16[1,2,2,2,16,1024]{5,4,0,1,2,3:T(8,128)(2,1)}) fusion(bf16[2,2,2,2,16,1024]{5,4,0,1,2,3:T(8,128)(2,1)} %bitcast.290, pred[]{:T(512)S(6)} %eq.170), kind=kLoop, calls=%fused_computation.303 | loop fusion | flops 131072 | bytes 1310721 | tf_op jit(solution)/shard_map/slice | solution.py:70
  32.5 6.4 %collective-permute-done.24 = bf16[2,2,2,2,16,1024]{5,4,3,2,1,0:T(8,128)(2,1)} collective-permute-done((bf16[2,2,2,2,16,1024]{5,4,3,2,1,0:T(8,128)(2,1)}, bf16[2,2,2,2,16,1024]{5,4,3,2,1,0:T(8,128)(2,1)}, u32[]{:S(2)}, u32[]{:S(2)}) %collective-permute-start.24) | collective-permute-done | bytes 524320 | tf_op jit(solution)/shard_map/ppermute | solution.py:73
  42.8 3.4 %collective-permute-start.9 = (bf16[2,2,2,16,1024]{4,3,2,1,0:T(8,128)(2,1)S(1)}, bf16[2,2,2,16,1024]{4,3,2,1,0:T(8,128)(2,1)S(1)}, u32[]{:S(2)}, u32[]{:S(2)}) collective-permute-start(bf16[2,2,2,16,1024]{4,3,2,1,0:T(8,128)(2,1)S(1)} %pad_maximum_fusion.7), channel_id=1, source_target_pairs={{0,8},{2,10},{4,12},{6,14},{8,0},{10,2},{12,4},{14,6},{16,24},{18,... | collective-permute-start | bytes 786440 | tf_op jit(solution)/shard_map/ppermute | solution.py:73
  50.6 5.0 %collective-permute-done.17 = bf16[2,2,2,16,1024]{4,3,2,1,0:T(8,128)(2,1)S(1)} collective-permute-done((bf16[2,2,2,16,1024]{4,3,2,1,0:T(8,128)(2,1)S(1)}, bf16[2,2,2,16,1024]{4,3,2,1,0:T(8,128)(2,1)S(1)}, u32[]{:S(2)}, u32[]{:S(2)}) %collective-permute-start.17) | collective-permute-done | bytes 262176 | tf_op jit(solution)/shard_map/ppermute | solution.py:73
  55.7 1.8 %collective-permute-start.18 = (bf16[2,2,16,1024]{3,2,1,0:T(8,128)(2,1)S(1)}, bf16[2,2,16,1024]{3,2,1,0:T(8,128)(2,1)S(1)}, u32[]{:S(2)}, u32[]{:S(2)}) collective-permute-start(bf16[2,2,16,1024]{3,2,1,0:T(8,128)(2,1)S(1)} %pad_maximum_fusion.27), channel_id=1, source_target_pairs={{0,2},{2,0},{4,6},{6,4},{8,10},{10,8},{12,14},{14,12},{16,18},{18,... | collective-permute-start | bytes 393224 | tf_op jit(solution)/shard_map/ppermute | solution.py:73
  57.9 2.4 %collective-permute-start.2 = (bf16[2,2,16,1024]{3,2,1,0:T(8,128)(2,1)S(1)}, bf16[2,2,16,1024]{3,2,1,0:T(8,128)(2,1)S(1)}, u32[]{:S(2)}, u32[]{:S(2)}) collective-permute-start(bf16[2,2,16,1024]{3,2,1,0:T(8,128)(2,1)S(1)} %pad_maximum_fusion.21), channel_id=1, source_target_pairs={{0,8},{2,10},{4,12},{6,14},{8,0},{10,2},{12,4},{14,6},{16,24},{18,... | collective-permute-start | bytes 393224 | tf_op jit(solution)/shard_map/ppermute | solution.py:73
  61.5 3.7 %collective-permute-done.10 = bf16[2,2,16,1024]{3,2,1,0:T(8,128)(2,1)S(1)} collective-permute-done((bf16[2,2,16,1024]{3,2,1,0:T(8,128)(2,1)S(1)}, bf16[2,2,16,1024]{3,2,1,0:T(8,128)(2,1)S(1)}, u32[]{:S(2)}, u32[]{:S(2)}) %collective-permute-start.10) | collective-permute-done | bytes 131104 | tf_op jit(solution)/shard_map/ppermute | solution.py:73
  67.1 2.1 %collective-permute-start.28 = (bf16[2,16,1024]{2,1,0:T(8,128)(2,1)S(1)}, bf16[2,16,1024]{2,1,0:T(8,128)(2,1)S(1)}, u32[]{:S(2)}, u32[]{:S(2)}) collective-permute-start(bf16[2,16,1024]{2,1,0:T(8,128)(2,1)S(1)} %pad_maximum_fusion.50), channel_id=1, source_target_pairs={{0,8},{2,10},{4,12},{6,14},{8,0},{10,2},{12,4},{14,6},{16,24},{18,... | collective-permute-start | bytes 196616 | tf_op jit(solution)/shard_map/ppermute | solution.py:83
  75.3 1.6 collective-permute-start.13
  76.9 2.4 %collective-permute-done.4 = bf16[2,16,1024]{2,1,0:T(8,128)(2,1)S(1)} collective-permute-done((bf16[2,16,1024]{2,1,0:T(8,128)(2,1)S(1)}, bf16[2,16,1024]{2,1,0:T(8,128)(2,1)S(1)}, u32[]{:S(2)}, u32[]{:S(2)}) %collective-permute-start.4) | collective-permute-done | bytes 65568 | tf_op jit(solution)/shard_map/ppermute | solution.py:83
  79.6 1.6 %collective-permute-start.30 = (bf16[2,2,2,16,1024]{4,3,2,1,0:T(8,128)(2,1)S(1)}, bf16[2,2,2,16,1024]{4,3,2,1,0:T(8,128)(2,1)S(1)}, u32[]{:S(2)}, u32[]{:S(2)}) collective-permute-start(bf16[2,2,2,16,1024]{4,3,2,1,0:T(8,128)(2,1)S(1)} %pad_maximum_fusion.14), channel_id=1, source_target_pairs={{0,2},{2,0},{4,6},{6,4},{8,10},{10,8},{12,14},{14,12},{16,18},{18,... | collective-permute-start | bytes 786440 | tf_op jit(solution)/shard_map/ppermute | solution.py:83
  81.3 2.3 %collective-permute-start.22 = (bf16[2,2,2,16,1024]{4,3,2,1,0:T(8,128)(2,1)S(1)}, bf16[2,2,2,16,1024]{4,3,2,1,0:T(8,128)(2,1)S(1)}, u32[]{:S(2)}, u32[]{:S(2)}) collective-permute-start(bf16[2,2,2,16,1024]{4,3,2,1,0:T(8,128)(2,1)S(1)} %pad_maximum_fusion.11), channel_id=1, source_target_pairs={{0,16},{2,18},{4,20},{6,22},{8,24},{10,26},{12,28},{14,30},{16,0},... | collective-permute-start | bytes 786440 | tf_op jit(solution)/shard_map/ppermute | solution.py:83
  83.5 3.4 %collective-permute-done.13 = bf16[2,2,16,1024]{3,2,1,0:T(8,128)(2,1)S(1)} collective-permute-done((bf16[2,2,16,1024]{3,2,1,0:T(8,128)(2,1)S(1)}, bf16[2,2,16,1024]{3,2,1,0:T(8,128)(2,1)S(1)}, u32[]{:S(2)}, u32[]{:S(2)}) %collective-permute-start.13) | collective-permute-done | bytes 131104 | tf_op jit(solution)/shard_map/ppermute | solution.py:83
  87.1 2.9 %collective-permute-done.5 = bf16[2,2,16,1024]{3,2,1,0:T(8,128)(2,1)S(1)} collective-permute-done((bf16[2,2,16,1024]{3,2,1,0:T(8,128)(2,1)S(1)}, bf16[2,2,16,1024]{3,2,1,0:T(8,128)(2,1)S(1)}, u32[]{:S(2)}, u32[]{:S(2)}) %collective-permute-start.5) | collective-permute-done | bytes 131104 | tf_op jit(solution)/shard_map/ppermute | solution.py:83
  91.3 8.9 %collective-permute-done.22 = bf16[2,2,2,16,1024]{4,3,2,1,0:T(8,128)(2,1)S(1)} collective-permute-done((bf16[2,2,2,16,1024]{4,3,2,1,0:T(8,128)(2,1)S(1)}, bf16[2,2,2,16,1024]{4,3,2,1,0:T(8,128)(2,1)S(1)}, u32[]{:S(2)}, u32[]{:S(2)}) %collective-permute-start.22) | collective-permute-done | bytes 262176 | tf_op jit(solution)/shard_map/ppermute | solution.py:83
  100.4 2.0 %collective-permute-start.34 = (bf16[1,2,2,2,16,1024]{5,4,3,2,1,0:T(8,128)(2,1)S(1)}, bf16[1,2,2,2,16,1024]{5,4,3,2,1,0:T(8,128)(2,1)S(1)}, u32[]{:S(2)}, u32[]{:S(2)}) collective-permute-start(bf16[1,2,2,2,16,1024]{5,4,3,2,1,0:T(8,128)(2,1)S(1)} %maximum_bitcast_fusion.15), channel_id=1, source_target_pairs={{0,4},{2,6},{4,0},{6,2},{8,12},{10,14},{12,8},{14,10},{16,20},{18,... | collective-permute-start | bytes 786440 | tf_op jit(solution)/shard_map/ppermute | solution.py:83
  102.6 2.1 %collective-permute-start.7 = (bf16[1,2,2,2,16,1024]{5,4,3,2,1,0:T(8,128)(2,1)S(1)}, bf16[1,2,2,2,16,1024]{5,4,3,2,1,0:T(8,128)(2,1)S(1)}, u32[]{:S(2)}, u32[]{:S(2)}) collective-permute-start(bf16[1,2,2,2,16,1024]{5,4,3,2,1,0:T(8,128)(2,1)S(1)} %maximum_bitcast_fusion.10), channel_id=1, source_target_pairs={{0,2},{2,0},{4,6},{6,4},{8,10},{10,8},{12,14},{14,12},{16,18},{18,... | collective-permute-start | bytes 786440 | tf_op jit(solution)/shard_map/ppermute | solution.py:83
  104.8 1.3 collective-permute-start.31
  106.3 2.1 %collective-permute-done.35 = bf16[1,2,2,2,16,1024]{5,4,3,2,1,0:T(8,128)(2,1)S(1)} collective-permute-done((bf16[1,2,2,2,16,1024]{5,4,3,2,1,0:T(8,128)(2,1)S(1)}, bf16[1,2,2,2,16,1024]{5,4,3,2,1,0:T(8,128)(2,1)S(1)}, u32[]{:S(2)}, u32[]{:S(2)}) %collective-permute-start.35) | collective-permute-done | bytes 262176 | tf_op jit(solution)/shard_map/ppermute | solution.py:83
  108.5 1.8 %collective-permute-start.15 = (bf16[1,2,2,2,16,1024]{5,4,3,2,1,0:T(8,128)(2,1)S(1)}, bf16[1,2,2,2,16,1024]{5,4,3,2,1,0:T(8,128)(2,1)S(1)}, u32[]{:S(2)}, u32[]{:S(2)}) collective-permute-start(bf16[1,2,2,2,16,1024]{5,4,3,2,1,0:T(8,128)(2,1)S(1)} %maximum_bitcast_fusion.11), channel_id=1, source_target_pairs={{0,4},{2,6},{4,0},{6,2},{8,12},{10,14},{12,8},{14,10},{16,20},{18,... | collective-permute-start | bytes 786440 | tf_op jit(solution)/shard_map/ppermute | solution.py:83
  111.9 1.5 maximum_bitcast_fusion.1.blk_ref
  113.4 11.7 %shard_map.47 = (f32[4,4,1024]{2,1,0:T(4,128)}, f32[4,4,128]{2,1,0:T(4,128)}) custom-call(s32[64]{0:T(128)} %squeeze.19.meta_ref, bf16[1,1024,1024]{2,1,0:T(8,128)(2,1)} %maximum_bitcast_fusion.1.blk_ref, bf16[1024,1152]{1,0:T(8,128)(2,1)} %copy-done.3), custom_call_target="tpu_custom_call" | custom-call | flops 5435817984 | bytes 4521984 | tf_op jit(solution)/shard_map/pallas_call | solution.py:154
  126.6 1.5 maximum_bitcast_fusion.blk_ref
  128.1 11.9 %shard_map.46 = (f32[4,4,1024]{2,1,0:T(4,128)}, f32[4,4,128]{2,1,0:T(4,128)}) custom-call(s32[64]{0:T(128)} %squeeze.16.meta_ref, bf16[1,1024,1024]{2,1,0:T(8,128)(2,1)} %maximum_bitcast_fusion.blk_ref, bf16[1024,1152]{1,0:T(8,128)(2,1)} %copy-done.3), custom_call_target="tpu_custom_call" | custom-call | flops 5435817984 | bytes 4521984 | tf_op jit(solution)/shard_map/pallas_call | solution.py:154
  143.8 1.7 %collective-permute-start.39 = (f32[32]{0:T(128)S(1)}, f32[32]{0:T(128)S(1)}, u32[]{:S(2)}, u32[]{:S(2)}) collective-permute-start(f32[32]{0:T(128)S(1)} %fusion.11), channel_id=1, source_target_pairs={{0,6},{2,4},{4,2},{6,0},{8,14},{10,12},{12,10},{14,8},{16,22},{18,... | collective-permute-start | bytes 392 | tf_op jit(solution)/shard_map/ppermute | solution.py:33
  145.5 1.8 %collective-permute-start.41 = (f32[32]{0:T(128)S(1)}, f32[32]{0:T(128)S(1)}, u32[]{:S(2)}, u32[]{:S(2)}) collective-permute-start(f32[32]{0:T(128)S(1)} %fusion.11), channel_id=1, source_target_pairs={{0,2},{2,0},{4,6},{6,4},{8,10},{10,8},{12,14},{14,12},{16,18},{18,... | collective-permute-start | bytes 392 | tf_op jit(solution)/shard_map/ppermute | solution.py:33
  149.1 1.5 collective-permute-start.42
  150.6 2.0 %collective-permute-start.43 = (f32[32]{0:T(128)S(1)}, f32[32]{0:T(128)S(1)}, u32[]{:S(2)}, u32[]{:S(2)}) collective-permute-start(f32[32]{0:T(128)S(1)} %fusion.27), channel_id=1, source_target_pairs={{0,16},{2,18},{4,20},{6,22},{8,24},{10,26},{12,28},{14,30},{16,0},... | collective-permute-start | bytes 392 | tf_op jit(solution)/shard_map/ppermute | solution.py:33
  (260 shorter events, 48.9 us)
Async XLA Ops:
  1.7 27.0 %collective-permute-start.32 = (bf16[1024,128]{1,0:T(8,128)(2,1)}, bf16[1024,128]{1,0:T(8,128)(2,1)}, u32[]{:S(2)}, u32[]{:S(2)}) collective-permute-start(bf16[1024,128]{1,0:T(8,128)(2,1)} %slice.719), channel_id=1, source_target_pairs={{2,0},{4,2},{6,4},{8,6},{10,8},{12,10},{14,12},{16,14},{18,16},{20... | collective-permute-start | bytes 786440 | tf_op jit(solution)/shard_map/ppermute | solution.py:18
  8.0 30.8 %collective-permute-start.24 = (bf16[2,2,2,2,16,1024]{5,4,3,2,1,0:T(8,128)(2,1)}, bf16[2,2,2,2,16,1024]{5,4,3,2,1,0:T(8,128)(2,1)}, u32[]{:S(2)}, u32[]{:S(2)}) collective-permute-start(bf16[2,2,2,2,16,1024]{5,4,3,2,1,0:T(8,128)(2,1)} %pad_maximum_fusion.3), channel_id=1, source_target_pairs={{0,16},{2,18},{4,20},{6,22},{8,24},{10,26},{12,28},{14,30},{16,0},... | collective-permute-start | bytes 1572872 | tf_op jit(solution)/shard_map/ppermute | solution.py:73
  15.9 24.2 %collective-permute-start.16 = (bf16[2,2,2,2,16,1024]{5,4,3,2,1,0:T(8,128)(2,1)}, bf16[2,2,2,2,16,1024]{5,4,3,2,1,0:T(8,128)(2,1)}, u32[]{:S(2)}, u32[]{:S(2)}) collective-permute-start(bf16[2,2,2,2,16,1024]{5,4,3,2,1,0:T(8,128)(2,1)} %pad_maximum_fusion.2), channel_id=1, source_target_pairs={{0,8},{2,10},{4,12},{6,14},{8,0},{10,2},{12,4},{14,6},{16,24},{18,... | collective-permute-start | bytes 1572872 | tf_op jit(solution)/shard_map/ppermute | solution.py:73
  20.4 21.2 %collective-permute-start.8 = (bf16[2,2,2,2,16,1024]{5,4,3,2,1,0:T(8,128)(2,1)}, bf16[2,2,2,2,16,1024]{5,4,3,2,1,0:T(8,128)(2,1)}, u32[]{:S(2)}, u32[]{:S(2)}) collective-permute-start(bf16[2,2,2,2,16,1024]{5,4,3,2,1,0:T(8,128)(2,1)} %pad_maximum_fusion.1), channel_id=1, source_target_pairs={{0,4},{2,6},{4,0},{6,2},{8,12},{10,14},{12,8},{14,10},{16,20},{18,... | collective-permute-start | bytes 1572872 | tf_op jit(solution)/shard_map/ppermute | solution.py:73
  23.7 22.5 %collective-permute-start = (bf16[2,2,2,2,16,1024]{5,4,0,1,2,3:T(8,128)(2,1)}, bf16[2,2,2,2,16,1024]{5,4,0,1,2,3:T(8,128)(2,1)}, u32[]{:S(2)}, u32[]{:S(2)}) collective-permute-start(bf16[2,2,2,2,16,1024]{5,4,0,1,2,3:T(8,128)(2,1)} %pad_maximum_fusion), channel_id=1, source_target_pairs={{0,2},{2,0},{4,6},{6,4},{8,10},{10,8},{12,14},{14,12},{16,18},{18,... | collective-permute-start | bytes 1572872 | tf_op jit(solution)/shard_map/ppermute | solution.py:73
  40.0 9.6 %collective-permute-start.25 = (bf16[2,2,2,16,1024]{4,3,2,1,0:T(8,128)(2,1)S(1)}, bf16[2,2,2,16,1024]{4,3,2,1,0:T(8,128)(2,1)S(1)}, u32[]{:S(2)}, u32[]{:S(2)}) collective-permute-start(bf16[2,2,2,16,1024]{4,3,2,1,0:T(8,128)(2,1)S(1)} %pad_maximum_fusion.13), channel_id=1, source_target_pairs={{0,2},{2,0},{4,6},{6,4},{8,10},{10,8},{12,14},{14,12},{16,18},{18,... | collective-permute-start | bytes 786440 | tf_op jit(solution)/shard_map/ppermute | solution.py:73
  41.3 14.4 %collective-permute-start.17 = (bf16[2,2,2,16,1024]{4,3,2,1,0:T(8,128)(2,1)S(1)}, bf16[2,2,2,16,1024]{4,3,2,1,0:T(8,128)(2,1)S(1)}, u32[]{:S(2)}, u32[]{:S(2)}) collective-permute-start(bf16[2,2,2,16,1024]{4,3,2,1,0:T(8,128)(2,1)S(1)} %pad_maximum_fusion.10), channel_id=1, source_target_pairs={{0,16},{2,18},{4,20},{6,22},{8,24},{10,26},{12,28},{14,30},{16,0},... | collective-permute-start | bytes 786440 | tf_op jit(solution)/shard_map/ppermute | solution.py:73
  42.8 14.7 %collective-permute-start.9 = (bf16[2,2,2,16,1024]{4,3,2,1,0:T(8,128)(2,1)S(1)}, bf16[2,2,2,16,1024]{4,3,2,1,0:T(8,128)(2,1)S(1)}, u32[]{:S(2)}, u32[]{:S(2)}) collective-permute-start(bf16[2,2,2,16,1024]{4,3,2,1,0:T(8,128)(2,1)S(1)} %pad_maximum_fusion.7), channel_id=1, source_target_pairs={{0,8},{2,10},{4,12},{6,14},{8,0},{10,2},{12,4},{14,6},{16,24},{18,... | collective-permute-start | bytes 786440 | tf_op jit(solution)/shard_map/ppermute | solution.py:73
  48.4 9.4 %collective-permute-start.1 = (bf16[2,2,2,16,1024]{4,3,2,1,0:T(8,128)(2,1)S(1)}, bf16[2,2,2,16,1024]{4,3,2,1,0:T(8,128)(2,1)S(1)}, u32[]{:S(2)}, u32[]{:S(2)}) collective-permute-start(bf16[2,2,2,16,1024]{4,3,2,1,0:T(8,128)(2,1)S(1)} %pad_maximum_fusion.4), channel_id=1, source_target_pairs={{0,4},{2,6},{4,0},{6,2},{8,12},{10,14},{12,8},{14,10},{16,20},{18,... | collective-permute-start | bytes 786440 | tf_op jit(solution)/shard_map/ppermute | solution.py:73
  49.7 10.6 %collective-permute-start.26 = (bf16[2,2,16,1024]{3,2,1,0:T(8,128)(2,1)S(1)}, bf16[2,2,16,1024]{3,2,1,0:T(8,128)(2,1)S(1)}, u32[]{:S(2)}, u32[]{:S(2)}) collective-permute-start(bf16[2,2,16,1024]{3,2,1,0:T(8,128)(2,1)S(1)} %pad_maximum_fusion.30), channel_id=1, source_target_pairs={{0,4},{2,6},{4,0},{6,2},{8,12},{10,14},{12,8},{14,10},{16,20},{18,... | collective-permute-start | bytes 393224 | tf_op jit(solution)/shard_map/ppermute | solution.py:73
  57.6 7.6 %collective-permute-start.10 = (bf16[2,2,16,1024]{3,2,1,0:T(8,128)(2,1)S(1)}, bf16[2,2,16,1024]{3,2,1,0:T(8,128)(2,1)S(1)}, u32[]{:S(2)}, u32[]{:S(2)}) collective-permute-start(bf16[2,2,16,1024]{3,2,1,0:T(8,128)(2,1)S(1)} %pad_maximum_fusion.24), channel_id=1, source_target_pairs={{0,16},{2,18},{4,20},{6,22},{8,24},{10,26},{12,28},{14,30},{16,0},... | collective-permute-start | bytes 393224 | tf_op jit(solution)/shard_map/ppermute | solution.py:73
  57.9 8.5 %collective-permute-start.2 = (bf16[2,2,16,1024]{3,2,1,0:T(8,128)(2,1)S(1)}, bf16[2,2,16,1024]{3,2,1,0:T(8,128)(2,1)S(1)}, u32[]{:S(2)}, u32[]{:S(2)}) collective-permute-start(bf16[2,2,16,1024]{3,2,1,0:T(8,128)(2,1)S(1)} %pad_maximum_fusion.21), channel_id=1, source_target_pairs={{0,8},{2,10},{4,12},{6,14},{8,0},{10,2},{12,4},{14,6},{16,24},{18,... | collective-permute-start | bytes 393224 | tf_op jit(solution)/shard_map/ppermute | solution.py:73
  60.4 6.7 %collective-permute-start.27 = (bf16[2,16,1024]{2,1,0:T(8,128)(2,1)S(1)}, bf16[2,16,1024]{2,1,0:T(8,128)(2,1)S(1)}, u32[]{:S(2)}, u32[]{:S(2)}) collective-permute-start(bf16[2,16,1024]{2,1,0:T(8,128)(2,1)S(1)} %pad_maximum_fusion.49), channel_id=1, source_target_pairs={{0,8},{2,10},{4,12},{6,14},{8,0},{10,2},{12,4},{14,6},{16,24},{18,... | collective-permute-start | bytes 196616 | tf_op jit(solution)/shard_map/ppermute | solution.py:73
  60.8 8.4 %collective-permute-start.19 = (bf16[2,16,1024]{2,1,0:T(8,128)(2,1)S(1)}, bf16[2,16,1024]{2,1,0:T(8,128)(2,1)S(1)}, u32[]{:S(2)}, u32[]{:S(2)}) collective-permute-start(bf16[2,16,1024]{2,1,0:T(8,128)(2,1)S(1)} %pad_maximum_fusion.45), channel_id=1, source_target_pairs={{0,4},{2,6},{4,0},{6,2},{8,12},{10,14},{12,8},{14,10},{16,20},{18,... | collective-permute-start | bytes 196616 | tf_op jit(solution)/shard_map/ppermute | solution.py:73
  66.4 5.6 %collective-permute-start.3 = (bf16[2,16,1024]{2,1,0:T(8,128)(2,1)S(1)}, bf16[2,16,1024]{2,1,0:T(8,128)(2,1)S(1)}, u32[]{:S(2)}, u32[]{:S(2)}) collective-permute-start(bf16[2,16,1024]{2,1,0:T(8,128)(2,1)S(1)} %pad_maximum_fusion.37), channel_id=1, source_target_pairs={{0,16},{2,18},{4,20},{6,22},{8,24},{10,26},{12,28},{14,30},{16,0},... | collective-permute-start | bytes 196616 | tf_op jit(solution)/shard_map/ppermute | solution.py:73
  72.0 7.3 %collective-permute-start.4 = (bf16[2,16,1024]{2,1,0:T(8,128)(2,1)S(1)}, bf16[2,16,1024]{2,1,0:T(8,128)(2,1)S(1)}, u32[]{:S(2)}, u32[]{:S(2)}) collective-permute-start(bf16[2,16,1024]{2,1,0:T(8,128)(2,1)S(1)} %pad_maximum_fusion.38), channel_id=1, source_target_pairs={{0,16},{2,18},{4,20},{6,22},{8,24},{10,26},{12,28},{14,30},{16,0},... | collective-permute-start | bytes 196616 | tf_op jit(solution)/shard_map/ppermute | solution.py:83
  72.4 7.1 %collective-permute-start.29 = (bf16[2,2,16,1024]{3,2,1,0:T(8,128)(2,1)S(1)}, bf16[2,2,16,1024]{3,2,1,0:T(8,128)(2,1)S(1)}, u32[]{:S(2)}, u32[]{:S(2)}) collective-permute-start(bf16[2,2,16,1024]{3,2,1,0:T(8,128)(2,1)S(1)} %pad_maximum_fusion.31), channel_id=1, source_target_pairs={{0,4},{2,6},{4,0},{6,2},{8,12},{10,14},{12,8},{14,10},{16,20},{18,... | collective-permute-start | bytes 393224 | tf_op jit(solution)/shard_map/ppermute | solution.py:83
  74.2 6.9 %collective-permute-start.21 = (bf16[2,2,16,1024]{3,2,1,0:T(8,128)(2,1)S(1)}, bf16[2,2,16,1024]{3,2,1,0:T(8,128)(2,1)S(1)}, u32[]{:S(2)}, u32[]{:S(2)}) collective-permute-start(bf16[2,2,16,1024]{3,2,1,0:T(8,128)(2,1)S(1)} %pad_maximum_fusion.28), channel_id=1, source_target_pairs={{0,2},{2,0},{4,6},{6,4},{8,10},{10,8},{12,14},{14,12},{16,18},{18,... | collective-permute-start | bytes 393224 | tf_op jit(solution)/shard_map/ppermute | solution.py:83
  75.3 11.6 %collective-permute-start.13 = (bf16[2,2,16,1024]{3,2,1,0:T(8,128)(2,1)S(1)}, bf16[2,2,16,1024]{3,2,1,0:T(8,128)(2,1)S(1)}, u32[]{:S(2)}, u32[]{:S(2)}) collective-permute-start(bf16[2,2,16,1024]{3,2,1,0:T(8,128)(2,1)S(1)} %pad_maximum_fusion.25), channel_id=1, source_target_pairs={{0,16},{2,18},{4,20},{6,22},{8,24},{10,26},{12,28},{14,30},{16,0},... | collective-permute-start | bytes 393224 | tf_op jit(solution)/shard_map/ppermute | solution.py:83
  79.4 10.6 %collective-permute-start.5 = (bf16[2,2,16,1024]{3,2,1,0:T(8,128)(2,1)S(1)}, bf16[2,2,16,1024]{3,2,1,0:T(8,128)(2,1)S(1)}, u32[]{:S(2)}, u32[]{:S(2)}) collective-permute-start(bf16[2,2,16,1024]{3,2,1,0:T(8,128)(2,1)S(1)} %pad_maximum_fusion.22), channel_id=1, source_target_pairs={{0,8},{2,10},{4,12},{6,14},{8,0},{10,2},{12,4},{14,6},{16,24},{18,... | collective-permute-start | bytes 393224 | tf_op jit(solution)/shard_map/ppermute | solution.py:83
  79.6 11.1 %collective-permute-start.30 = (bf16[2,2,2,16,1024]{4,3,2,1,0:T(8,128)(2,1)S(1)}, bf16[2,2,2,16,1024]{4,3,2,1,0:T(8,128)(2,1)S(1)}, u32[]{:S(2)}, u32[]{:S(2)}) collective-permute-start(bf16[2,2,2,16,1024]{4,3,2,1,0:T(8,128)(2,1)S(1)} %pad_maximum_fusion.14), channel_id=1, source_target_pairs={{0,2},{2,0},{4,6},{6,4},{8,10},{10,8},{12,14},{14,12},{16,18},{18,... | collective-permute-start | bytes 786440 | tf_op jit(solution)/shard_map/ppermute | solution.py:83
  81.3 18.9 %collective-permute-start.22 = (bf16[2,2,2,16,1024]{4,3,2,1,0:T(8,128)(2,1)S(1)}, bf16[2,2,2,16,1024]{4,3,2,1,0:T(8,128)(2,1)S(1)}, u32[]{:S(2)}, u32[]{:S(2)}) collective-permute-start(bf16[2,2,2,16,1024]{4,3,2,1,0:T(8,128)(2,1)S(1)} %pad_maximum_fusion.11), channel_id=1, source_target_pairs={{0,16},{2,18},{4,20},{6,22},{8,24},{10,26},{12,28},{14,30},{16,0},... | collective-permute-start | bytes 786440 | tf_op jit(solution)/shard_map/ppermute | solution.py:83
  87.0 13.3 %collective-permute-start.14 = (bf16[2,2,2,16,1024]{4,3,2,1,0:T(8,128)(2,1)S(1)}, bf16[2,2,2,16,1024]{4,3,2,1,0:T(8,128)(2,1)S(1)}, u32[]{:S(2)}, u32[]{:S(2)}) collective-permute-start(bf16[2,2,2,16,1024]{4,3,2,1,0:T(8,128)(2,1)S(1)} %pad_maximum_fusion.8), channel_id=1, source_target_pairs={{0,8},{2,10},{4,12},{6,14},{8,0},{10,2},{12,4},{14,6},{16,24},{18,... | collective-permute-start | bytes 786440 | tf_op jit(solution)/shard_map/ppermute | solution.py:83
  90.1 12.2 %collective-permute-start.6 = (bf16[2,2,2,16,1024]{4,3,2,1,0:T(8,128)(2,1)S(1)}, bf16[2,2,2,16,1024]{4,3,2,1,0:T(8,128)(2,1)S(1)}, u32[]{:S(2)}, u32[]{:S(2)}) collective-permute-start(bf16[2,2,2,16,1024]{4,3,2,1,0:T(8,128)(2,1)S(1)} %pad_maximum_fusion.5), channel_id=1, source_target_pairs={{0,4},{2,6},{4,0},{6,2},{8,12},{10,14},{12,8},{14,10},{16,20},{18,... | collective-permute-start | bytes 786440 | tf_op jit(solution)/shard_map/ppermute | solution.py:83
  90.7 14.1 %collective-permute-start.36 = (bf16[1,2,2,2,16,1024]{5,4,3,2,1,0:T(8,128)(2,1)S(1)}, bf16[1,2,2,2,16,1024]{5,4,3,2,1,0:T(8,128)(2,1)S(1)}, u32[]{:S(2)}, u32[]{:S(2)}) collective-permute-start(bf16[1,2,2,2,16,1024]{5,4,3,2,1,0:T(8,128)(2,1)S(1)} %maximum_bitcast_fusion.17), channel_id=1, source_target_pairs={{0,16},{2,18},{4,20},{6,22},{8,24},{10,26},{12,28},{14,30},{16,0},... | collective-permute-start | bytes 786440 | tf_op jit(solution)/shard_map/ppermute | solution.py:83
  100.2 8.1 %collective-permute-start.35 = (bf16[1,2,2,2,16,1024]{5,4,3,2,1,0:T(8,128)(2,1)S(1)}, bf16[1,2,2,2,16,1024]{5,4,3,2,1,0:T(8,128)(2,1)S(1)}, u32[]{:S(2)}, u32[]{:S(2)}) collective-permute-start(bf16[1,2,2,2,16,1024]{5,4,3,2,1,0:T(8,128)(2,1)S(1)} %maximum_bitcast_fusion.16), channel_id=1, source_target_pairs={{0,8},{2,10},{4,12},{6,14},{8,0},{10,2},{12,4},{14,6},{16,24},{18,... | collective-permute-start | bytes 786440 | tf_op jit(solution)/shard_map/ppermute | solution.py:83
  100.4 8.1 %collective-permute-start.34 = (bf16[1,2,2,2,16,1024]{5,4,3,2,1,0:T(8,128)(2,1)S(1)}, bf16[1,2,2,2,16,1024]{5,4,3,2,1,0:T(8,128)(2,1)S(1)}, u32[]{:S(2)}, u32[]{:S(2)}) collective-permute-start(bf16[1,2,2,2,16,1024]{5,4,3,2,1,0:T(8,128)(2,1)S(1)} %maximum_bitcast_fusion.15), channel_id=1, source_target_pairs={{0,4},{2,6},{4,0},{6,2},{8,12},{10,14},{12,8},{14,10},{16,20},{18,... | collective-permute-start | bytes 786440 | tf_op jit(solution)/shard_map/ppermute | solution.py:83
  102.5 8.0 %collective-permute-start.33 = (bf16[1,2,2,2,16,1024]{5,4,3,2,1,0:T(8,128)(2,1)S(1)}, bf16[1,2,2,2,16,1024]{5,4,3,2,1,0:T(8,128)(2,1)S(1)}, u32[]{:S(2)}, u32[]{:S(2)}) collective-permute-start(bf16[1,2,2,2,16,1024]{5,4,3,2,1,0:T(8,128)(2,1)S(1)} %maximum_bitcast_fusion.14), channel_id=1, source_target_pairs={{0,2},{2,0},{4,6},{6,4},{8,10},{10,8},{12,14},{14,12},{16,18},{18,... | collective-permute-start | bytes 786440 | tf_op jit(solution)/shard_map/ppermute | solution.py:83
  102.6 9.1 %collective-permute-start.7 = (bf16[1,2,2,2,16,1024]{5,4,3,2,1,0:T(8,128)(2,1)S(1)}, bf16[1,2,2,2,16,1024]{5,4,3,2,1,0:T(8,128)(2,1)S(1)}, u32[]{:S(2)}, u32[]{:S(2)}) collective-permute-start(bf16[1,2,2,2,16,1024]{5,4,3,2,1,0:T(8,128)(2,1)S(1)} %maximum_bitcast_fusion.10), channel_id=1, source_target_pairs={{0,2},{2,0},{4,6},{6,4},{8,10},{10,8},{12,14},{14,12},{16,18},{18,... | collective-permute-start | bytes 786440 | tf_op jit(solution)/shard_map/ppermute | solution.py:83
  104.8 21.2 %collective-permute-start.31 = (bf16[1,2,2,2,16,1024]{5,4,3,2,1,0:T(8,128)(2,1)S(1)}, bf16[1,2,2,2,16,1024]{5,4,3,2,1,0:T(8,128)(2,1)S(1)}, u32[]{:S(2)}, u32[]{:S(2)}) collective-permute-start(bf16[1,2,2,2,16,1024]{5,4,3,2,1,0:T(8,128)(2,1)S(1)} %maximum_bitcast_fusion.13), channel_id=1, source_target_pairs={{0,16},{2,18},{4,20},{6,22},{8,24},{10,26},{12,28},{14,30},{16,0},... | collective-permute-start | bytes 786440 | tf_op jit(solution)/shard_map/ppermute | solution.py:83
  108.4 17.8 %collective-permute-start.23 = (bf16[1,2,2,2,16,1024]{5,4,3,2,1,0:T(8,128)(2,1)S(1)}, bf16[1,2,2,2,16,1024]{5,4,3,2,1,0:T(8,128)(2,1)S(1)}, u32[]{:S(2)}, u32[]{:S(2)}) collective-permute-start(bf16[1,2,2,2,16,1024]{5,4,3,2,1,0:T(8,128)(2,1)S(1)} %maximum_bitcast_fusion.12), channel_id=1, source_target_pairs={{0,8},{2,10},{4,12},{6,14},{8,0},{10,2},{12,4},{14,6},{16,24},{18,... | collective-permute-start | bytes 786440 | tf_op jit(solution)/shard_map/ppermute | solution.py:83
  108.5 17.8 %collective-permute-start.15 = (bf16[1,2,2,2,16,1024]{5,4,3,2,1,0:T(8,128)(2,1)S(1)}, bf16[1,2,2,2,16,1024]{5,4,3,2,1,0:T(8,128)(2,1)S(1)}, u32[]{:S(2)}, u32[]{:S(2)}) collective-permute-start(bf16[1,2,2,2,16,1024]{5,4,3,2,1,0:T(8,128)(2,1)S(1)} %maximum_bitcast_fusion.11), channel_id=1, source_target_pairs={{0,4},{2,6},{4,0},{6,2},{8,12},{10,14},{12,8},{14,10},{16,20},{18,... | collective-permute-start | bytes 786440 | tf_op jit(solution)/shard_map/ppermute | solution.py:83
  (22 other events, 113.0 us)

commit v7 on v6

--- a/solution.py
+++ b/solution.py
@@ -8,6 +8,7 @@
 L = 128
 GROUP = 4
 REACH = L + 16
+SPLIT = 3
 
 EPS = 1e-06
 
@@ -78,7 +79,7 @@
     for s in reversed(range(nbits)):
         sends = {}
         for (p, r), buf in bufs.items():
-            sends.setdefault((r if s == 0 else 0, orders[p][s]), []).append(((p, r), buf))
+            sends.setdefault((r if s <= SPLIT else 0, orders[p][s]), []).append(((p, r), buf))
         for (_, mask), items in sorted(sends.items()):
             got = lax.ppermute(jnp.stack([v for _, v in items]), axis, [(i, i ^ mask) for i in range(size)])
             bit = (place // mask) % 2

time: 158 us -> 167 us (1.057)
  starting transfers between devices: 52.3 us -> 72.6 us
  waiting for transfers between devices: 44 us -> 33.1 us
    ppermute x36 -> x48, starting transfers between devices: 42.5 us -> 62.8 us  [spread_blocks(): lax.ppermute(jnp.stack([v for _, v in items]), axis, [(i, i ^ mask) for i...]
    ppermute x36 -> x48, waiting for transfers between devices: 38.8 us -> 27.6 us  [spread_blocks(): lax.ppermute(jnp.stack([v for _, v in items]), axis, [(i, i ^ mask) for i...]
    another operation x52 -> x40, other arithmetic: 4.2 us -> 4.03 us  [spread_blocks(): jnp.stack([v for _, v in items])]
  transfers between devices with their start and end apart: 45 -> 57, of which waited for: 21 -> 17; matrix products, arithmetic and copies ran while one was open for 18% -> 17% of each run, Pallas kernels for 7% -> 7%
where the time goes in v7:
time: 167 us
  starting transfers between devices  72.6 us (43%)
  waiting for transfers between devices  33.1 us (20%)
  Pallas kernels  23.8 us (14%)
  other arithmetic  17.8 us (11%)
  local copies, waits for them, and re-layouts  15.1 us (9%)
  between operations  2.71 us (2%)
    ppermute x48, starting transfers between devices, spread_blocks(): lax.ppermute(jnp.stack([v for _, v in items]), axis, [(i, i ^ mask) for i...  62.8 us
    ppermute x48, waiting for transfers between devices, spread_blocks(): lax.ppermute(jnp.stack([v for _, v in items]), axis, [(i, i ^ mask) for i...  27.6 us
    pallas_call x2, Pallas kernels, correlate(): pl.pallas_call(correlate_kernel, grid_spec=grid_spec, out_shape=[jax.Shap...  23.8 us
    ppermute x8, starting transfers between devices, group_sum(): got[d] = lax.ppermute(value, axis, pairs)  8.57 us
    select_n x18, other arithmetic, spread_blocks(): bufs[key] = jnp.where(holder, keeps[key], got[n])  5.69 us
    ppermute x8, waiting for transfers between devices, group_sum(): got[d] = lax.ppermute(value, axis, pairs)  5.56 us
    unnamed x20, local copies, waits for them, and re-layouts  4.38 us
    another operation x40, other arithmetic, spread_blocks(): jnp.stack([v for _, v in items])  4.03 us
  transfers between devices with their start and end apart: 57, of which 17 were waited for; matrix products, arithmetic and copies ran while one was open for 17% of the time, Pallas kernels for 7%

profile of v7, /device:TPU:0, one launch (start us, length us, event | category | flops | bytes accessed | tf_op | source)
XLA Modules:
  0.0 166.6 jit_solution(1313964111640546571)
XLA Ops:
  0.0 1.7 %slice.599 = bf16[1024,128]{1,0:T(8,128)(2,1)} slice(bf16[1024,1024]{1,0:T(8,128)(2,1)} %param.4), slice={[0:1024], [0:128]} | slice | bytes 524288 | tf_op jit(solution)/shard_map/slice | solution.py:182
  3.0 2.9 %copy.32 = bf16[1024,1024]{0,1:T(8,128)(2,1)S(1)} copy(bf16[1024,1024]{1,0:T(8,128)(2,1)} %param.4) | data formatting | bytes 4194304 | tf_op args[0]
  8.0 7.0 %collective-permute-start.24 = (bf16[2,2,2,2,16,1024]{5,4,3,2,1,0:T(8,128)(2,1)}, bf16[2,2,2,2,16,1024]{5,4,3,2,1,0:T(8,128)(2,1)}, u32[]{:S(2)}, u32[]{:S(2)}) collective-permute-start(bf16[2,2,2,2,16,1024]{5,4,3,2,1,0:T(8,128)(2,1)} %pad_maximum_fusion.3), channel_id=1, source_target_pairs={{0,16},{2,18},{4,20},{6,22},{8,24},{10,26},{12,28},{14,30},{16,0},... | collective-permute-start | bytes 1572872 | tf_op jit(solution)/shard_map/ppermute | solution.py:74
  16.0 1.6 collective-permute-start.16
  21.1 1.8 %fusion.29 = (bf16[1,2,2,2,16,1024]{5,4,0,1,2,3:T(8,128)(2,1)S(1)}, bf16[1,2,2,2,16,1024]{5,4,0,1,2,3:T(8,128)(2,1)S(1)}, bf16[1,2,2,2,16,1024]{5,4,0,1,2,3:T(8,128)(2,1)}) fusion(bf16[2,2,2,2,16,1024]{5,4,0,1,2,3:T(8,128)(2,1)} %bitcast.290, pred[]{:T(512)S(6)} %eq.182), kind=kLoop, calls=%fused_computation.291 | loop fusion | flops 131072 | bytes 1310721 | tf_op jit(solution)/shard_map/slice | solution.py:71
  32.6 6.3 %collective-permute-done.24 = bf16[2,2,2,2,16,1024]{5,4,3,2,1,0:T(8,128)(2,1)} collective-permute-done((bf16[2,2,2,2,16,1024]{5,4,3,2,1,0:T(8,128)(2,1)}, bf16[2,2,2,2,16,1024]{5,4,3,2,1,0:T(8,128)(2,1)}, u32[]{:S(2)}, u32[]{:S(2)}) %collective-permute-start.24) | collective-permute-done | bytes 524320 | tf_op jit(solution)/shard_map/ppermute | solution.py:74
  42.8 3.4 %collective-permute-start.9 = (bf16[2,2,2,16,1024]{4,3,2,1,0:T(8,128)(2,1)S(1)}, bf16[2,2,2,16,1024]{4,3,2,1,0:T(8,128)(2,1)S(1)}, u32[]{:S(2)}, u32[]{:S(2)}) collective-permute-start(bf16[2,2,2,16,1024]{4,3,2,1,0:T(8,128)(2,1)S(1)} %pad_maximum_fusion.6), channel_id=1, source_target_pairs={{0,8},{2,10},{4,12},{6,14},{8,0},{10,2},{12,4},{14,6},{16,24},{18,... | collective-permute-start | bytes 786440 | tf_op jit(solution)/shard_map/ppermute | solution.py:74
  50.6 5.0 %collective-permute-done.17 = bf16[2,2,2,16,1024]{4,3,2,1,0:T(8,128)(2,1)S(1)} collective-permute-done((bf16[2,2,2,16,1024]{4,3,2,1,0:T(8,128)(2,1)S(1)}, bf16[2,2,2,16,1024]{4,3,2,1,0:T(8,128)(2,1)S(1)}, u32[]{:S(2)}, u32[]{:S(2)}) %collective-permute-start.17) | collective-permute-done | bytes 262176 | tf_op jit(solution)/shard_map/ppermute | solution.py:74
  55.7 1.8 %collective-permute-start.18 = (bf16[2,2,16,1024]{3,2,1,0:T(8,128)(2,1)S(1)}, bf16[2,2,16,1024]{3,2,1,0:T(8,128)(2,1)S(1)}, u32[]{:S(2)}, u32[]{:S(2)}) collective-permute-start(bf16[2,2,16,1024]{3,2,1,0:T(8,128)(2,1)S(1)} %pad_maximum_fusion.21), channel_id=1, source_target_pairs={{0,2},{2,0},{4,6},{6,4},{8,10},{10,8},{12,14},{14,12},{16,18},{18,... | collective-permute-start | bytes 393224 | tf_op jit(solution)/shard_map/ppermute | solution.py:74
  57.9 2.5 %collective-permute-start.2 = (bf16[2,2,16,1024]{3,2,1,0:T(8,128)(2,1)S(1)}, bf16[2,2,16,1024]{3,2,1,0:T(8,128)(2,1)S(1)}, u32[]{:S(2)}, u32[]{:S(2)}) collective-permute-start(bf16[2,2,16,1024]{3,2,1,0:T(8,128)(2,1)S(1)} %pad_maximum_fusion.17), channel_id=1, source_target_pairs={{0,8},{2,10},{4,12},{6,14},{8,0},{10,2},{12,4},{14,6},{16,24},{18,... | collective-permute-start | bytes 393224 | tf_op jit(solution)/shard_map/ppermute | solution.py:74
  61.6 3.7 %collective-permute-done.10 = bf16[2,2,16,1024]{3,2,1,0:T(8,128)(2,1)S(1)} collective-permute-done((bf16[2,2,16,1024]{3,2,1,0:T(8,128)(2,1)S(1)}, bf16[2,2,16,1024]{3,2,1,0:T(8,128)(2,1)S(1)}, u32[]{:S(2)}, u32[]{:S(2)}) %collective-permute-start.10) | collective-permute-done | bytes 131104 | tf_op jit(solution)/shard_map/ppermute | solution.py:74
  67.1 2.1 %collective-permute-start.45 = (bf16[1,16,1024]{2,1,0:T(8,128)(2,1)S(1)}, bf16[1,16,1024]{2,1,0:T(8,128)(2,1)S(1)}, u32[]{:S(2)}, u32[]{:S(2)}) collective-permute-start(bf16[1,16,1024]{2,1,0:T(8,128)(2,1)S(1)} %get-tuple-element.115), channel_id=1, source_target_pairs={{0,8},{2,10},{4,12},{6,14},{8,0},{10,2},{12,4},{14,6},{16,24},{18,... | collective-permute-start | bytes 98312 | tf_op jit(solution)/shard_map/ppermute | solution.py:84
  72.0 2.4 %collective-permute-start.28 = (bf16[1,16,1024]{2,1,0:T(8,128)(2,1)S(1)}, bf16[1,16,1024]{2,1,0:T(8,128)(2,1)S(1)}, u32[]{:S(2)}, u32[]{:S(2)}) collective-permute-start(bf16[1,16,1024]{2,1,0:T(8,128)(2,1)S(1)} %get-tuple-element.114), channel_id=1, source_target_pairs={{0,8},{2,10},{4,12},{6,14},{8,0},{10,2},{12,4},{14,6},{16,24},{18,... | collective-permute-start | bytes 98312 | tf_op jit(solution)/shard_map/ppermute | solution.py:84
  77.1 1.6 collective-permute-start.46
  79.4 2.5 %collective-permute-start.38 = (bf16[1,2,16,1024]{3,2,1,0:T(8,128)(2,1)S(1)}, bf16[1,2,16,1024]{3,2,1,0:T(8,128)(2,1)S(1)}, u32[]{:S(2)}, u32[]{:S(2)}) collective-permute-start(bf16[1,2,16,1024]{3,2,1,0:T(8,128)(2,1)S(1)} %maximum_bitcast_fusion.32), channel_id=1, source_target_pairs={{0,16},{2,18},{4,20},{6,22},{8,24},{10,26},{12,28},{14,30},{16,0},... | collective-permute-start | bytes 196616 | tf_op jit(solution)/shard_map/ppermute | solution.py:84
  84.1 2.3 %collective-permute-start.13 = (bf16[1,2,16,1024]{3,2,1,0:T(8,128)(2,1)S(1)}, bf16[1,2,16,1024]{3,2,1,0:T(8,128)(2,1)S(1)}, u32[]{:S(2)}, u32[]{:S(2)}) collective-permute-start(bf16[1,2,16,1024]{3,2,1,0:T(8,128)(2,1)S(1)} %maximum_bitcast_fusion.28), channel_id=1, source_target_pairs={{0,16},{2,18},{4,20},{6,22},{8,24},{10,26},{12,28},{14,30},{16,0},... | collective-permute-start | bytes 196616 | tf_op jit(solution)/shard_map/ppermute | solution.py:84
  86.9 1.6 collective-permute-start.47
  88.5 1.7 %collective-permute-start.43 = (bf16[1,2,2,16,1024]{4,3,2,1,0:T(8,128)(2,1)S(1)}, bf16[1,2,2,16,1024]{4,3,2,1,0:T(8,128)(2,1)S(1)}, u32[]{:S(2)}, u32[]{:S(2)}) collective-permute-start(bf16[1,2,2,16,1024]{4,3,2,1,0:T(8,128)(2,1)S(1)} %maximum_bitcast_fusion.24), channel_id=1, source_target_pairs={{0,16},{2,18},{4,20},{6,22},{8,24},{10,26},{12,28},{14,30},{16,0},... | collective-permute-start | bytes 393224 | tf_op jit(solution)/shard_map/ppermute | solution.py:84
  93.3 2.8 %collective-permute-start.22 = (bf16[1,2,2,16,1024]{4,3,2,1,0:T(8,128)(2,1)S(1)}, bf16[1,2,2,16,1024]{4,3,2,1,0:T(8,128)(2,1)S(1)}, u32[]{:S(2)}, u32[]{:S(2)}) collective-permute-start(bf16[1,2,2,16,1024]{4,3,2,1,0:T(8,128)(2,1)S(1)} %maximum_bitcast_fusion.20), channel_id=1, source_target_pairs={{0,16},{2,18},{4,20},{6,22},{8,24},{10,26},{12,28},{14,30},{16,0},... | collective-permute-start | bytes 393224 | tf_op jit(solution)/shard_map/ppermute | solution.py:84
  96.1 2.1 %collective-permute-done.43 = bf16[1,2,2,16,1024]{4,3,2,1,0:T(8,128)(2,1)S(1)} collective-permute-done((bf16[1,2,2,16,1024]{4,3,2,1,0:T(8,128)(2,1)S(1)}, bf16[1,2,2,16,1024]{4,3,2,1,0:T(8,128)(2,1)S(1)}, u32[]{:S(2)}, u32[]{:S(2)}) %collective-permute-start.43) | collective-permute-done | bytes 131104 | tf_op jit(solution)/shard_map/ppermute | solution.py:84
  98.2 1.5 collective-permute-start.14
  99.9 3.9 %collective-permute-start.48 = (bf16[1,2,2,2,16,1024]{5,4,3,2,1,0:T(8,128)(2,1)S(1)}, bf16[1,2,2,2,16,1024]{5,4,3,2,1,0:T(8,128)(2,1)S(1)}, u32[]{:S(2)}, u32[]{:S(2)}) collective-permute-start(bf16[1,2,2,2,16,1024]{5,4,3,2,1,0:T(8,128)(2,1)S(1)} %maximum_bitcast_fusion.17), channel_id=1, source_target_pairs={{0,16},{2,18},{4,20},{6,22},{8,24},{10,26},{12,28},{14,30},{16,0},... | collective-permute-start | bytes 786440 | tf_op jit(solution)/shard_map/ppermute | solution.py:84
  104.1 2.1 %collective-permute-start.40 = (bf16[1,2,2,2,16,1024]{5,4,3,2,1,0:T(8,128)(2,1)S(1)}, bf16[1,2,2,2,16,1024]{5,4,3,2,1,0:T(8,128)(2,1)S(1)}, u32[]{:S(2)}, u32[]{:S(2)}) collective-permute-start(bf16[1,2,2,2,16,1024]{5,4,3,2,1,0:T(8,128)(2,1)S(1)} %maximum_bitcast_fusion.15), channel_id=1, source_target_pairs={{0,4},{2,6},{4,0},{6,2},{8,12},{10,14},{12,8},{14,10},{16,20},{18,... | collective-permute-start | bytes 786440 | tf_op jit(solution)/shard_map/ppermute | solution.py:84
  106.2 1.8 %collective-permute-start.36 = (bf16[1,2,2,2,16,1024]{5,4,3,2,1,0:T(8,128)(2,1)S(1)}, bf16[1,2,2,2,16,1024]{5,4,3,2,1,0:T(8,128)(2,1)S(1)}, u32[]{:S(2)}, u32[]{:S(2)}) collective-permute-start(bf16[1,2,2,2,16,1024]{5,4,3,2,1,0:T(8,128)(2,1)S(1)} %maximum_bitcast_fusion.14), channel_id=1, source_target_pairs={{0,2},{2,0},{4,6},{6,4},{8,10},{10,8},{12,14},{14,12},{16,18},{18,... | collective-permute-start | bytes 786440 | tf_op jit(solution)/shard_map/ppermute | solution.py:84
  109.4 6.5 %collective-permute-done.48 = bf16[1,2,2,2,16,1024]{5,4,3,2,1,0:T(8,128)(2,1)S(1)} collective-permute-done((bf16[1,2,2,2,16,1024]{5,4,3,2,1,0:T(8,128)(2,1)S(1)}, bf16[1,2,2,2,16,1024]{5,4,3,2,1,0:T(8,128)(2,1)S(1)}, u32[]{:S(2)}, u32[]{:S(2)}) %collective-permute-start.48) | collective-permute-done | bytes 262176 | tf_op jit(solution)/shard_map/ppermute | solution.py:84
  116.0 2.0 %collective-permute-done.44 = bf16[1,2,2,2,16,1024]{5,4,3,2,1,0:T(8,128)(2,1)S(1)} collective-permute-done((bf16[1,2,2,2,16,1024]{5,4,3,2,1,0:T(8,128)(2,1)S(1)}, bf16[1,2,2,2,16,1024]{5,4,3,2,1,0:T(8,128)(2,1)S(1)}, u32[]{:S(2)}, u32[]{:S(2)}) %collective-permute-start.44) | collective-permute-done | bytes 262176 | tf_op jit(solution)/shard_map/ppermute | solution.py:84
  120.9 1.5 maximum_bitcast_fusion.1.blk_ref
  122.4 11.9 %shard_map.47 = (f32[4,4,1024]{2,1,0:T(4,128)}, f32[4,4,128]{2,1,0:T(4,128)}) custom-call(s32[64]{0:T(128)} %squeeze.19.meta_ref, bf16[1,1024,1024]{2,1,0:T(8,128)(2,1)} %maximum_bitcast_fusion.1.blk_ref, bf16[1024,1152]{1,0:T(8,128)(2,1)} %copy-done.3), custom_call_target="tpu_custom_call" | custom-call | flops 5435817984 | bytes 4521984 | tf_op jit(solution)/shard_map/pallas_call | solution.py:155
  135.8 1.5 maximum_bitcast_fusion.blk_ref
  137.3 11.9 %shard_map.46 = (f32[4,4,1024]{2,1,0:T(4,128)}, f32[4,4,128]{2,1,0:T(4,128)}) custom-call(s32[64]{0:T(128)} %squeeze.16.meta_ref, bf16[1,1024,1024]{2,1,0:T(8,128)(2,1)} %maximum_bitcast_fusion.blk_ref, bf16[1024,1152]{1,0:T(8,128)(2,1)} %copy-done.3), custom_call_target="tpu_custom_call" | custom-call | flops 5435817984 | bytes 4521984 | tf_op jit(solution)/shard_map/pallas_call | solution.py:155
  159.1 2.3 %collective-permute-start.54 = (f32[32]{0:T(128)S(1)}, f32[32]{0:T(128)S(1)}, u32[]{:S(2)}, u32[]{:S(2)}) collective-permute-start(f32[32]{0:T(128)S(1)} %fusion.27), channel_id=1, source_target_pairs={{0,24},{2,26},{4,28},{6,30},{8,16},{10,18},{12,20},{14,22},{16,8},... | collective-permute-start | bytes 392 | tf_op jit(solution)/shard_map/ppermute | solution.py:34
  161.3 2.2 %collective-permute-start.56 = (f32[32]{0:T(128)S(1)}, f32[32]{0:T(128)S(1)}, u32[]{:S(2)}, u32[]{:S(2)}) collective-permute-start(f32[32]{0:T(128)S(1)} %fusion.27), channel_id=1, source_target_pairs={{0,8},{2,10},{4,12},{6,14},{8,0},{10,2},{12,4},{14,6},{16,24},{18,... | collective-permute-start | bytes 392 | tf_op jit(solution)/shard_map/ppermute | solution.py:34
  (284 shorter events, 58.3 us)
Async XLA Ops:
  1.7 27.1 %collective-permute-start.32 = (bf16[1024,128]{1,0:T(8,128)(2,1)}, bf16[1024,128]{1,0:T(8,128)(2,1)}, u32[]{:S(2)}, u32[]{:S(2)}) collective-permute-start(bf16[1024,128]{1,0:T(8,128)(2,1)} %slice.599), channel_id=1, source_target_pairs={{2,0},{4,2},{6,4},{8,6},{10,8},{12,10},{14,12},{16,14},{18,16},{20... | collective-permute-start | bytes 786440 | tf_op jit(solution)/shard_map/ppermute | solution.py:19
  8.0 30.8 %collective-permute-start.24 = (bf16[2,2,2,2,16,1024]{5,4,3,2,1,0:T(8,128)(2,1)}, bf16[2,2,2,2,16,1024]{5,4,3,2,1,0:T(8,128)(2,1)}, u32[]{:S(2)}, u32[]{:S(2)}) collective-permute-start(bf16[2,2,2,2,16,1024]{5,4,3,2,1,0:T(8,128)(2,1)} %pad_maximum_fusion.3), channel_id=1, source_target_pairs={{0,16},{2,18},{4,20},{6,22},{8,24},{10,26},{12,28},{14,30},{16,0},... | collective-permute-start | bytes 1572872 | tf_op jit(solution)/shard_map/ppermute | solution.py:74
  16.0 24.1 %collective-permute-start.16 = (bf16[2,2,2,2,16,1024]{5,4,3,2,1,0:T(8,128)(2,1)}, bf16[2,2,2,2,16,1024]{5,4,3,2,1,0:T(8,128)(2,1)}, u32[]{:S(2)}, u32[]{:S(2)}) collective-permute-start(bf16[2,2,2,2,16,1024]{5,4,3,2,1,0:T(8,128)(2,1)} %pad_maximum_fusion.2), channel_id=1, source_target_pairs={{0,8},{2,10},{4,12},{6,14},{8,0},{10,2},{12,4},{14,6},{16,24},{18,... | collective-permute-start | bytes 1572872 | tf_op jit(solution)/shard_map/ppermute | solution.py:74
  20.5 21.2 %collective-permute-start.8 = (bf16[2,2,2,2,16,1024]{5,4,3,2,1,0:T(8,128)(2,1)}, bf16[2,2,2,2,16,1024]{5,4,3,2,1,0:T(8,128)(2,1)}, u32[]{:S(2)}, u32[]{:S(2)}) collective-permute-start(bf16[2,2,2,2,16,1024]{5,4,3,2,1,0:T(8,128)(2,1)} %pad_maximum_fusion.1), channel_id=1, source_target_pairs={{0,4},{2,6},{4,0},{6,2},{8,12},{10,14},{12,8},{14,10},{16,20},{18,... | collective-permute-start | bytes 1572872 | tf_op jit(solution)/shard_map/ppermute | solution.py:74
  23.8 22.4 %collective-permute-start = (bf16[2,2,2,2,16,1024]{5,4,0,1,2,3:T(8,128)(2,1)}, bf16[2,2,2,2,16,1024]{5,4,0,1,2,3:T(8,128)(2,1)}, u32[]{:S(2)}, u32[]{:S(2)}) collective-permute-start(bf16[2,2,2,2,16,1024]{5,4,0,1,2,3:T(8,128)(2,1)} %pad_maximum_fusion), channel_id=1, source_target_pairs={{0,2},{2,0},{4,6},{6,4},{8,10},{10,8},{12,14},{14,12},{16,18},{18,... | collective-permute-start | bytes 1572872 | tf_op jit(solution)/shard_map/ppermute | solution.py:74
  40.0 9.6 %collective-permute-start.25 = (bf16[2,2,2,16,1024]{4,3,2,1,0:T(8,128)(2,1)S(1)}, bf16[2,2,2,16,1024]{4,3,2,1,0:T(8,128)(2,1)S(1)}, u32[]{:S(2)}, u32[]{:S(2)}) collective-permute-start(bf16[2,2,2,16,1024]{4,3,2,1,0:T(8,128)(2,1)S(1)} %pad_maximum_fusion.10), channel_id=1, source_target_pairs={{0,2},{2,0},{4,6},{6,4},{8,10},{10,8},{12,14},{14,12},{16,18},{18,... | collective-permute-start | bytes 786440 | tf_op jit(solution)/shard_map/ppermute | solution.py:74
  41.3 14.3 %collective-permute-start.17 = (bf16[2,2,2,16,1024]{4,3,2,1,0:T(8,128)(2,1)S(1)}, bf16[2,2,2,16,1024]{4,3,2,1,0:T(8,128)(2,1)S(1)}, u32[]{:S(2)}, u32[]{:S(2)}) collective-permute-start(bf16[2,2,2,16,1024]{4,3,2,1,0:T(8,128)(2,1)S(1)} %pad_maximum_fusion.8), channel_id=1, source_target_pairs={{0,16},{2,18},{4,20},{6,22},{8,24},{10,26},{12,28},{14,30},{16,0},... | collective-permute-start | bytes 786440 | tf_op jit(solution)/shard_map/ppermute | solution.py:74
  42.8 14.7 %collective-permute-start.9 = (bf16[2,2,2,16,1024]{4,3,2,1,0:T(8,128)(2,1)S(1)}, bf16[2,2,2,16,1024]{4,3,2,1,0:T(8,128)(2,1)S(1)}, u32[]{:S(2)}, u32[]{:S(2)}) collective-permute-start(bf16[2,2,2,16,1024]{4,3,2,1,0:T(8,128)(2,1)S(1)} %pad_maximum_fusion.6), channel_id=1, source_target_pairs={{0,8},{2,10},{4,12},{6,14},{8,0},{10,2},{12,4},{14,6},{16,24},{18,... | collective-permute-start | bytes 786440 | tf_op jit(solution)/shard_map/ppermute | solution.py:74
  48.4 9.3 %collective-permute-start.1 = (bf16[2,2,2,16,1024]{4,3,2,1,0:T(8,128)(2,1)S(1)}, bf16[2,2,2,16,1024]{4,3,2,1,0:T(8,128)(2,1)S(1)}, u32[]{:S(2)}, u32[]{:S(2)}) collective-permute-start(bf16[2,2,2,16,1024]{4,3,2,1,0:T(8,128)(2,1)S(1)} %pad_maximum_fusion.4), channel_id=1, source_target_pairs={{0,4},{2,6},{4,0},{6,2},{8,12},{10,14},{12,8},{14,10},{16,20},{18,... | collective-permute-start | bytes 786440 | tf_op jit(solution)/shard_map/ppermute | solution.py:74
  49.7 10.6 %collective-permute-start.26 = (bf16[2,2,16,1024]{3,2,1,0:T(8,128)(2,1)S(1)}, bf16[2,2,16,1024]{3,2,1,0:T(8,128)(2,1)S(1)}, u32[]{:S(2)}, u32[]{:S(2)}) collective-permute-start(bf16[2,2,16,1024]{3,2,1,0:T(8,128)(2,1)S(1)} %pad_maximum_fusion.23), channel_id=1, source_target_pairs={{0,4},{2,6},{4,0},{6,2},{8,12},{10,14},{12,8},{14,10},{16,20},{18,... | collective-permute-start | bytes 393224 | tf_op jit(solution)/shard_map/ppermute | solution.py:74
  57.6 7.6 %collective-permute-start.10 = (bf16[2,2,16,1024]{3,2,1,0:T(8,128)(2,1)S(1)}, bf16[2,2,16,1024]{3,2,1,0:T(8,128)(2,1)S(1)}, u32[]{:S(2)}, u32[]{:S(2)}) collective-permute-start(bf16[2,2,16,1024]{3,2,1,0:T(8,128)(2,1)S(1)} %pad_maximum_fusion.19), channel_id=1, source_target_pairs={{0,16},{2,18},{4,20},{6,22},{8,24},{10,26},{12,28},{14,30},{16,0},... | collective-permute-start | bytes 393224 | tf_op jit(solution)/shard_map/ppermute | solution.py:74
  57.9 8.5 %collective-permute-start.2 = (bf16[2,2,16,1024]{3,2,1,0:T(8,128)(2,1)S(1)}, bf16[2,2,16,1024]{3,2,1,0:T(8,128)(2,1)S(1)}, u32[]{:S(2)}, u32[]{:S(2)}) collective-permute-start(bf16[2,2,16,1024]{3,2,1,0:T(8,128)(2,1)S(1)} %pad_maximum_fusion.17), channel_id=1, source_target_pairs={{0,8},{2,10},{4,12},{6,14},{8,0},{10,2},{12,4},{14,6},{16,24},{18,... | collective-permute-start | bytes 393224 | tf_op jit(solution)/shard_map/ppermute | solution.py:74
  60.8 8.4 %collective-permute-start.19 = (bf16[2,16,1024]{2,1,0:T(8,128)(2,1)S(1)}, bf16[2,16,1024]{2,1,0:T(8,128)(2,1)S(1)}, u32[]{:S(2)}, u32[]{:S(2)}) collective-permute-start(bf16[2,16,1024]{2,1,0:T(8,128)(2,1)S(1)} %pad_maximum_fusion.33), channel_id=1, source_target_pairs={{0,4},{2,6},{4,0},{6,2},{8,12},{10,14},{12,8},{14,10},{16,20},{18,... | collective-permute-start | bytes 196616 | tf_op jit(solution)/shard_map/ppermute | solution.py:74
  67.1 7.3 %collective-permute-start.45 = (bf16[1,16,1024]{2,1,0:T(8,128)(2,1)S(1)}, bf16[1,16,1024]{2,1,0:T(8,128)(2,1)S(1)}, u32[]{:S(2)}, u32[]{:S(2)}) collective-permute-start(bf16[1,16,1024]{2,1,0:T(8,128)(2,1)S(1)} %get-tuple-element.115), channel_id=1, source_target_pairs={{0,8},{2,10},{4,12},{6,14},{8,0},{10,2},{12,4},{14,6},{16,24},{18,... | collective-permute-start | bytes 98312 | tf_op jit(solution)/shard_map/ppermute | solution.py:84
  79.4 7.1 %collective-permute-start.38 = (bf16[1,2,16,1024]{3,2,1,0:T(8,128)(2,1)S(1)}, bf16[1,2,16,1024]{3,2,1,0:T(8,128)(2,1)S(1)}, u32[]{:S(2)}, u32[]{:S(2)}) collective-permute-start(bf16[1,2,16,1024]{3,2,1,0:T(8,128)(2,1)S(1)} %maximum_bitcast_fusion.32), channel_id=1, source_target_pairs={{0,16},{2,18},{4,20},{6,22},{8,24},{10,26},{12,28},{14,30},{16,0},... | collective-permute-start | bytes 196616 | tf_op jit(solution)/shard_map/ppermute | solution.py:84
  83.3 7.0 %collective-permute-start.21 = (bf16[1,2,16,1024]{3,2,1,0:T(8,128)(2,1)S(1)}, bf16[1,2,16,1024]{3,2,1,0:T(8,128)(2,1)S(1)}, u32[]{:S(2)}, u32[]{:S(2)}) collective-permute-start(bf16[1,2,16,1024]{3,2,1,0:T(8,128)(2,1)S(1)} %maximum_bitcast_fusion.29), channel_id=1, source_target_pairs={{0,2},{2,0},{4,6},{6,4},{8,10},{10,8},{12,14},{14,12},{16,18},{18,... | collective-permute-start | bytes 196616 | tf_op jit(solution)/shard_map/ppermute | solution.py:84
  84.1 7.4 %collective-permute-start.13 = (bf16[1,2,16,1024]{3,2,1,0:T(8,128)(2,1)S(1)}, bf16[1,2,16,1024]{3,2,1,0:T(8,128)(2,1)S(1)}, u32[]{:S(2)}, u32[]{:S(2)}) collective-permute-start(bf16[1,2,16,1024]{3,2,1,0:T(8,128)(2,1)S(1)} %maximum_bitcast_fusion.28), channel_id=1, source_target_pairs={{0,16},{2,18},{4,20},{6,22},{8,24},{10,26},{12,28},{14,30},{16,0},... | collective-permute-start | bytes 196616 | tf_op jit(solution)/shard_map/ppermute | solution.py:84
  88.5 9.7 %collective-permute-start.43 = (bf16[1,2,2,16,1024]{4,3,2,1,0:T(8,128)(2,1)S(1)}, bf16[1,2,2,16,1024]{4,3,2,1,0:T(8,128)(2,1)S(1)}, u32[]{:S(2)}, u32[]{:S(2)}) collective-permute-start(bf16[1,2,2,16,1024]{4,3,2,1,0:T(8,128)(2,1)S(1)} %maximum_bitcast_fusion.24), channel_id=1, source_target_pairs={{0,16},{2,18},{4,20},{6,22},{8,24},{10,26},{12,28},{14,30},{16,0},... | collective-permute-start | bytes 393224 | tf_op jit(solution)/shard_map/ppermute | solution.py:84
  90.3 9.5 %collective-permute-start.39 = (bf16[1,2,2,16,1024]{4,3,2,1,0:T(8,128)(2,1)S(1)}, bf16[1,2,2,16,1024]{4,3,2,1,0:T(8,128)(2,1)S(1)}, u32[]{:S(2)}, u32[]{:S(2)}) collective-permute-start(bf16[1,2,2,16,1024]{4,3,2,1,0:T(8,128)(2,1)S(1)} %maximum_bitcast_fusion.23), channel_id=1, source_target_pairs={{0,8},{2,10},{4,12},{6,14},{8,0},{10,2},{12,4},{14,6},{16,24},{18,... | collective-permute-start | bytes 393224 | tf_op jit(solution)/shard_map/ppermute | solution.py:84
  91.5 8.4 %collective-permute-start.35 = (bf16[1,2,2,16,1024]{4,3,2,1,0:T(8,128)(2,1)S(1)}, bf16[1,2,2,16,1024]{4,3,2,1,0:T(8,128)(2,1)S(1)}, u32[]{:S(2)}, u32[]{:S(2)}) collective-permute-start(bf16[1,2,2,16,1024]{4,3,2,1,0:T(8,128)(2,1)S(1)} %maximum_bitcast_fusion.22), channel_id=1, source_target_pairs={{0,4},{2,6},{4,0},{6,2},{8,12},{10,14},{12,8},{14,10},{16,20},{18,... | collective-permute-start | bytes 393224 | tf_op jit(solution)/shard_map/ppermute | solution.py:84
  91.9 12.0 %collective-permute-start.30 = (bf16[1,2,2,16,1024]{4,3,2,1,0:T(8,128)(2,1)S(1)}, bf16[1,2,2,16,1024]{4,3,2,1,0:T(8,128)(2,1)S(1)}, u32[]{:S(2)}, u32[]{:S(2)}) collective-permute-start(bf16[1,2,2,16,1024]{4,3,2,1,0:T(8,128)(2,1)S(1)} %maximum_bitcast_fusion.21), channel_id=1, source_target_pairs={{0,2},{2,0},{4,6},{6,4},{8,10},{10,8},{12,14},{14,12},{16,18},{18,... | collective-permute-start | bytes 393224 | tf_op jit(solution)/shard_map/ppermute | solution.py:84
  93.3 10.8 %collective-permute-start.22 = (bf16[1,2,2,16,1024]{4,3,2,1,0:T(8,128)(2,1)S(1)}, bf16[1,2,2,16,1024]{4,3,2,1,0:T(8,128)(2,1)S(1)}, u32[]{:S(2)}, u32[]{:S(2)}) collective-permute-start(bf16[1,2,2,16,1024]{4,3,2,1,0:T(8,128)(2,1)S(1)} %maximum_bitcast_fusion.20), channel_id=1, source_target_pairs={{0,16},{2,18},{4,20},{6,22},{8,24},{10,26},{12,28},{14,30},{16,0},... | collective-permute-start | bytes 393224 | tf_op jit(solution)/shard_map/ppermute | solution.py:84
  98.2 8.0 %collective-permute-start.14 = (bf16[1,2,2,16,1024]{4,3,2,1,0:T(8,128)(2,1)S(1)}, bf16[1,2,2,16,1024]{4,3,2,1,0:T(8,128)(2,1)S(1)}, u32[]{:S(2)}, u32[]{:S(2)}) collective-permute-start(bf16[1,2,2,16,1024]{4,3,2,1,0:T(8,128)(2,1)S(1)} %maximum_bitcast_fusion.19), channel_id=1, source_target_pairs={{0,8},{2,10},{4,12},{6,14},{8,0},{10,2},{12,4},{14,6},{16,24},{18,... | collective-permute-start | bytes 393224 | tf_op jit(solution)/shard_map/ppermute | solution.py:84
  99.8 8.4 %collective-permute-start.6 = (bf16[1,2,2,16,1024]{4,3,2,1,0:T(8,128)(2,1)S(1)}, bf16[1,2,2,16,1024]{4,3,2,1,0:T(8,128)(2,1)S(1)}, u32[]{:S(2)}, u32[]{:S(2)}) collective-permute-start(bf16[1,2,2,16,1024]{4,3,2,1,0:T(8,128)(2,1)S(1)} %maximum_bitcast_fusion.18), channel_id=1, source_target_pairs={{0,4},{2,6},{4,0},{6,2},{8,12},{10,14},{12,8},{14,10},{16,20},{18,... | collective-permute-start | bytes 393224 | tf_op jit(solution)/shard_map/ppermute | solution.py:84
  99.9 15.9 %collective-permute-start.48 = (bf16[1,2,2,2,16,1024]{5,4,3,2,1,0:T(8,128)(2,1)S(1)}, bf16[1,2,2,2,16,1024]{5,4,3,2,1,0:T(8,128)(2,1)S(1)}, u32[]{:S(2)}, u32[]{:S(2)}) collective-permute-start(bf16[1,2,2,2,16,1024]{5,4,3,2,1,0:T(8,128)(2,1)S(1)} %maximum_bitcast_fusion.17), channel_id=1, source_target_pairs={{0,16},{2,18},{4,20},{6,22},{8,24},{10,26},{12,28},{14,30},{16,0},... | collective-permute-start | bytes 786440 | tf_op jit(solution)/shard_map/ppermute | solution.py:84
  103.9 14.1 %collective-permute-start.44 = (bf16[1,2,2,2,16,1024]{5,4,3,2,1,0:T(8,128)(2,1)S(1)}, bf16[1,2,2,2,16,1024]{5,4,3,2,1,0:T(8,128)(2,1)S(1)}, u32[]{:S(2)}, u32[]{:S(2)}) collective-permute-start(bf16[1,2,2,2,16,1024]{5,4,3,2,1,0:T(8,128)(2,1)S(1)} %maximum_bitcast_fusion.16), channel_id=1, source_target_pairs={{0,8},{2,10},{4,12},{6,14},{8,0},{10,2},{12,4},{14,6},{16,24},{18,... | collective-permute-start | bytes 786440 | tf_op jit(solution)/shard_map/ppermute | solution.py:84
  104.1 15.4 %collective-permute-start.40 = (bf16[1,2,2,2,16,1024]{5,4,3,2,1,0:T(8,128)(2,1)S(1)}, bf16[1,2,2,2,16,1024]{5,4,3,2,1,0:T(8,128)(2,1)S(1)}, u32[]{:S(2)}, u32[]{:S(2)}) collective-permute-start(bf16[1,2,2,2,16,1024]{5,4,3,2,1,0:T(8,128)(2,1)S(1)} %maximum_bitcast_fusion.15), channel_id=1, source_target_pairs={{0,4},{2,6},{4,0},{6,2},{8,12},{10,14},{12,8},{14,10},{16,20},{18,... | collective-permute-start | bytes 786440 | tf_op jit(solution)/shard_map/ppermute | solution.py:84
  106.2 14.5 %collective-permute-start.36 = (bf16[1,2,2,2,16,1024]{5,4,3,2,1,0:T(8,128)(2,1)S(1)}, bf16[1,2,2,2,16,1024]{5,4,3,2,1,0:T(8,128)(2,1)S(1)}, u32[]{:S(2)}, u32[]{:S(2)}) collective-permute-start(bf16[1,2,2,2,16,1024]{5,4,3,2,1,0:T(8,128)(2,1)S(1)} %maximum_bitcast_fusion.14), channel_id=1, source_target_pairs={{0,2},{2,0},{4,6},{6,4},{8,10},{10,8},{12,14},{14,12},{16,18},{18,... | collective-permute-start | bytes 786440 | tf_op jit(solution)/shard_map/ppermute | solution.py:84
  108.1 27.0 %collective-permute-start.31 = (bf16[1,2,2,2,16,1024]{5,4,3,2,1,0:T(8,128)(2,1)S(1)}, bf16[1,2,2,2,16,1024]{5,4,3,2,1,0:T(8,128)(2,1)S(1)}, u32[]{:S(2)}, u32[]{:S(2)}) collective-permute-start(bf16[1,2,2,2,16,1024]{5,4,3,2,1,0:T(8,128)(2,1)S(1)} %maximum_bitcast_fusion.13), channel_id=1, source_target_pairs={{0,16},{2,18},{4,20},{6,22},{8,24},{10,26},{12,28},{14,30},{16,0},... | collective-permute-start | bytes 786440 | tf_op jit(solution)/shard_map/ppermute | solution.py:84
  115.9 19.4 %collective-permute-start.23 = (bf16[1,2,2,2,16,1024]{5,4,3,2,1,0:T(8,128)(2,1)S(1)}, bf16[1,2,2,2,16,1024]{5,4,3,2,1,0:T(8,128)(2,1)S(1)}, u32[]{:S(2)}, u32[]{:S(2)}) collective-permute-start(bf16[1,2,2,2,16,1024]{5,4,3,2,1,0:T(8,128)(2,1)S(1)} %maximum_bitcast_fusion.12), channel_id=1, source_target_pairs={{0,8},{2,10},{4,12},{6,14},{8,0},{10,2},{12,4},{14,6},{16,24},{18,... | collective-permute-start | bytes 786440 | tf_op jit(solution)/shard_map/ppermute | solution.py:84
  118.0 17.4 %collective-permute-start.15 = (bf16[1,2,2,2,16,1024]{5,4,3,2,1,0:T(8,128)(2,1)S(1)}, bf16[1,2,2,2,16,1024]{5,4,3,2,1,0:T(8,128)(2,1)S(1)}, u32[]{:S(2)}, u32[]{:S(2)}) collective-permute-start(bf16[1,2,2,2,16,1024]{5,4,3,2,1,0:T(8,128)(2,1)S(1)} %maximum_bitcast_fusion.11), channel_id=1, source_target_pairs={{0,4},{2,6},{4,0},{6,2},{8,12},{10,14},{12,8},{14,10},{16,20},{18,... | collective-permute-start | bytes 786440 | tf_op jit(solution)/shard_map/ppermute | solution.py:84
  119.5 16.2 %collective-permute-start.7 = (bf16[1,2,2,2,16,1024]{5,4,3,2,1,0:T(8,128)(2,1)S(1)}, bf16[1,2,2,2,16,1024]{5,4,3,2,1,0:T(8,128)(2,1)S(1)}, u32[]{:S(2)}, u32[]{:S(2)}) collective-permute-start(bf16[1,2,2,2,16,1024]{5,4,3,2,1,0:T(8,128)(2,1)S(1)} %maximum_bitcast_fusion.10), channel_id=1, source_target_pairs={{0,2},{2,0},{4,6},{6,4},{8,10},{10,8},{12,14},{14,12},{16,18},{18,... | collective-permute-start | bytes 786440 | tf_op jit(solution)/shard_map/ppermute | solution.py:84
  (34 other events, 187.2 us)

commit v8 on v6

--- a/solution.py
+++ b/solution.py
@@ -200,16 +200,18 @@
     energy_local = window_sum(summed, L, lag_count)
 
     meta = meta.astype(jnp.int32).reshape(rounds, -1)
-    pieces = [correlate(meta[r], blocks[r : r + 1], extended, count) for r in range(rounds)]
-    corr_local = jnp.concatenate([c for c, _ in pieces])
-    local_power = jnp.concatenate([p for _, p in pieces])
-    tmpl_power = group_sum(local_power, "sec")
-    both = group_sum(jnp.stack([corr_local, energy_local]), "sec")
-    corr, energy = both[0], both[1]
-    normed = corr / jnp.sqrt(energy * tmpl_power[:, None] + EPS)
-    power_sum = group_sum(jnp.sum(normed * normed, axis=1), "tm")
+    energy = group_sum(energy_local, "sec").reshape(rounds, count, lag_count)
+    normed, power = [], []
+    for r in range(rounds):
+        corr_local, local_power = correlate(meta[r], blocks[r : r + 1], extended, count)
+        corr = group_sum(corr_local, "sec")
+        tmpl_power = group_sum(local_power, "sec")
+        cc = corr / jnp.sqrt(energy[r] * tmpl_power[:, None] + EPS)
+        normed.append(cc)
+        power.append(jnp.sum(cc * cc, axis=1))
+    power_sum = group_sum(jnp.stack(power), "tm")
     meansq = power_sum / total_lags
-    scored = normed / jnp.sqrt(meansq[:, None] + EPS)
+    scored = jnp.stack(normed) / jnp.sqrt(meansq[:, :, None] + EPS)
     return scored.reshape(rounds, count, lag_count)
 
 

time: 158 us -> 177 us (1.12)
  starting transfers between devices: 52.3 us -> 81 us
  waiting for transfers between devices: 44 us -> 36.6 us
    ppermute x36, starting transfers between devices: 42.5 us -> 67.9 us  [spread_blocks(): lax.ppermute(jnp.stack([v for _, v in items]), axis, [(i, i ^ mask) for i...]
    ppermute x36, waiting for transfers between devices: 38.8 us -> 26.6 us  [spread_blocks(): lax.ppermute(jnp.stack([v for _, v in items]), axis, [(i, i ^ mask) for i...]
    ppermute x1, waiting for transfers between devices: 0.01 us -> 5.51 us  [from_behind(): return lax.ppermute(value, axis, pairs)]
    ppermute x8 -> x11, starting transfers between devices: 8.57 us -> 11.8 us  [group_sum(): got[d] = lax.ppermute(value, axis, pairs)]
    ppermute x8 -> x11, waiting for transfers between devices: 5.15 us -> 4.55 us  [group_sum(): got[d] = lax.ppermute(value, axis, pairs)]
    unnamed x20 -> x18, local copies, waits for them, and re-layouts: 4.37 us -> 4.35 us
  transfers between devices with their start and end apart: 45 -> 48, of which waited for: 21 -> 17; matrix products, arithmetic and copies ran while one was open for 18% -> 14% of each run, Pallas kernels for 7% -> 13%
where the time goes in v8:
time: 177 us
  starting transfers between devices  81 us (46%)
  waiting for transfers between devices  36.6 us (21%)
  Pallas kernels  23.6 us (13%)
  other arithmetic  16.9 us (10%)
  local copies, waits for them, and re-layouts  14.3 us (8%)
  between operations  2.68 us (2%)
    ppermute x36, starting transfers between devices, spread_blocks(): lax.ppermute(jnp.stack([v for _, v in items]), axis, [(i, i ^ mask) for i...  67.9 us
    ppermute x36, waiting for transfers between devices, spread_blocks(): lax.ppermute(jnp.stack([v for _, v in items]), axis, [(i, i ^ mask) for i...  26.6 us
    pallas_call x2, Pallas kernels, correlate(): pl.pallas_call(correlate_kernel, grid_spec=grid_spec, out_shape=[jax.Shap...  23.6 us
    ppermute x11, starting transfers between devices, group_sum(): got[d] = lax.ppermute(value, axis, pairs)  11.8 us
    select_n x18, other arithmetic, spread_blocks(): bufs[key] = jnp.where(holder, keeps[key], got[n])  5.7 us
    ppermute x1, waiting for transfers between devices, from_behind(): return lax.ppermute(value, axis, pairs)  5.51 us
    ppermute x11, waiting for transfers between devices, group_sum(): got[d] = lax.ppermute(value, axis, pairs)  4.55 us
    unnamed x18, local copies, waits for them, and re-layouts  4.35 us
  transfers between devices with their start and end apart: 48, of which 17 were waited for; matrix products, arithmetic and copies ran while one was open for 14% of the time, Pallas kernels for 13%

profile of v8, /device:TPU:0, one launch (start us, length us, event | category | flops | bytes accessed | tf_op | source)
XLA Modules:
  0.0 176.5 jit_solution(4569405422941899800)
XLA Ops:
  0.0 2.9 %copy.32 = bf16[1024,1024]{0,1:T(8,128)(2,1)S(1)} copy(bf16[1024,1024]{1,0:T(8,128)(2,1)} %param.4) | data formatting | bytes 4194304 | tf_op args[0]
  5.5 2.9 %collective-permute-start = (bf16[2,2,2,2,16,1024]{5,4,0,1,2,3:T(8,128)(2,1)}, bf16[2,2,2,2,16,1024]{5,4,0,1,2,3:T(8,128)(2,1)}, u32[]{:S(2)}, u32[]{:S(2)}) collective-permute-start(bf16[2,2,2,2,16,1024]{5,4,0,1,2,3:T(8,128)(2,1)} %pad_maximum_fusion), channel_id=1, source_target_pairs={{0,2},{2,0},{4,6},{6,4},{8,10},{10,8},{12,14},{14,12},{16,18},{18,... | collective-permute-start | bytes 1572872 | tf_op jit(solution)/shard_map/ppermute | solution.py:73
  9.4 1.5 collective-permute-start.8
  11.9 1.6 collective-permute-start.16
  16.2 2.6 %collective-permute-start.24 = (bf16[2,2,2,2,16,1024]{5,4,3,2,1,0:T(8,128)(2,1)}, bf16[2,2,2,2,16,1024]{5,4,3,2,1,0:T(8,128)(2,1)}, u32[]{:S(2)}, u32[]{:S(2)}) collective-permute-start(bf16[2,2,2,2,16,1024]{5,4,3,2,1,0:T(8,128)(2,1)} %pad_maximum_fusion.3), channel_id=1, source_target_pairs={{0,16},{2,18},{4,20},{6,22},{8,24},{10,26},{12,28},{14,30},{16,0},... | collective-permute-start | bytes 1572872 | tf_op jit(solution)/shard_map/ppermute | solution.py:73
  23.2 5.5 %collective-permute-done.32 = bf16[1024,128]{1,0:T(8,128)(2,1)} collective-permute-done((bf16[1024,128]{1,0:T(8,128)(2,1)}, bf16[1024,128]{1,0:T(8,128)(2,1)}, u32[]{:S(2)}, u32[]{:S(2)}) %collective-permute-start.32) | collective-permute-done | bytes 262176 | tf_op jit(solution)/shard_map/ppermute | solution.py:18
  38.0 11.0 %collective-permute-start.9 = (bf16[2,2,2,16,1024]{4,3,2,1,0:T(8,128)(2,1)S(1)}, bf16[2,2,2,16,1024]{4,3,2,1,0:T(8,128)(2,1)S(1)}, u32[]{:S(2)}, u32[]{:S(2)}) collective-permute-start(bf16[2,2,2,16,1024]{4,3,2,1,0:T(8,128)(2,1)S(1)} %pad_maximum_fusion.7), channel_id=1, source_target_pairs={{0,8},{2,10},{4,12},{6,14},{8,0},{10,2},{12,4},{14,6},{16,24},{18,... | collective-permute-start | bytes 786440 | tf_op jit(solution)/shard_map/ppermute | solution.py:73
  50.2 6.6 %collective-permute-start.17 = (bf16[2,2,2,16,1024]{4,3,2,1,0:T(8,128)(2,1)S(1)}, bf16[2,2,2,16,1024]{4,3,2,1,0:T(8,128)(2,1)S(1)}, u32[]{:S(2)}, u32[]{:S(2)}) collective-permute-start(bf16[2,2,2,16,1024]{4,3,2,1,0:T(8,128)(2,1)S(1)} %pad_maximum_fusion.10), channel_id=1, source_target_pairs={{0,16},{2,18},{4,20},{6,22},{8,24},{10,26},{12,28},{14,30},{16,0},... | collective-permute-start | bytes 786440 | tf_op jit(solution)/shard_map/ppermute | solution.py:73
  58.0 4.0 %collective-permute-start.25 = (bf16[2,2,2,16,1024]{4,3,2,1,0:T(8,128)(2,1)S(1)}, bf16[2,2,2,16,1024]{4,3,2,1,0:T(8,128)(2,1)S(1)}, u32[]{:S(2)}, u32[]{:S(2)}) collective-permute-start(bf16[2,2,2,16,1024]{4,3,2,1,0:T(8,128)(2,1)S(1)} %pad_maximum_fusion.13), channel_id=1, source_target_pairs={{0,2},{2,0},{4,6},{6,4},{8,10},{10,8},{12,14},{14,12},{16,18},{18,... | collective-permute-start | bytes 786440 | tf_op jit(solution)/shard_map/ppermute | solution.py:73
  62.3 3.0 %collective-permute-start.10 = (bf16[2,2,16,1024]{3,2,1,0:T(8,128)(2,1)S(1)}, bf16[2,2,16,1024]{3,2,1,0:T(8,128)(2,1)S(1)}, u32[]{:S(2)}, u32[]{:S(2)}) collective-permute-start(bf16[2,2,16,1024]{3,2,1,0:T(8,128)(2,1)S(1)} %pad_maximum_fusion.23), channel_id=1, source_target_pairs={{0,16},{2,18},{4,20},{6,22},{8,24},{10,26},{12,28},{14,30},{16,0},... | collective-permute-start | bytes 393224 | tf_op jit(solution)/shard_map/ppermute | solution.py:73
  65.4 13.3 %collective-permute-start.18 = (bf16[2,2,16,1024]{3,2,1,0:T(8,128)(2,1)S(1)}, bf16[2,2,16,1024]{3,2,1,0:T(8,128)(2,1)S(1)}, u32[]{:S(2)}, u32[]{:S(2)}) collective-permute-start(bf16[2,2,16,1024]{3,2,1,0:T(8,128)(2,1)S(1)} %pad_maximum_fusion.26), channel_id=1, source_target_pairs={{0,2},{2,0},{4,6},{6,4},{8,10},{10,8},{12,14},{14,12},{16,18},{18,... | collective-permute-start | bytes 393224 | tf_op jit(solution)/shard_map/ppermute | solution.py:73
  79.4 2.3 %collective-permute-start.11 = (bf16[2,16,1024]{2,1,0:T(8,128)(2,1)S(1)}, bf16[2,16,1024]{2,1,0:T(8,128)(2,1)S(1)}, u32[]{:S(2)}, u32[]{:S(2)}) collective-permute-start(bf16[2,16,1024]{2,1,0:T(8,128)(2,1)S(1)} %pad_maximum_fusion.40), channel_id=1, source_target_pairs={{0,2},{2,0},{4,6},{6,4},{8,10},{10,8},{12,14},{14,12},{16,18},{18,... | collective-permute-start | bytes 196616 | tf_op jit(solution)/shard_map/ppermute | solution.py:73
  82.2 2.3 %collective-permute-done.26 = bf16[2,2,16,1024]{3,2,1,0:T(8,128)(2,1)S(1)} collective-permute-done((bf16[2,2,16,1024]{3,2,1,0:T(8,128)(2,1)S(1)}, bf16[2,2,16,1024]{3,2,1,0:T(8,128)(2,1)S(1)}, u32[]{:S(2)}, u32[]{:S(2)}) %collective-permute-start.26) | collective-permute-done | bytes 131104 | tf_op jit(solution)/shard_map/ppermute | solution.py:73
  84.9 1.8 collective-permute-start.12
  87.0 3.1 %collective-permute-done.27 = bf16[2,16,1024]{2,1,0:T(8,128)(2,1)S(1)} collective-permute-done((bf16[2,16,1024]{2,1,0:T(8,128)(2,1)S(1)}, bf16[2,16,1024]{2,1,0:T(8,128)(2,1)S(1)}, u32[]{:S(2)}, u32[]{:S(2)}) %collective-permute-start.27) | collective-permute-done | bytes 65568 | tf_op jit(solution)/shard_map/ppermute | solution.py:73
  90.4 2.6 %collective-permute-start.5 = (bf16[2,2,16,1024]{3,2,1,0:T(8,128)(2,1)S(1)}, bf16[2,2,16,1024]{3,2,1,0:T(8,128)(2,1)S(1)}, u32[]{:S(2)}, u32[]{:S(2)}) collective-permute-start(bf16[2,2,16,1024]{3,2,1,0:T(8,128)(2,1)S(1)} %pad_maximum_fusion.21), channel_id=1, source_target_pairs={{0,8},{2,10},{4,12},{6,14},{8,0},{10,2},{12,4},{14,6},{16,24},{18,... | collective-permute-start | bytes 393224 | tf_op jit(solution)/shard_map/ppermute | solution.py:83
  96.7 2.1 %collective-permute-start.6 = (bf16[2,2,2,16,1024]{4,3,2,1,0:T(8,128)(2,1)S(1)}, bf16[2,2,2,16,1024]{4,3,2,1,0:T(8,128)(2,1)S(1)}, u32[]{:S(2)}, u32[]{:S(2)}) collective-permute-start(bf16[2,2,2,16,1024]{4,3,2,1,0:T(8,128)(2,1)S(1)} %pad_maximum_fusion.5), channel_id=1, source_target_pairs={{0,4},{2,6},{4,0},{6,2},{8,12},{10,14},{12,8},{14,10},{16,20},{18,... | collective-permute-start | bytes 786440 | tf_op jit(solution)/shard_map/ppermute | solution.py:83
  98.8 1.8 %collective-permute-done.13 = bf16[2,2,16,1024]{3,2,1,0:T(8,128)(2,1)S(1)} collective-permute-done((bf16[2,2,16,1024]{3,2,1,0:T(8,128)(2,1)S(1)}, bf16[2,2,16,1024]{3,2,1,0:T(8,128)(2,1)S(1)}, u32[]{:S(2)}, u32[]{:S(2)}) %collective-permute-start.13) | collective-permute-done | bytes 131104 | tf_op jit(solution)/shard_map/ppermute | solution.py:83
  105.7 8.3 %collective-permute-done.14 = bf16[2,2,2,16,1024]{4,3,2,1,0:T(8,128)(2,1)S(1)} collective-permute-done((bf16[2,2,2,16,1024]{4,3,2,1,0:T(8,128)(2,1)S(1)}, bf16[2,2,2,16,1024]{4,3,2,1,0:T(8,128)(2,1)S(1)}, u32[]{:S(2)}, u32[]{:S(2)}) %collective-permute-start.14) | collective-permute-done | bytes 262176 | tf_op jit(solution)/shard_map/ppermute | solution.py:83
  114.9 1.8 %collective-permute-start.15 = (bf16[1,2,2,2,16,1024]{5,4,3,2,1,0:T(8,128)(2,1)S(1)}, bf16[1,2,2,2,16,1024]{5,4,3,2,1,0:T(8,128)(2,1)S(1)}, u32[]{:S(2)}, u32[]{:S(2)}) collective-permute-start(bf16[1,2,2,2,16,1024]{5,4,3,2,1,0:T(8,128)(2,1)S(1)} %maximum_bitcast_fusion.11), channel_id=1, source_target_pairs={{0,4},{2,6},{4,0},{6,2},{8,12},{10,14},{12,8},{14,10},{16,20},{18,... | collective-permute-start | bytes 786440 | tf_op jit(solution)/shard_map/ppermute | solution.py:83
  116.8 1.9 %collective-permute-start.23 = (bf16[1,2,2,2,16,1024]{5,4,3,2,1,0:T(8,128)(2,1)S(1)}, bf16[1,2,2,2,16,1024]{5,4,3,2,1,0:T(8,128)(2,1)S(1)}, u32[]{:S(2)}, u32[]{:S(2)}) collective-permute-start(bf16[1,2,2,2,16,1024]{5,4,3,2,1,0:T(8,128)(2,1)S(1)} %maximum_bitcast_fusion.12), channel_id=1, source_target_pairs={{0,8},{2,10},{4,12},{6,14},{8,0},{10,2},{12,4},{14,6},{16,24},{18,... | collective-permute-start | bytes 786440 | tf_op jit(solution)/shard_map/ppermute | solution.py:83
  118.9 1.6 collective-permute-done.37
  122.0 4.8 %collective-permute-done.38 = bf16[1,2,2,2,16,1024]{5,4,3,2,1,0:T(8,128)(2,1)S(1)} collective-permute-done((bf16[1,2,2,2,16,1024]{5,4,3,2,1,0:T(8,128)(2,1)S(1)}, bf16[1,2,2,2,16,1024]{5,4,3,2,1,0:T(8,128)(2,1)S(1)}, u32[]{:S(2)}, u32[]{:S(2)}) %collective-permute-start.38) | collective-permute-done | bytes 262176 | tf_op jit(solution)/shard_map/ppermute | solution.py:83
  126.9 1.5 collective-permute-done.39
  128.5 1.5 maximum_bitcast_fusion.1.blk_ref
  130.1 11.9 %shard_map.47 = (f32[4,4,1024]{2,1,0:T(4,128)}, f32[4,4,128]{2,1,0:T(4,128)}) custom-call(s32[64]{0:T(128)} %squeeze.11.meta_ref, bf16[1,1024,1024]{2,1,0:T(8,128)(2,1)} %maximum_bitcast_fusion.1.blk_ref, bf16[1024,1152]{1,0:T(8,128)(2,1)} %copy-done.3), custom_call_target="tpu_custom_call" | custom-call | flops 5435817984 | bytes 4521984 | tf_op jit(solution)/shard_map/pallas_call | solution.py:154
  144.9 1.5 maximum_bitcast_fusion.blk_ref
  146.4 11.7 %shard_map.46 = (f32[4,4,1024]{2,1,0:T(4,128)}, f32[4,4,128]{2,1,0:T(4,128)}) custom-call(s32[64]{0:T(128)} %squeeze.8.meta_ref, bf16[1,1024,1024]{2,1,0:T(8,128)(2,1)} %maximum_bitcast_fusion.blk_ref, bf16[1024,1152]{1,0:T(8,128)(2,1)} %copy-done.3), custom_call_target="tpu_custom_call" | custom-call | flops 5435817984 | bytes 4521984 | tf_op jit(solution)/shard_map/pallas_call | solution.py:154
  162.7 3.4 %collective-permute-start.43 = (f32[2,16]{1,0:T(2,128)S(1)}, f32[2,16]{1,0:T(2,128)S(1)}, u32[]{:S(2)}, u32[]{:S(2)}) collective-permute-start(f32[2,16]{1,0:T(2,128)S(1)} %pad_maximum_fusion.52), channel_id=1, source_target_pairs={{0,4},{2,6},{4,0},{6,2},{8,12},{10,14},{12,8},{14,10},{16,20},{18,... | collective-permute-start | bytes 392 | tf_op jit(solution)/shard_map/ppermute | solution.py:33
  166.2 1.4 collective-permute-start.44
  167.7 2.0 %collective-permute-done.44 = f32[2,16]{1,0:T(2,128)S(1)} collective-permute-done((f32[2,16]{1,0:T(2,128)S(1)}, f32[2,16]{1,0:T(2,128)S(1)}, u32[]{:S(2)}, u32[]{:S(2)}) %collective-permute-start.44) | collective-permute-done | bytes 160 | tf_op jit(solution)/shard_map/ppermute | solution.py:33
  169.9 4.3 %collective-permute-start.47 = (f32[2,16]{1,0:T(2,128)S(1)}, f32[2,16]{1,0:T(2,128)S(1)}, u32[]{:S(2)}, u32[]{:S(2)}) collective-permute-start(f32[2,16]{1,0:T(2,128)S(1)} %select_add_fusion.1), channel_id=1, source_target_pairs={{0,8},{2,10},{4,12},{6,14},{8,0},{10,2},{12,4},{14,6},{16,24},{18,... | collective-permute-start | bytes 392 | tf_op jit(solution)/shard_map/ppermute | solution.py:33
  (260 shorter events, 45.2 us)
Async XLA Ops:
  5.5 28.5 %collective-permute-start = (bf16[2,2,2,2,16,1024]{5,4,0,1,2,3:T(8,128)(2,1)}, bf16[2,2,2,2,16,1024]{5,4,0,1,2,3:T(8,128)(2,1)}, u32[]{:S(2)}, u32[]{:S(2)}) collective-permute-start(bf16[2,2,2,2,16,1024]{5,4,0,1,2,3:T(8,128)(2,1)} %pad_maximum_fusion), channel_id=1, source_target_pairs={{0,2},{2,0},{4,6},{6,4},{8,10},{10,8},{12,14},{14,12},{16,18},{18,... | collective-permute-start | bytes 1572872 | tf_op jit(solution)/shard_map/ppermute | solution.py:73
  9.4 27.4 %collective-permute-start.8 = (bf16[2,2,2,2,16,1024]{5,4,3,2,1,0:T(8,128)(2,1)}, bf16[2,2,2,2,16,1024]{5,4,3,2,1,0:T(8,128)(2,1)}, u32[]{:S(2)}, u32[]{:S(2)}) collective-permute-start(bf16[2,2,2,2,16,1024]{5,4,3,2,1,0:T(8,128)(2,1)} %pad_maximum_fusion.1), channel_id=1, source_target_pairs={{0,4},{2,6},{4,0},{6,2},{8,12},{10,14},{12,8},{14,10},{16,20},{18,... | collective-permute-start | bytes 1572872 | tf_op jit(solution)/shard_map/ppermute | solution.py:73
  11.9 37.2 %collective-permute-start.16 = (bf16[2,2,2,2,16,1024]{5,4,3,2,1,0:T(8,128)(2,1)}, bf16[2,2,2,2,16,1024]{5,4,3,2,1,0:T(8,128)(2,1)}, u32[]{:S(2)}, u32[]{:S(2)}) collective-permute-start(bf16[2,2,2,2,16,1024]{5,4,3,2,1,0:T(8,128)(2,1)} %pad_maximum_fusion.2), channel_id=1, source_target_pairs={{0,8},{2,10},{4,12},{6,14},{8,0},{10,2},{12,4},{14,6},{16,24},{18,... | collective-permute-start | bytes 1572872 | tf_op jit(solution)/shard_map/ppermute | solution.py:73
  16.2 40.6 %collective-permute-start.24 = (bf16[2,2,2,2,16,1024]{5,4,3,2,1,0:T(8,128)(2,1)}, bf16[2,2,2,2,16,1024]{5,4,3,2,1,0:T(8,128)(2,1)}, u32[]{:S(2)}, u32[]{:S(2)}) collective-permute-start(bf16[2,2,2,2,16,1024]{5,4,3,2,1,0:T(8,128)(2,1)} %pad_maximum_fusion.3), channel_id=1, source_target_pairs={{0,16},{2,18},{4,20},{6,22},{8,24},{10,26},{12,28},{14,30},{16,0},... | collective-permute-start | bytes 1572872 | tf_op jit(solution)/shard_map/ppermute | solution.py:73
  19.6 9.1 %collective-permute-start.32 = (bf16[1024,128]{1,0:T(8,128)(2,1)}, bf16[1024,128]{1,0:T(8,128)(2,1)}, u32[]{:S(2)}, u32[]{:S(2)}) collective-permute-start(bf16[1024,128]{1,0:T(8,128)(2,1)} %slice.721), channel_id=1, source_target_pairs={{2,0},{4,2},{6,4},{8,6},{10,8},{12,10},{14,12},{16,14},{18,16},{20... | collective-permute-start | bytes 786440 | tf_op jit(solution)/shard_map/ppermute | solution.py:18
  36.2 25.8 %collective-permute-start.1 = (bf16[2,2,2,16,1024]{4,3,2,1,0:T(8,128)(2,1)S(1)}, bf16[2,2,2,16,1024]{4,3,2,1,0:T(8,128)(2,1)S(1)}, u32[]{:S(2)}, u32[]{:S(2)}) collective-permute-start(bf16[2,2,2,16,1024]{4,3,2,1,0:T(8,128)(2,1)S(1)} %pad_maximum_fusion.4), channel_id=1, source_target_pairs={{0,4},{2,6},{4,0},{6,2},{8,12},{10,14},{12,8},{14,10},{16,20},{18,... | collective-permute-start | bytes 786440 | tf_op jit(solution)/shard_map/ppermute | solution.py:73
  38.0 24.2 %collective-permute-start.9 = (bf16[2,2,2,16,1024]{4,3,2,1,0:T(8,128)(2,1)S(1)}, bf16[2,2,2,16,1024]{4,3,2,1,0:T(8,128)(2,1)S(1)}, u32[]{:S(2)}, u32[]{:S(2)}) collective-permute-start(bf16[2,2,2,16,1024]{4,3,2,1,0:T(8,128)(2,1)S(1)} %pad_maximum_fusion.7), channel_id=1, source_target_pairs={{0,8},{2,10},{4,12},{6,14},{8,0},{10,2},{12,4},{14,6},{16,24},{18,... | collective-permute-start | bytes 786440 | tf_op jit(solution)/shard_map/ppermute | solution.py:73
  50.2 15.1 %collective-permute-start.17 = (bf16[2,2,2,16,1024]{4,3,2,1,0:T(8,128)(2,1)S(1)}, bf16[2,2,2,16,1024]{4,3,2,1,0:T(8,128)(2,1)S(1)}, u32[]{:S(2)}, u32[]{:S(2)}) collective-permute-start(bf16[2,2,2,16,1024]{4,3,2,1,0:T(8,128)(2,1)S(1)} %pad_maximum_fusion.10), channel_id=1, source_target_pairs={{0,16},{2,18},{4,20},{6,22},{8,24},{10,26},{12,28},{14,30},{16,0},... | collective-permute-start | bytes 786440 | tf_op jit(solution)/shard_map/ppermute | solution.py:73
  58.0 20.7 %collective-permute-start.25 = (bf16[2,2,2,16,1024]{4,3,2,1,0:T(8,128)(2,1)S(1)}, bf16[2,2,2,16,1024]{4,3,2,1,0:T(8,128)(2,1)S(1)}, u32[]{:S(2)}, u32[]{:S(2)}) collective-permute-start(bf16[2,2,2,16,1024]{4,3,2,1,0:T(8,128)(2,1)S(1)} %pad_maximum_fusion.13), channel_id=1, source_target_pairs={{0,2},{2,0},{4,6},{6,4},{8,10},{10,8},{12,14},{14,12},{16,18},{18,... | collective-permute-start | bytes 786440 | tf_op jit(solution)/shard_map/ppermute | solution.py:73
  62.1 17.1 %collective-permute-start.2 = (bf16[2,2,16,1024]{3,2,1,0:T(8,128)(2,1)S(1)}, bf16[2,2,16,1024]{3,2,1,0:T(8,128)(2,1)S(1)}, u32[]{:S(2)}, u32[]{:S(2)}) collective-permute-start(bf16[2,2,16,1024]{3,2,1,0:T(8,128)(2,1)S(1)} %pad_maximum_fusion.20), channel_id=1, source_target_pairs={{0,8},{2,10},{4,12},{6,14},{8,0},{10,2},{12,4},{14,6},{16,24},{18,... | collective-permute-start | bytes 393224 | tf_op jit(solution)/shard_map/ppermute | solution.py:73
  62.3 17.0 %collective-permute-start.10 = (bf16[2,2,16,1024]{3,2,1,0:T(8,128)(2,1)S(1)}, bf16[2,2,16,1024]{3,2,1,0:T(8,128)(2,1)S(1)}, u32[]{:S(2)}, u32[]{:S(2)}) collective-permute-start(bf16[2,2,16,1024]{3,2,1,0:T(8,128)(2,1)S(1)} %pad_maximum_fusion.23), channel_id=1, source_target_pairs={{0,16},{2,18},{4,20},{6,22},{8,24},{10,26},{12,28},{14,30},{16,0},... | collective-permute-start | bytes 393224 | tf_op jit(solution)/shard_map/ppermute | solution.py:73
  65.4 16.4 %collective-permute-start.18 = (bf16[2,2,16,1024]{3,2,1,0:T(8,128)(2,1)S(1)}, bf16[2,2,16,1024]{3,2,1,0:T(8,128)(2,1)S(1)}, u32[]{:S(2)}, u32[]{:S(2)}) collective-permute-start(bf16[2,2,16,1024]{3,2,1,0:T(8,128)(2,1)S(1)} %pad_maximum_fusion.26), channel_id=1, source_target_pairs={{0,2},{2,0},{4,6},{6,4},{8,10},{10,8},{12,14},{14,12},{16,18},{18,... | collective-permute-start | bytes 393224 | tf_op jit(solution)/shard_map/ppermute | solution.py:73
  84.9 8.0 %collective-permute-start.12 = (bf16[2,16,1024]{2,1,0:T(8,128)(2,1)S(1)}, bf16[2,16,1024]{2,1,0:T(8,128)(2,1)S(1)}, u32[]{:S(2)}, u32[]{:S(2)}) collective-permute-start(bf16[2,16,1024]{2,1,0:T(8,128)(2,1)S(1)} %pad_maximum_fusion.41), channel_id=1, source_target_pairs={{0,2},{2,0},{4,6},{6,4},{8,10},{10,8},{12,14},{14,12},{16,18},{18,... | collective-permute-start | bytes 196616 | tf_op jit(solution)/shard_map/ppermute | solution.py:83
  86.7 6.4 %collective-permute-start.20 = (bf16[2,16,1024]{2,1,0:T(8,128)(2,1)S(1)}, bf16[2,16,1024]{2,1,0:T(8,128)(2,1)S(1)}, u32[]{:S(2)}, u32[]{:S(2)}) collective-permute-start(bf16[2,16,1024]{2,1,0:T(8,128)(2,1)S(1)} %pad_maximum_fusion.45), channel_id=1, source_target_pairs={{0,4},{2,6},{4,0},{6,2},{8,12},{10,14},{12,8},{14,10},{16,20},{18,... | collective-permute-start | bytes 196616 | tf_op jit(solution)/shard_map/ppermute | solution.py:83
  90.4 6.2 %collective-permute-start.5 = (bf16[2,2,16,1024]{3,2,1,0:T(8,128)(2,1)S(1)}, bf16[2,2,16,1024]{3,2,1,0:T(8,128)(2,1)S(1)}, u32[]{:S(2)}, u32[]{:S(2)}) collective-permute-start(bf16[2,2,16,1024]{3,2,1,0:T(8,128)(2,1)S(1)} %pad_maximum_fusion.21), channel_id=1, source_target_pairs={{0,8},{2,10},{4,12},{6,14},{8,0},{10,2},{12,4},{14,6},{16,24},{18,... | collective-permute-start | bytes 393224 | tf_op jit(solution)/shard_map/ppermute | solution.py:83
  93.0 7.6 %collective-permute-start.13 = (bf16[2,2,16,1024]{3,2,1,0:T(8,128)(2,1)S(1)}, bf16[2,2,16,1024]{3,2,1,0:T(8,128)(2,1)S(1)}, u32[]{:S(2)}, u32[]{:S(2)}) collective-permute-start(bf16[2,2,16,1024]{3,2,1,0:T(8,128)(2,1)S(1)} %pad_maximum_fusion.24), channel_id=1, source_target_pairs={{0,16},{2,18},{4,20},{6,22},{8,24},{10,26},{12,28},{14,30},{16,0},... | collective-permute-start | bytes 393224 | tf_op jit(solution)/shard_map/ppermute | solution.py:83
  93.2 7.7 %collective-permute-start.21 = (bf16[2,2,16,1024]{3,2,1,0:T(8,128)(2,1)S(1)}, bf16[2,2,16,1024]{3,2,1,0:T(8,128)(2,1)S(1)}, u32[]{:S(2)}, u32[]{:S(2)}) collective-permute-start(bf16[2,2,16,1024]{3,2,1,0:T(8,128)(2,1)S(1)} %pad_maximum_fusion.27), channel_id=1, source_target_pairs={{0,2},{2,0},{4,6},{6,4},{8,10},{10,8},{12,14},{14,12},{16,18},{18,... | collective-permute-start | bytes 393224 | tf_op jit(solution)/shard_map/ppermute | solution.py:83
  95.2 7.0 %collective-permute-start.29 = (bf16[2,2,16,1024]{3,2,1,0:T(8,128)(2,1)S(1)}, bf16[2,2,16,1024]{3,2,1,0:T(8,128)(2,1)S(1)}, u32[]{:S(2)}, u32[]{:S(2)}) collective-permute-start(bf16[2,2,16,1024]{3,2,1,0:T(8,128)(2,1)S(1)} %pad_maximum_fusion.30), channel_id=1, source_target_pairs={{0,4},{2,6},{4,0},{6,2},{8,12},{10,14},{12,8},{14,10},{16,20},{18,... | collective-permute-start | bytes 393224 | tf_op jit(solution)/shard_map/ppermute | solution.py:83
  96.7 6.8 %collective-permute-start.6 = (bf16[2,2,2,16,1024]{4,3,2,1,0:T(8,128)(2,1)S(1)}, bf16[2,2,2,16,1024]{4,3,2,1,0:T(8,128)(2,1)S(1)}, u32[]{:S(2)}, u32[]{:S(2)}) collective-permute-start(bf16[2,2,2,16,1024]{4,3,2,1,0:T(8,128)(2,1)S(1)} %pad_maximum_fusion.5), channel_id=1, source_target_pairs={{0,4},{2,6},{4,0},{6,2},{8,12},{10,14},{12,8},{14,10},{16,20},{18,... | collective-permute-start | bytes 786440 | tf_op jit(solution)/shard_map/ppermute | solution.py:83
  100.8 13.2 %collective-permute-start.14 = (bf16[2,2,2,16,1024]{4,3,2,1,0:T(8,128)(2,1)S(1)}, bf16[2,2,2,16,1024]{4,3,2,1,0:T(8,128)(2,1)S(1)}, u32[]{:S(2)}, u32[]{:S(2)}) collective-permute-start(bf16[2,2,2,16,1024]{4,3,2,1,0:T(8,128)(2,1)S(1)} %pad_maximum_fusion.8), channel_id=1, source_target_pairs={{0,8},{2,10},{4,12},{6,14},{8,0},{10,2},{12,4},{14,6},{16,24},{18,... | collective-permute-start | bytes 786440 | tf_op jit(solution)/shard_map/ppermute | solution.py:83
  101.0 13.2 %collective-permute-start.22 = (bf16[2,2,2,16,1024]{4,3,2,1,0:T(8,128)(2,1)S(1)}, bf16[2,2,2,16,1024]{4,3,2,1,0:T(8,128)(2,1)S(1)}, u32[]{:S(2)}, u32[]{:S(2)}) collective-permute-start(bf16[2,2,2,16,1024]{4,3,2,1,0:T(8,128)(2,1)S(1)} %pad_maximum_fusion.11), channel_id=1, source_target_pairs={{0,16},{2,18},{4,20},{6,22},{8,24},{10,26},{12,28},{14,30},{16,0},... | collective-permute-start | bytes 786440 | tf_op jit(solution)/shard_map/ppermute | solution.py:83
  102.3 12.0 %collective-permute-start.30 = (bf16[2,2,2,16,1024]{4,3,2,1,0:T(8,128)(2,1)S(1)}, bf16[2,2,2,16,1024]{4,3,2,1,0:T(8,128)(2,1)S(1)}, u32[]{:S(2)}, u32[]{:S(2)}) collective-permute-start(bf16[2,2,2,16,1024]{4,3,2,1,0:T(8,128)(2,1)S(1)} %pad_maximum_fusion.14), channel_id=1, source_target_pairs={{0,2},{2,0},{4,6},{6,4},{8,10},{10,8},{12,14},{14,12},{16,18},{18,... | collective-permute-start | bytes 786440 | tf_op jit(solution)/shard_map/ppermute | solution.py:83
  103.5 11.3 %collective-permute-start.7 = (bf16[1,2,2,2,16,1024]{5,4,3,2,1,0:T(8,128)(2,1)S(1)}, bf16[1,2,2,2,16,1024]{5,4,3,2,1,0:T(8,128)(2,1)S(1)}, u32[]{:S(2)}, u32[]{:S(2)}) collective-permute-start(bf16[1,2,2,2,16,1024]{5,4,3,2,1,0:T(8,128)(2,1)S(1)} %maximum_bitcast_fusion.10), channel_id=1, source_target_pairs={{0,2},{2,0},{4,6},{6,4},{8,10},{10,8},{12,14},{14,12},{16,18},{18,... | collective-permute-start | bytes 786440 | tf_op jit(solution)/shard_map/ppermute | solution.py:83
  104.6 12.2 %collective-permute-start.36 = (bf16[1,2,2,2,16,1024]{5,4,3,2,1,0:T(8,128)(2,1)S(1)}, bf16[1,2,2,2,16,1024]{5,4,3,2,1,0:T(8,128)(2,1)S(1)}, u32[]{:S(2)}, u32[]{:S(2)}) collective-permute-start(bf16[1,2,2,2,16,1024]{5,4,3,2,1,0:T(8,128)(2,1)S(1)} %maximum_bitcast_fusion.14), channel_id=1, source_target_pairs={{0,2},{2,0},{4,6},{6,4},{8,10},{10,8},{12,14},{14,12},{16,18},{18,... | collective-permute-start | bytes 786440 | tf_op jit(solution)/shard_map/ppermute | solution.py:83
  114.1 6.4 %collective-permute-start.37 = (bf16[1,2,2,2,16,1024]{5,4,3,2,1,0:T(8,128)(2,1)S(1)}, bf16[1,2,2,2,16,1024]{5,4,3,2,1,0:T(8,128)(2,1)S(1)}, u32[]{:S(2)}, u32[]{:S(2)}) collective-permute-start(bf16[1,2,2,2,16,1024]{5,4,3,2,1,0:T(8,128)(2,1)S(1)} %maximum_bitcast_fusion.15), channel_id=1, source_target_pairs={{0,4},{2,6},{4,0},{6,2},{8,12},{10,14},{12,8},{14,10},{16,20},{18,... | collective-permute-start | bytes 786440 | tf_op jit(solution)/shard_map/ppermute | solution.py:83
  114.2 12.5 %collective-permute-start.38 = (bf16[1,2,2,2,16,1024]{5,4,3,2,1,0:T(8,128)(2,1)S(1)}, bf16[1,2,2,2,16,1024]{5,4,3,2,1,0:T(8,128)(2,1)S(1)}, u32[]{:S(2)}, u32[]{:S(2)}) collective-permute-start(bf16[1,2,2,2,16,1024]{5,4,3,2,1,0:T(8,128)(2,1)S(1)} %maximum_bitcast_fusion.16), channel_id=1, source_target_pairs={{0,8},{2,10},{4,12},{6,14},{8,0},{10,2},{12,4},{14,6},{16,24},{18,... | collective-permute-start | bytes 786440 | tf_op jit(solution)/shard_map/ppermute | solution.py:83
  114.4 14.0 %collective-permute-start.39 = (bf16[1,2,2,2,16,1024]{5,4,3,2,1,0:T(8,128)(2,1)S(1)}, bf16[1,2,2,2,16,1024]{5,4,3,2,1,0:T(8,128)(2,1)S(1)}, u32[]{:S(2)}, u32[]{:S(2)}) collective-permute-start(bf16[1,2,2,2,16,1024]{5,4,3,2,1,0:T(8,128)(2,1)S(1)} %maximum_bitcast_fusion.17), channel_id=1, source_target_pairs={{0,16},{2,18},{4,20},{6,22},{8,24},{10,26},{12,28},{14,30},{16,0},... | collective-permute-start | bytes 786440 | tf_op jit(solution)/shard_map/ppermute | solution.py:83
  114.9 29.5 %collective-permute-start.15 = (bf16[1,2,2,2,16,1024]{5,4,3,2,1,0:T(8,128)(2,1)S(1)}, bf16[1,2,2,2,16,1024]{5,4,3,2,1,0:T(8,128)(2,1)S(1)}, u32[]{:S(2)}, u32[]{:S(2)}) collective-permute-start(bf16[1,2,2,2,16,1024]{5,4,3,2,1,0:T(8,128)(2,1)S(1)} %maximum_bitcast_fusion.11), channel_id=1, source_target_pairs={{0,4},{2,6},{4,0},{6,2},{8,12},{10,14},{12,8},{14,10},{16,20},{18,... | collective-permute-start | bytes 786440 | tf_op jit(solution)/shard_map/ppermute | solution.py:83
  116.8 27.7 %collective-permute-start.23 = (bf16[1,2,2,2,16,1024]{5,4,3,2,1,0:T(8,128)(2,1)S(1)}, bf16[1,2,2,2,16,1024]{5,4,3,2,1,0:T(8,128)(2,1)S(1)}, u32[]{:S(2)}, u32[]{:S(2)}) collective-permute-start(bf16[1,2,2,2,16,1024]{5,4,3,2,1,0:T(8,128)(2,1)S(1)} %maximum_bitcast_fusion.12), channel_id=1, source_target_pairs={{0,8},{2,10},{4,12},{6,14},{8,0},{10,2},{12,4},{14,6},{16,24},{18,... | collective-permute-start | bytes 786440 | tf_op jit(solution)/shard_map/ppermute | solution.py:83
  120.5 24.2 %collective-permute-start.31 = (bf16[1,2,2,2,16,1024]{5,4,3,2,1,0:T(8,128)(2,1)S(1)}, bf16[1,2,2,2,16,1024]{5,4,3,2,1,0:T(8,128)(2,1)S(1)}, u32[]{:S(2)}, u32[]{:S(2)}) collective-permute-start(bf16[1,2,2,2,16,1024]{5,4,3,2,1,0:T(8,128)(2,1)S(1)} %maximum_bitcast_fusion.13), channel_id=1, source_target_pairs={{0,16},{2,18},{4,20},{6,22},{8,24},{10,26},{12,28},{14,30},{16,0},... | collective-permute-start | bytes 786440 | tf_op jit(solution)/shard_map/ppermute | solution.py:83
  142.8 18.4 %collective-permute-start.40 = (f32[16,1024]{1,0:T(8,128)S(1)}, f32[16,1024]{1,0:T(8,128)S(1)}, u32[]{:S(2)}, u32[]{:S(2)}) collective-permute-start(f32[16,1024]{1,0:T(8,128)S(1)} %reshape.406), channel_id=1, source_target_pairs={{0,1},{1,0},{2,3},{3,2},{4,5},{5,4},{6,7},{7,6},{8,9},{9,8},{10,11... | collective-permute-start | bytes 196616 | tf_op jit(solution)/shard_map/ppermute | solution.py:33
  143.8 16.6 %collective-permute-start.41 = (f32[16]{0:T(128)S(1)}, f32[16]{0:T(128)S(1)}, u32[]{:S(2)}, u32[]{:S(2)}) collective-permute-start(f32[16]{0:T(128)S(1)} %reshape_squeeze.7), channel_id=1, source_target_pairs={{0,1},{1,0},{2,3},{3,2},{4,5},{5,4},{6,7},{7,6},{8,9},{9,8},{10,11... | collective-permute-start | bytes 200 | tf_op jit(solution)/shard_map/ppermute | solution.py:33
  (24 other events, 138.8 us)

commit v9 on v6

--- a/solution.py
+++ b/solution.py
@@ -54,7 +54,9 @@
         masked = jnp.where(own[:, None, None], block[None], jnp.zeros_like(block)[None])
         return lax.psum(masked, axis)
     piece = rows // (parts * size)
-    orders = [[1 << ((p + s) % nbits) for s in range(nbits)] for p in range(parts)]
+    low_bits = max(nbits - 1, 1)
+    orders = [[1 << ((p + s) % low_bits) for s in range(low_bits)] for p in range(parts)]
+    orders = [o + [1 << (nbits - 1)] if nbits > 1 else o for o in orders]
     bufs = {}
     for p in range(parts):
         seg = block[p * piece * size : (p + 1) * piece * size].reshape([2] * nbits + [piece, chans])

time: 158 us -> 181 us (1.15)
  waiting for transfers between devices: 44 us -> 76.4 us
  starting transfers between devices: 52.3 us -> 45.8 us
  other arithmetic: 18 us -> 15.9 us
    ppermute x36 -> x23, waiting for transfers between devices: 38.8 us -> 71.5 us  [spread_blocks(): lax.ppermute(jnp.stack([v for _, v in items]), axis, [(i, i ^ mask) for i...]
    ppermute x36 -> x23, starting transfers between devices: 42.5 us -> 35.9 us  [spread_blocks(): lax.ppermute(jnp.stack([v for _, v in items]), axis, [(i, i ^ mask) for i...]
    select_n x18 -> x11, other arithmetic: 5.69 us -> 3.61 us  [spread_blocks(): bufs[key] = jnp.where(holder, keeps[key], got[n])]
    another operation x52 -> x43, other arithmetic: 4.2 us -> 3.78 us  [spread_blocks(): jnp.stack([v for _, v in items])]
  transfers between devices with their start and end apart: 45 -> 32, of which waited for: 21 -> 19; matrix products, arithmetic and copies ran while one was open for 18% -> 14% of each run, Pallas kernels for 7% -> 7%
where the time goes in v9:
time: 181 us; the launch traced here: 180 us
  waiting for transfers between devices  76.4 us (42%)
  starting transfers between devices  45.8 us (25%)
  Pallas kernels  23.8 us (13%)
  other arithmetic  15.9 us (9%)
  local copies, waits for them, and re-layouts  14.1 us (8%)
  between operations  2.55 us (1%)
    ppermute x23, waiting for transfers between devices, spread_blocks(): lax.ppermute(jnp.stack([v for _, v in items]), axis, [(i, i ^ mask) for i...  71.5 us
    ppermute x23, starting transfers between devices, spread_blocks(): lax.ppermute(jnp.stack([v for _, v in items]), axis, [(i, i ^ mask) for i...  35.9 us
    pallas_call x2, Pallas kernels, correlate(): pl.pallas_call(correlate_kernel, grid_spec=grid_spec, out_shape=[jax.Shap...  23.8 us
    ppermute x8, starting transfers between devices, group_sum(): got[d] = lax.ppermute(value, axis, pairs)  8.57 us
    ppermute x8, waiting for transfers between devices, group_sum(): got[d] = lax.ppermute(value, axis, pairs)  4.86 us
    another operation x43, other arithmetic, spread_blocks(): jnp.stack([v for _, v in items])  3.78 us
  transfers between devices with their start and end apart: 32, of which 19 were waited for; matrix products, arithmetic and copies ran while one was open for 14% of the time, Pallas kernels for 7%

profile of v9, /device:TPU:0, one launch (start us, length us, event | category | flops | bytes accessed | tf_op | source)
XLA Modules:
  0.0 179.9 jit_solution(8576136923381302204)
XLA Ops:
  0.0 1.7 slice.737
  3.0 2.9 %copy.38 = bf16[1024,1024]{0,1:T(8,128)(2,1)S(1)} copy(bf16[1024,1024]{1,0:T(8,128)(2,1)} %param.4) | data formatting | bytes 4194304 | tf_op args[0]
  9.0 3.6 %collective-permute-start = (bf16[4,2,2,2,16,1024]{5,4,0,1,2,3:T(8,128)(2,1)}, bf16[4,2,2,2,16,1024]{5,4,0,1,2,3:T(8,128)(2,1)}, u32[]{:S(2)}, u32[]{:S(2)}) collective-permute-start(bf16[4,2,2,2,16,1024]{5,4,0,1,2,3:T(8,128)(2,1)} %pad_maximum_fusion), channel_id=1, source_target_pairs={{0,2},{2,0},{4,6},{6,4},{8,10},{10,8},{12,14},{14,12},{16,18},{18,... | collective-permute-start | bytes 3145736 | tf_op jit(solution)/shard_map/ppermute | solution.py:75
  13.6 2.0 %collective-permute-start.3 = (bf16[2,2,2,2,16,1024]{5,4,3,2,1,0:T(8,128)(2,1)}, bf16[2,2,2,2,16,1024]{5,4,3,2,1,0:T(8,128)(2,1)}, u32[]{:S(2)}, u32[]{:S(2)}) collective-permute-start(bf16[2,2,2,2,16,1024]{5,4,3,2,1,0:T(8,128)(2,1)} %pad_maximum_fusion.2), channel_id=1, source_target_pairs={{0,4},{2,6},{4,0},{6,2},{8,12},{10,14},{12,8},{14,10},{16,20},{18,... | collective-permute-start | bytes 1572872 | tf_op jit(solution)/shard_map/ppermute | solution.py:75
  17.6 1.6 collective-permute-start.6
  28.5 2.5 %collective-permute-start.4 = (bf16[2,2,2,16,1024]{4,3,2,1,0:T(8,128)(2,1)S(1)}, bf16[2,2,2,16,1024]{4,3,2,1,0:T(8,128)(2,1)S(1)}, u32[]{:S(2)}, u32[]{:S(2)}) collective-permute-start(bf16[2,2,2,16,1024]{4,3,2,1,0:T(8,128)(2,1)S(1)} %pad_maximum_fusion.8), channel_id=1, source_target_pairs={{0,8},{2,10},{4,12},{6,14},{8,0},{10,2},{12,4},{14,6},{16,24},{18,... | collective-permute-start | bytes 786440 | tf_op jit(solution)/shard_map/ppermute | solution.py:75
  32.1 1.8 %collective-permute-start.7 = (bf16[2,2,2,16,1024]{4,3,2,1,0:T(8,128)(2,1)S(1)}, bf16[2,2,2,16,1024]{4,3,2,1,0:T(8,128)(2,1)S(1)}, u32[]{:S(2)}, u32[]{:S(2)}) collective-permute-start(bf16[2,2,2,16,1024]{4,3,2,1,0:T(8,128)(2,1)S(1)} %pad_maximum_fusion.9), channel_id=1, source_target_pairs={{0,2},{2,0},{4,6},{6,4},{8,10},{10,8},{12,14},{14,12},{16,18},{18,... | collective-permute-start | bytes 786440 | tf_op jit(solution)/shard_map/ppermute | solution.py:75
  33.9 2.3 %collective-permute-done.4 = bf16[2,2,2,16,1024]{4,3,2,1,0:T(8,128)(2,1)S(1)} collective-permute-done((bf16[2,2,2,16,1024]{4,3,2,1,0:T(8,128)(2,1)S(1)}, bf16[2,2,2,16,1024]{4,3,2,1,0:T(8,128)(2,1)S(1)}, u32[]{:S(2)}, u32[]{:S(2)}) %collective-permute-start.4) | collective-permute-done | bytes 262176 | tf_op jit(solution)/shard_map/ppermute | solution.py:75
  37.8 4.6 %collective-permute-done.7 = bf16[2,2,2,16,1024]{4,3,2,1,0:T(8,128)(2,1)S(1)} collective-permute-done((bf16[2,2,2,16,1024]{4,3,2,1,0:T(8,128)(2,1)S(1)}, bf16[2,2,2,16,1024]{4,3,2,1,0:T(8,128)(2,1)S(1)}, u32[]{:S(2)}, u32[]{:S(2)}) %collective-permute-start.7) | collective-permute-done | bytes 262176 | tf_op jit(solution)/shard_map/ppermute | solution.py:75
  45.0 3.6 %collective-permute-start.1 = (bf16[4,2,2,16,1024]{4,3,2,1,0:T(8,128)(2,1)S(1)}, bf16[4,2,2,16,1024]{4,3,2,1,0:T(8,128)(2,1)S(1)}, u32[]{:S(2)}, u32[]{:S(2)}) collective-permute-start(bf16[4,2,2,16,1024]{4,3,2,1,0:T(8,128)(2,1)S(1)} %pad_maximum_fusion.1), channel_id=1, source_target_pairs={{0,4},{2,6},{4,0},{6,2},{8,12},{10,14},{12,8},{14,10},{16,20},{18,... | collective-permute-start | bytes 1572872 | tf_op jit(solution)/shard_map/ppermute | solution.py:75
  48.7 11.4 %collective-permute-done.1 = bf16[4,2,2,16,1024]{4,3,2,1,0:T(8,128)(2,1)S(1)} collective-permute-done((bf16[4,2,2,16,1024]{4,3,2,1,0:T(8,128)(2,1)S(1)}, bf16[4,2,2,16,1024]{4,3,2,1,0:T(8,128)(2,1)S(1)}, u32[]{:S(2)}, u32[]{:S(2)}) %collective-permute-start.1) | collective-permute-done | bytes 524320 | tf_op jit(solution)/shard_map/ppermute | solution.py:75
  60.4 1.9 %collective-permute-start.2 = (bf16[4,2,16,1024]{3,2,1,0:T(8,128)(2,1)S(1)}, bf16[4,2,16,1024]{3,2,1,0:T(8,128)(2,1)S(1)}, u32[]{:S(2)}, u32[]{:S(2)}) collective-permute-start(bf16[4,2,16,1024]{3,2,1,0:T(8,128)(2,1)S(1)} %pad_maximum_fusion.7), channel_id=1, source_target_pairs={{0,8},{2,10},{4,12},{6,14},{8,0},{10,2},{12,4},{14,6},{16,24},{18,... | collective-permute-start | bytes 786440 | tf_op jit(solution)/shard_map/ppermute | solution.py:75
  62.4 6.0 %collective-permute-done.2 = bf16[4,2,16,1024]{3,2,1,0:T(8,128)(2,1)S(1)} collective-permute-done((bf16[4,2,16,1024]{3,2,1,0:T(8,128)(2,1)S(1)}, bf16[4,2,16,1024]{3,2,1,0:T(8,128)(2,1)S(1)}, u32[]{:S(2)}, u32[]{:S(2)}) %collective-permute-start.2) | collective-permute-done | bytes 262176 | tf_op jit(solution)/shard_map/ppermute | solution.py:75
  68.6 3.8 %collective-permute-start.9 = (bf16[8,16,1024]{2,1,0:T(8,128)(2,1)S(1)}, bf16[8,16,1024]{2,1,0:T(8,128)(2,1)S(1)}, u32[]{:S(2)}, u32[]{:S(2)}) collective-permute-start(bf16[8,16,1024]{2,1,0:T(8,128)(2,1)S(1)} %constant_dynamic-update-slice_fusion), channel_id=1, source_target_pairs={{0,16},{2,18},{4,20},{6,22},{8,24},{10,26},{12,28},{14,30},{16,0},... | collective-permute-start | bytes 786440 | tf_op jit(solution)/shard_map/ppermute | solution.py:75
  72.5 12.3 %collective-permute-done.9 = bf16[8,16,1024]{2,1,0:T(8,128)(2,1)S(1)} collective-permute-done((bf16[8,16,1024]{2,1,0:T(8,128)(2,1)S(1)}, bf16[8,16,1024]{2,1,0:T(8,128)(2,1)S(1)}, u32[]{:S(2)}, u32[]{:S(2)}) %collective-permute-start.9) | collective-permute-done | bytes 262176 | tf_op jit(solution)/shard_map/ppermute | solution.py:75
  85.3 9.9 %collective-permute-done.10 = bf16[8,16,1024]{2,1,0:T(8,128)(2,1)S(1)} collective-permute-done((bf16[8,16,1024]{2,1,0:T(8,128)(2,1)S(1)}, bf16[8,16,1024]{2,1,0:T(8,128)(2,1)S(1)}, u32[]{:S(2)}, u32[]{:S(2)}) %collective-permute-start.10) | collective-permute-done | bytes 262176 | tf_op jit(solution)/shard_map/ppermute | solution.py:85
  96.6 1.8 %collective-permute-start.14 = (bf16[2,2,16,1024]{3,2,1,0:T(8,128)(2,1)S(1)}, bf16[2,2,16,1024]{3,2,1,0:T(8,128)(2,1)S(1)}, u32[]{:S(2)}, u32[]{:S(2)}) collective-permute-start(bf16[2,2,16,1024]{3,2,1,0:T(8,128)(2,1)S(1)} %pad_maximum_fusion.26), channel_id=1, source_target_pairs={{0,2},{2,0},{4,6},{6,4},{8,10},{10,8},{12,14},{14,12},{16,18},{18,... | collective-permute-start | bytes 393224 | tf_op jit(solution)/shard_map/ppermute | solution.py:85
  98.4 3.8 %collective-permute-done.17 = bf16[2,2,16,1024]{3,2,1,0:T(8,128)(2,1)S(1)} collective-permute-done((bf16[2,2,16,1024]{3,2,1,0:T(8,128)(2,1)S(1)}, bf16[2,2,16,1024]{3,2,1,0:T(8,128)(2,1)S(1)}, u32[]{:S(2)}, u32[]{:S(2)}) %collective-permute-start.17) | collective-permute-done | bytes 131104 | tf_op jit(solution)/shard_map/ppermute | solution.py:85
  102.9 1.5 collective-permute-start.15
  105.3 3.5 %collective-permute-done.18 = bf16[2,2,2,16,1024]{4,3,2,1,0:T(8,128)(2,1)S(1)} collective-permute-done((bf16[2,2,2,16,1024]{4,3,2,1,0:T(8,128)(2,1)S(1)}, bf16[2,2,2,16,1024]{4,3,2,1,0:T(8,128)(2,1)S(1)}, u32[]{:S(2)}, u32[]{:S(2)}) %collective-permute-start.18) | collective-permute-done | bytes 262176 | tf_op jit(solution)/shard_map/ppermute | solution.py:85
  108.9 1.8 %collective-permute-start.23 = (bf16[1,2,2,2,16,1024]{5,4,3,2,1,0:T(8,128)(2,1)S(1)}, bf16[1,2,2,2,16,1024]{5,4,3,2,1,0:T(8,128)(2,1)S(1)}, u32[]{:S(2)}, u32[]{:S(2)}) collective-permute-start(bf16[1,2,2,2,16,1024]{5,4,3,2,1,0:T(8,128)(2,1)S(1)} %maximum_bitcast_fusion.17), channel_id=1, source_target_pairs={{0,8},{2,10},{4,12},{6,14},{8,0},{10,2},{12,4},{14,6},{16,24},{18,... | collective-permute-start | bytes 786440 | tf_op jit(solution)/shard_map/ppermute | solution.py:85
  111.4 1.6 collective-permute-start.22
  115.5 4.6 %collective-permute-done.22 = bf16[1,2,2,2,16,1024]{5,4,3,2,1,0:T(8,128)(2,1)S(1)} collective-permute-done((bf16[1,2,2,2,16,1024]{5,4,3,2,1,0:T(8,128)(2,1)S(1)}, bf16[1,2,2,2,16,1024]{5,4,3,2,1,0:T(8,128)(2,1)S(1)}, u32[]{:S(2)}, u32[]{:S(2)}) %collective-permute-start.22) | collective-permute-done | bytes 262176 | tf_op jit(solution)/shard_map/ppermute | solution.py:85
  120.3 2.6 %collective-permute-done.16 = bf16[1,2,2,2,16,1024]{5,4,3,2,1,0:T(8,128)(2,1)S(1)} collective-permute-done((bf16[1,2,2,2,16,1024]{5,4,3,2,1,0:T(8,128)(2,1)S(1)}, bf16[1,2,2,2,16,1024]{5,4,3,2,1,0:T(8,128)(2,1)S(1)}, u32[]{:S(2)}, u32[]{:S(2)}) %collective-permute-start.16) | collective-permute-done | bytes 262176 | tf_op jit(solution)/shard_map/ppermute | solution.py:85
  124.0 1.8 collective-permute-start.13
  125.8 9.1 %collective-permute-done.21 = bf16[2,2,2,2,16,1024]{5,4,3,2,1,0:T(8,128)(2,1)S(1)} collective-permute-done((bf16[2,2,2,2,16,1024]{5,4,3,2,1,0:T(8,128)(2,1)S(1)}, bf16[2,2,2,2,16,1024]{5,4,3,2,1,0:T(8,128)(2,1)S(1)}, u32[]{:S(2)}, u32[]{:S(2)}) %collective-permute-start.21) | collective-permute-done | bytes 524320 | tf_op jit(solution)/shard_map/ppermute | solution.py:85
  135.1 1.5 maximum_bitcast_fusion.1.blk_ref
  136.6 11.7 %shard_map.47 = (f32[4,4,1024]{2,1,0:T(4,128)}, f32[4,4,128]{2,1,0:T(4,128)}) custom-call(s32[64]{0:T(128)} %squeeze.19.meta_ref, bf16[1,1024,1024]{2,1,0:T(8,128)(2,1)} %maximum_bitcast_fusion.1.blk_ref, bf16[1024,1152]{1,0:T(8,128)(2,1)} %copy-done.3), custom_call_target="tpu_custom_call" | custom-call | flops 5435817984 | bytes 4521984 | tf_op jit(solution)/shard_map/pallas_call | solution.py:156
  151.1 12.0 %shard_map.46 = (f32[4,4,1024]{2,1,0:T(4,128)}, f32[4,4,128]{2,1,0:T(4,128)}) custom-call(s32[64]{0:T(128)} %squeeze.16.meta_ref, bf16[1,1024,1024]{2,1,0:T(8,128)(2,1)} %maximum_bitcast_fusion.blk_ref, bf16[1024,1152]{1,0:T(8,128)(2,1)} %copy-done.3), custom_call_target="tpu_custom_call" | custom-call | flops 5435817984 | bytes 4521984 | tf_op jit(solution)/shard_map/pallas_call | solution.py:156
  168.8 1.7 collective-permute-start.28
  172.3 1.6 collective-permute-start.29
  173.9 1.6 collective-permute-start.30
  (220 shorter events, 43.2 us)
Async XLA Ops:
  1.7 21.3 %collective-permute-start.20 = (bf16[1024,128]{1,0:T(8,128)(2,1)}, bf16[1024,128]{1,0:T(8,128)(2,1)}, u32[]{:S(2)}, u32[]{:S(2)}) collective-permute-start(bf16[1024,128]{1,0:T(8,128)(2,1)} %slice.737), channel_id=1, source_target_pairs={{2,0},{4,2},{6,4},{8,6},{10,8},{12,10},{14,12},{16,14},{18,16},{20... | collective-permute-start | bytes 786440 | tf_op jit(solution)/shard_map/ppermute | solution.py:18
  9.0 33.4 %collective-permute-start = (bf16[4,2,2,2,16,1024]{5,4,0,1,2,3:T(8,128)(2,1)}, bf16[4,2,2,2,16,1024]{5,4,0,1,2,3:T(8,128)(2,1)}, u32[]{:S(2)}, u32[]{:S(2)}) collective-permute-start(bf16[4,2,2,2,16,1024]{5,4,0,1,2,3:T(8,128)(2,1)} %pad_maximum_fusion), channel_id=1, source_target_pairs={{0,2},{2,0},{4,6},{6,4},{8,10},{10,8},{12,14},{14,12},{16,18},{18,... | collective-permute-start | bytes 3145736 | tf_op jit(solution)/shard_map/ppermute | solution.py:75
  13.6 13.7 %collective-permute-start.3 = (bf16[2,2,2,2,16,1024]{5,4,3,2,1,0:T(8,128)(2,1)}, bf16[2,2,2,2,16,1024]{5,4,3,2,1,0:T(8,128)(2,1)}, u32[]{:S(2)}, u32[]{:S(2)}) collective-permute-start(bf16[2,2,2,2,16,1024]{5,4,3,2,1,0:T(8,128)(2,1)} %pad_maximum_fusion.2), channel_id=1, source_target_pairs={{0,4},{2,6},{4,0},{6,2},{8,12},{10,14},{12,8},{14,10},{16,20},{18,... | collective-permute-start | bytes 1572872 | tf_op jit(solution)/shard_map/ppermute | solution.py:75
  17.6 13.4 %collective-permute-start.6 = (bf16[2,2,2,2,16,1024]{5,4,3,2,1,0:T(8,128)(2,1)}, bf16[2,2,2,2,16,1024]{5,4,3,2,1,0:T(8,128)(2,1)}, u32[]{:S(2)}, u32[]{:S(2)}) collective-permute-start(bf16[2,2,2,2,16,1024]{5,4,3,2,1,0:T(8,128)(2,1)} %pad_maximum_fusion.3), channel_id=1, source_target_pairs={{0,8},{2,10},{4,12},{6,14},{8,0},{10,2},{12,4},{14,6},{16,24},{18,... | collective-permute-start | bytes 1572872 | tf_op jit(solution)/shard_map/ppermute | solution.py:75
  28.5 7.7 %collective-permute-start.4 = (bf16[2,2,2,16,1024]{4,3,2,1,0:T(8,128)(2,1)S(1)}, bf16[2,2,2,16,1024]{4,3,2,1,0:T(8,128)(2,1)S(1)}, u32[]{:S(2)}, u32[]{:S(2)}) collective-permute-start(bf16[2,2,2,16,1024]{4,3,2,1,0:T(8,128)(2,1)S(1)} %pad_maximum_fusion.8), channel_id=1, source_target_pairs={{0,8},{2,10},{4,12},{6,14},{8,0},{10,2},{12,4},{14,6},{16,24},{18,... | collective-permute-start | bytes 786440 | tf_op jit(solution)/shard_map/ppermute | solution.py:75
  32.1 10.3 %collective-permute-start.7 = (bf16[2,2,2,16,1024]{4,3,2,1,0:T(8,128)(2,1)S(1)}, bf16[2,2,2,16,1024]{4,3,2,1,0:T(8,128)(2,1)S(1)}, u32[]{:S(2)}, u32[]{:S(2)}) collective-permute-start(bf16[2,2,2,16,1024]{4,3,2,1,0:T(8,128)(2,1)S(1)} %pad_maximum_fusion.9), channel_id=1, source_target_pairs={{0,2},{2,0},{4,6},{6,4},{8,10},{10,8},{12,14},{14,12},{16,18},{18,... | collective-permute-start | bytes 786440 | tf_op jit(solution)/shard_map/ppermute | solution.py:75
  36.3 26.0 %collective-permute-start.5 = (bf16[2,2,16,1024]{3,2,1,0:T(8,128)(2,1)S(1)}, bf16[2,2,16,1024]{3,2,1,0:T(8,128)(2,1)S(1)}, u32[]{:S(2)}, u32[]{:S(2)}) collective-permute-start(bf16[2,2,16,1024]{3,2,1,0:T(8,128)(2,1)S(1)} %pad_maximum_fusion.22), channel_id=1, source_target_pairs={{0,2},{2,0},{4,6},{6,4},{8,10},{10,8},{12,14},{14,12},{16,18},{18,... | collective-permute-start | bytes 393224 | tf_op jit(solution)/shard_map/ppermute | solution.py:75
  45.0 15.1 %collective-permute-start.1 = (bf16[4,2,2,16,1024]{4,3,2,1,0:T(8,128)(2,1)S(1)}, bf16[4,2,2,16,1024]{4,3,2,1,0:T(8,128)(2,1)S(1)}, u32[]{:S(2)}, u32[]{:S(2)}) collective-permute-start(bf16[4,2,2,16,1024]{4,3,2,1,0:T(8,128)(2,1)S(1)} %pad_maximum_fusion.1), channel_id=1, source_target_pairs={{0,4},{2,6},{4,0},{6,2},{8,12},{10,14},{12,8},{14,10},{16,20},{18,... | collective-permute-start | bytes 1572872 | tf_op jit(solution)/shard_map/ppermute | solution.py:75
  48.6 13.7 %collective-permute-start.8 = (bf16[2,2,16,1024]{3,2,1,0:T(8,128)(2,1)S(1)}, bf16[2,2,16,1024]{3,2,1,0:T(8,128)(2,1)S(1)}, u32[]{:S(2)}, u32[]{:S(2)}) collective-permute-start(bf16[2,2,16,1024]{3,2,1,0:T(8,128)(2,1)S(1)} %pad_maximum_fusion.23), channel_id=1, source_target_pairs={{0,4},{2,6},{4,0},{6,2},{8,12},{10,14},{12,8},{14,10},{16,20},{18,... | collective-permute-start | bytes 393224 | tf_op jit(solution)/shard_map/ppermute | solution.py:75
  60.4 8.0 %collective-permute-start.2 = (bf16[4,2,16,1024]{3,2,1,0:T(8,128)(2,1)S(1)}, bf16[4,2,16,1024]{3,2,1,0:T(8,128)(2,1)S(1)}, u32[]{:S(2)}, u32[]{:S(2)}) collective-permute-start(bf16[4,2,16,1024]{3,2,1,0:T(8,128)(2,1)S(1)} %pad_maximum_fusion.7), channel_id=1, source_target_pairs={{0,8},{2,10},{4,12},{6,14},{8,0},{10,2},{12,4},{14,6},{16,24},{18,... | collective-permute-start | bytes 786440 | tf_op jit(solution)/shard_map/ppermute | solution.py:75
  68.6 16.2 %collective-permute-start.9 = (bf16[8,16,1024]{2,1,0:T(8,128)(2,1)S(1)}, bf16[8,16,1024]{2,1,0:T(8,128)(2,1)S(1)}, u32[]{:S(2)}, u32[]{:S(2)}) collective-permute-start(bf16[8,16,1024]{2,1,0:T(8,128)(2,1)S(1)} %constant_dynamic-update-slice_fusion), channel_id=1, source_target_pairs={{0,16},{2,18},{4,20},{6,22},{8,24},{10,26},{12,28},{14,30},{16,0},... | collective-permute-start | bytes 786440 | tf_op jit(solution)/shard_map/ppermute | solution.py:75
  85.1 10.1 %collective-permute-start.10 = (bf16[8,16,1024]{2,1,0:T(8,128)(2,1)S(1)}, bf16[8,16,1024]{2,1,0:T(8,128)(2,1)S(1)}, u32[]{:S(2)}, u32[]{:S(2)}) collective-permute-start(bf16[8,16,1024]{2,1,0:T(8,128)(2,1)S(1)} %get-tuple-element.13), channel_id=1, source_target_pairs={{0,16},{2,18},{4,20},{6,22},{8,24},{10,26},{12,28},{14,30},{16,0},... | collective-permute-start | bytes 786440 | tf_op jit(solution)/shard_map/ppermute | solution.py:85
  95.4 9.0 %collective-permute-start.11 = (bf16[4,2,16,1024]{3,2,1,0:T(8,128)(2,1)S(1)}, bf16[4,2,16,1024]{3,2,1,0:T(8,128)(2,1)S(1)}, u32[]{:S(2)}, u32[]{:S(2)}) collective-permute-start(bf16[4,2,16,1024]{3,2,1,0:T(8,128)(2,1)S(1)} %pad_maximum_fusion.10), channel_id=1, source_target_pairs={{0,8},{2,10},{4,12},{6,14},{8,0},{10,2},{12,4},{14,6},{16,24},{18,... | collective-permute-start | bytes 786440 | tf_op jit(solution)/shard_map/ppermute | solution.py:85
  95.9 6.4 %collective-permute-start.17 = (bf16[2,2,16,1024]{3,2,1,0:T(8,128)(2,1)S(1)}, bf16[2,2,16,1024]{3,2,1,0:T(8,128)(2,1)S(1)}, u32[]{:S(2)}, u32[]{:S(2)}) collective-permute-start(bf16[2,2,16,1024]{3,2,1,0:T(8,128)(2,1)S(1)} %pad_maximum_fusion.28), channel_id=1, source_target_pairs={{0,4},{2,6},{4,0},{6,2},{8,12},{10,14},{12,8},{14,10},{16,20},{18,... | collective-permute-start | bytes 393224 | tf_op jit(solution)/shard_map/ppermute | solution.py:85
  96.6 6.1 %collective-permute-start.14 = (bf16[2,2,16,1024]{3,2,1,0:T(8,128)(2,1)S(1)}, bf16[2,2,16,1024]{3,2,1,0:T(8,128)(2,1)S(1)}, u32[]{:S(2)}, u32[]{:S(2)}) collective-permute-start(bf16[2,2,16,1024]{3,2,1,0:T(8,128)(2,1)S(1)} %pad_maximum_fusion.26), channel_id=1, source_target_pairs={{0,2},{2,0},{4,6},{6,4},{8,10},{10,8},{12,14},{14,12},{16,18},{18,... | collective-permute-start | bytes 393224 | tf_op jit(solution)/shard_map/ppermute | solution.py:85
  102.3 6.4 %collective-permute-start.18 = (bf16[2,2,2,16,1024]{4,3,2,1,0:T(8,128)(2,1)S(1)}, bf16[2,2,2,16,1024]{4,3,2,1,0:T(8,128)(2,1)S(1)}, u32[]{:S(2)}, u32[]{:S(2)}) collective-permute-start(bf16[2,2,2,16,1024]{4,3,2,1,0:T(8,128)(2,1)S(1)} %pad_maximum_fusion.14), channel_id=1, source_target_pairs={{0,2},{2,0},{4,6},{6,4},{8,10},{10,8},{12,14},{14,12},{16,18},{18,... | collective-permute-start | bytes 786440 | tf_op jit(solution)/shard_map/ppermute | solution.py:85
  102.9 8.5 %collective-permute-start.15 = (bf16[2,2,2,16,1024]{4,3,2,1,0:T(8,128)(2,1)S(1)}, bf16[2,2,2,16,1024]{4,3,2,1,0:T(8,128)(2,1)S(1)}, u32[]{:S(2)}, u32[]{:S(2)}) collective-permute-start(bf16[2,2,2,16,1024]{4,3,2,1,0:T(8,128)(2,1)S(1)} %pad_maximum_fusion.12), channel_id=1, source_target_pairs={{0,8},{2,10},{4,12},{6,14},{8,0},{10,2},{12,4},{14,6},{16,24},{18,... | collective-permute-start | bytes 786440 | tf_op jit(solution)/shard_map/ppermute | solution.py:85
  104.7 18.3 %collective-permute-start.12 = (bf16[4,2,2,16,1024]{4,3,2,1,0:T(8,128)(2,1)S(1)}, bf16[4,2,2,16,1024]{4,3,2,1,0:T(8,128)(2,1)S(1)}, u32[]{:S(2)}, u32[]{:S(2)}) collective-permute-start(bf16[4,2,2,16,1024]{4,3,2,1,0:T(8,128)(2,1)S(1)} %pad_maximum_fusion.4), channel_id=1, source_target_pairs={{0,4},{2,6},{4,0},{6,2},{8,12},{10,14},{12,8},{14,10},{16,20},{18,... | collective-permute-start | bytes 1572872 | tf_op jit(solution)/shard_map/ppermute | solution.py:85
  108.9 6.6 %collective-permute-start.23 = (bf16[1,2,2,2,16,1024]{5,4,3,2,1,0:T(8,128)(2,1)S(1)}, bf16[1,2,2,2,16,1024]{5,4,3,2,1,0:T(8,128)(2,1)S(1)}, u32[]{:S(2)}, u32[]{:S(2)}) collective-permute-start(bf16[1,2,2,2,16,1024]{5,4,3,2,1,0:T(8,128)(2,1)S(1)} %maximum_bitcast_fusion.17), channel_id=1, source_target_pairs={{0,8},{2,10},{4,12},{6,14},{8,0},{10,2},{12,4},{14,6},{16,24},{18,... | collective-permute-start | bytes 786440 | tf_op jit(solution)/shard_map/ppermute | solution.py:85
  111.4 8.6 %collective-permute-start.22 = (bf16[1,2,2,2,16,1024]{5,4,3,2,1,0:T(8,128)(2,1)S(1)}, bf16[1,2,2,2,16,1024]{5,4,3,2,1,0:T(8,128)(2,1)S(1)}, u32[]{:S(2)}, u32[]{:S(2)}) collective-permute-start(bf16[1,2,2,2,16,1024]{5,4,3,2,1,0:T(8,128)(2,1)S(1)} %maximum_bitcast_fusion.16), channel_id=1, source_target_pairs={{0,4},{2,6},{4,0},{6,2},{8,12},{10,14},{12,8},{14,10},{16,20},{18,... | collective-permute-start | bytes 786440 | tf_op jit(solution)/shard_map/ppermute | solution.py:85
  113.0 7.2 %collective-permute-start.19 = (bf16[1,2,2,2,16,1024]{5,4,3,2,1,0:T(8,128)(2,1)S(1)}, bf16[1,2,2,2,16,1024]{5,4,3,2,1,0:T(8,128)(2,1)S(1)}, u32[]{:S(2)}, u32[]{:S(2)}) collective-permute-start(bf16[1,2,2,2,16,1024]{5,4,3,2,1,0:T(8,128)(2,1)S(1)} %maximum_bitcast_fusion.13), channel_id=1, source_target_pairs={{0,8},{2,10},{4,12},{6,14},{8,0},{10,2},{12,4},{14,6},{16,24},{18,... | collective-permute-start | bytes 786440 | tf_op jit(solution)/shard_map/ppermute | solution.py:85
  114.2 8.7 %collective-permute-start.16 = (bf16[1,2,2,2,16,1024]{5,4,3,2,1,0:T(8,128)(2,1)S(1)}, bf16[1,2,2,2,16,1024]{5,4,3,2,1,0:T(8,128)(2,1)S(1)}, u32[]{:S(2)}, u32[]{:S(2)}) collective-permute-start(bf16[1,2,2,2,16,1024]{5,4,3,2,1,0:T(8,128)(2,1)S(1)} %maximum_bitcast_fusion.12), channel_id=1, source_target_pairs={{0,4},{2,6},{4,0},{6,2},{8,12},{10,14},{12,8},{14,10},{16,20},{18,... | collective-permute-start | bytes 786440 | tf_op jit(solution)/shard_map/ppermute | solution.py:85
  123.2 11.7 %collective-permute-start.21 = (bf16[2,2,2,2,16,1024]{5,4,3,2,1,0:T(8,128)(2,1)S(1)}, bf16[2,2,2,2,16,1024]{5,4,3,2,1,0:T(8,128)(2,1)S(1)}, u32[]{:S(2)}, u32[]{:S(2)}) collective-permute-start(bf16[2,2,2,2,16,1024]{5,4,3,2,1,0:T(8,128)(2,1)S(1)} %pad_maximum_fusion.6), channel_id=1, source_target_pairs={{0,2},{2,0},{4,6},{6,4},{8,10},{10,8},{12,14},{14,12},{16,18},{18,... | collective-permute-start | bytes 1572872 | tf_op jit(solution)/shard_map/ppermute | solution.py:85
  124.0 25.3 %collective-permute-start.13 = (bf16[2,2,2,2,16,1024]{5,4,3,2,1,0:T(8,128)(2,1)S(1)}, bf16[2,2,2,2,16,1024]{5,4,3,2,1,0:T(8,128)(2,1)S(1)}, u32[]{:S(2)}, u32[]{:S(2)}) collective-permute-start(bf16[2,2,2,2,16,1024]{5,4,3,2,1,0:T(8,128)(2,1)S(1)} %pad_maximum_fusion.5), channel_id=1, source_target_pairs={{0,2},{2,0},{4,6},{6,4},{8,10},{10,8},{12,14},{14,12},{16,18},{18,... | collective-permute-start | bytes 1572872 | tf_op jit(solution)/shard_map/ppermute | solution.py:85
  164.0 2.7 %collective-permute-start.24 = (f32[2,32,1024]{2,1,0:T(8,128)S(1)}, f32[2,32,1024]{2,1,0:T(8,128)S(1)}, u32[]{:S(2)}, u32[]{:S(2)}) collective-permute-start(f32[2,32,1024]{2,1,0:T(8,128)S(1)} %pad_maximum_fusion.21), channel_id=1, source_target_pairs={{0,1},{1,0},{2,3},{3,2},{4,5},{5,4},{6,7},{7,6},{8,9},{9,8},{10,11... | collective-permute-start | bytes 786440 | tf_op jit(solution)/shard_map/ppermute | solution.py:33
  165.2 1.3 collective-permute-start.25
  167.0 4.5 %collective-permute-start.26 = (f32[32]{0:T(128)S(1)}, f32[32]{0:T(128)S(1)}, u32[]{:S(2)}, u32[]{:S(2)}) collective-permute-start(f32[32]{0:T(128)S(1)} %fusion.11), channel_id=1, source_target_pairs={{0,6},{2,4},{4,2},{6,0},{8,14},{10,12},{12,10},{14,8},{16,22},{18,... | collective-permute-start | bytes 392 | tf_op jit(solution)/shard_map/ppermute | solution.py:33
  167.9 3.6 %collective-permute-start.27 = (f32[32]{0:T(128)S(1)}, f32[32]{0:T(128)S(1)}, u32[]{:S(2)}, u32[]{:S(2)}) collective-permute-start(f32[32]{0:T(128)S(1)} %fusion.11), channel_id=1, source_target_pairs={{0,4},{2,6},{4,0},{6,2},{8,12},{10,14},{12,8},{14,10},{16,20},{18,... | collective-permute-start | bytes 392 | tf_op jit(solution)/shard_map/ppermute | solution.py:33
  168.8 3.5 %collective-permute-start.28 = (f32[32]{0:T(128)S(1)}, f32[32]{0:T(128)S(1)}, u32[]{:S(2)}, u32[]{:S(2)}) collective-permute-start(f32[32]{0:T(128)S(1)} %fusion.11), channel_id=1, source_target_pairs={{0,2},{2,0},{4,6},{6,4},{8,10},{10,8},{12,14},{14,12},{16,18},{18,... | collective-permute-start | bytes 392 | tf_op jit(solution)/shard_map/ppermute | solution.py:33
  172.3 5.4 %collective-permute-start.29 = (f32[32]{0:T(128)S(1)}, f32[32]{0:T(128)S(1)}, u32[]{:S(2)}, u32[]{:S(2)}) collective-permute-start(f32[32]{0:T(128)S(1)} %fusion.27), channel_id=1, source_target_pairs={{0,24},{2,26},{4,28},{6,30},{8,16},{10,18},{12,20},{14,22},{16,8},... | collective-permute-start | bytes 392 | tf_op jit(solution)/shard_map/ppermute | solution.py:33
  173.9 4.4 %collective-permute-start.30 = (f32[32]{0:T(128)S(1)}, f32[32]{0:T(128)S(1)}, u32[]{:S(2)}, u32[]{:S(2)}) collective-permute-start(f32[32]{0:T(128)S(1)} %fusion.27), channel_id=1, source_target_pairs={{0,16},{2,18},{4,20},{6,22},{8,24},{10,26},{12,28},{14,30},{16,0},... | collective-permute-start | bytes 392 | tf_op jit(solution)/shard_map/ppermute | solution.py:33
  175.5 3.5 %collective-permute-start.31 = (f32[32]{0:T(128)S(1)}, f32[32]{0:T(128)S(1)}, u32[]{:S(2)}, u32[]{:S(2)}) collective-permute-start(f32[32]{0:T(128)S(1)} %fusion.27), channel_id=1, source_target_pairs={{0,8},{2,10},{4,12},{6,14},{8,0},{10,2},{12,4},{14,6},{16,24},{18,... | collective-permute-start | bytes 392 | tf_op jit(solution)/shard_map/ppermute | solution.py:33
  (9 other events, 67.9 us)

commit v10 on v6

--- a/solution.py
+++ b/solution.py
@@ -69,7 +69,7 @@
             bit = (place // mask) % 2
             keeps[p, r] = jnp.where(bit == 1, buf[1], buf[0])
             sends.setdefault(mask, []).append(((p, r), jnp.where(bit == 1, buf[0], buf[1])))
-        for mask, items in sends.items():
+        for mask, items in sorted(sends.items(), key=lambda kv: -kv[0]):
             got = lax.ppermute(jnp.stack([v for _, v in items]), axis, [(i, i ^ mask) for i in range(size)])
             for n, (key, _) in enumerate(items):
                 held = sum(orders[key[0]][:s])
@@ -79,7 +79,7 @@
         sends = {}
         for (p, r), buf in bufs.items():
             sends.setdefault((r if s == 0 else 0, orders[p][s]), []).append(((p, r), buf))
-        for (_, mask), items in sorted(sends.items()):
+        for (_, mask), items in sorted(sends.items(), key=lambda kv: (kv[0][0], -kv[0][1])):
             got = lax.ppermute(jnp.stack([v for _, v in items]), axis, [(i, i ^ mask) for i in range(size)])
             bit = (place // mask) % 2
             for n, (key, buf) in enumerate(items):

time: 158 us -> 158 us (level)
  no operation moved by 1% of the time
where the time goes in v10:
time: 158 us; the launch traced here: 157 us
  starting transfers between devices  52.3 us (33%)
  waiting for transfers between devices  44 us (28%)
  Pallas kernels  23.6 us (15%)
  other arithmetic  18 us (11%)
  local copies, waits for them, and re-layouts  15.1 us (10%)
  between operations  2.59 us (2%)
    ppermute x36, starting transfers between devices, spread_blocks(): lax.ppermute(jnp.stack([v for _, v in items]), axis, [(i, i ^ mask) for i...  42.5 us
    ppermute x36, waiting for transfers between devices, spread_blocks(): lax.ppermute(jnp.stack([v for _, v in items]), axis, [(i, i ^ mask) for i...  38.8 us
    pallas_call x2, Pallas kernels, correlate(): pl.pallas_call(correlate_kernel, grid_spec=grid_spec, out_shape=[jax.Shap...  23.6 us
    ppermute x8, starting transfers between devices, group_sum(): got[d] = lax.ppermute(value, axis, pairs)  8.57 us
    select_n x18, other arithmetic, spread_blocks(): bufs[key] = jnp.where(holder, keeps[key], got[n])  5.69 us
    ppermute x8, waiting for transfers between devices, group_sum(): got[d] = lax.ppermute(value, axis, pairs)  5.15 us
    unnamed x20, local copies, waits for them, and re-layouts  4.37 us
    another operation x52, other arithmetic, spread_blocks(): jnp.stack([v for _, v in items])  4.2 us
  transfers between devices with their start and end apart: 45, of which 21 were waited for; matrix products, arithmetic and copies ran while one was open for 18% of the time, Pallas kernels for 7%

profile of v10, /device:TPU:0, one launch (start us, length us, event | category | flops | bytes accessed | tf_op | source)
XLA Modules:
  0.0 157.0 jit_solution(17145707625160787396)
XLA Ops:
  0.0 1.7 %slice.719 = bf16[1024,128]{1,0:T(8,128)(2,1)} slice(bf16[1024,1024]{1,0:T(8,128)(2,1)} %param.4), slice={[0:1024], [0:128]} | slice | bytes 524288 | tf_op jit(solution)/shard_map/slice | solution.py:181
  3.0 2.9 %copy.32 = bf16[1024,1024]{0,1:T(8,128)(2,1)S(1)} copy(bf16[1024,1024]{1,0:T(8,128)(2,1)} %param.4) | data formatting | bytes 4194304 | tf_op args[0]
  8.0 7.0 %collective-permute-start.24 = (bf16[2,2,2,2,16,1024]{5,4,3,2,1,0:T(8,128)(2,1)}, bf16[2,2,2,2,16,1024]{5,4,3,2,1,0:T(8,128)(2,1)}, u32[]{:S(2)}, u32[]{:S(2)}) collective-permute-start(bf16[2,2,2,2,16,1024]{5,4,3,2,1,0:T(8,128)(2,1)} %pad_maximum_fusion.3), channel_id=1, source_target_pairs={{0,16},{2,18},{4,20},{6,22},{8,24},{10,26},{12,28},{14,30},{16,0},... | collective-permute-start | bytes 1572872 | tf_op jit(solution)/shard_map/ppermute | solution.py:73
  15.9 1.6 %collective-permute-start.16 = (bf16[2,2,2,2,16,1024]{5,4,3,2,1,0:T(8,128)(2,1)}, bf16[2,2,2,2,16,1024]{5,4,3,2,1,0:T(8,128)(2,1)}, u32[]{:S(2)}, u32[]{:S(2)}) collective-permute-start(bf16[2,2,2,2,16,1024]{5,4,3,2,1,0:T(8,128)(2,1)} %pad_maximum_fusion.2), channel_id=1, source_target_pairs={{0,8},{2,10},{4,12},{6,14},{8,0},{10,2},{12,4},{14,6},{16,24},{18,... | collective-permute-start | bytes 1572872 | tf_op jit(solution)/shard_map/ppermute | solution.py:73
  21.0 1.8 %fusion.29 = (bf16[1,2,2,2,16,1024]{5,4,0,1,2,3:T(8,128)(2,1)S(1)}, bf16[1,2,2,2,16,1024]{5,4,0,1,2,3:T(8,128)(2,1)S(1)}, bf16[1,2,2,2,16,1024]{5,4,0,1,2,3:T(8,128)(2,1)}) fusion(bf16[2,2,2,2,16,1024]{5,4,0,1,2,3:T(8,128)(2,1)} %bitcast.290, pred[]{:T(512)S(6)} %eq.170), kind=kLoop, calls=%fused_computation.303 | loop fusion | flops 131072 | bytes 1310721 | tf_op jit(solution)/shard_map/slice | solution.py:70
  32.5 6.4 %collective-permute-done.24 = bf16[2,2,2,2,16,1024]{5,4,3,2,1,0:T(8,128)(2,1)} collective-permute-done((bf16[2,2,2,2,16,1024]{5,4,3,2,1,0:T(8,128)(2,1)}, bf16[2,2,2,2,16,1024]{5,4,3,2,1,0:T(8,128)(2,1)}, u32[]{:S(2)}, u32[]{:S(2)}) %collective-permute-start.24) | collective-permute-done | bytes 524320 | tf_op jit(solution)/shard_map/ppermute | solution.py:73
  42.8 3.4 %collective-permute-start.9 = (bf16[2,2,2,16,1024]{4,3,2,1,0:T(8,128)(2,1)S(1)}, bf16[2,2,2,16,1024]{4,3,2,1,0:T(8,128)(2,1)S(1)}, u32[]{:S(2)}, u32[]{:S(2)}) collective-permute-start(bf16[2,2,2,16,1024]{4,3,2,1,0:T(8,128)(2,1)S(1)} %pad_maximum_fusion.7), channel_id=1, source_target_pairs={{0,8},{2,10},{4,12},{6,14},{8,0},{10,2},{12,4},{14,6},{16,24},{18,... | collective-permute-start | bytes 786440 | tf_op jit(solution)/shard_map/ppermute | solution.py:73
  50.6 5.0 %collective-permute-done.17 = bf16[2,2,2,16,1024]{4,3,2,1,0:T(8,128)(2,1)S(1)} collective-permute-done((bf16[2,2,2,16,1024]{4,3,2,1,0:T(8,128)(2,1)S(1)}, bf16[2,2,2,16,1024]{4,3,2,1,0:T(8,128)(2,1)S(1)}, u32[]{:S(2)}, u32[]{:S(2)}) %collective-permute-start.17) | collective-permute-done | bytes 262176 | tf_op jit(solution)/shard_map/ppermute | solution.py:73
  55.7 1.8 %collective-permute-start.18 = (bf16[2,2,16,1024]{3,2,1,0:T(8,128)(2,1)S(1)}, bf16[2,2,16,1024]{3,2,1,0:T(8,128)(2,1)S(1)}, u32[]{:S(2)}, u32[]{:S(2)}) collective-permute-start(bf16[2,2,16,1024]{3,2,1,0:T(8,128)(2,1)S(1)} %pad_maximum_fusion.27), channel_id=1, source_target_pairs={{0,2},{2,0},{4,6},{6,4},{8,10},{10,8},{12,14},{14,12},{16,18},{18,... | collective-permute-start | bytes 393224 | tf_op jit(solution)/shard_map/ppermute | solution.py:73
  57.9 2.4 %collective-permute-start.2 = (bf16[2,2,16,1024]{3,2,1,0:T(8,128)(2,1)S(1)}, bf16[2,2,16,1024]{3,2,1,0:T(8,128)(2,1)S(1)}, u32[]{:S(2)}, u32[]{:S(2)}) collective-permute-start(bf16[2,2,16,1024]{3,2,1,0:T(8,128)(2,1)S(1)} %pad_maximum_fusion.21), channel_id=1, source_target_pairs={{0,8},{2,10},{4,12},{6,14},{8,0},{10,2},{12,4},{14,6},{16,24},{18,... | collective-permute-start | bytes 393224 | tf_op jit(solution)/shard_map/ppermute | solution.py:73
  61.5 3.7 %collective-permute-done.10 = bf16[2,2,16,1024]{3,2,1,0:T(8,128)(2,1)S(1)} collective-permute-done((bf16[2,2,16,1024]{3,2,1,0:T(8,128)(2,1)S(1)}, bf16[2,2,16,1024]{3,2,1,0:T(8,128)(2,1)S(1)}, u32[]{:S(2)}, u32[]{:S(2)}) %collective-permute-start.10) | collective-permute-done | bytes 131104 | tf_op jit(solution)/shard_map/ppermute | solution.py:73
  67.1 2.1 %collective-permute-start.28 = (bf16[2,16,1024]{2,1,0:T(8,128)(2,1)S(1)}, bf16[2,16,1024]{2,1,0:T(8,128)(2,1)S(1)}, u32[]{:S(2)}, u32[]{:S(2)}) collective-permute-start(bf16[2,16,1024]{2,1,0:T(8,128)(2,1)S(1)} %pad_maximum_fusion.50), channel_id=1, source_target_pairs={{0,8},{2,10},{4,12},{6,14},{8,0},{10,2},{12,4},{14,6},{16,24},{18,... | collective-permute-start | bytes 196616 | tf_op jit(solution)/shard_map/ppermute | solution.py:83
  75.3 1.6 collective-permute-start.13
  76.9 2.4 %collective-permute-done.4 = bf16[2,16,1024]{2,1,0:T(8,128)(2,1)S(1)} collective-permute-done((bf16[2,16,1024]{2,1,0:T(8,128)(2,1)S(1)}, bf16[2,16,1024]{2,1,0:T(8,128)(2,1)S(1)}, u32[]{:S(2)}, u32[]{:S(2)}) %collective-permute-start.4) | collective-permute-done | bytes 65568 | tf_op jit(solution)/shard_map/ppermute | solution.py:83
  79.6 1.6 %collective-permute-start.30 = (bf16[2,2,2,16,1024]{4,3,2,1,0:T(8,128)(2,1)S(1)}, bf16[2,2,2,16,1024]{4,3,2,1,0:T(8,128)(2,1)S(1)}, u32[]{:S(2)}, u32[]{:S(2)}) collective-permute-start(bf16[2,2,2,16,1024]{4,3,2,1,0:T(8,128)(2,1)S(1)} %pad_maximum_fusion.14), channel_id=1, source_target_pairs={{0,2},{2,0},{4,6},{6,4},{8,10},{10,8},{12,14},{14,12},{16,18},{18,... | collective-permute-start | bytes 786440 | tf_op jit(solution)/shard_map/ppermute | solution.py:83
  81.3 2.3 %collective-permute-start.22 = (bf16[2,2,2,16,1024]{4,3,2,1,0:T(8,128)(2,1)S(1)}, bf16[2,2,2,16,1024]{4,3,2,1,0:T(8,128)(2,1)S(1)}, u32[]{:S(2)}, u32[]{:S(2)}) collective-permute-start(bf16[2,2,2,16,1024]{4,3,2,1,0:T(8,128)(2,1)S(1)} %pad_maximum_fusion.11), channel_id=1, source_target_pairs={{0,16},{2,18},{4,20},{6,22},{8,24},{10,26},{12,28},{14,30},{16,0},... | collective-permute-start | bytes 786440 | tf_op jit(solution)/shard_map/ppermute | solution.py:83
  83.5 3.4 %collective-permute-done.13 = bf16[2,2,16,1024]{3,2,1,0:T(8,128)(2,1)S(1)} collective-permute-done((bf16[2,2,16,1024]{3,2,1,0:T(8,128)(2,1)S(1)}, bf16[2,2,16,1024]{3,2,1,0:T(8,128)(2,1)S(1)}, u32[]{:S(2)}, u32[]{:S(2)}) %collective-permute-start.13) | collective-permute-done | bytes 131104 | tf_op jit(solution)/shard_map/ppermute | solution.py:83
  87.1 2.9 %collective-permute-done.5 = bf16[2,2,16,1024]{3,2,1,0:T(8,128)(2,1)S(1)} collective-permute-done((bf16[2,2,16,1024]{3,2,1,0:T(8,128)(2,1)S(1)}, bf16[2,2,16,1024]{3,2,1,0:T(8,128)(2,1)S(1)}, u32[]{:S(2)}, u32[]{:S(2)}) %collective-permute-start.5) | collective-permute-done | bytes 131104 | tf_op jit(solution)/shard_map/ppermute | solution.py:83
  91.3 8.9 %collective-permute-done.22 = bf16[2,2,2,16,1024]{4,3,2,1,0:T(8,128)(2,1)S(1)} collective-permute-done((bf16[2,2,2,16,1024]{4,3,2,1,0:T(8,128)(2,1)S(1)}, bf16[2,2,2,16,1024]{4,3,2,1,0:T(8,128)(2,1)S(1)}, u32[]{:S(2)}, u32[]{:S(2)}) %collective-permute-start.22) | collective-permute-done | bytes 262176 | tf_op jit(solution)/shard_map/ppermute | solution.py:83
  100.4 2.0 %collective-permute-start.34 = (bf16[1,2,2,2,16,1024]{5,4,3,2,1,0:T(8,128)(2,1)S(1)}, bf16[1,2,2,2,16,1024]{5,4,3,2,1,0:T(8,128)(2,1)S(1)}, u32[]{:S(2)}, u32[]{:S(2)}) collective-permute-start(bf16[1,2,2,2,16,1024]{5,4,3,2,1,0:T(8,128)(2,1)S(1)} %maximum_bitcast_fusion.15), channel_id=1, source_target_pairs={{0,4},{2,6},{4,0},{6,2},{8,12},{10,14},{12,8},{14,10},{16,20},{18,... | collective-permute-start | bytes 786440 | tf_op jit(solution)/shard_map/ppermute | solution.py:83
  102.6 2.1 %collective-permute-start.7 = (bf16[1,2,2,2,16,1024]{5,4,3,2,1,0:T(8,128)(2,1)S(1)}, bf16[1,2,2,2,16,1024]{5,4,3,2,1,0:T(8,128)(2,1)S(1)}, u32[]{:S(2)}, u32[]{:S(2)}) collective-permute-start(bf16[1,2,2,2,16,1024]{5,4,3,2,1,0:T(8,128)(2,1)S(1)} %maximum_bitcast_fusion.10), channel_id=1, source_target_pairs={{0,2},{2,0},{4,6},{6,4},{8,10},{10,8},{12,14},{14,12},{16,18},{18,... | collective-permute-start | bytes 786440 | tf_op jit(solution)/shard_map/ppermute | solution.py:83
  104.8 1.3 collective-permute-start.31
  106.3 2.1 %collective-permute-done.35 = bf16[1,2,2,2,16,1024]{5,4,3,2,1,0:T(8,128)(2,1)S(1)} collective-permute-done((bf16[1,2,2,2,16,1024]{5,4,3,2,1,0:T(8,128)(2,1)S(1)}, bf16[1,2,2,2,16,1024]{5,4,3,2,1,0:T(8,128)(2,1)S(1)}, u32[]{:S(2)}, u32[]{:S(2)}) %collective-permute-start.35) | collective-permute-done | bytes 262176 | tf_op jit(solution)/shard_map/ppermute | solution.py:83
  108.5 1.8 %collective-permute-start.15 = (bf16[1,2,2,2,16,1024]{5,4,3,2,1,0:T(8,128)(2,1)S(1)}, bf16[1,2,2,2,16,1024]{5,4,3,2,1,0:T(8,128)(2,1)S(1)}, u32[]{:S(2)}, u32[]{:S(2)}) collective-permute-start(bf16[1,2,2,2,16,1024]{5,4,3,2,1,0:T(8,128)(2,1)S(1)} %maximum_bitcast_fusion.11), channel_id=1, source_target_pairs={{0,4},{2,6},{4,0},{6,2},{8,12},{10,14},{12,8},{14,10},{16,20},{18,... | collective-permute-start | bytes 786440 | tf_op jit(solution)/shard_map/ppermute | solution.py:83
  111.9 1.5 maximum_bitcast_fusion.1.blk_ref
  113.4 11.7 %shard_map.47 = (f32[4,4,1024]{2,1,0:T(4,128)}, f32[4,4,128]{2,1,0:T(4,128)}) custom-call(s32[64]{0:T(128)} %squeeze.19.meta_ref, bf16[1,1024,1024]{2,1,0:T(8,128)(2,1)} %maximum_bitcast_fusion.1.blk_ref, bf16[1024,1152]{1,0:T(8,128)(2,1)} %copy-done.3), custom_call_target="tpu_custom_call" | custom-call | flops 5435817984 | bytes 4521984 | tf_op jit(solution)/shard_map/pallas_call | solution.py:154
  126.6 1.5 maximum_bitcast_fusion.blk_ref
  128.1 11.9 %shard_map.46 = (f32[4,4,1024]{2,1,0:T(4,128)}, f32[4,4,128]{2,1,0:T(4,128)}) custom-call(s32[64]{0:T(128)} %squeeze.16.meta_ref, bf16[1,1024,1024]{2,1,0:T(8,128)(2,1)} %maximum_bitcast_fusion.blk_ref, bf16[1024,1152]{1,0:T(8,128)(2,1)} %copy-done.3), custom_call_target="tpu_custom_call" | custom-call | flops 5435817984 | bytes 4521984 | tf_op jit(solution)/shard_map/pallas_call | solution.py:154
  143.8 1.7 %collective-permute-start.39 = (f32[32]{0:T(128)S(1)}, f32[32]{0:T(128)S(1)}, u32[]{:S(2)}, u32[]{:S(2)}) collective-permute-start(f32[32]{0:T(128)S(1)} %fusion.11), channel_id=1, source_target_pairs={{0,6},{2,4},{4,2},{6,0},{8,14},{10,12},{12,10},{14,8},{16,22},{18,... | collective-permute-start | bytes 392 | tf_op jit(solution)/shard_map/ppermute | solution.py:33
  145.5 1.8 %collective-permute-start.41 = (f32[32]{0:T(128)S(1)}, f32[32]{0:T(128)S(1)}, u32[]{:S(2)}, u32[]{:S(2)}) collective-permute-start(f32[32]{0:T(128)S(1)} %fusion.11), channel_id=1, source_target_pairs={{0,2},{2,0},{4,6},{6,4},{8,10},{10,8},{12,14},{14,12},{16,18},{18,... | collective-permute-start | bytes 392 | tf_op jit(solution)/shard_map/ppermute | solution.py:33
  149.1 1.5 collective-permute-start.42
  150.6 2.0 %collective-permute-start.43 = (f32[32]{0:T(128)S(1)}, f32[32]{0:T(128)S(1)}, u32[]{:S(2)}, u32[]{:S(2)}) collective-permute-start(f32[32]{0:T(128)S(1)} %fusion.27), channel_id=1, source_target_pairs={{0,16},{2,18},{4,20},{6,22},{8,24},{10,26},{12,28},{14,30},{16,0},... | collective-permute-start | bytes 392 | tf_op jit(solution)/shard_map/ppermute | solution.py:33
  (260 shorter events, 48.9 us)
Async XLA Ops:
  1.7 27.0 %collective-permute-start.32 = (bf16[1024,128]{1,0:T(8,128)(2,1)}, bf16[1024,128]{1,0:T(8,128)(2,1)}, u32[]{:S(2)}, u32[]{:S(2)}) collective-permute-start(bf16[1024,128]{1,0:T(8,128)(2,1)} %slice.719), channel_id=1, source_target_pairs={{2,0},{4,2},{6,4},{8,6},{10,8},{12,10},{14,12},{16,14},{18,16},{20... | collective-permute-start | bytes 786440 | tf_op jit(solution)/shard_map/ppermute | solution.py:18
  8.0 30.8 %collective-permute-start.24 = (bf16[2,2,2,2,16,1024]{5,4,3,2,1,0:T(8,128)(2,1)}, bf16[2,2,2,2,16,1024]{5,4,3,2,1,0:T(8,128)(2,1)}, u32[]{:S(2)}, u32[]{:S(2)}) collective-permute-start(bf16[2,2,2,2,16,1024]{5,4,3,2,1,0:T(8,128)(2,1)} %pad_maximum_fusion.3), channel_id=1, source_target_pairs={{0,16},{2,18},{4,20},{6,22},{8,24},{10,26},{12,28},{14,30},{16,0},... | collective-permute-start | bytes 1572872 | tf_op jit(solution)/shard_map/ppermute | solution.py:73
  15.9 24.2 %collective-permute-start.16 = (bf16[2,2,2,2,16,1024]{5,4,3,2,1,0:T(8,128)(2,1)}, bf16[2,2,2,2,16,1024]{5,4,3,2,1,0:T(8,128)(2,1)}, u32[]{:S(2)}, u32[]{:S(2)}) collective-permute-start(bf16[2,2,2,2,16,1024]{5,4,3,2,1,0:T(8,128)(2,1)} %pad_maximum_fusion.2), channel_id=1, source_target_pairs={{0,8},{2,10},{4,12},{6,14},{8,0},{10,2},{12,4},{14,6},{16,24},{18,... | collective-permute-start | bytes 1572872 | tf_op jit(solution)/shard_map/ppermute | solution.py:73
  20.4 21.2 %collective-permute-start.8 = (bf16[2,2,2,2,16,1024]{5,4,3,2,1,0:T(8,128)(2,1)}, bf16[2,2,2,2,16,1024]{5,4,3,2,1,0:T(8,128)(2,1)}, u32[]{:S(2)}, u32[]{:S(2)}) collective-permute-start(bf16[2,2,2,2,16,1024]{5,4,3,2,1,0:T(8,128)(2,1)} %pad_maximum_fusion.1), channel_id=1, source_target_pairs={{0,4},{2,6},{4,0},{6,2},{8,12},{10,14},{12,8},{14,10},{16,20},{18,... | collective-permute-start | bytes 1572872 | tf_op jit(solution)/shard_map/ppermute | solution.py:73
  23.7 22.5 %collective-permute-start = (bf16[2,2,2,2,16,1024]{5,4,0,1,2,3:T(8,128)(2,1)}, bf16[2,2,2,2,16,1024]{5,4,0,1,2,3:T(8,128)(2,1)}, u32[]{:S(2)}, u32[]{:S(2)}) collective-permute-start(bf16[2,2,2,2,16,1024]{5,4,0,1,2,3:T(8,128)(2,1)} %pad_maximum_fusion), channel_id=1, source_target_pairs={{0,2},{2,0},{4,6},{6,4},{8,10},{10,8},{12,14},{14,12},{16,18},{18,... | collective-permute-start | bytes 1572872 | tf_op jit(solution)/shard_map/ppermute | solution.py:73
  40.0 9.6 %collective-permute-start.25 = (bf16[2,2,2,16,1024]{4,3,2,1,0:T(8,128)(2,1)S(1)}, bf16[2,2,2,16,1024]{4,3,2,1,0:T(8,128)(2,1)S(1)}, u32[]{:S(2)}, u32[]{:S(2)}) collective-permute-start(bf16[2,2,2,16,1024]{4,3,2,1,0:T(8,128)(2,1)S(1)} %pad_maximum_fusion.13), channel_id=1, source_target_pairs={{0,2},{2,0},{4,6},{6,4},{8,10},{10,8},{12,14},{14,12},{16,18},{18,... | collective-permute-start | bytes 786440 | tf_op jit(solution)/shard_map/ppermute | solution.py:73
  41.3 14.4 %collective-permute-start.17 = (bf16[2,2,2,16,1024]{4,3,2,1,0:T(8,128)(2,1)S(1)}, bf16[2,2,2,16,1024]{4,3,2,1,0:T(8,128)(2,1)S(1)}, u32[]{:S(2)}, u32[]{:S(2)}) collective-permute-start(bf16[2,2,2,16,1024]{4,3,2,1,0:T(8,128)(2,1)S(1)} %pad_maximum_fusion.10), channel_id=1, source_target_pairs={{0,16},{2,18},{4,20},{6,22},{8,24},{10,26},{12,28},{14,30},{16,0},... | collective-permute-start | bytes 786440 | tf_op jit(solution)/shard_map/ppermute | solution.py:73
  42.8 14.7 %collective-permute-start.9 = (bf16[2,2,2,16,1024]{4,3,2,1,0:T(8,128)(2,1)S(1)}, bf16[2,2,2,16,1024]{4,3,2,1,0:T(8,128)(2,1)S(1)}, u32[]{:S(2)}, u32[]{:S(2)}) collective-permute-start(bf16[2,2,2,16,1024]{4,3,2,1,0:T(8,128)(2,1)S(1)} %pad_maximum_fusion.7), channel_id=1, source_target_pairs={{0,8},{2,10},{4,12},{6,14},{8,0},{10,2},{12,4},{14,6},{16,24},{18,... | collective-permute-start | bytes 786440 | tf_op jit(solution)/shard_map/ppermute | solution.py:73
  48.4 9.4 %collective-permute-start.1 = (bf16[2,2,2,16,1024]{4,3,2,1,0:T(8,128)(2,1)S(1)}, bf16[2,2,2,16,1024]{4,3,2,1,0:T(8,128)(2,1)S(1)}, u32[]{:S(2)}, u32[]{:S(2)}) collective-permute-start(bf16[2,2,2,16,1024]{4,3,2,1,0:T(8,128)(2,1)S(1)} %pad_maximum_fusion.4), channel_id=1, source_target_pairs={{0,4},{2,6},{4,0},{6,2},{8,12},{10,14},{12,8},{14,10},{16,20},{18,... | collective-permute-start | bytes 786440 | tf_op jit(solution)/shard_map/ppermute | solution.py:73
  49.7 10.6 %collective-permute-start.26 = (bf16[2,2,16,1024]{3,2,1,0:T(8,128)(2,1)S(1)}, bf16[2,2,16,1024]{3,2,1,0:T(8,128)(2,1)S(1)}, u32[]{:S(2)}, u32[]{:S(2)}) collective-permute-start(bf16[2,2,16,1024]{3,2,1,0:T(8,128)(2,1)S(1)} %pad_maximum_fusion.30), channel_id=1, source_target_pairs={{0,4},{2,6},{4,0},{6,2},{8,12},{10,14},{12,8},{14,10},{16,20},{18,... | collective-permute-start | bytes 393224 | tf_op jit(solution)/shard_map/ppermute | solution.py:73
  57.6 7.6 %collective-permute-start.10 = (bf16[2,2,16,1024]{3,2,1,0:T(8,128)(2,1)S(1)}, bf16[2,2,16,1024]{3,2,1,0:T(8,128)(2,1)S(1)}, u32[]{:S(2)}, u32[]{:S(2)}) collective-permute-start(bf16[2,2,16,1024]{3,2,1,0:T(8,128)(2,1)S(1)} %pad_maximum_fusion.24), channel_id=1, source_target_pairs={{0,16},{2,18},{4,20},{6,22},{8,24},{10,26},{12,28},{14,30},{16,0},... | collective-permute-start | bytes 393224 | tf_op jit(solution)/shard_map/ppermute | solution.py:73
  57.9 8.5 %collective-permute-start.2 = (bf16[2,2,16,1024]{3,2,1,0:T(8,128)(2,1)S(1)}, bf16[2,2,16,1024]{3,2,1,0:T(8,128)(2,1)S(1)}, u32[]{:S(2)}, u32[]{:S(2)}) collective-permute-start(bf16[2,2,16,1024]{3,2,1,0:T(8,128)(2,1)S(1)} %pad_maximum_fusion.21), channel_id=1, source_target_pairs={{0,8},{2,10},{4,12},{6,14},{8,0},{10,2},{12,4},{14,6},{16,24},{18,... | collective-permute-start | bytes 393224 | tf_op jit(solution)/shard_map/ppermute | solution.py:73
  60.4 6.7 %collective-permute-start.27 = (bf16[2,16,1024]{2,1,0:T(8,128)(2,1)S(1)}, bf16[2,16,1024]{2,1,0:T(8,128)(2,1)S(1)}, u32[]{:S(2)}, u32[]{:S(2)}) collective-permute-start(bf16[2,16,1024]{2,1,0:T(8,128)(2,1)S(1)} %pad_maximum_fusion.49), channel_id=1, source_target_pairs={{0,8},{2,10},{4,12},{6,14},{8,0},{10,2},{12,4},{14,6},{16,24},{18,... | collective-permute-start | bytes 196616 | tf_op jit(solution)/shard_map/ppermute | solution.py:73
  60.8 8.4 %collective-permute-start.19 = (bf16[2,16,1024]{2,1,0:T(8,128)(2,1)S(1)}, bf16[2,16,1024]{2,1,0:T(8,128)(2,1)S(1)}, u32[]{:S(2)}, u32[]{:S(2)}) collective-permute-start(bf16[2,16,1024]{2,1,0:T(8,128)(2,1)S(1)} %pad_maximum_fusion.45), channel_id=1, source_target_pairs={{0,4},{2,6},{4,0},{6,2},{8,12},{10,14},{12,8},{14,10},{16,20},{18,... | collective-permute-start | bytes 196616 | tf_op jit(solution)/shard_map/ppermute | solution.py:73
  66.4 5.6 %collective-permute-start.3 = (bf16[2,16,1024]{2,1,0:T(8,128)(2,1)S(1)}, bf16[2,16,1024]{2,1,0:T(8,128)(2,1)S(1)}, u32[]{:S(2)}, u32[]{:S(2)}) collective-permute-start(bf16[2,16,1024]{2,1,0:T(8,128)(2,1)S(1)} %pad_maximum_fusion.37), channel_id=1, source_target_pairs={{0,16},{2,18},{4,20},{6,22},{8,24},{10,26},{12,28},{14,30},{16,0},... | collective-permute-start | bytes 196616 | tf_op jit(solution)/shard_map/ppermute | solution.py:73
  72.0 7.3 %collective-permute-start.4 = (bf16[2,16,1024]{2,1,0:T(8,128)(2,1)S(1)}, bf16[2,16,1024]{2,1,0:T(8,128)(2,1)S(1)}, u32[]{:S(2)}, u32[]{:S(2)}) collective-permute-start(bf16[2,16,1024]{2,1,0:T(8,128)(2,1)S(1)} %pad_maximum_fusion.38), channel_id=1, source_target_pairs={{0,16},{2,18},{4,20},{6,22},{8,24},{10,26},{12,28},{14,30},{16,0},... | collective-permute-start | bytes 196616 | tf_op jit(solution)/shard_map/ppermute | solution.py:83
  72.4 7.1 %collective-permute-start.29 = (bf16[2,2,16,1024]{3,2,1,0:T(8,128)(2,1)S(1)}, bf16[2,2,16,1024]{3,2,1,0:T(8,128)(2,1)S(1)}, u32[]{:S(2)}, u32[]{:S(2)}) collective-permute-start(bf16[2,2,16,1024]{3,2,1,0:T(8,128)(2,1)S(1)} %pad_maximum_fusion.31), channel_id=1, source_target_pairs={{0,4},{2,6},{4,0},{6,2},{8,12},{10,14},{12,8},{14,10},{16,20},{18,... | collective-permute-start | bytes 393224 | tf_op jit(solution)/shard_map/ppermute | solution.py:83
  74.2 6.9 %collective-permute-start.21 = (bf16[2,2,16,1024]{3,2,1,0:T(8,128)(2,1)S(1)}, bf16[2,2,16,1024]{3,2,1,0:T(8,128)(2,1)S(1)}, u32[]{:S(2)}, u32[]{:S(2)}) collective-permute-start(bf16[2,2,16,1024]{3,2,1,0:T(8,128)(2,1)S(1)} %pad_maximum_fusion.28), channel_id=1, source_target_pairs={{0,2},{2,0},{4,6},{6,4},{8,10},{10,8},{12,14},{14,12},{16,18},{18,... | collective-permute-start | bytes 393224 | tf_op jit(solution)/shard_map/ppermute | solution.py:83
  75.3 11.6 %collective-permute-start.13 = (bf16[2,2,16,1024]{3,2,1,0:T(8,128)(2,1)S(1)}, bf16[2,2,16,1024]{3,2,1,0:T(8,128)(2,1)S(1)}, u32[]{:S(2)}, u32[]{:S(2)}) collective-permute-start(bf16[2,2,16,1024]{3,2,1,0:T(8,128)(2,1)S(1)} %pad_maximum_fusion.25), channel_id=1, source_target_pairs={{0,16},{2,18},{4,20},{6,22},{8,24},{10,26},{12,28},{14,30},{16,0},... | collective-permute-start | bytes 393224 | tf_op jit(solution)/shard_map/ppermute | solution.py:83
  79.4 10.6 %collective-permute-start.5 = (bf16[2,2,16,1024]{3,2,1,0:T(8,128)(2,1)S(1)}, bf16[2,2,16,1024]{3,2,1,0:T(8,128)(2,1)S(1)}, u32[]{:S(2)}, u32[]{:S(2)}) collective-permute-start(bf16[2,2,16,1024]{3,2,1,0:T(8,128)(2,1)S(1)} %pad_maximum_fusion.22), channel_id=1, source_target_pairs={{0,8},{2,10},{4,12},{6,14},{8,0},{10,2},{12,4},{14,6},{16,24},{18,... | collective-permute-start | bytes 393224 | tf_op jit(solution)/shard_map/ppermute | solution.py:83
  79.6 11.1 %collective-permute-start.30 = (bf16[2,2,2,16,1024]{4,3,2,1,0:T(8,128)(2,1)S(1)}, bf16[2,2,2,16,1024]{4,3,2,1,0:T(8,128)(2,1)S(1)}, u32[]{:S(2)}, u32[]{:S(2)}) collective-permute-start(bf16[2,2,2,16,1024]{4,3,2,1,0:T(8,128)(2,1)S(1)} %pad_maximum_fusion.14), channel_id=1, source_target_pairs={{0,2},{2,0},{4,6},{6,4},{8,10},{10,8},{12,14},{14,12},{16,18},{18,... | collective-permute-start | bytes 786440 | tf_op jit(solution)/shard_map/ppermute | solution.py:83
  81.3 18.9 %collective-permute-start.22 = (bf16[2,2,2,16,1024]{4,3,2,1,0:T(8,128)(2,1)S(1)}, bf16[2,2,2,16,1024]{4,3,2,1,0:T(8,128)(2,1)S(1)}, u32[]{:S(2)}, u32[]{:S(2)}) collective-permute-start(bf16[2,2,2,16,1024]{4,3,2,1,0:T(8,128)(2,1)S(1)} %pad_maximum_fusion.11), channel_id=1, source_target_pairs={{0,16},{2,18},{4,20},{6,22},{8,24},{10,26},{12,28},{14,30},{16,0},... | collective-permute-start | bytes 786440 | tf_op jit(solution)/shard_map/ppermute | solution.py:83
  87.0 13.3 %collective-permute-start.14 = (bf16[2,2,2,16,1024]{4,3,2,1,0:T(8,128)(2,1)S(1)}, bf16[2,2,2,16,1024]{4,3,2,1,0:T(8,128)(2,1)S(1)}, u32[]{:S(2)}, u32[]{:S(2)}) collective-permute-start(bf16[2,2,2,16,1024]{4,3,2,1,0:T(8,128)(2,1)S(1)} %pad_maximum_fusion.8), channel_id=1, source_target_pairs={{0,8},{2,10},{4,12},{6,14},{8,0},{10,2},{12,4},{14,6},{16,24},{18,... | collective-permute-start | bytes 786440 | tf_op jit(solution)/shard_map/ppermute | solution.py:83
  90.1 12.2 %collective-permute-start.6 = (bf16[2,2,2,16,1024]{4,3,2,1,0:T(8,128)(2,1)S(1)}, bf16[2,2,2,16,1024]{4,3,2,1,0:T(8,128)(2,1)S(1)}, u32[]{:S(2)}, u32[]{:S(2)}) collective-permute-start(bf16[2,2,2,16,1024]{4,3,2,1,0:T(8,128)(2,1)S(1)} %pad_maximum_fusion.5), channel_id=1, source_target_pairs={{0,4},{2,6},{4,0},{6,2},{8,12},{10,14},{12,8},{14,10},{16,20},{18,... | collective-permute-start | bytes 786440 | tf_op jit(solution)/shard_map/ppermute | solution.py:83
  90.7 14.1 %collective-permute-start.36 = (bf16[1,2,2,2,16,1024]{5,4,3,2,1,0:T(8,128)(2,1)S(1)}, bf16[1,2,2,2,16,1024]{5,4,3,2,1,0:T(8,128)(2,1)S(1)}, u32[]{:S(2)}, u32[]{:S(2)}) collective-permute-start(bf16[1,2,2,2,16,1024]{5,4,3,2,1,0:T(8,128)(2,1)S(1)} %maximum_bitcast_fusion.17), channel_id=1, source_target_pairs={{0,16},{2,18},{4,20},{6,22},{8,24},{10,26},{12,28},{14,30},{16,0},... | collective-permute-start | bytes 786440 | tf_op jit(solution)/shard_map/ppermute | solution.py:83
  100.2 8.1 %collective-permute-start.35 = (bf16[1,2,2,2,16,1024]{5,4,3,2,1,0:T(8,128)(2,1)S(1)}, bf16[1,2,2,2,16,1024]{5,4,3,2,1,0:T(8,128)(2,1)S(1)}, u32[]{:S(2)}, u32[]{:S(2)}) collective-permute-start(bf16[1,2,2,2,16,1024]{5,4,3,2,1,0:T(8,128)(2,1)S(1)} %maximum_bitcast_fusion.16), channel_id=1, source_target_pairs={{0,8},{2,10},{4,12},{6,14},{8,0},{10,2},{12,4},{14,6},{16,24},{18,... | collective-permute-start | bytes 786440 | tf_op jit(solution)/shard_map/ppermute | solution.py:83
  100.4 8.1 %collective-permute-start.34 = (bf16[1,2,2,2,16,1024]{5,4,3,2,1,0:T(8,128)(2,1)S(1)}, bf16[1,2,2,2,16,1024]{5,4,3,2,1,0:T(8,128)(2,1)S(1)}, u32[]{:S(2)}, u32[]{:S(2)}) collective-permute-start(bf16[1,2,2,2,16,1024]{5,4,3,2,1,0:T(8,128)(2,1)S(1)} %maximum_bitcast_fusion.15), channel_id=1, source_target_pairs={{0,4},{2,6},{4,0},{6,2},{8,12},{10,14},{12,8},{14,10},{16,20},{18,... | collective-permute-start | bytes 786440 | tf_op jit(solution)/shard_map/ppermute | solution.py:83
  102.5 8.0 %collective-permute-start.33 = (bf16[1,2,2,2,16,1024]{5,4,3,2,1,0:T(8,128)(2,1)S(1)}, bf16[1,2,2,2,16,1024]{5,4,3,2,1,0:T(8,128)(2,1)S(1)}, u32[]{:S(2)}, u32[]{:S(2)}) collective-permute-start(bf16[1,2,2,2,16,1024]{5,4,3,2,1,0:T(8,128)(2,1)S(1)} %maximum_bitcast_fusion.14), channel_id=1, source_target_pairs={{0,2},{2,0},{4,6},{6,4},{8,10},{10,8},{12,14},{14,12},{16,18},{18,... | collective-permute-start | bytes 786440 | tf_op jit(solution)/shard_map/ppermute | solution.py:83
  102.6 9.1 %collective-permute-start.7 = (bf16[1,2,2,2,16,1024]{5,4,3,2,1,0:T(8,128)(2,1)S(1)}, bf16[1,2,2,2,16,1024]{5,4,3,2,1,0:T(8,128)(2,1)S(1)}, u32[]{:S(2)}, u32[]{:S(2)}) collective-permute-start(bf16[1,2,2,2,16,1024]{5,4,3,2,1,0:T(8,128)(2,1)S(1)} %maximum_bitcast_fusion.10), channel_id=1, source_target_pairs={{0,2},{2,0},{4,6},{6,4},{8,10},{10,8},{12,14},{14,12},{16,18},{18,... | collective-permute-start | bytes 786440 | tf_op jit(solution)/shard_map/ppermute | solution.py:83
  104.8 21.2 %collective-permute-start.31 = (bf16[1,2,2,2,16,1024]{5,4,3,2,1,0:T(8,128)(2,1)S(1)}, bf16[1,2,2,2,16,1024]{5,4,3,2,1,0:T(8,128)(2,1)S(1)}, u32[]{:S(2)}, u32[]{:S(2)}) collective-permute-start(bf16[1,2,2,2,16,1024]{5,4,3,2,1,0:T(8,128)(2,1)S(1)} %maximum_bitcast_fusion.13), channel_id=1, source_target_pairs={{0,16},{2,18},{4,20},{6,22},{8,24},{10,26},{12,28},{14,30},{16,0},... | collective-permute-start | bytes 786440 | tf_op jit(solution)/shard_map/ppermute | solution.py:83
  108.4 17.8 %collective-permute-start.23 = (bf16[1,2,2,2,16,1024]{5,4,3,2,1,0:T(8,128)(2,1)S(1)}, bf16[1,2,2,2,16,1024]{5,4,3,2,1,0:T(8,128)(2,1)S(1)}, u32[]{:S(2)}, u32[]{:S(2)}) collective-permute-start(bf16[1,2,2,2,16,1024]{5,4,3,2,1,0:T(8,128)(2,1)S(1)} %maximum_bitcast_fusion.12), channel_id=1, source_target_pairs={{0,8},{2,10},{4,12},{6,14},{8,0},{10,2},{12,4},{14,6},{16,24},{18,... | collective-permute-start | bytes 786440 | tf_op jit(solution)/shard_map/ppermute | solution.py:83
  108.5 17.8 %collective-permute-start.15 = (bf16[1,2,2,2,16,1024]{5,4,3,2,1,0:T(8,128)(2,1)S(1)}, bf16[1,2,2,2,16,1024]{5,4,3,2,1,0:T(8,128)(2,1)S(1)}, u32[]{:S(2)}, u32[]{:S(2)}) collective-permute-start(bf16[1,2,2,2,16,1024]{5,4,3,2,1,0:T(8,128)(2,1)S(1)} %maximum_bitcast_fusion.11), channel_id=1, source_target_pairs={{0,4},{2,6},{4,0},{6,2},{8,12},{10,14},{12,8},{14,10},{16,20},{18,... | collective-permute-start | bytes 786440 | tf_op jit(solution)/shard_map/ppermute | solution.py:83
  (22 other events, 113.0 us)

commit v11 on v10

--- a/solution.py
+++ b/solution.py
@@ -78,7 +78,7 @@
     for s in reversed(range(nbits)):
         sends = {}
         for (p, r), buf in bufs.items():
-            sends.setdefault((r if s == 0 else 0, orders[p][s]), []).append(((p, r), buf))
+            sends.setdefault((r if s <= 1 else 0, orders[p][s]), []).append(((p, r), buf))
         for (_, mask), items in sorted(sends.items(), key=lambda kv: (kv[0][0], -kv[0][1])):
             got = lax.ppermute(jnp.stack([v for _, v in items]), axis, [(i, i ^ mask) for i in range(size)])
             bit = (place // mask) % 2

time: 158 us -> 160 us (1.013)
  starting transfers between devices: 52.3 us -> 55.6 us
    ppermute x36 -> x40, starting transfers between devices: 42.5 us -> 45.8 us  [spread_blocks(): lax.ppermute(jnp.stack([v for _, v in items]), axis, [(i, i ^ mask) for i...]
    ppermute x36 -> x40, waiting for transfers between devices: 38.8 us -> 38.5 us  [spread_blocks(): lax.ppermute(jnp.stack([v for _, v in items]), axis, [(i, i ^ mask) for i...]
    another operation x52 -> x48, other arithmetic: 4.2 us -> 4.07 us  [spread_blocks(): jnp.stack([v for _, v in items])]
  transfers between devices with their start and end apart: 45 -> 49, of which waited for: 21 -> 22; matrix products, arithmetic and copies ran while one was open for 18% -> 17% of each run, Pallas kernels for 7% -> 7%
where the time goes in v11:
time: 160 us
  starting transfers between devices  55.6 us (35%)
  waiting for transfers between devices  43.4 us (27%)
  Pallas kernels  23.6 us (15%)
  other arithmetic  17.9 us (11%)
  local copies, waits for them, and re-layouts  15.1 us (9%)
  between operations  2.63 us (2%)
    ppermute x40, starting transfers between devices, spread_blocks(): lax.ppermute(jnp.stack([v for _, v in items]), axis, [(i, i ^ mask) for i...  45.8 us
    ppermute x40, waiting for transfers between devices, spread_blocks(): lax.ppermute(jnp.stack([v for _, v in items]), axis, [(i, i ^ mask) for i...  38.5 us
    pallas_call x2, Pallas kernels, correlate(): pl.pallas_call(correlate_kernel, grid_spec=grid_spec, out_shape=[jax.Shap...  23.6 us
    ppermute x8, starting transfers between devices, group_sum(): got[d] = lax.ppermute(value, axis, pairs)  8.57 us
    select_n x18, other arithmetic, spread_blocks(): bufs[key] = jnp.where(holder, keeps[key], got[n])  5.69 us
    ppermute x8, waiting for transfers between devices, group_sum(): got[d] = lax.ppermute(value, axis, pairs)  4.87 us
    unnamed x20, local copies, waits for them, and re-layouts  4.36 us
    another operation x48, other arithmetic, spread_blocks(): jnp.stack([v for _, v in items])  4.07 us
  transfers between devices with their start and end apart: 49, of which 22 were waited for; matrix products, arithmetic and copies ran while one was open for 17% of the time, Pallas kernels for 7%

profile of v11, /device:TPU:0, one launch (start us, length us, event | category | flops | bytes accessed | tf_op | source)
XLA Modules:
  0.0 159.7 jit_solution(12210900759758337465)
XLA Ops:
  0.0 1.7 %slice.679 = bf16[1024,128]{1,0:T(8,128)(2,1)} slice(bf16[1024,1024]{1,0:T(8,128)(2,1)} %param.4), slice={[0:1024], [0:128]} | slice | bytes 524288 | tf_op jit(solution)/shard_map/slice | solution.py:181
  3.0 2.9 %copy.32 = bf16[1024,1024]{0,1:T(8,128)(2,1)S(1)} copy(bf16[1024,1024]{1,0:T(8,128)(2,1)} %param.4) | data formatting | bytes 4194304 | tf_op args[0]
  8.0 7.0 %collective-permute-start.24 = (bf16[2,2,2,2,16,1024]{5,4,3,2,1,0:T(8,128)(2,1)}, bf16[2,2,2,2,16,1024]{5,4,3,2,1,0:T(8,128)(2,1)}, u32[]{:S(2)}, u32[]{:S(2)}) collective-permute-start(bf16[2,2,2,2,16,1024]{5,4,3,2,1,0:T(8,128)(2,1)} %pad_maximum_fusion.3), channel_id=1, source_target_pairs={{0,16},{2,18},{4,20},{6,22},{8,24},{10,26},{12,28},{14,30},{16,0},... | collective-permute-start | bytes 1572872 | tf_op jit(solution)/shard_map/ppermute | solution.py:73
  15.9 1.6 collective-permute-start.16
  21.0 1.8 %fusion.29 = (bf16[1,2,2,2,16,1024]{5,4,0,1,2,3:T(8,128)(2,1)S(1)}, bf16[1,2,2,2,16,1024]{5,4,0,1,2,3:T(8,128)(2,1)S(1)}, bf16[1,2,2,2,16,1024]{5,4,0,1,2,3:T(8,128)(2,1)}) fusion(bf16[2,2,2,2,16,1024]{5,4,0,1,2,3:T(8,128)(2,1)} %bitcast.290, pred[]{:T(512)S(6)} %eq.174), kind=kLoop, calls=%fused_computation.299 | loop fusion | flops 131072 | bytes 1310721 | tf_op jit(solution)/shard_map/slice | solution.py:70
  32.5 6.3 %collective-permute-done.24 = bf16[2,2,2,2,16,1024]{5,4,3,2,1,0:T(8,128)(2,1)} collective-permute-done((bf16[2,2,2,2,16,1024]{5,4,3,2,1,0:T(8,128)(2,1)}, bf16[2,2,2,2,16,1024]{5,4,3,2,1,0:T(8,128)(2,1)}, u32[]{:S(2)}, u32[]{:S(2)}) %collective-permute-start.24) | collective-permute-done | bytes 524320 | tf_op jit(solution)/shard_map/ppermute | solution.py:73
  42.8 3.4 %collective-permute-start.9 = (bf16[2,2,2,16,1024]{4,3,2,1,0:T(8,128)(2,1)S(1)}, bf16[2,2,2,16,1024]{4,3,2,1,0:T(8,128)(2,1)S(1)}, u32[]{:S(2)}, u32[]{:S(2)}) collective-permute-start(bf16[2,2,2,16,1024]{4,3,2,1,0:T(8,128)(2,1)S(1)} %pad_maximum_fusion.6), channel_id=1, source_target_pairs={{0,8},{2,10},{4,12},{6,14},{8,0},{10,2},{12,4},{14,6},{16,24},{18,... | collective-permute-start | bytes 786440 | tf_op jit(solution)/shard_map/ppermute | solution.py:73
  50.6 5.0 %collective-permute-done.17 = bf16[2,2,2,16,1024]{4,3,2,1,0:T(8,128)(2,1)S(1)} collective-permute-done((bf16[2,2,2,16,1024]{4,3,2,1,0:T(8,128)(2,1)S(1)}, bf16[2,2,2,16,1024]{4,3,2,1,0:T(8,128)(2,1)S(1)}, u32[]{:S(2)}, u32[]{:S(2)}) %collective-permute-start.17) | collective-permute-done | bytes 262176 | tf_op jit(solution)/shard_map/ppermute | solution.py:73
  55.7 1.8 %collective-permute-start.18 = (bf16[2,2,16,1024]{3,2,1,0:T(8,128)(2,1)S(1)}, bf16[2,2,16,1024]{3,2,1,0:T(8,128)(2,1)S(1)}, u32[]{:S(2)}, u32[]{:S(2)}) collective-permute-start(bf16[2,2,16,1024]{3,2,1,0:T(8,128)(2,1)S(1)} %pad_maximum_fusion.23), channel_id=1, source_target_pairs={{0,2},{2,0},{4,6},{6,4},{8,10},{10,8},{12,14},{14,12},{16,18},{18,... | collective-permute-start | bytes 393224 | tf_op jit(solution)/shard_map/ppermute | solution.py:73
  57.9 2.4 %collective-permute-start.2 = (bf16[2,2,16,1024]{3,2,1,0:T(8,128)(2,1)S(1)}, bf16[2,2,16,1024]{3,2,1,0:T(8,128)(2,1)S(1)}, u32[]{:S(2)}, u32[]{:S(2)}) collective-permute-start(bf16[2,2,16,1024]{3,2,1,0:T(8,128)(2,1)S(1)} %pad_maximum_fusion.17), channel_id=1, source_target_pairs={{0,8},{2,10},{4,12},{6,14},{8,0},{10,2},{12,4},{14,6},{16,24},{18,... | collective-permute-start | bytes 393224 | tf_op jit(solution)/shard_map/ppermute | solution.py:73
  61.5 3.7 %collective-permute-done.10 = bf16[2,2,16,1024]{3,2,1,0:T(8,128)(2,1)S(1)} collective-permute-done((bf16[2,2,16,1024]{3,2,1,0:T(8,128)(2,1)S(1)}, bf16[2,2,16,1024]{3,2,1,0:T(8,128)(2,1)S(1)}, u32[]{:S(2)}, u32[]{:S(2)}) %collective-permute-start.10) | collective-permute-done | bytes 131104 | tf_op jit(solution)/shard_map/ppermute | solution.py:73
  67.1 2.1 %collective-permute-start.28 = (bf16[2,16,1024]{2,1,0:T(8,128)(2,1)S(1)}, bf16[2,16,1024]{2,1,0:T(8,128)(2,1)S(1)}, u32[]{:S(2)}, u32[]{:S(2)}) collective-permute-start(bf16[2,16,1024]{2,1,0:T(8,128)(2,1)S(1)} %pad_maximum_fusion.43), channel_id=1, source_target_pairs={{0,8},{2,10},{4,12},{6,14},{8,0},{10,2},{12,4},{14,6},{16,24},{18,... | collective-permute-start | bytes 196616 | tf_op jit(solution)/shard_map/ppermute | solution.py:83
  75.4 1.6 collective-permute-start.13
  76.9 2.4 %collective-permute-done.4 = bf16[2,16,1024]{2,1,0:T(8,128)(2,1)S(1)} collective-permute-done((bf16[2,16,1024]{2,1,0:T(8,128)(2,1)S(1)}, bf16[2,16,1024]{2,1,0:T(8,128)(2,1)S(1)}, u32[]{:S(2)}, u32[]{:S(2)}) %collective-permute-start.4) | collective-permute-done | bytes 65568 | tf_op jit(solution)/shard_map/ppermute | solution.py:83
  79.5 1.8 %collective-permute-start.39 = (bf16[1,2,2,16,1024]{4,3,2,1,0:T(8,128)(2,1)S(1)}, bf16[1,2,2,16,1024]{4,3,2,1,0:T(8,128)(2,1)S(1)}, u32[]{:S(2)}, u32[]{:S(2)}) collective-permute-start(bf16[1,2,2,16,1024]{4,3,2,1,0:T(8,128)(2,1)S(1)} %maximum_bitcast_fusion.25), channel_id=1, source_target_pairs={{0,2},{2,0},{4,6},{6,4},{8,10},{10,8},{12,14},{14,12},{16,18},{18,... | collective-permute-start | bytes 393224 | tf_op jit(solution)/shard_map/ppermute | solution.py:83
  81.3 2.1 %collective-permute-start.37 = (bf16[1,2,2,16,1024]{4,3,2,1,0:T(8,128)(2,1)S(1)}, bf16[1,2,2,16,1024]{4,3,2,1,0:T(8,128)(2,1)S(1)}, u32[]{:S(2)}, u32[]{:S(2)}) collective-permute-start(bf16[1,2,2,16,1024]{4,3,2,1,0:T(8,128)(2,1)S(1)} %maximum_bitcast_fusion.24), channel_id=1, source_target_pairs={{0,16},{2,18},{4,20},{6,22},{8,24},{10,26},{12,28},{14,30},{16,0},... | collective-permute-start | bytes 393224 | tf_op jit(solution)/shard_map/ppermute | solution.py:83
  83.5 1.6 collective-permute-done.13
  85.1 3.1 %collective-permute-done.5 = bf16[2,2,16,1024]{3,2,1,0:T(8,128)(2,1)S(1)} collective-permute-done((bf16[2,2,16,1024]{3,2,1,0:T(8,128)(2,1)S(1)}, bf16[2,2,16,1024]{3,2,1,0:T(8,128)(2,1)S(1)}, u32[]{:S(2)}, u32[]{:S(2)}) %collective-permute-start.5) | collective-permute-done | bytes 131104 | tf_op jit(solution)/shard_map/ppermute | solution.py:83
  88.3 1.5 collective-permute-start.33
  91.8 1.9 %collective-permute-done.35 = bf16[1,2,2,16,1024]{4,3,2,1,0:T(8,128)(2,1)S(1)} collective-permute-done((bf16[1,2,2,16,1024]{4,3,2,1,0:T(8,128)(2,1)S(1)}, bf16[1,2,2,16,1024]{4,3,2,1,0:T(8,128)(2,1)S(1)}, u32[]{:S(2)}, u32[]{:S(2)}) %collective-permute-start.35) | collective-permute-done | bytes 131104 | tf_op jit(solution)/shard_map/ppermute | solution.py:83
  95.7 2.2 %collective-permute-start.38 = (bf16[1,2,2,2,16,1024]{5,4,3,2,1,0:T(8,128)(2,1)S(1)}, bf16[1,2,2,2,16,1024]{5,4,3,2,1,0:T(8,128)(2,1)S(1)}, u32[]{:S(2)}, u32[]{:S(2)}) collective-permute-start(bf16[1,2,2,2,16,1024]{5,4,3,2,1,0:T(8,128)(2,1)S(1)} %maximum_bitcast_fusion.16), channel_id=1, source_target_pairs={{0,8},{2,10},{4,12},{6,14},{8,0},{10,2},{12,4},{14,6},{16,24},{18,... | collective-permute-start | bytes 786440 | tf_op jit(solution)/shard_map/ppermute | solution.py:83
  98.6 1.9 %collective-permute-done.22 = bf16[1,2,2,16,1024]{4,3,2,1,0:T(8,128)(2,1)S(1)} collective-permute-done((bf16[1,2,2,16,1024]{4,3,2,1,0:T(8,128)(2,1)S(1)}, bf16[1,2,2,16,1024]{4,3,2,1,0:T(8,128)(2,1)S(1)}, u32[]{:S(2)}, u32[]{:S(2)}) %collective-permute-start.22) | collective-permute-done | bytes 131104 | tf_op jit(solution)/shard_map/ppermute | solution.py:83
  100.6 2.2 %collective-permute-done.14 = bf16[1,2,2,16,1024]{4,3,2,1,0:T(8,128)(2,1)S(1)} collective-permute-done((bf16[1,2,2,16,1024]{4,3,2,1,0:T(8,128)(2,1)S(1)}, bf16[1,2,2,16,1024]{4,3,2,1,0:T(8,128)(2,1)S(1)}, u32[]{:S(2)}, u32[]{:S(2)}) %collective-permute-start.14) | collective-permute-done | bytes 131104 | tf_op jit(solution)/shard_map/ppermute | solution.py:83
  103.6 7.3 %collective-permute-done.40 = bf16[1,2,2,2,16,1024]{5,4,3,2,1,0:T(8,128)(2,1)S(1)} collective-permute-done((bf16[1,2,2,2,16,1024]{5,4,3,2,1,0:T(8,128)(2,1)S(1)}, bf16[1,2,2,2,16,1024]{5,4,3,2,1,0:T(8,128)(2,1)S(1)}, u32[]{:S(2)}, u32[]{:S(2)}) %collective-permute-start.40) | collective-permute-done | bytes 262176 | tf_op jit(solution)/shard_map/ppermute | solution.py:83
  111.0 2.9 %collective-permute-start.23 = (bf16[1,2,2,2,16,1024]{5,4,3,2,1,0:T(8,128)(2,1)S(1)}, bf16[1,2,2,2,16,1024]{5,4,3,2,1,0:T(8,128)(2,1)S(1)}, u32[]{:S(2)}, u32[]{:S(2)}) collective-permute-start(bf16[1,2,2,2,16,1024]{5,4,3,2,1,0:T(8,128)(2,1)S(1)} %maximum_bitcast_fusion.12), channel_id=1, source_target_pairs={{0,8},{2,10},{4,12},{6,14},{8,0},{10,2},{12,4},{14,6},{16,24},{18,... | collective-permute-start | bytes 786440 | tf_op jit(solution)/shard_map/ppermute | solution.py:83
  114.9 1.5 maximum_bitcast_fusion.1.blk_ref
  116.4 11.7 %shard_map.47 = (f32[4,4,1024]{2,1,0:T(4,128)}, f32[4,4,128]{2,1,0:T(4,128)}) custom-call(s32[64]{0:T(128)} %squeeze.19.meta_ref, bf16[1,1024,1024]{2,1,0:T(8,128)(2,1)} %maximum_bitcast_fusion.1.blk_ref, bf16[1024,1152]{1,0:T(8,128)(2,1)} %copy-done.3), custom_call_target="tpu_custom_call" | custom-call | flops 5435817984 | bytes 4521984 | tf_op jit(solution)/shard_map/pallas_call | solution.py:154
  129.6 1.5 maximum_bitcast_fusion.blk_ref
  131.1 11.9 %shard_map.46 = (f32[4,4,1024]{2,1,0:T(4,128)}, f32[4,4,128]{2,1,0:T(4,128)}) custom-call(s32[64]{0:T(128)} %squeeze.16.meta_ref, bf16[1,1024,1024]{2,1,0:T(8,128)(2,1)} %maximum_bitcast_fusion.blk_ref, bf16[1024,1152]{1,0:T(8,128)(2,1)} %copy-done.3), custom_call_target="tpu_custom_call" | custom-call | flops 5435817984 | bytes 4521984 | tf_op jit(solution)/shard_map/pallas_call | solution.py:154
  147.9 1.4 collective-permute-start.44
  152.9 1.6 collective-permute-start.46
  154.4 2.9 %collective-permute-start.48 = (f32[32]{0:T(128)S(1)}, f32[32]{0:T(128)S(1)}, u32[]{:S(2)}, u32[]{:S(2)}) collective-permute-start(f32[32]{0:T(128)S(1)} %fusion.27), channel_id=1, source_target_pairs={{0,8},{2,10},{4,12},{6,14},{8,0},{10,2},{12,4},{14,6},{16,24},{18,... | collective-permute-start | bytes 392 | tf_op jit(solution)/shard_map/ppermute | solution.py:33
  (268 shorter events, 52.6 us)
Async XLA Ops:
  1.7 27.0 %collective-permute-start.32 = (bf16[1024,128]{1,0:T(8,128)(2,1)}, bf16[1024,128]{1,0:T(8,128)(2,1)}, u32[]{:S(2)}, u32[]{:S(2)}) collective-permute-start(bf16[1024,128]{1,0:T(8,128)(2,1)} %slice.679), channel_id=1, source_target_pairs={{2,0},{4,2},{6,4},{8,6},{10,8},{12,10},{14,12},{16,14},{18,16},{20... | collective-permute-start | bytes 786440 | tf_op jit(solution)/shard_map/ppermute | solution.py:18
  8.0 30.8 %collective-permute-start.24 = (bf16[2,2,2,2,16,1024]{5,4,3,2,1,0:T(8,128)(2,1)}, bf16[2,2,2,2,16,1024]{5,4,3,2,1,0:T(8,128)(2,1)}, u32[]{:S(2)}, u32[]{:S(2)}) collective-permute-start(bf16[2,2,2,2,16,1024]{5,4,3,2,1,0:T(8,128)(2,1)} %pad_maximum_fusion.3), channel_id=1, source_target_pairs={{0,16},{2,18},{4,20},{6,22},{8,24},{10,26},{12,28},{14,30},{16,0},... | collective-permute-start | bytes 1572872 | tf_op jit(solution)/shard_map/ppermute | solution.py:73
  15.9 24.2 %collective-permute-start.16 = (bf16[2,2,2,2,16,1024]{5,4,3,2,1,0:T(8,128)(2,1)}, bf16[2,2,2,2,16,1024]{5,4,3,2,1,0:T(8,128)(2,1)}, u32[]{:S(2)}, u32[]{:S(2)}) collective-permute-start(bf16[2,2,2,2,16,1024]{5,4,3,2,1,0:T(8,128)(2,1)} %pad_maximum_fusion.2), channel_id=1, source_target_pairs={{0,8},{2,10},{4,12},{6,14},{8,0},{10,2},{12,4},{14,6},{16,24},{18,... | collective-permute-start | bytes 1572872 | tf_op jit(solution)/shard_map/ppermute | solution.py:73
  20.4 21.2 %collective-permute-start.8 = (bf16[2,2,2,2,16,1024]{5,4,3,2,1,0:T(8,128)(2,1)}, bf16[2,2,2,2,16,1024]{5,4,3,2,1,0:T(8,128)(2,1)}, u32[]{:S(2)}, u32[]{:S(2)}) collective-permute-start(bf16[2,2,2,2,16,1024]{5,4,3,2,1,0:T(8,128)(2,1)} %pad_maximum_fusion.1), channel_id=1, source_target_pairs={{0,4},{2,6},{4,0},{6,2},{8,12},{10,14},{12,8},{14,10},{16,20},{18,... | collective-permute-start | bytes 1572872 | tf_op jit(solution)/shard_map/ppermute | solution.py:73
  23.7 22.5 %collective-permute-start = (bf16[2,2,2,2,16,1024]{5,4,0,1,2,3:T(8,128)(2,1)}, bf16[2,2,2,2,16,1024]{5,4,0,1,2,3:T(8,128)(2,1)}, u32[]{:S(2)}, u32[]{:S(2)}) collective-permute-start(bf16[2,2,2,2,16,1024]{5,4,0,1,2,3:T(8,128)(2,1)} %pad_maximum_fusion), channel_id=1, source_target_pairs={{0,2},{2,0},{4,6},{6,4},{8,10},{10,8},{12,14},{14,12},{16,18},{18,... | collective-permute-start | bytes 1572872 | tf_op jit(solution)/shard_map/ppermute | solution.py:73
  40.0 9.6 %collective-permute-start.25 = (bf16[2,2,2,16,1024]{4,3,2,1,0:T(8,128)(2,1)S(1)}, bf16[2,2,2,16,1024]{4,3,2,1,0:T(8,128)(2,1)S(1)}, u32[]{:S(2)}, u32[]{:S(2)}) collective-permute-start(bf16[2,2,2,16,1024]{4,3,2,1,0:T(8,128)(2,1)S(1)} %pad_maximum_fusion.10), channel_id=1, source_target_pairs={{0,2},{2,0},{4,6},{6,4},{8,10},{10,8},{12,14},{14,12},{16,18},{18,... | collective-permute-start | bytes 786440 | tf_op jit(solution)/shard_map/ppermute | solution.py:73
  41.3 14.4 %collective-permute-start.17 = (bf16[2,2,2,16,1024]{4,3,2,1,0:T(8,128)(2,1)S(1)}, bf16[2,2,2,16,1024]{4,3,2,1,0:T(8,128)(2,1)S(1)}, u32[]{:S(2)}, u32[]{:S(2)}) collective-permute-start(bf16[2,2,2,16,1024]{4,3,2,1,0:T(8,128)(2,1)S(1)} %pad_maximum_fusion.8), channel_id=1, source_target_pairs={{0,16},{2,18},{4,20},{6,22},{8,24},{10,26},{12,28},{14,30},{16,0},... | collective-permute-start | bytes 786440 | tf_op jit(solution)/shard_map/ppermute | solution.py:73
  42.8 14.7 %collective-permute-start.9 = (bf16[2,2,2,16,1024]{4,3,2,1,0:T(8,128)(2,1)S(1)}, bf16[2,2,2,16,1024]{4,3,2,1,0:T(8,128)(2,1)S(1)}, u32[]{:S(2)}, u32[]{:S(2)}) collective-permute-start(bf16[2,2,2,16,1024]{4,3,2,1,0:T(8,128)(2,1)S(1)} %pad_maximum_fusion.6), channel_id=1, source_target_pairs={{0,8},{2,10},{4,12},{6,14},{8,0},{10,2},{12,4},{14,6},{16,24},{18,... | collective-permute-start | bytes 786440 | tf_op jit(solution)/shard_map/ppermute | solution.py:73
  48.4 9.4 %collective-permute-start.1 = (bf16[2,2,2,16,1024]{4,3,2,1,0:T(8,128)(2,1)S(1)}, bf16[2,2,2,16,1024]{4,3,2,1,0:T(8,128)(2,1)S(1)}, u32[]{:S(2)}, u32[]{:S(2)}) collective-permute-start(bf16[2,2,2,16,1024]{4,3,2,1,0:T(8,128)(2,1)S(1)} %pad_maximum_fusion.4), channel_id=1, source_target_pairs={{0,4},{2,6},{4,0},{6,2},{8,12},{10,14},{12,8},{14,10},{16,20},{18,... | collective-permute-start | bytes 786440 | tf_op jit(solution)/shard_map/ppermute | solution.py:73
  49.7 10.6 %collective-permute-start.26 = (bf16[2,2,16,1024]{3,2,1,0:T(8,128)(2,1)S(1)}, bf16[2,2,16,1024]{3,2,1,0:T(8,128)(2,1)S(1)}, u32[]{:S(2)}, u32[]{:S(2)}) collective-permute-start(bf16[2,2,16,1024]{3,2,1,0:T(8,128)(2,1)S(1)} %pad_maximum_fusion.26), channel_id=1, source_target_pairs={{0,4},{2,6},{4,0},{6,2},{8,12},{10,14},{12,8},{14,10},{16,20},{18,... | collective-permute-start | bytes 393224 | tf_op jit(solution)/shard_map/ppermute | solution.py:73
  57.6 7.6 %collective-permute-start.10 = (bf16[2,2,16,1024]{3,2,1,0:T(8,128)(2,1)S(1)}, bf16[2,2,16,1024]{3,2,1,0:T(8,128)(2,1)S(1)}, u32[]{:S(2)}, u32[]{:S(2)}) collective-permute-start(bf16[2,2,16,1024]{3,2,1,0:T(8,128)(2,1)S(1)} %pad_maximum_fusion.20), channel_id=1, source_target_pairs={{0,16},{2,18},{4,20},{6,22},{8,24},{10,26},{12,28},{14,30},{16,0},... | collective-permute-start | bytes 393224 | tf_op jit(solution)/shard_map/ppermute | solution.py:73
  57.9 8.5 %collective-permute-start.2 = (bf16[2,2,16,1024]{3,2,1,0:T(8,128)(2,1)S(1)}, bf16[2,2,16,1024]{3,2,1,0:T(8,128)(2,1)S(1)}, u32[]{:S(2)}, u32[]{:S(2)}) collective-permute-start(bf16[2,2,16,1024]{3,2,1,0:T(8,128)(2,1)S(1)} %pad_maximum_fusion.17), channel_id=1, source_target_pairs={{0,8},{2,10},{4,12},{6,14},{8,0},{10,2},{12,4},{14,6},{16,24},{18,... | collective-permute-start | bytes 393224 | tf_op jit(solution)/shard_map/ppermute | solution.py:73
  60.8 8.4 %collective-permute-start.19 = (bf16[2,16,1024]{2,1,0:T(8,128)(2,1)S(1)}, bf16[2,16,1024]{2,1,0:T(8,128)(2,1)S(1)}, u32[]{:S(2)}, u32[]{:S(2)}) collective-permute-start(bf16[2,16,1024]{2,1,0:T(8,128)(2,1)S(1)} %pad_maximum_fusion.39), channel_id=1, source_target_pairs={{0,4},{2,6},{4,0},{6,2},{8,12},{10,14},{12,8},{14,10},{16,20},{18,... | collective-permute-start | bytes 196616 | tf_op jit(solution)/shard_map/ppermute | solution.py:73
  72.0 7.3 %collective-permute-start.4 = (bf16[2,16,1024]{2,1,0:T(8,128)(2,1)S(1)}, bf16[2,16,1024]{2,1,0:T(8,128)(2,1)S(1)}, u32[]{:S(2)}, u32[]{:S(2)}) collective-permute-start(bf16[2,16,1024]{2,1,0:T(8,128)(2,1)S(1)} %pad_maximum_fusion.34), channel_id=1, source_target_pairs={{0,16},{2,18},{4,20},{6,22},{8,24},{10,26},{12,28},{14,30},{16,0},... | collective-permute-start | bytes 196616 | tf_op jit(solution)/shard_map/ppermute | solution.py:83
  72.4 7.0 %collective-permute-start.29 = (bf16[2,2,16,1024]{3,2,1,0:T(8,128)(2,1)S(1)}, bf16[2,2,16,1024]{3,2,1,0:T(8,128)(2,1)S(1)}, u32[]{:S(2)}, u32[]{:S(2)}) collective-permute-start(bf16[2,2,16,1024]{3,2,1,0:T(8,128)(2,1)S(1)} %pad_maximum_fusion.27), channel_id=1, source_target_pairs={{0,4},{2,6},{4,0},{6,2},{8,12},{10,14},{12,8},{14,10},{16,20},{18,... | collective-permute-start | bytes 393224 | tf_op jit(solution)/shard_map/ppermute | solution.py:83
  74.3 7.0 %collective-permute-start.21 = (bf16[2,2,16,1024]{3,2,1,0:T(8,128)(2,1)S(1)}, bf16[2,2,16,1024]{3,2,1,0:T(8,128)(2,1)S(1)}, u32[]{:S(2)}, u32[]{:S(2)}) collective-permute-start(bf16[2,2,16,1024]{3,2,1,0:T(8,128)(2,1)S(1)} %pad_maximum_fusion.24), channel_id=1, source_target_pairs={{0,2},{2,0},{4,6},{6,4},{8,10},{10,8},{12,14},{14,12},{16,18},{18,... | collective-permute-start | bytes 393224 | tf_op jit(solution)/shard_map/ppermute | solution.py:83
  75.4 9.7 %collective-permute-start.13 = (bf16[2,2,16,1024]{3,2,1,0:T(8,128)(2,1)S(1)}, bf16[2,2,16,1024]{3,2,1,0:T(8,128)(2,1)S(1)}, u32[]{:S(2)}, u32[]{:S(2)}) collective-permute-start(bf16[2,2,16,1024]{3,2,1,0:T(8,128)(2,1)S(1)} %pad_maximum_fusion.21), channel_id=1, source_target_pairs={{0,16},{2,18},{4,20},{6,22},{8,24},{10,26},{12,28},{14,30},{16,0},... | collective-permute-start | bytes 393224 | tf_op jit(solution)/shard_map/ppermute | solution.py:83
  79.4 8.8 %collective-permute-start.5 = (bf16[2,2,16,1024]{3,2,1,0:T(8,128)(2,1)S(1)}, bf16[2,2,16,1024]{3,2,1,0:T(8,128)(2,1)S(1)}, u32[]{:S(2)}, u32[]{:S(2)}) collective-permute-start(bf16[2,2,16,1024]{3,2,1,0:T(8,128)(2,1)S(1)} %pad_maximum_fusion.18), channel_id=1, source_target_pairs={{0,8},{2,10},{4,12},{6,14},{8,0},{10,2},{12,4},{14,6},{16,24},{18,... | collective-permute-start | bytes 393224 | tf_op jit(solution)/shard_map/ppermute | solution.py:83
  79.5 11.0 %collective-permute-start.39 = (bf16[1,2,2,16,1024]{4,3,2,1,0:T(8,128)(2,1)S(1)}, bf16[1,2,2,16,1024]{4,3,2,1,0:T(8,128)(2,1)S(1)}, u32[]{:S(2)}, u32[]{:S(2)}) collective-permute-start(bf16[1,2,2,16,1024]{4,3,2,1,0:T(8,128)(2,1)S(1)} %maximum_bitcast_fusion.25), channel_id=1, source_target_pairs={{0,2},{2,0},{4,6},{6,4},{8,10},{10,8},{12,14},{14,12},{16,18},{18,... | collective-permute-start | bytes 393224 | tf_op jit(solution)/shard_map/ppermute | solution.py:83
  81.3 10.3 %collective-permute-start.37 = (bf16[1,2,2,16,1024]{4,3,2,1,0:T(8,128)(2,1)S(1)}, bf16[1,2,2,16,1024]{4,3,2,1,0:T(8,128)(2,1)S(1)}, u32[]{:S(2)}, u32[]{:S(2)}) collective-permute-start(bf16[1,2,2,16,1024]{4,3,2,1,0:T(8,128)(2,1)S(1)} %maximum_bitcast_fusion.24), channel_id=1, source_target_pairs={{0,16},{2,18},{4,20},{6,22},{8,24},{10,26},{12,28},{14,30},{16,0},... | collective-permute-start | bytes 393224 | tf_op jit(solution)/shard_map/ppermute | solution.py:83
  85.1 8.7 %collective-permute-start.35 = (bf16[1,2,2,16,1024]{4,3,2,1,0:T(8,128)(2,1)S(1)}, bf16[1,2,2,16,1024]{4,3,2,1,0:T(8,128)(2,1)S(1)}, u32[]{:S(2)}, u32[]{:S(2)}) collective-permute-start(bf16[1,2,2,16,1024]{4,3,2,1,0:T(8,128)(2,1)S(1)} %maximum_bitcast_fusion.23), channel_id=1, source_target_pairs={{0,8},{2,10},{4,12},{6,14},{8,0},{10,2},{12,4},{14,6},{16,24},{18,... | collective-permute-start | bytes 393224 | tf_op jit(solution)/shard_map/ppermute | solution.py:83
  90.5 7.5 %collective-permute-start.30 = (bf16[1,2,2,16,1024]{4,3,2,1,0:T(8,128)(2,1)S(1)}, bf16[1,2,2,16,1024]{4,3,2,1,0:T(8,128)(2,1)S(1)}, u32[]{:S(2)}, u32[]{:S(2)}) collective-permute-start(bf16[1,2,2,16,1024]{4,3,2,1,0:T(8,128)(2,1)S(1)} %maximum_bitcast_fusion.21), channel_id=1, source_target_pairs={{0,2},{2,0},{4,6},{6,4},{8,10},{10,8},{12,14},{14,12},{16,18},{18,... | collective-permute-start | bytes 393224 | tf_op jit(solution)/shard_map/ppermute | solution.py:83
  91.6 8.9 %collective-permute-start.22 = (bf16[1,2,2,16,1024]{4,3,2,1,0:T(8,128)(2,1)S(1)}, bf16[1,2,2,16,1024]{4,3,2,1,0:T(8,128)(2,1)S(1)}, u32[]{:S(2)}, u32[]{:S(2)}) collective-permute-start(bf16[1,2,2,16,1024]{4,3,2,1,0:T(8,128)(2,1)S(1)} %maximum_bitcast_fusion.20), channel_id=1, source_target_pairs={{0,16},{2,18},{4,20},{6,22},{8,24},{10,26},{12,28},{14,30},{16,0},... | collective-permute-start | bytes 393224 | tf_op jit(solution)/shard_map/ppermute | solution.py:83
  93.8 9.0 %collective-permute-start.14 = (bf16[1,2,2,16,1024]{4,3,2,1,0:T(8,128)(2,1)S(1)}, bf16[1,2,2,16,1024]{4,3,2,1,0:T(8,128)(2,1)S(1)}, u32[]{:S(2)}, u32[]{:S(2)}) collective-permute-start(bf16[1,2,2,16,1024]{4,3,2,1,0:T(8,128)(2,1)S(1)} %maximum_bitcast_fusion.19), channel_id=1, source_target_pairs={{0,8},{2,10},{4,12},{6,14},{8,0},{10,2},{12,4},{14,6},{16,24},{18,... | collective-permute-start | bytes 393224 | tf_op jit(solution)/shard_map/ppermute | solution.py:83
  94.5 16.4 %collective-permute-start.40 = (bf16[1,2,2,2,16,1024]{5,4,3,2,1,0:T(8,128)(2,1)S(1)}, bf16[1,2,2,2,16,1024]{5,4,3,2,1,0:T(8,128)(2,1)S(1)}, u32[]{:S(2)}, u32[]{:S(2)}) collective-permute-start(bf16[1,2,2,2,16,1024]{5,4,3,2,1,0:T(8,128)(2,1)S(1)} %maximum_bitcast_fusion.17), channel_id=1, source_target_pairs={{0,16},{2,18},{4,20},{6,22},{8,24},{10,26},{12,28},{14,30},{16,0},... | collective-permute-start | bytes 786440 | tf_op jit(solution)/shard_map/ppermute | solution.py:83
  95.7 15.3 %collective-permute-start.38 = (bf16[1,2,2,2,16,1024]{5,4,3,2,1,0:T(8,128)(2,1)S(1)}, bf16[1,2,2,2,16,1024]{5,4,3,2,1,0:T(8,128)(2,1)S(1)}, u32[]{:S(2)}, u32[]{:S(2)}) collective-permute-start(bf16[1,2,2,2,16,1024]{5,4,3,2,1,0:T(8,128)(2,1)S(1)} %maximum_bitcast_fusion.16), channel_id=1, source_target_pairs={{0,8},{2,10},{4,12},{6,14},{8,0},{10,2},{12,4},{14,6},{16,24},{18,... | collective-permute-start | bytes 786440 | tf_op jit(solution)/shard_map/ppermute | solution.py:83
  98.0 16.1 %collective-permute-start.36 = (bf16[1,2,2,2,16,1024]{5,4,3,2,1,0:T(8,128)(2,1)S(1)}, bf16[1,2,2,2,16,1024]{5,4,3,2,1,0:T(8,128)(2,1)S(1)}, u32[]{:S(2)}, u32[]{:S(2)}) collective-permute-start(bf16[1,2,2,2,16,1024]{5,4,3,2,1,0:T(8,128)(2,1)S(1)} %maximum_bitcast_fusion.15), channel_id=1, source_target_pairs={{0,4},{2,6},{4,0},{6,2},{8,12},{10,14},{12,8},{14,10},{16,20},{18,... | collective-permute-start | bytes 786440 | tf_op jit(solution)/shard_map/ppermute | solution.py:83
  100.5 14.2 %collective-permute-start.34 = (bf16[1,2,2,2,16,1024]{5,4,3,2,1,0:T(8,128)(2,1)S(1)}, bf16[1,2,2,2,16,1024]{5,4,3,2,1,0:T(8,128)(2,1)S(1)}, u32[]{:S(2)}, u32[]{:S(2)}) collective-permute-start(bf16[1,2,2,2,16,1024]{5,4,3,2,1,0:T(8,128)(2,1)S(1)} %maximum_bitcast_fusion.14), channel_id=1, source_target_pairs={{0,2},{2,0},{4,6},{6,4},{8,10},{10,8},{12,14},{14,12},{16,18},{18,... | collective-permute-start | bytes 786440 | tf_op jit(solution)/shard_map/ppermute | solution.py:83
  102.7 11.9 %collective-permute-start.7 = (bf16[1,2,2,2,16,1024]{5,4,3,2,1,0:T(8,128)(2,1)S(1)}, bf16[1,2,2,2,16,1024]{5,4,3,2,1,0:T(8,128)(2,1)S(1)}, u32[]{:S(2)}, u32[]{:S(2)}) collective-permute-start(bf16[1,2,2,2,16,1024]{5,4,3,2,1,0:T(8,128)(2,1)S(1)} %maximum_bitcast_fusion.10), channel_id=1, source_target_pairs={{0,2},{2,0},{4,6},{6,4},{8,10},{10,8},{12,14},{14,12},{16,18},{18,... | collective-permute-start | bytes 786440 | tf_op jit(solution)/shard_map/ppermute | solution.py:83
  110.8 18.1 %collective-permute-start.31 = (bf16[1,2,2,2,16,1024]{5,4,3,2,1,0:T(8,128)(2,1)S(1)}, bf16[1,2,2,2,16,1024]{5,4,3,2,1,0:T(8,128)(2,1)S(1)}, u32[]{:S(2)}, u32[]{:S(2)}) collective-permute-start(bf16[1,2,2,2,16,1024]{5,4,3,2,1,0:T(8,128)(2,1)S(1)} %maximum_bitcast_fusion.13), channel_id=1, source_target_pairs={{0,16},{2,18},{4,20},{6,22},{8,24},{10,26},{12,28},{14,30},{16,0},... | collective-permute-start | bytes 786440 | tf_op jit(solution)/shard_map/ppermute | solution.py:83
  111.0 18.1 %collective-permute-start.23 = (bf16[1,2,2,2,16,1024]{5,4,3,2,1,0:T(8,128)(2,1)S(1)}, bf16[1,2,2,2,16,1024]{5,4,3,2,1,0:T(8,128)(2,1)S(1)}, u32[]{:S(2)}, u32[]{:S(2)}) collective-permute-start(bf16[1,2,2,2,16,1024]{5,4,3,2,1,0:T(8,128)(2,1)S(1)} %maximum_bitcast_fusion.12), channel_id=1, source_target_pairs={{0,8},{2,10},{4,12},{6,14},{8,0},{10,2},{12,4},{14,6},{16,24},{18,... | collective-permute-start | bytes 786440 | tf_op jit(solution)/shard_map/ppermute | solution.py:83
  114.1 15.2 %collective-permute-start.15 = (bf16[1,2,2,2,16,1024]{5,4,3,2,1,0:T(8,128)(2,1)S(1)}, bf16[1,2,2,2,16,1024]{5,4,3,2,1,0:T(8,128)(2,1)S(1)}, u32[]{:S(2)}, u32[]{:S(2)}) collective-permute-start(bf16[1,2,2,2,16,1024]{5,4,3,2,1,0:T(8,128)(2,1)S(1)} %maximum_bitcast_fusion.11), channel_id=1, source_target_pairs={{0,4},{2,6},{4,0},{6,2},{8,12},{10,14},{12,8},{14,10},{16,20},{18,... | collective-permute-start | bytes 786440 | tf_op jit(solution)/shard_map/ppermute | solution.py:83
  (26 other events, 138.5 us)

commit v12 on v10

--- a/solution.py
+++ b/solution.py
@@ -23,7 +23,7 @@
     place = lax.axis_index(axis)
     stride = 1
     while stride < size:
-        fan = 4 if size % (stride * 4) == 0 else 2 if size % (stride * 2) == 0 else 0
+        fan = 4 if stride == 1 and size % 4 == 0 else 2 if size % (stride * 2) == 0 else 0
         if fan == 0:
             return lax.psum(value, axis)
         member = (place // stride) % fan

time: 158 us -> 159 us (level)
    ppermute x8 -> x7, waiting for transfers between devices: 5.15 us -> 6.37 us  [group_sum(): got[d] = lax.ppermute(value, axis, pairs)]
    ppermute x8 -> x7, starting transfers between devices: 8.57 us -> 8.2 us  [group_sum(): got[d] = lax.ppermute(value, axis, pairs)]
  transfers between devices with their start and end apart: 45 -> 44, of which waited for: 21 -> 20; matrix products, arithmetic and copies ran while one was open for 18% -> 18% of each run, Pallas kernels for 7% -> 7%
where the time goes in v12:
time: 159 us; the launch traced here: 158 us
  starting transfers between devices  51.9 us (33%)
  waiting for transfers between devices  45.1 us (28%)
  Pallas kernels  23.6 us (15%)
  other arithmetic  18 us (11%)
  local copies, waits for them, and re-layouts  15.1 us (9%)
  between operations  2.7 us (2%)
    ppermute x36, starting transfers between devices, spread_blocks(): lax.ppermute(jnp.stack([v for _, v in items]), axis, [(i, i ^ mask) for i...  42.4 us
    ppermute x36, waiting for transfers between devices, spread_blocks(): lax.ppermute(jnp.stack([v for _, v in items]), axis, [(i, i ^ mask) for i...  38.7 us
    pallas_call x2, Pallas kernels, correlate(): pl.pallas_call(correlate_kernel, grid_spec=grid_spec, out_shape=[jax.Shap...  23.6 us
    ppermute x7, starting transfers between devices, group_sum(): got[d] = lax.ppermute(value, axis, pairs)  8.2 us
    ppermute x7, waiting for transfers between devices, group_sum(): got[d] = lax.ppermute(value, axis, pairs)  6.37 us
    select_n x18, other arithmetic, spread_blocks(): bufs[key] = jnp.where(holder, keeps[key], got[n])  5.69 us
    unnamed x20, local copies, waits for them, and re-layouts  4.38 us
    another operation x52, other arithmetic, spread_blocks(): jnp.stack([v for _, v in items])  4.18 us
  transfers between devices with their start and end apart: 44, of which 20 were waited for; matrix products, arithmetic and copies ran while one was open for 18% of the time, Pallas kernels for 7%

profile of v12, /device:TPU:0, one launch (start us, length us, event | category | flops | bytes accessed | tf_op | source)
XLA Modules:
  0.0 157.9 jit_solution(3677610433462604428)
XLA Ops:
  0.0 1.7 %slice.719 = bf16[1024,128]{1,0:T(8,128)(2,1)} slice(bf16[1024,1024]{1,0:T(8,128)(2,1)} %param.4), slice={[0:1024], [0:128]} | slice | bytes 524288 | tf_op jit(solution)/shard_map/slice | solution.py:181
  3.0 2.9 %copy.32 = bf16[1024,1024]{0,1:T(8,128)(2,1)S(1)} copy(bf16[1024,1024]{1,0:T(8,128)(2,1)} %param.4) | data formatting | bytes 4194304 | tf_op args[0]
  8.0 7.0 %collective-permute-start.24 = (bf16[2,2,2,2,16,1024]{5,4,3,2,1,0:T(8,128)(2,1)}, bf16[2,2,2,2,16,1024]{5,4,3,2,1,0:T(8,128)(2,1)}, u32[]{:S(2)}, u32[]{:S(2)}) collective-permute-start(bf16[2,2,2,2,16,1024]{5,4,3,2,1,0:T(8,128)(2,1)} %pad_maximum_fusion.3), channel_id=1, source_target_pairs={{0,16},{2,18},{4,20},{6,22},{8,24},{10,26},{12,28},{14,30},{16,0},... | collective-permute-start | bytes 1572872 | tf_op jit(solution)/shard_map/ppermute | solution.py:73
  15.9 1.6 collective-permute-start.16
  21.0 1.8 %fusion.29 = (bf16[1,2,2,2,16,1024]{5,4,0,1,2,3:T(8,128)(2,1)S(1)}, bf16[1,2,2,2,16,1024]{5,4,0,1,2,3:T(8,128)(2,1)S(1)}, bf16[1,2,2,2,16,1024]{5,4,0,1,2,3:T(8,128)(2,1)}) fusion(bf16[2,2,2,2,16,1024]{5,4,0,1,2,3:T(8,128)(2,1)} %bitcast.290, pred[]{:T(512)S(6)} %eq.155), kind=kLoop, calls=%fused_computation.295 | loop fusion | flops 131072 | bytes 1310721 | tf_op jit(solution)/shard_map/slice | solution.py:70
  32.6 6.2 %collective-permute-done.24 = bf16[2,2,2,2,16,1024]{5,4,3,2,1,0:T(8,128)(2,1)} collective-permute-done((bf16[2,2,2,2,16,1024]{5,4,3,2,1,0:T(8,128)(2,1)}, bf16[2,2,2,2,16,1024]{5,4,3,2,1,0:T(8,128)(2,1)}, u32[]{:S(2)}, u32[]{:S(2)}) %collective-permute-start.24) | collective-permute-done | bytes 524320 | tf_op jit(solution)/shard_map/ppermute | solution.py:73
  42.8 3.4 %collective-permute-start.9 = (bf16[2,2,2,16,1024]{4,3,2,1,0:T(8,128)(2,1)S(1)}, bf16[2,2,2,16,1024]{4,3,2,1,0:T(8,128)(2,1)S(1)}, u32[]{:S(2)}, u32[]{:S(2)}) collective-permute-start(bf16[2,2,2,16,1024]{4,3,2,1,0:T(8,128)(2,1)S(1)} %pad_maximum_fusion.7), channel_id=1, source_target_pairs={{0,8},{2,10},{4,12},{6,14},{8,0},{10,2},{12,4},{14,6},{16,24},{18,... | collective-permute-start | bytes 786440 | tf_op jit(solution)/shard_map/ppermute | solution.py:73
  50.6 5.0 %collective-permute-done.17 = bf16[2,2,2,16,1024]{4,3,2,1,0:T(8,128)(2,1)S(1)} collective-permute-done((bf16[2,2,2,16,1024]{4,3,2,1,0:T(8,128)(2,1)S(1)}, bf16[2,2,2,16,1024]{4,3,2,1,0:T(8,128)(2,1)S(1)}, u32[]{:S(2)}, u32[]{:S(2)}) %collective-permute-start.17) | collective-permute-done | bytes 262176 | tf_op jit(solution)/shard_map/ppermute | solution.py:73
  55.7 1.8 %collective-permute-start.18 = (bf16[2,2,16,1024]{3,2,1,0:T(8,128)(2,1)S(1)}, bf16[2,2,16,1024]{3,2,1,0:T(8,128)(2,1)S(1)}, u32[]{:S(2)}, u32[]{:S(2)}) collective-permute-start(bf16[2,2,16,1024]{3,2,1,0:T(8,128)(2,1)S(1)} %pad_maximum_fusion.27), channel_id=1, source_target_pairs={{0,2},{2,0},{4,6},{6,4},{8,10},{10,8},{12,14},{14,12},{16,18},{18,... | collective-permute-start | bytes 393224 | tf_op jit(solution)/shard_map/ppermute | solution.py:73
  57.9 2.4 %collective-permute-start.2 = (bf16[2,2,16,1024]{3,2,1,0:T(8,128)(2,1)S(1)}, bf16[2,2,16,1024]{3,2,1,0:T(8,128)(2,1)S(1)}, u32[]{:S(2)}, u32[]{:S(2)}) collective-permute-start(bf16[2,2,16,1024]{3,2,1,0:T(8,128)(2,1)S(1)} %pad_maximum_fusion.21), channel_id=1, source_target_pairs={{0,8},{2,10},{4,12},{6,14},{8,0},{10,2},{12,4},{14,6},{16,24},{18,... | collective-permute-start | bytes 393224 | tf_op jit(solution)/shard_map/ppermute | solution.py:73
  61.5 3.7 %collective-permute-done.10 = bf16[2,2,16,1024]{3,2,1,0:T(8,128)(2,1)S(1)} collective-permute-done((bf16[2,2,16,1024]{3,2,1,0:T(8,128)(2,1)S(1)}, bf16[2,2,16,1024]{3,2,1,0:T(8,128)(2,1)S(1)}, u32[]{:S(2)}, u32[]{:S(2)}) %collective-permute-start.10) | collective-permute-done | bytes 131104 | tf_op jit(solution)/shard_map/ppermute | solution.py:73
  67.1 2.1 %collective-permute-start.28 = (bf16[2,16,1024]{2,1,0:T(8,128)(2,1)S(1)}, bf16[2,16,1024]{2,1,0:T(8,128)(2,1)S(1)}, u32[]{:S(2)}, u32[]{:S(2)}) collective-permute-start(bf16[2,16,1024]{2,1,0:T(8,128)(2,1)S(1)} %pad_maximum_fusion.50), channel_id=1, source_target_pairs={{0,8},{2,10},{4,12},{6,14},{8,0},{10,2},{12,4},{14,6},{16,24},{18,... | collective-permute-start | bytes 196616 | tf_op jit(solution)/shard_map/ppermute | solution.py:83
  75.3 1.6 collective-permute-start.13
  76.9 2.4 %collective-permute-done.4 = bf16[2,16,1024]{2,1,0:T(8,128)(2,1)S(1)} collective-permute-done((bf16[2,16,1024]{2,1,0:T(8,128)(2,1)S(1)}, bf16[2,16,1024]{2,1,0:T(8,128)(2,1)S(1)}, u32[]{:S(2)}, u32[]{:S(2)}) %collective-permute-start.4) | collective-permute-done | bytes 65568 | tf_op jit(solution)/shard_map/ppermute | solution.py:83
  79.6 1.6 %collective-permute-start.30 = (bf16[2,2,2,16,1024]{4,3,2,1,0:T(8,128)(2,1)S(1)}, bf16[2,2,2,16,1024]{4,3,2,1,0:T(8,128)(2,1)S(1)}, u32[]{:S(2)}, u32[]{:S(2)}) collective-permute-start(bf16[2,2,2,16,1024]{4,3,2,1,0:T(8,128)(2,1)S(1)} %pad_maximum_fusion.14), channel_id=1, source_target_pairs={{0,2},{2,0},{4,6},{6,4},{8,10},{10,8},{12,14},{14,12},{16,18},{18,... | collective-permute-start | bytes 786440 | tf_op jit(solution)/shard_map/ppermute | solution.py:83
  81.3 2.3 %collective-permute-start.22 = (bf16[2,2,2,16,1024]{4,3,2,1,0:T(8,128)(2,1)S(1)}, bf16[2,2,2,16,1024]{4,3,2,1,0:T(8,128)(2,1)S(1)}, u32[]{:S(2)}, u32[]{:S(2)}) collective-permute-start(bf16[2,2,2,16,1024]{4,3,2,1,0:T(8,128)(2,1)S(1)} %pad_maximum_fusion.11), channel_id=1, source_target_pairs={{0,16},{2,18},{4,20},{6,22},{8,24},{10,26},{12,28},{14,30},{16,0},... | collective-permute-start | bytes 786440 | tf_op jit(solution)/shard_map/ppermute | solution.py:83
  83.5 3.4 %collective-permute-done.13 = bf16[2,2,16,1024]{3,2,1,0:T(8,128)(2,1)S(1)} collective-permute-done((bf16[2,2,16,1024]{3,2,1,0:T(8,128)(2,1)S(1)}, bf16[2,2,16,1024]{3,2,1,0:T(8,128)(2,1)S(1)}, u32[]{:S(2)}, u32[]{:S(2)}) %collective-permute-start.13) | collective-permute-done | bytes 131104 | tf_op jit(solution)/shard_map/ppermute | solution.py:83
  87.1 2.9 %collective-permute-done.5 = bf16[2,2,16,1024]{3,2,1,0:T(8,128)(2,1)S(1)} collective-permute-done((bf16[2,2,16,1024]{3,2,1,0:T(8,128)(2,1)S(1)}, bf16[2,2,16,1024]{3,2,1,0:T(8,128)(2,1)S(1)}, u32[]{:S(2)}, u32[]{:S(2)}) %collective-permute-start.5) | collective-permute-done | bytes 131104 | tf_op jit(solution)/shard_map/ppermute | solution.py:83
  91.3 8.9 %collective-permute-done.22 = bf16[2,2,2,16,1024]{4,3,2,1,0:T(8,128)(2,1)S(1)} collective-permute-done((bf16[2,2,2,16,1024]{4,3,2,1,0:T(8,128)(2,1)S(1)}, bf16[2,2,2,16,1024]{4,3,2,1,0:T(8,128)(2,1)S(1)}, u32[]{:S(2)}, u32[]{:S(2)}) %collective-permute-start.22) | collective-permute-done | bytes 262176 | tf_op jit(solution)/shard_map/ppermute | solution.py:83
  100.4 2.0 %collective-permute-start.34 = (bf16[1,2,2,2,16,1024]{5,4,3,2,1,0:T(8,128)(2,1)S(1)}, bf16[1,2,2,2,16,1024]{5,4,3,2,1,0:T(8,128)(2,1)S(1)}, u32[]{:S(2)}, u32[]{:S(2)}) collective-permute-start(bf16[1,2,2,2,16,1024]{5,4,3,2,1,0:T(8,128)(2,1)S(1)} %maximum_bitcast_fusion.15), channel_id=1, source_target_pairs={{0,4},{2,6},{4,0},{6,2},{8,12},{10,14},{12,8},{14,10},{16,20},{18,... | collective-permute-start | bytes 786440 | tf_op jit(solution)/shard_map/ppermute | solution.py:83
  102.6 2.1 %collective-permute-start.7 = (bf16[1,2,2,2,16,1024]{5,4,3,2,1,0:T(8,128)(2,1)S(1)}, bf16[1,2,2,2,16,1024]{5,4,3,2,1,0:T(8,128)(2,1)S(1)}, u32[]{:S(2)}, u32[]{:S(2)}) collective-permute-start(bf16[1,2,2,2,16,1024]{5,4,3,2,1,0:T(8,128)(2,1)S(1)} %maximum_bitcast_fusion.10), channel_id=1, source_target_pairs={{0,2},{2,0},{4,6},{6,4},{8,10},{10,8},{12,14},{14,12},{16,18},{18,... | collective-permute-start | bytes 786440 | tf_op jit(solution)/shard_map/ppermute | solution.py:83
  106.3 2.1 %collective-permute-done.35 = bf16[1,2,2,2,16,1024]{5,4,3,2,1,0:T(8,128)(2,1)S(1)} collective-permute-done((bf16[1,2,2,2,16,1024]{5,4,3,2,1,0:T(8,128)(2,1)S(1)}, bf16[1,2,2,2,16,1024]{5,4,3,2,1,0:T(8,128)(2,1)S(1)}, u32[]{:S(2)}, u32[]{:S(2)}) %collective-permute-start.35) | collective-permute-done | bytes 262176 | tf_op jit(solution)/shard_map/ppermute | solution.py:83
  108.5 1.8 %collective-permute-start.15 = (bf16[1,2,2,2,16,1024]{5,4,3,2,1,0:T(8,128)(2,1)S(1)}, bf16[1,2,2,2,16,1024]{5,4,3,2,1,0:T(8,128)(2,1)S(1)}, u32[]{:S(2)}, u32[]{:S(2)}) collective-permute-start(bf16[1,2,2,2,16,1024]{5,4,3,2,1,0:T(8,128)(2,1)S(1)} %maximum_bitcast_fusion.11), channel_id=1, source_target_pairs={{0,4},{2,6},{4,0},{6,2},{8,12},{10,14},{12,8},{14,10},{16,20},{18,... | collective-permute-start | bytes 786440 | tf_op jit(solution)/shard_map/ppermute | solution.py:83
  111.9 1.5 maximum_bitcast_fusion.1.blk_ref
  113.4 11.7 %shard_map.47 = (f32[4,4,1024]{2,1,0:T(4,128)}, f32[4,4,128]{2,1,0:T(4,128)}) custom-call(s32[64]{0:T(128)} %squeeze.19.meta_ref, bf16[1,1024,1024]{2,1,0:T(8,128)(2,1)} %maximum_bitcast_fusion.1.blk_ref, bf16[1024,1152]{1,0:T(8,128)(2,1)} %copy-done.3), custom_call_target="tpu_custom_call" | custom-call | flops 5435817984 | bytes 4521984 | tf_op jit(solution)/shard_map/pallas_call | solution.py:154
  126.6 1.5 maximum_bitcast_fusion.blk_ref
  128.1 11.9 %shard_map.46 = (f32[4,4,1024]{2,1,0:T(4,128)}, f32[4,4,128]{2,1,0:T(4,128)}) custom-call(s32[64]{0:T(128)} %squeeze.16.meta_ref, bf16[1,1024,1024]{2,1,0:T(8,128)(2,1)} %maximum_bitcast_fusion.blk_ref, bf16[1024,1152]{1,0:T(8,128)(2,1)} %copy-done.3), custom_call_target="tpu_custom_call" | custom-call | flops 5435817984 | bytes 4521984 | tf_op jit(solution)/shard_map/pallas_call | solution.py:154
  143.7 1.7 %collective-permute-start.39 = (f32[32]{0:T(128)S(1)}, f32[32]{0:T(128)S(1)}, u32[]{:S(2)}, u32[]{:S(2)}) collective-permute-start(f32[32]{0:T(128)S(1)} %fusion.11), channel_id=1, source_target_pairs={{0,6},{2,4},{4,2},{6,0},{8,14},{10,12},{12,10},{14,8},{16,22},{18,... | collective-permute-start | bytes 392 | tf_op jit(solution)/shard_map/ppermute | solution.py:33
  145.4 1.8 %collective-permute-start.41 = (f32[32]{0:T(128)S(1)}, f32[32]{0:T(128)S(1)}, u32[]{:S(2)}, u32[]{:S(2)}) collective-permute-start(f32[32]{0:T(128)S(1)} %fusion.11), channel_id=1, source_target_pairs={{0,2},{2,0},{4,6},{6,4},{8,10},{10,8},{12,14},{14,12},{16,18},{18,... | collective-permute-start | bytes 392 | tf_op jit(solution)/shard_map/ppermute | solution.py:33
  149.0 2.1 %collective-permute-start.42 = (f32[32]{0:T(128)S(1)}, f32[32]{0:T(128)S(1)}, u32[]{:S(2)}, u32[]{:S(2)}) collective-permute-start(f32[32]{0:T(128)S(1)} %fusion.27), channel_id=1, source_target_pairs={{0,8},{2,10},{4,12},{6,14},{8,0},{10,2},{12,4},{14,6},{16,24},{18,... | collective-permute-start | bytes 392 | tf_op jit(solution)/shard_map/ppermute | solution.py:33
  152.6 2.0 %collective-permute-start.43 = (f32[32]{0:T(128)S(1)}, f32[32]{0:T(128)S(1)}, u32[]{:S(2)}, u32[]{:S(2)}) collective-permute-start(f32[32]{0:T(128)S(1)} %fusion.24), channel_id=1, source_target_pairs={{0,16},{2,18},{4,20},{6,22},{8,24},{10,26},{12,28},{14,30},{16,0},... | collective-permute-start | bytes 392 | tf_op jit(solution)/shard_map/ppermute | solution.py:33
  154.6 2.4 %collective-permute-done.43 = f32[32]{0:T(128)S(1)} collective-permute-done((f32[32]{0:T(128)S(1)}, f32[32]{0:T(128)S(1)}, u32[]{:S(2)}, u32[]{:S(2)}) %collective-permute-start.43) | collective-permute-done | bytes 160 | tf_op jit(solution)/shard_map/ppermute | solution.py:33
  (259 shorter events, 48.2 us)
Async XLA Ops:
  1.7 27.1 %collective-permute-start.32 = (bf16[1024,128]{1,0:T(8,128)(2,1)}, bf16[1024,128]{1,0:T(8,128)(2,1)}, u32[]{:S(2)}, u32[]{:S(2)}) collective-permute-start(bf16[1024,128]{1,0:T(8,128)(2,1)} %slice.719), channel_id=1, source_target_pairs={{2,0},{4,2},{6,4},{8,6},{10,8},{12,10},{14,12},{16,14},{18,16},{20... | collective-permute-start | bytes 786440 | tf_op jit(solution)/shard_map/ppermute | solution.py:18
  8.0 30.8 %collective-permute-start.24 = (bf16[2,2,2,2,16,1024]{5,4,3,2,1,0:T(8,128)(2,1)}, bf16[2,2,2,2,16,1024]{5,4,3,2,1,0:T(8,128)(2,1)}, u32[]{:S(2)}, u32[]{:S(2)}) collective-permute-start(bf16[2,2,2,2,16,1024]{5,4,3,2,1,0:T(8,128)(2,1)} %pad_maximum_fusion.3), channel_id=1, source_target_pairs={{0,16},{2,18},{4,20},{6,22},{8,24},{10,26},{12,28},{14,30},{16,0},... | collective-permute-start | bytes 1572872 | tf_op jit(solution)/shard_map/ppermute | solution.py:73
  15.9 24.2 %collective-permute-start.16 = (bf16[2,2,2,2,16,1024]{5,4,3,2,1,0:T(8,128)(2,1)}, bf16[2,2,2,2,16,1024]{5,4,3,2,1,0:T(8,128)(2,1)}, u32[]{:S(2)}, u32[]{:S(2)}) collective-permute-start(bf16[2,2,2,2,16,1024]{5,4,3,2,1,0:T(8,128)(2,1)} %pad_maximum_fusion.2), channel_id=1, source_target_pairs={{0,8},{2,10},{4,12},{6,14},{8,0},{10,2},{12,4},{14,6},{16,24},{18,... | collective-permute-start | bytes 1572872 | tf_op jit(solution)/shard_map/ppermute | solution.py:73
  20.4 21.2 %collective-permute-start.8 = (bf16[2,2,2,2,16,1024]{5,4,3,2,1,0:T(8,128)(2,1)}, bf16[2,2,2,2,16,1024]{5,4,3,2,1,0:T(8,128)(2,1)}, u32[]{:S(2)}, u32[]{:S(2)}) collective-permute-start(bf16[2,2,2,2,16,1024]{5,4,3,2,1,0:T(8,128)(2,1)} %pad_maximum_fusion.1), channel_id=1, source_target_pairs={{0,4},{2,6},{4,0},{6,2},{8,12},{10,14},{12,8},{14,10},{16,20},{18,... | collective-permute-start | bytes 1572872 | tf_op jit(solution)/shard_map/ppermute | solution.py:73
  23.7 22.5 %collective-permute-start = (bf16[2,2,2,2,16,1024]{5,4,0,1,2,3:T(8,128)(2,1)}, bf16[2,2,2,2,16,1024]{5,4,0,1,2,3:T(8,128)(2,1)}, u32[]{:S(2)}, u32[]{:S(2)}) collective-permute-start(bf16[2,2,2,2,16,1024]{5,4,0,1,2,3:T(8,128)(2,1)} %pad_maximum_fusion), channel_id=1, source_target_pairs={{0,2},{2,0},{4,6},{6,4},{8,10},{10,8},{12,14},{14,12},{16,18},{18,... | collective-permute-start | bytes 1572872 | tf_op jit(solution)/shard_map/ppermute | solution.py:73
  40.0 9.6 %collective-permute-start.25 = (bf16[2,2,2,16,1024]{4,3,2,1,0:T(8,128)(2,1)S(1)}, bf16[2,2,2,16,1024]{4,3,2,1,0:T(8,128)(2,1)S(1)}, u32[]{:S(2)}, u32[]{:S(2)}) collective-permute-start(bf16[2,2,2,16,1024]{4,3,2,1,0:T(8,128)(2,1)S(1)} %pad_maximum_fusion.13), channel_id=1, source_target_pairs={{0,2},{2,0},{4,6},{6,4},{8,10},{10,8},{12,14},{14,12},{16,18},{18,... | collective-permute-start | bytes 786440 | tf_op jit(solution)/shard_map/ppermute | solution.py:73
  41.3 14.4 %collective-permute-start.17 = (bf16[2,2,2,16,1024]{4,3,2,1,0:T(8,128)(2,1)S(1)}, bf16[2,2,2,16,1024]{4,3,2,1,0:T(8,128)(2,1)S(1)}, u32[]{:S(2)}, u32[]{:S(2)}) collective-permute-start(bf16[2,2,2,16,1024]{4,3,2,1,0:T(8,128)(2,1)S(1)} %pad_maximum_fusion.10), channel_id=1, source_target_pairs={{0,16},{2,18},{4,20},{6,22},{8,24},{10,26},{12,28},{14,30},{16,0},... | collective-permute-start | bytes 786440 | tf_op jit(solution)/shard_map/ppermute | solution.py:73
  42.8 14.8 %collective-permute-start.9 = (bf16[2,2,2,16,1024]{4,3,2,1,0:T(8,128)(2,1)S(1)}, bf16[2,2,2,16,1024]{4,3,2,1,0:T(8,128)(2,1)S(1)}, u32[]{:S(2)}, u32[]{:S(2)}) collective-permute-start(bf16[2,2,2,16,1024]{4,3,2,1,0:T(8,128)(2,1)S(1)} %pad_maximum_fusion.7), channel_id=1, source_target_pairs={{0,8},{2,10},{4,12},{6,14},{8,0},{10,2},{12,4},{14,6},{16,24},{18,... | collective-permute-start | bytes 786440 | tf_op jit(solution)/shard_map/ppermute | solution.py:73
  48.4 9.4 %collective-permute-start.1 = (bf16[2,2,2,16,1024]{4,3,2,1,0:T(8,128)(2,1)S(1)}, bf16[2,2,2,16,1024]{4,3,2,1,0:T(8,128)(2,1)S(1)}, u32[]{:S(2)}, u32[]{:S(2)}) collective-permute-start(bf16[2,2,2,16,1024]{4,3,2,1,0:T(8,128)(2,1)S(1)} %pad_maximum_fusion.4), channel_id=1, source_target_pairs={{0,4},{2,6},{4,0},{6,2},{8,12},{10,14},{12,8},{14,10},{16,20},{18,... | collective-permute-start | bytes 786440 | tf_op jit(solution)/shard_map/ppermute | solution.py:73
  49.7 10.6 %collective-permute-start.26 = (bf16[2,2,16,1024]{3,2,1,0:T(8,128)(2,1)S(1)}, bf16[2,2,16,1024]{3,2,1,0:T(8,128)(2,1)S(1)}, u32[]{:S(2)}, u32[]{:S(2)}) collective-permute-start(bf16[2,2,16,1024]{3,2,1,0:T(8,128)(2,1)S(1)} %pad_maximum_fusion.30), channel_id=1, source_target_pairs={{0,4},{2,6},{4,0},{6,2},{8,12},{10,14},{12,8},{14,10},{16,20},{18,... | collective-permute-start | bytes 393224 | tf_op jit(solution)/shard_map/ppermute | solution.py:73
  57.7 7.6 %collective-permute-start.10 = (bf16[2,2,16,1024]{3,2,1,0:T(8,128)(2,1)S(1)}, bf16[2,2,16,1024]{3,2,1,0:T(8,128)(2,1)S(1)}, u32[]{:S(2)}, u32[]{:S(2)}) collective-permute-start(bf16[2,2,16,1024]{3,2,1,0:T(8,128)(2,1)S(1)} %pad_maximum_fusion.24), channel_id=1, source_target_pairs={{0,16},{2,18},{4,20},{6,22},{8,24},{10,26},{12,28},{14,30},{16,0},... | collective-permute-start | bytes 393224 | tf_op jit(solution)/shard_map/ppermute | solution.py:73
  57.9 8.5 %collective-permute-start.2 = (bf16[2,2,16,1024]{3,2,1,0:T(8,128)(2,1)S(1)}, bf16[2,2,16,1024]{3,2,1,0:T(8,128)(2,1)S(1)}, u32[]{:S(2)}, u32[]{:S(2)}) collective-permute-start(bf16[2,2,16,1024]{3,2,1,0:T(8,128)(2,1)S(1)} %pad_maximum_fusion.21), channel_id=1, source_target_pairs={{0,8},{2,10},{4,12},{6,14},{8,0},{10,2},{12,4},{14,6},{16,24},{18,... | collective-permute-start | bytes 393224 | tf_op jit(solution)/shard_map/ppermute | solution.py:73
  60.4 6.7 %collective-permute-start.27 = (bf16[2,16,1024]{2,1,0:T(8,128)(2,1)S(1)}, bf16[2,16,1024]{2,1,0:T(8,128)(2,1)S(1)}, u32[]{:S(2)}, u32[]{:S(2)}) collective-permute-start(bf16[2,16,1024]{2,1,0:T(8,128)(2,1)S(1)} %pad_maximum_fusion.49), channel_id=1, source_target_pairs={{0,8},{2,10},{4,12},{6,14},{8,0},{10,2},{12,4},{14,6},{16,24},{18,... | collective-permute-start | bytes 196616 | tf_op jit(solution)/shard_map/ppermute | solution.py:73
  60.8 8.3 %collective-permute-start.19 = (bf16[2,16,1024]{2,1,0:T(8,128)(2,1)S(1)}, bf16[2,16,1024]{2,1,0:T(8,128)(2,1)S(1)}, u32[]{:S(2)}, u32[]{:S(2)}) collective-permute-start(bf16[2,16,1024]{2,1,0:T(8,128)(2,1)S(1)} %pad_maximum_fusion.45), channel_id=1, source_target_pairs={{0,4},{2,6},{4,0},{6,2},{8,12},{10,14},{12,8},{14,10},{16,20},{18,... | collective-permute-start | bytes 196616 | tf_op jit(solution)/shard_map/ppermute | solution.py:73
  66.4 5.6 %collective-permute-start.3 = (bf16[2,16,1024]{2,1,0:T(8,128)(2,1)S(1)}, bf16[2,16,1024]{2,1,0:T(8,128)(2,1)S(1)}, u32[]{:S(2)}, u32[]{:S(2)}) collective-permute-start(bf16[2,16,1024]{2,1,0:T(8,128)(2,1)S(1)} %pad_maximum_fusion.37), channel_id=1, source_target_pairs={{0,16},{2,18},{4,20},{6,22},{8,24},{10,26},{12,28},{14,30},{16,0},... | collective-permute-start | bytes 196616 | tf_op jit(solution)/shard_map/ppermute | solution.py:73
  72.0 7.3 %collective-permute-start.4 = (bf16[2,16,1024]{2,1,0:T(8,128)(2,1)S(1)}, bf16[2,16,1024]{2,1,0:T(8,128)(2,1)S(1)}, u32[]{:S(2)}, u32[]{:S(2)}) collective-permute-start(bf16[2,16,1024]{2,1,0:T(8,128)(2,1)S(1)} %pad_maximum_fusion.38), channel_id=1, source_target_pairs={{0,16},{2,18},{4,20},{6,22},{8,24},{10,26},{12,28},{14,30},{16,0},... | collective-permute-start | bytes 196616 | tf_op jit(solution)/shard_map/ppermute | solution.py:83
  72.4 7.1 %collective-permute-start.29 = (bf16[2,2,16,1024]{3,2,1,0:T(8,128)(2,1)S(1)}, bf16[2,2,16,1024]{3,2,1,0:T(8,128)(2,1)S(1)}, u32[]{:S(2)}, u32[]{:S(2)}) collective-permute-start(bf16[2,2,16,1024]{3,2,1,0:T(8,128)(2,1)S(1)} %pad_maximum_fusion.31), channel_id=1, source_target_pairs={{0,4},{2,6},{4,0},{6,2},{8,12},{10,14},{12,8},{14,10},{16,20},{18,... | collective-permute-start | bytes 393224 | tf_op jit(solution)/shard_map/ppermute | solution.py:83
  74.2 6.9 %collective-permute-start.21 = (bf16[2,2,16,1024]{3,2,1,0:T(8,128)(2,1)S(1)}, bf16[2,2,16,1024]{3,2,1,0:T(8,128)(2,1)S(1)}, u32[]{:S(2)}, u32[]{:S(2)}) collective-permute-start(bf16[2,2,16,1024]{3,2,1,0:T(8,128)(2,1)S(1)} %pad_maximum_fusion.28), channel_id=1, source_target_pairs={{0,2},{2,0},{4,6},{6,4},{8,10},{10,8},{12,14},{14,12},{16,18},{18,... | collective-permute-start | bytes 393224 | tf_op jit(solution)/shard_map/ppermute | solution.py:83
  75.3 11.6 %collective-permute-start.13 = (bf16[2,2,16,1024]{3,2,1,0:T(8,128)(2,1)S(1)}, bf16[2,2,16,1024]{3,2,1,0:T(8,128)(2,1)S(1)}, u32[]{:S(2)}, u32[]{:S(2)}) collective-permute-start(bf16[2,2,16,1024]{3,2,1,0:T(8,128)(2,1)S(1)} %pad_maximum_fusion.25), channel_id=1, source_target_pairs={{0,16},{2,18},{4,20},{6,22},{8,24},{10,26},{12,28},{14,30},{16,0},... | collective-permute-start | bytes 393224 | tf_op jit(solution)/shard_map/ppermute | solution.py:83
  79.4 10.6 %collective-permute-start.5 = (bf16[2,2,16,1024]{3,2,1,0:T(8,128)(2,1)S(1)}, bf16[2,2,16,1024]{3,2,1,0:T(8,128)(2,1)S(1)}, u32[]{:S(2)}, u32[]{:S(2)}) collective-permute-start(bf16[2,2,16,1024]{3,2,1,0:T(8,128)(2,1)S(1)} %pad_maximum_fusion.22), channel_id=1, source_target_pairs={{0,8},{2,10},{4,12},{6,14},{8,0},{10,2},{12,4},{14,6},{16,24},{18,... | collective-permute-start | bytes 393224 | tf_op jit(solution)/shard_map/ppermute | solution.py:83
  79.6 11.0 %collective-permute-start.30 = (bf16[2,2,2,16,1024]{4,3,2,1,0:T(8,128)(2,1)S(1)}, bf16[2,2,2,16,1024]{4,3,2,1,0:T(8,128)(2,1)S(1)}, u32[]{:S(2)}, u32[]{:S(2)}) collective-permute-start(bf16[2,2,2,16,1024]{4,3,2,1,0:T(8,128)(2,1)S(1)} %pad_maximum_fusion.14), channel_id=1, source_target_pairs={{0,2},{2,0},{4,6},{6,4},{8,10},{10,8},{12,14},{14,12},{16,18},{18,... | collective-permute-start | bytes 786440 | tf_op jit(solution)/shard_map/ppermute | solution.py:83
  81.3 18.9 %collective-permute-start.22 = (bf16[2,2,2,16,1024]{4,3,2,1,0:T(8,128)(2,1)S(1)}, bf16[2,2,2,16,1024]{4,3,2,1,0:T(8,128)(2,1)S(1)}, u32[]{:S(2)}, u32[]{:S(2)}) collective-permute-start(bf16[2,2,2,16,1024]{4,3,2,1,0:T(8,128)(2,1)S(1)} %pad_maximum_fusion.11), channel_id=1, source_target_pairs={{0,16},{2,18},{4,20},{6,22},{8,24},{10,26},{12,28},{14,30},{16,0},... | collective-permute-start | bytes 786440 | tf_op jit(solution)/shard_map/ppermute | solution.py:83
  87.0 13.3 %collective-permute-start.14 = (bf16[2,2,2,16,1024]{4,3,2,1,0:T(8,128)(2,1)S(1)}, bf16[2,2,2,16,1024]{4,3,2,1,0:T(8,128)(2,1)S(1)}, u32[]{:S(2)}, u32[]{:S(2)}) collective-permute-start(bf16[2,2,2,16,1024]{4,3,2,1,0:T(8,128)(2,1)S(1)} %pad_maximum_fusion.8), channel_id=1, source_target_pairs={{0,8},{2,10},{4,12},{6,14},{8,0},{10,2},{12,4},{14,6},{16,24},{18,... | collective-permute-start | bytes 786440 | tf_op jit(solution)/shard_map/ppermute | solution.py:83
  90.1 12.2 %collective-permute-start.6 = (bf16[2,2,2,16,1024]{4,3,2,1,0:T(8,128)(2,1)S(1)}, bf16[2,2,2,16,1024]{4,3,2,1,0:T(8,128)(2,1)S(1)}, u32[]{:S(2)}, u32[]{:S(2)}) collective-permute-start(bf16[2,2,2,16,1024]{4,3,2,1,0:T(8,128)(2,1)S(1)} %pad_maximum_fusion.5), channel_id=1, source_target_pairs={{0,4},{2,6},{4,0},{6,2},{8,12},{10,14},{12,8},{14,10},{16,20},{18,... | collective-permute-start | bytes 786440 | tf_op jit(solution)/shard_map/ppermute | solution.py:83
  90.7 14.1 %collective-permute-start.36 = (bf16[1,2,2,2,16,1024]{5,4,3,2,1,0:T(8,128)(2,1)S(1)}, bf16[1,2,2,2,16,1024]{5,4,3,2,1,0:T(8,128)(2,1)S(1)}, u32[]{:S(2)}, u32[]{:S(2)}) collective-permute-start(bf16[1,2,2,2,16,1024]{5,4,3,2,1,0:T(8,128)(2,1)S(1)} %maximum_bitcast_fusion.17), channel_id=1, source_target_pairs={{0,16},{2,18},{4,20},{6,22},{8,24},{10,26},{12,28},{14,30},{16,0},... | collective-permute-start | bytes 786440 | tf_op jit(solution)/shard_map/ppermute | solution.py:83
  100.2 8.1 %collective-permute-start.35 = (bf16[1,2,2,2,16,1024]{5,4,3,2,1,0:T(8,128)(2,1)S(1)}, bf16[1,2,2,2,16,1024]{5,4,3,2,1,0:T(8,128)(2,1)S(1)}, u32[]{:S(2)}, u32[]{:S(2)}) collective-permute-start(bf16[1,2,2,2,16,1024]{5,4,3,2,1,0:T(8,128)(2,1)S(1)} %maximum_bitcast_fusion.16), channel_id=1, source_target_pairs={{0,8},{2,10},{4,12},{6,14},{8,0},{10,2},{12,4},{14,6},{16,24},{18,... | collective-permute-start | bytes 786440 | tf_op jit(solution)/shard_map/ppermute | solution.py:83
  100.4 8.1 %collective-permute-start.34 = (bf16[1,2,2,2,16,1024]{5,4,3,2,1,0:T(8,128)(2,1)S(1)}, bf16[1,2,2,2,16,1024]{5,4,3,2,1,0:T(8,128)(2,1)S(1)}, u32[]{:S(2)}, u32[]{:S(2)}) collective-permute-start(bf16[1,2,2,2,16,1024]{5,4,3,2,1,0:T(8,128)(2,1)S(1)} %maximum_bitcast_fusion.15), channel_id=1, source_target_pairs={{0,4},{2,6},{4,0},{6,2},{8,12},{10,14},{12,8},{14,10},{16,20},{18,... | collective-permute-start | bytes 786440 | tf_op jit(solution)/shard_map/ppermute | solution.py:83
  102.5 8.0 %collective-permute-start.33 = (bf16[1,2,2,2,16,1024]{5,4,3,2,1,0:T(8,128)(2,1)S(1)}, bf16[1,2,2,2,16,1024]{5,4,3,2,1,0:T(8,128)(2,1)S(1)}, u32[]{:S(2)}, u32[]{:S(2)}) collective-permute-start(bf16[1,2,2,2,16,1024]{5,4,3,2,1,0:T(8,128)(2,1)S(1)} %maximum_bitcast_fusion.14), channel_id=1, source_target_pairs={{0,2},{2,0},{4,6},{6,4},{8,10},{10,8},{12,14},{14,12},{16,18},{18,... | collective-permute-start | bytes 786440 | tf_op jit(solution)/shard_map/ppermute | solution.py:83
  102.6 9.1 %collective-permute-start.7 = (bf16[1,2,2,2,16,1024]{5,4,3,2,1,0:T(8,128)(2,1)S(1)}, bf16[1,2,2,2,16,1024]{5,4,3,2,1,0:T(8,128)(2,1)S(1)}, u32[]{:S(2)}, u32[]{:S(2)}) collective-permute-start(bf16[1,2,2,2,16,1024]{5,4,3,2,1,0:T(8,128)(2,1)S(1)} %maximum_bitcast_fusion.10), channel_id=1, source_target_pairs={{0,2},{2,0},{4,6},{6,4},{8,10},{10,8},{12,14},{14,12},{16,18},{18,... | collective-permute-start | bytes 786440 | tf_op jit(solution)/shard_map/ppermute | solution.py:83
  104.8 21.2 %collective-permute-start.31 = (bf16[1,2,2,2,16,1024]{5,4,3,2,1,0:T(8,128)(2,1)S(1)}, bf16[1,2,2,2,16,1024]{5,4,3,2,1,0:T(8,128)(2,1)S(1)}, u32[]{:S(2)}, u32[]{:S(2)}) collective-permute-start(bf16[1,2,2,2,16,1024]{5,4,3,2,1,0:T(8,128)(2,1)S(1)} %maximum_bitcast_fusion.13), channel_id=1, source_target_pairs={{0,16},{2,18},{4,20},{6,22},{8,24},{10,26},{12,28},{14,30},{16,0},... | collective-permute-start | bytes 786440 | tf_op jit(solution)/shard_map/ppermute | solution.py:83
  108.4 17.8 %collective-permute-start.23 = (bf16[1,2,2,2,16,1024]{5,4,3,2,1,0:T(8,128)(2,1)S(1)}, bf16[1,2,2,2,16,1024]{5,4,3,2,1,0:T(8,128)(2,1)S(1)}, u32[]{:S(2)}, u32[]{:S(2)}) collective-permute-start(bf16[1,2,2,2,16,1024]{5,4,3,2,1,0:T(8,128)(2,1)S(1)} %maximum_bitcast_fusion.12), channel_id=1, source_target_pairs={{0,8},{2,10},{4,12},{6,14},{8,0},{10,2},{12,4},{14,6},{16,24},{18,... | collective-permute-start | bytes 786440 | tf_op jit(solution)/shard_map/ppermute | solution.py:83
  108.5 17.8 %collective-permute-start.15 = (bf16[1,2,2,2,16,1024]{5,4,3,2,1,0:T(8,128)(2,1)S(1)}, bf16[1,2,2,2,16,1024]{5,4,3,2,1,0:T(8,128)(2,1)S(1)}, u32[]{:S(2)}, u32[]{:S(2)}) collective-permute-start(bf16[1,2,2,2,16,1024]{5,4,3,2,1,0:T(8,128)(2,1)S(1)} %maximum_bitcast_fusion.11), channel_id=1, source_target_pairs={{0,4},{2,6},{4,0},{6,2},{8,12},{10,14},{12,8},{14,10},{16,20},{18,... | collective-permute-start | bytes 786440 | tf_op jit(solution)/shard_map/ppermute | solution.py:83
  (21 other events, 108.2 us)

commit v13 on v10

--- a/solution.py
+++ b/solution.py
@@ -47,17 +47,19 @@
     place = lax.axis_index(axis)
     nbits = size.bit_length() - 1
     rounds = roots.shape[0]
-    rows, chans = block.shape
+    chans, rows = block.shape
     parts = next(p for p in (4, 2, 1) if rows % (p * size) == 0)
     if size & (size - 1) or rows % (parts * size) or nbits == 0:
         own = place == roots
-        masked = jnp.where(own[:, None, None], block[None], jnp.zeros_like(block)[None])
+        flipped = jnp.transpose(block)
+        masked = jnp.where(own[:, None, None], flipped[None], jnp.zeros_like(flipped)[None])
         return lax.psum(masked, axis)
     piece = rows // (parts * size)
     orders = [[1 << ((p + s) % nbits) for s in range(nbits)] for p in range(parts)]
     bufs = {}
     for p in range(parts):
-        seg = block[p * piece * size : (p + 1) * piece * size].reshape([2] * nbits + [piece, chans])
+        seg = jnp.transpose(block[:, p * piece * size : (p + 1) * piece * size])
+        seg = seg.reshape([2] * nbits + [piece, chans])
         perm = [nbits - 1 - (m.bit_length() - 1) for m in orders[p]] + [nbits, nbits + 1]
         seg = jnp.transpose(seg, perm)
         for r in range(rounds):
@@ -185,7 +187,7 @@
     upper = chan_range[:, :, 1]
     inside = (channel >= lower[:, :, None]) & (channel < upper[:, :, None])
 
-    blocks = spread_blocks(jnp.transpose(signal), round_shard, "tm")
+    blocks = spread_blocks(signal, round_shard, "tm")
     offs = jnp.clip(offsets, 0, lag_count - L)
     first = jnp.minimum((offs // 16) * 16, lag_count - REACH)
     base = section * chan_local

time: 158 us -> 156 us (0.987)
  waiting for transfers between devices: 44 us -> 41.1 us
    ppermute x36, waiting for transfers between devices: 38.8 us -> 35.9 us  [spread_blocks(): lax.ppermute(jnp.stack([v for _, v in items]), axis, [(i, i ^ mask) for i...]
    unnamed x20 -> x23, local copies, waits for them, and re-layouts: 4.37 us -> 4.15 us
  transfers between devices with their start and end apart: 45 -> 45, of which waited for: 21 -> 21; matrix products, arithmetic and copies ran while one was open for 18% -> 18% of each run, Pallas kernels for 7% -> 8%
where the time goes in v13:
time: 156 us; the launch traced here: 155 us
  starting transfers between devices  53.1 us (34%)
  waiting for transfers between devices  41.1 us (26%)
  Pallas kernels  23.8 us (15%)
  other arithmetic  18.1 us (12%)
  local copies, waits for them, and re-layouts  15 us (10%)
  between operations  2.62 us (2%)
    ppermute x36, starting transfers between devices, spread_blocks(): lax.ppermute(jnp.stack([v for _, v in items]), axis, [(i, i ^ mask) for i...  43.3 us
    ppermute x36, waiting for transfers between devices, spread_blocks(): lax.ppermute(jnp.stack([v for _, v in items]), axis, [(i, i ^ mask) for i...  35.9 us
    pallas_call x2, Pallas kernels, correlate(): pl.pallas_call(correlate_kernel, grid_spec=grid_spec, out_shape=[jax.Shap...  23.8 us
    ppermute x8, starting transfers between devices, group_sum(): got[d] = lax.ppermute(value, axis, pairs)  8.57 us
    select_n x18, other arithmetic, spread_blocks(): bufs[key] = jnp.where(holder, keeps[key], got[n])  5.7 us
    ppermute x8, waiting for transfers between devices, group_sum(): got[d] = lax.ppermute(value, axis, pairs)  5.14 us
    another operation x52, other arithmetic, spread_blocks(): jnp.stack([v for _, v in items])  4.23 us
    unnamed x23, local copies, waits for them, and re-layouts  4.15 us
  transfers between devices with their start and end apart: 45, of which 21 were waited for; matrix products, arithmetic and copies ran while one was open for 18% of the time, Pallas kernels for 8%

profile of v13, /device:TPU:0, one launch (start us, length us, event | category | flops | bytes accessed | tf_op | source)
XLA Modules:
  0.0 155.1 jit_solution(2728242743195249506)
XLA Ops:
  0.0 1.7 %slice.719 = bf16[1024,128]{1,0:T(8,128)(2,1)} slice(bf16[1024,1024]{1,0:T(8,128)(2,1)} %param.4), slice={[0:1024], [0:128]} | slice | bytes 524288 | tf_op jit(solution)/shard_map/slice | solution.py:183
  3.0 2.5 %fusion.28 = (bf16[1024,256]{1,0:T(8,128)(2,1)}, bf16[1024,256]{1,0:T(8,128)(2,1)S(1)}, bf16[1024,256]{1,0:T(8,128)(2,1)S(1)}, bf16[1024,256]{1,0:T(8,128)(2,1)S(1)}) fusion(bf16[1024,1024]{1,0:T(8,128)(2,1)} %param.4), kind=kLoop, calls=%fused_computation.302 | loop fusion | bytes 4194304 | tf_op jit(solution)/shard_map/slice | solution.py:61
  6.6 7.0 %collective-permute-start.24 = (bf16[2,2,2,2,16,1024]{5,4,3,2,1,0:T(8,128)(2,1)}, bf16[2,2,2,2,16,1024]{5,4,3,2,1,0:T(8,128)(2,1)}, u32[]{:S(2)}, u32[]{:S(2)}) collective-permute-start(bf16[2,2,2,2,16,1024]{5,4,3,2,1,0:T(8,128)(2,1)} %pad_maximum_fusion.3), channel_id=1, source_target_pairs={{0,16},{2,18},{4,20},{6,22},{8,24},{10,26},{12,28},{14,30},{16,0},... | collective-permute-start | bytes 1572872 | tf_op jit(solution)/shard_map/ppermute | solution.py:75
  14.8 1.6 %collective-permute-start.16 = (bf16[2,2,2,2,16,1024]{5,4,3,2,1,0:T(8,128)(2,1)}, bf16[2,2,2,2,16,1024]{5,4,3,2,1,0:T(8,128)(2,1)}, u32[]{:S(2)}, u32[]{:S(2)}) collective-permute-start(bf16[2,2,2,2,16,1024]{5,4,3,2,1,0:T(8,128)(2,1)} %pad_maximum_fusion.2), channel_id=1, source_target_pairs={{0,8},{2,10},{4,12},{6,14},{8,0},{10,2},{12,4},{14,6},{16,24},{18,... | collective-permute-start | bytes 1572872 | tf_op jit(solution)/shard_map/ppermute | solution.py:75
  18.9 2.0 %copy.66 = bf16[1024,256]{0,1:T(8,128)(2,1)} copy(bf16[1024,256]{1,0:T(8,128)(2,1)} %get-tuple-element.17) | data formatting | bytes 1048576
  20.9 1.8 %fusion.29 = (bf16[1,2,2,2,16,1024]{5,4,0,1,2,3:T(8,128)(2,1)S(1)}, bf16[1,2,2,2,16,1024]{5,4,0,1,2,3:T(8,128)(2,1)S(1)}, bf16[1,2,2,2,16,1024]{5,4,0,1,2,3:T(8,128)(2,1)}) fusion(bf16[2,2,2,2,16,1024]{5,4,0,1,2,3:T(8,128)(2,1)} %bitcast.296, pred[]{:T(512)S(6)} %eq.170), kind=kLoop, calls=%fused_computation.303 | loop fusion | flops 131072 | bytes 1310721 | tf_op jit(solution)/shard_map/slice | solution.py:72
  32.4 6.3 %collective-permute-done.24 = bf16[2,2,2,2,16,1024]{5,4,3,2,1,0:T(8,128)(2,1)} collective-permute-done((bf16[2,2,2,2,16,1024]{5,4,3,2,1,0:T(8,128)(2,1)}, bf16[2,2,2,2,16,1024]{5,4,3,2,1,0:T(8,128)(2,1)}, u32[]{:S(2)}, u32[]{:S(2)}) %collective-permute-start.24) | collective-permute-done | bytes 524320 | tf_op jit(solution)/shard_map/ppermute | solution.py:75
  42.8 2.0 %collective-permute-start.9 = (bf16[2,2,2,16,1024]{4,3,2,1,0:T(8,128)(2,1)S(1)}, bf16[2,2,2,16,1024]{4,3,2,1,0:T(8,128)(2,1)S(1)}, u32[]{:S(2)}, u32[]{:S(2)}) collective-permute-start(bf16[2,2,2,16,1024]{4,3,2,1,0:T(8,128)(2,1)S(1)} %pad_maximum_fusion.7), channel_id=1, source_target_pairs={{0,8},{2,10},{4,12},{6,14},{8,0},{10,2},{12,4},{14,6},{16,24},{18,... | collective-permute-start | bytes 786440 | tf_op jit(solution)/shard_map/ppermute | solution.py:75
  49.2 5.8 %collective-permute-done.17 = bf16[2,2,2,16,1024]{4,3,2,1,0:T(8,128)(2,1)S(1)} collective-permute-done((bf16[2,2,2,16,1024]{4,3,2,1,0:T(8,128)(2,1)S(1)}, bf16[2,2,2,16,1024]{4,3,2,1,0:T(8,128)(2,1)S(1)}, u32[]{:S(2)}, u32[]{:S(2)}) %collective-permute-start.17) | collective-permute-done | bytes 262176 | tf_op jit(solution)/shard_map/ppermute | solution.py:75
  55.1 1.8 %collective-permute-start.18 = (bf16[2,2,16,1024]{3,2,1,0:T(8,128)(2,1)S(1)}, bf16[2,2,16,1024]{3,2,1,0:T(8,128)(2,1)S(1)}, u32[]{:S(2)}, u32[]{:S(2)}) collective-permute-start(bf16[2,2,16,1024]{3,2,1,0:T(8,128)(2,1)S(1)} %pad_maximum_fusion.27), channel_id=1, source_target_pairs={{0,2},{2,0},{4,6},{6,4},{8,10},{10,8},{12,14},{14,12},{16,18},{18,... | collective-permute-start | bytes 393224 | tf_op jit(solution)/shard_map/ppermute | solution.py:75
  57.3 1.8 %collective-permute-start.2 = (bf16[2,2,16,1024]{3,2,1,0:T(8,128)(2,1)S(1)}, bf16[2,2,16,1024]{3,2,1,0:T(8,128)(2,1)S(1)}, u32[]{:S(2)}, u32[]{:S(2)}) collective-permute-start(bf16[2,2,16,1024]{3,2,1,0:T(8,128)(2,1)S(1)} %pad_maximum_fusion.21), channel_id=1, source_target_pairs={{0,8},{2,10},{4,12},{6,14},{8,0},{10,2},{12,4},{14,6},{16,24},{18,... | collective-permute-start | bytes 393224 | tf_op jit(solution)/shard_map/ppermute | solution.py:75
  60.6 3.9 %collective-permute-done.10 = bf16[2,2,16,1024]{3,2,1,0:T(8,128)(2,1)S(1)} collective-permute-done((bf16[2,2,16,1024]{3,2,1,0:T(8,128)(2,1)S(1)}, bf16[2,2,16,1024]{3,2,1,0:T(8,128)(2,1)S(1)}, u32[]{:S(2)}, u32[]{:S(2)}) %collective-permute-start.10) | collective-permute-done | bytes 131104 | tf_op jit(solution)/shard_map/ppermute | solution.py:75
  66.6 2.4 %collective-permute-start.28 = (bf16[2,16,1024]{2,1,0:T(8,128)(2,1)S(1)}, bf16[2,16,1024]{2,1,0:T(8,128)(2,1)S(1)}, u32[]{:S(2)}, u32[]{:S(2)}) collective-permute-start(bf16[2,16,1024]{2,1,0:T(8,128)(2,1)S(1)} %pad_maximum_fusion.50), channel_id=1, source_target_pairs={{0,8},{2,10},{4,12},{6,14},{8,0},{10,2},{12,4},{14,6},{16,24},{18,... | collective-permute-start | bytes 196616 | tf_op jit(solution)/shard_map/ppermute | solution.py:85
  72.6 1.4 collective-permute-done.20
  74.7 2.0 %collective-permute-start.13 = (bf16[2,2,16,1024]{3,2,1,0:T(8,128)(2,1)S(1)}, bf16[2,2,16,1024]{3,2,1,0:T(8,128)(2,1)S(1)}, u32[]{:S(2)}, u32[]{:S(2)}) collective-permute-start(bf16[2,2,16,1024]{3,2,1,0:T(8,128)(2,1)S(1)} %pad_maximum_fusion.25), channel_id=1, source_target_pairs={{0,16},{2,18},{4,20},{6,22},{8,24},{10,26},{12,28},{14,30},{16,0},... | collective-permute-start | bytes 393224 | tf_op jit(solution)/shard_map/ppermute | solution.py:85
  78.0 2.5 %collective-permute-start.30 = (bf16[2,2,2,16,1024]{4,3,2,1,0:T(8,128)(2,1)S(1)}, bf16[2,2,2,16,1024]{4,3,2,1,0:T(8,128)(2,1)S(1)}, u32[]{:S(2)}, u32[]{:S(2)}) collective-permute-start(bf16[2,2,2,16,1024]{4,3,2,1,0:T(8,128)(2,1)S(1)} %pad_maximum_fusion.14), channel_id=1, source_target_pairs={{0,2},{2,0},{4,6},{6,4},{8,10},{10,8},{12,14},{14,12},{16,18},{18,... | collective-permute-start | bytes 786440 | tf_op jit(solution)/shard_map/ppermute | solution.py:85
  80.7 2.6 %collective-permute-start.22 = (bf16[2,2,2,16,1024]{4,3,2,1,0:T(8,128)(2,1)S(1)}, bf16[2,2,2,16,1024]{4,3,2,1,0:T(8,128)(2,1)S(1)}, u32[]{:S(2)}, u32[]{:S(2)}) collective-permute-start(bf16[2,2,2,16,1024]{4,3,2,1,0:T(8,128)(2,1)S(1)} %pad_maximum_fusion.11), channel_id=1, source_target_pairs={{0,16},{2,18},{4,20},{6,22},{8,24},{10,26},{12,28},{14,30},{16,0},... | collective-permute-start | bytes 786440 | tf_op jit(solution)/shard_map/ppermute | solution.py:85
  84.6 4.0 %collective-permute-start.6 = (bf16[2,2,2,16,1024]{4,3,2,1,0:T(8,128)(2,1)S(1)}, bf16[2,2,2,16,1024]{4,3,2,1,0:T(8,128)(2,1)S(1)}, u32[]{:S(2)}, u32[]{:S(2)}) collective-permute-start(bf16[2,2,2,16,1024]{4,3,2,1,0:T(8,128)(2,1)S(1)} %pad_maximum_fusion.5), channel_id=1, source_target_pairs={{0,4},{2,6},{4,0},{6,2},{8,12},{10,14},{12,8},{14,10},{16,20},{18,... | collective-permute-start | bytes 786440 | tf_op jit(solution)/shard_map/ppermute | solution.py:85
  88.7 1.6 %collective-permute-start.36 = (bf16[1,2,2,2,16,1024]{5,4,3,2,1,0:T(8,128)(2,1)S(1)}, bf16[1,2,2,2,16,1024]{5,4,3,2,1,0:T(8,128)(2,1)S(1)}, u32[]{:S(2)}, u32[]{:S(2)}) collective-permute-start(bf16[1,2,2,2,16,1024]{5,4,3,2,1,0:T(8,128)(2,1)S(1)} %maximum_bitcast_fusion.17), channel_id=1, source_target_pairs={{0,16},{2,18},{4,20},{6,22},{8,24},{10,26},{12,28},{14,30},{16,0},... | collective-permute-start | bytes 786440 | tf_op jit(solution)/shard_map/ppermute | solution.py:85
  90.3 7.3 %collective-permute-done.22 = bf16[2,2,2,16,1024]{4,3,2,1,0:T(8,128)(2,1)S(1)} collective-permute-done((bf16[2,2,2,16,1024]{4,3,2,1,0:T(8,128)(2,1)S(1)}, bf16[2,2,2,16,1024]{4,3,2,1,0:T(8,128)(2,1)S(1)}, u32[]{:S(2)}, u32[]{:S(2)}) %collective-permute-start.22) | collective-permute-done | bytes 262176 | tf_op jit(solution)/shard_map/ppermute | solution.py:85
  97.8 1.7 %collective-permute-start.34 = (bf16[1,2,2,2,16,1024]{5,4,3,2,1,0:T(8,128)(2,1)S(1)}, bf16[1,2,2,2,16,1024]{5,4,3,2,1,0:T(8,128)(2,1)S(1)}, u32[]{:S(2)}, u32[]{:S(2)}) collective-permute-start(bf16[1,2,2,2,16,1024]{5,4,3,2,1,0:T(8,128)(2,1)S(1)} %maximum_bitcast_fusion.15), channel_id=1, source_target_pairs={{0,4},{2,6},{4,0},{6,2},{8,12},{10,14},{12,8},{14,10},{16,20},{18,... | collective-permute-start | bytes 786440 | tf_op jit(solution)/shard_map/ppermute | solution.py:85
  101.9 3.3 %collective-permute-done.36 = bf16[1,2,2,2,16,1024]{5,4,3,2,1,0:T(8,128)(2,1)S(1)} collective-permute-done((bf16[1,2,2,2,16,1024]{5,4,3,2,1,0:T(8,128)(2,1)S(1)}, bf16[1,2,2,2,16,1024]{5,4,3,2,1,0:T(8,128)(2,1)S(1)}, u32[]{:S(2)}, u32[]{:S(2)}) %collective-permute-start.36) | collective-permute-done | bytes 262176 | tf_op jit(solution)/shard_map/ppermute | solution.py:85
  105.4 2.6 %collective-permute-done.35 = bf16[1,2,2,2,16,1024]{5,4,3,2,1,0:T(8,128)(2,1)S(1)} collective-permute-done((bf16[1,2,2,2,16,1024]{5,4,3,2,1,0:T(8,128)(2,1)S(1)}, bf16[1,2,2,2,16,1024]{5,4,3,2,1,0:T(8,128)(2,1)S(1)}, u32[]{:S(2)}, u32[]{:S(2)}) %collective-permute-start.35) | collective-permute-done | bytes 262176 | tf_op jit(solution)/shard_map/ppermute | solution.py:85
  108.1 1.3 collective-permute-start.15
  109.8 1.5 maximum_bitcast_fusion.1.blk_ref
  111.3 11.9 %shard_map.47 = (f32[4,4,1024]{2,1,0:T(4,128)}, f32[4,4,128]{2,1,0:T(4,128)}) custom-call(s32[64]{0:T(128)} %squeeze.19.meta_ref, bf16[1,1024,1024]{2,1,0:T(8,128)(2,1)} %maximum_bitcast_fusion.1.blk_ref, bf16[1024,1152]{1,0:T(8,128)(2,1)} %copy-done.3), custom_call_target="tpu_custom_call" | custom-call | flops 5435817984 | bytes 4521984 | tf_op jit(solution)/shard_map/pallas_call | solution.py:156
  124.7 1.5 maximum_bitcast_fusion.blk_ref
  126.2 11.9 %shard_map.46 = (f32[4,4,1024]{2,1,0:T(4,128)}, f32[4,4,128]{2,1,0:T(4,128)}) custom-call(s32[64]{0:T(128)} %squeeze.16.meta_ref, bf16[1,1024,1024]{2,1,0:T(8,128)(2,1)} %maximum_bitcast_fusion.blk_ref, bf16[1024,1152]{1,0:T(8,128)(2,1)} %copy-done.3), custom_call_target="tpu_custom_call" | custom-call | flops 5435817984 | bytes 4521984 | tf_op jit(solution)/shard_map/pallas_call | solution.py:156
  141.9 1.7 %collective-permute-start.39 = (f32[32]{0:T(128)S(1)}, f32[32]{0:T(128)S(1)}, u32[]{:S(2)}, u32[]{:S(2)}) collective-permute-start(f32[32]{0:T(128)S(1)} %fusion.11), channel_id=1, source_target_pairs={{0,6},{2,4},{4,2},{6,0},{8,14},{10,12},{12,10},{14,8},{16,22},{18,... | collective-permute-start | bytes 392 | tf_op jit(solution)/shard_map/ppermute | solution.py:33
  143.9 1.6 %collective-permute-start.41 = (f32[32]{0:T(128)S(1)}, f32[32]{0:T(128)S(1)}, u32[]{:S(2)}, u32[]{:S(2)}) collective-permute-start(f32[32]{0:T(128)S(1)} %fusion.11), channel_id=1, source_target_pairs={{0,2},{2,0},{4,6},{6,4},{8,10},{10,8},{12,14},{14,12},{16,18},{18,... | collective-permute-start | bytes 392 | tf_op jit(solution)/shard_map/ppermute | solution.py:33
  147.4 1.9 %collective-permute-start.42 = (f32[32]{0:T(128)S(1)}, f32[32]{0:T(128)S(1)}, u32[]{:S(2)}, u32[]{:S(2)}) collective-permute-start(f32[32]{0:T(128)S(1)} %fusion.27), channel_id=1, source_target_pairs={{0,24},{2,26},{4,28},{6,30},{8,16},{10,18},{12,20},{14,22},{16,8},... | collective-permute-start | bytes 392 | tf_op jit(solution)/shard_map/ppermute | solution.py:33
  149.4 1.3 collective-permute-start.43
  (263 shorter events, 48.3 us)
Async XLA Ops:
  1.7 26.9 %collective-permute-start.32 = (bf16[1024,128]{1,0:T(8,128)(2,1)}, bf16[1024,128]{1,0:T(8,128)(2,1)}, u32[]{:S(2)}, u32[]{:S(2)}) collective-permute-start(bf16[1024,128]{1,0:T(8,128)(2,1)} %slice.719), channel_id=1, source_target_pairs={{2,0},{4,2},{6,4},{8,6},{10,8},{12,10},{14,12},{16,14},{18,16},{20... | collective-permute-start | bytes 786440 | tf_op jit(solution)/shard_map/ppermute | solution.py:18
  6.6 32.1 %collective-permute-start.24 = (bf16[2,2,2,2,16,1024]{5,4,3,2,1,0:T(8,128)(2,1)}, bf16[2,2,2,2,16,1024]{5,4,3,2,1,0:T(8,128)(2,1)}, u32[]{:S(2)}, u32[]{:S(2)}) collective-permute-start(bf16[2,2,2,2,16,1024]{5,4,3,2,1,0:T(8,128)(2,1)} %pad_maximum_fusion.3), channel_id=1, source_target_pairs={{0,16},{2,18},{4,20},{6,22},{8,24},{10,26},{12,28},{14,30},{16,0},... | collective-permute-start | bytes 1572872 | tf_op jit(solution)/shard_map/ppermute | solution.py:75
  14.8 25.2 %collective-permute-start.16 = (bf16[2,2,2,2,16,1024]{5,4,3,2,1,0:T(8,128)(2,1)}, bf16[2,2,2,2,16,1024]{5,4,3,2,1,0:T(8,128)(2,1)}, u32[]{:S(2)}, u32[]{:S(2)}) collective-permute-start(bf16[2,2,2,2,16,1024]{5,4,3,2,1,0:T(8,128)(2,1)} %pad_maximum_fusion.2), channel_id=1, source_target_pairs={{0,8},{2,10},{4,12},{6,14},{8,0},{10,2},{12,4},{14,6},{16,24},{18,... | collective-permute-start | bytes 1572872 | tf_op jit(solution)/shard_map/ppermute | solution.py:75
  18.3 23.3 %collective-permute-start.8 = (bf16[2,2,2,2,16,1024]{5,4,3,2,1,0:T(8,128)(2,1)}, bf16[2,2,2,2,16,1024]{5,4,3,2,1,0:T(8,128)(2,1)}, u32[]{:S(2)}, u32[]{:S(2)}) collective-permute-start(bf16[2,2,2,2,16,1024]{5,4,3,2,1,0:T(8,128)(2,1)} %pad_maximum_fusion.1), channel_id=1, source_target_pairs={{0,4},{2,6},{4,0},{6,2},{8,12},{10,14},{12,8},{14,10},{16,20},{18,... | collective-permute-start | bytes 1572872 | tf_op jit(solution)/shard_map/ppermute | solution.py:75
  23.6 21.2 %collective-permute-start = (bf16[2,2,2,2,16,1024]{5,4,0,1,2,3:T(8,128)(2,1)}, bf16[2,2,2,2,16,1024]{5,4,0,1,2,3:T(8,128)(2,1)}, u32[]{:S(2)}, u32[]{:S(2)}) collective-permute-start(bf16[2,2,2,2,16,1024]{5,4,0,1,2,3:T(8,128)(2,1)} %pad_maximum_fusion), channel_id=1, source_target_pairs={{0,2},{2,0},{4,6},{6,4},{8,10},{10,8},{12,14},{14,12},{16,18},{18,... | collective-permute-start | bytes 1572872 | tf_op jit(solution)/shard_map/ppermute | solution.py:75
  39.9 8.3 %collective-permute-start.25 = (bf16[2,2,2,16,1024]{4,3,2,1,0:T(8,128)(2,1)S(1)}, bf16[2,2,2,16,1024]{4,3,2,1,0:T(8,128)(2,1)S(1)}, u32[]{:S(2)}, u32[]{:S(2)}) collective-permute-start(bf16[2,2,2,16,1024]{4,3,2,1,0:T(8,128)(2,1)S(1)} %pad_maximum_fusion.13), channel_id=1, source_target_pairs={{0,2},{2,0},{4,6},{6,4},{8,10},{10,8},{12,14},{14,12},{16,18},{18,... | collective-permute-start | bytes 786440 | tf_op jit(solution)/shard_map/ppermute | solution.py:75
  41.2 13.9 %collective-permute-start.17 = (bf16[2,2,2,16,1024]{4,3,2,1,0:T(8,128)(2,1)S(1)}, bf16[2,2,2,16,1024]{4,3,2,1,0:T(8,128)(2,1)S(1)}, u32[]{:S(2)}, u32[]{:S(2)}) collective-permute-start(bf16[2,2,2,16,1024]{4,3,2,1,0:T(8,128)(2,1)S(1)} %pad_maximum_fusion.10), channel_id=1, source_target_pairs={{0,16},{2,18},{4,20},{6,22},{8,24},{10,26},{12,28},{14,30},{16,0},... | collective-permute-start | bytes 786440 | tf_op jit(solution)/shard_map/ppermute | solution.py:75
  42.8 14.1 %collective-permute-start.9 = (bf16[2,2,2,16,1024]{4,3,2,1,0:T(8,128)(2,1)S(1)}, bf16[2,2,2,16,1024]{4,3,2,1,0:T(8,128)(2,1)S(1)}, u32[]{:S(2)}, u32[]{:S(2)}) collective-permute-start(bf16[2,2,2,16,1024]{4,3,2,1,0:T(8,128)(2,1)S(1)} %pad_maximum_fusion.7), channel_id=1, source_target_pairs={{0,8},{2,10},{4,12},{6,14},{8,0},{10,2},{12,4},{14,6},{16,24},{18,... | collective-permute-start | bytes 786440 | tf_op jit(solution)/shard_map/ppermute | solution.py:75
  47.0 10.1 %collective-permute-start.1 = (bf16[2,2,2,16,1024]{4,3,2,1,0:T(8,128)(2,1)S(1)}, bf16[2,2,2,16,1024]{4,3,2,1,0:T(8,128)(2,1)S(1)}, u32[]{:S(2)}, u32[]{:S(2)}) collective-permute-start(bf16[2,2,2,16,1024]{4,3,2,1,0:T(8,128)(2,1)S(1)} %pad_maximum_fusion.4), channel_id=1, source_target_pairs={{0,4},{2,6},{4,0},{6,2},{8,12},{10,14},{12,8},{14,10},{16,20},{18,... | collective-permute-start | bytes 786440 | tf_op jit(solution)/shard_map/ppermute | solution.py:75
  48.3 10.7 %collective-permute-start.26 = (bf16[2,2,16,1024]{3,2,1,0:T(8,128)(2,1)S(1)}, bf16[2,2,16,1024]{3,2,1,0:T(8,128)(2,1)S(1)}, u32[]{:S(2)}, u32[]{:S(2)}) collective-permute-start(bf16[2,2,16,1024]{3,2,1,0:T(8,128)(2,1)S(1)} %pad_maximum_fusion.30), channel_id=1, source_target_pairs={{0,4},{2,6},{4,0},{6,2},{8,12},{10,14},{12,8},{14,10},{16,20},{18,... | collective-permute-start | bytes 393224 | tf_op jit(solution)/shard_map/ppermute | solution.py:75
  57.0 7.5 %collective-permute-start.10 = (bf16[2,2,16,1024]{3,2,1,0:T(8,128)(2,1)S(1)}, bf16[2,2,16,1024]{3,2,1,0:T(8,128)(2,1)S(1)}, u32[]{:S(2)}, u32[]{:S(2)}) collective-permute-start(bf16[2,2,16,1024]{3,2,1,0:T(8,128)(2,1)S(1)} %pad_maximum_fusion.24), channel_id=1, source_target_pairs={{0,16},{2,18},{4,20},{6,22},{8,24},{10,26},{12,28},{14,30},{16,0},... | collective-permute-start | bytes 393224 | tf_op jit(solution)/shard_map/ppermute | solution.py:75
  57.3 8.6 %collective-permute-start.2 = (bf16[2,2,16,1024]{3,2,1,0:T(8,128)(2,1)S(1)}, bf16[2,2,16,1024]{3,2,1,0:T(8,128)(2,1)S(1)}, u32[]{:S(2)}, u32[]{:S(2)}) collective-permute-start(bf16[2,2,16,1024]{3,2,1,0:T(8,128)(2,1)S(1)} %pad_maximum_fusion.21), channel_id=1, source_target_pairs={{0,8},{2,10},{4,12},{6,14},{8,0},{10,2},{12,4},{14,6},{16,24},{18,... | collective-permute-start | bytes 393224 | tf_op jit(solution)/shard_map/ppermute | solution.py:75
  59.1 7.4 %collective-permute-start.27 = (bf16[2,16,1024]{2,1,0:T(8,128)(2,1)S(1)}, bf16[2,16,1024]{2,1,0:T(8,128)(2,1)S(1)}, u32[]{:S(2)}, u32[]{:S(2)}) collective-permute-start(bf16[2,16,1024]{2,1,0:T(8,128)(2,1)S(1)} %pad_maximum_fusion.49), channel_id=1, source_target_pairs={{0,8},{2,10},{4,12},{6,14},{8,0},{10,2},{12,4},{14,6},{16,24},{18,... | collective-permute-start | bytes 196616 | tf_op jit(solution)/shard_map/ppermute | solution.py:75
  60.6 8.4 %collective-permute-start.19 = (bf16[2,16,1024]{2,1,0:T(8,128)(2,1)S(1)}, bf16[2,16,1024]{2,1,0:T(8,128)(2,1)S(1)}, u32[]{:S(2)}, u32[]{:S(2)}) collective-permute-start(bf16[2,16,1024]{2,1,0:T(8,128)(2,1)S(1)} %pad_maximum_fusion.45), channel_id=1, source_target_pairs={{0,4},{2,6},{4,0},{6,2},{8,12},{10,14},{12,8},{14,10},{16,20},{18,... | collective-permute-start | bytes 196616 | tf_op jit(solution)/shard_map/ppermute | solution.py:75
  65.9 5.7 %collective-permute-start.3 = (bf16[2,16,1024]{2,1,0:T(8,128)(2,1)S(1)}, bf16[2,16,1024]{2,1,0:T(8,128)(2,1)S(1)}, u32[]{:S(2)}, u32[]{:S(2)}) collective-permute-start(bf16[2,16,1024]{2,1,0:T(8,128)(2,1)S(1)} %pad_maximum_fusion.37), channel_id=1, source_target_pairs={{0,16},{2,18},{4,20},{6,22},{8,24},{10,26},{12,28},{14,30},{16,0},... | collective-permute-start | bytes 196616 | tf_op jit(solution)/shard_map/ppermute | solution.py:75
  71.7 6.1 %collective-permute-start.4 = (bf16[2,16,1024]{2,1,0:T(8,128)(2,1)S(1)}, bf16[2,16,1024]{2,1,0:T(8,128)(2,1)S(1)}, u32[]{:S(2)}, u32[]{:S(2)}) collective-permute-start(bf16[2,16,1024]{2,1,0:T(8,128)(2,1)S(1)} %pad_maximum_fusion.38), channel_id=1, source_target_pairs={{0,16},{2,18},{4,20},{6,22},{8,24},{10,26},{12,28},{14,30},{16,0},... | collective-permute-start | bytes 196616 | tf_op jit(solution)/shard_map/ppermute | solution.py:85
  72.1 5.8 %collective-permute-start.29 = (bf16[2,2,16,1024]{3,2,1,0:T(8,128)(2,1)S(1)}, bf16[2,2,16,1024]{3,2,1,0:T(8,128)(2,1)S(1)}, u32[]{:S(2)}, u32[]{:S(2)}) collective-permute-start(bf16[2,2,16,1024]{3,2,1,0:T(8,128)(2,1)S(1)} %pad_maximum_fusion.31), channel_id=1, source_target_pairs={{0,4},{2,6},{4,0},{6,2},{8,12},{10,14},{12,8},{14,10},{16,20},{18,... | collective-permute-start | bytes 393224 | tf_op jit(solution)/shard_map/ppermute | solution.py:85
  74.1 6.5 %collective-permute-start.21 = (bf16[2,2,16,1024]{3,2,1,0:T(8,128)(2,1)S(1)}, bf16[2,2,16,1024]{3,2,1,0:T(8,128)(2,1)S(1)}, u32[]{:S(2)}, u32[]{:S(2)}) collective-permute-start(bf16[2,2,16,1024]{3,2,1,0:T(8,128)(2,1)S(1)} %pad_maximum_fusion.28), channel_id=1, source_target_pairs={{0,2},{2,0},{4,6},{6,4},{8,10},{10,8},{12,14},{14,12},{16,18},{18,... | collective-permute-start | bytes 393224 | tf_op jit(solution)/shard_map/ppermute | solution.py:85
  74.7 9.1 %collective-permute-start.13 = (bf16[2,2,16,1024]{3,2,1,0:T(8,128)(2,1)S(1)}, bf16[2,2,16,1024]{3,2,1,0:T(8,128)(2,1)S(1)}, u32[]{:S(2)}, u32[]{:S(2)}) collective-permute-start(bf16[2,2,16,1024]{3,2,1,0:T(8,128)(2,1)S(1)} %pad_maximum_fusion.25), channel_id=1, source_target_pairs={{0,16},{2,18},{4,20},{6,22},{8,24},{10,26},{12,28},{14,30},{16,0},... | collective-permute-start | bytes 393224 | tf_op jit(solution)/shard_map/ppermute | solution.py:85
  77.8 6.6 %collective-permute-start.5 = (bf16[2,2,16,1024]{3,2,1,0:T(8,128)(2,1)S(1)}, bf16[2,2,16,1024]{3,2,1,0:T(8,128)(2,1)S(1)}, u32[]{:S(2)}, u32[]{:S(2)}) collective-permute-start(bf16[2,2,16,1024]{3,2,1,0:T(8,128)(2,1)S(1)} %pad_maximum_fusion.22), channel_id=1, source_target_pairs={{0,8},{2,10},{4,12},{6,14},{8,0},{10,2},{12,4},{14,6},{16,24},{18,... | collective-permute-start | bytes 393224 | tf_op jit(solution)/shard_map/ppermute | solution.py:85
  78.0 10.6 %collective-permute-start.30 = (bf16[2,2,2,16,1024]{4,3,2,1,0:T(8,128)(2,1)S(1)}, bf16[2,2,2,16,1024]{4,3,2,1,0:T(8,128)(2,1)S(1)}, u32[]{:S(2)}, u32[]{:S(2)}) collective-permute-start(bf16[2,2,2,16,1024]{4,3,2,1,0:T(8,128)(2,1)S(1)} %pad_maximum_fusion.14), channel_id=1, source_target_pairs={{0,2},{2,0},{4,6},{6,4},{8,10},{10,8},{12,14},{14,12},{16,18},{18,... | collective-permute-start | bytes 786440 | tf_op jit(solution)/shard_map/ppermute | solution.py:85
  80.7 16.8 %collective-permute-start.22 = (bf16[2,2,2,16,1024]{4,3,2,1,0:T(8,128)(2,1)S(1)}, bf16[2,2,2,16,1024]{4,3,2,1,0:T(8,128)(2,1)S(1)}, u32[]{:S(2)}, u32[]{:S(2)}) collective-permute-start(bf16[2,2,2,16,1024]{4,3,2,1,0:T(8,128)(2,1)S(1)} %pad_maximum_fusion.11), channel_id=1, source_target_pairs={{0,16},{2,18},{4,20},{6,22},{8,24},{10,26},{12,28},{14,30},{16,0},... | collective-permute-start | bytes 786440 | tf_op jit(solution)/shard_map/ppermute | solution.py:85
  83.8 13.9 %collective-permute-start.14 = (bf16[2,2,2,16,1024]{4,3,2,1,0:T(8,128)(2,1)S(1)}, bf16[2,2,2,16,1024]{4,3,2,1,0:T(8,128)(2,1)S(1)}, u32[]{:S(2)}, u32[]{:S(2)}) collective-permute-start(bf16[2,2,2,16,1024]{4,3,2,1,0:T(8,128)(2,1)S(1)} %pad_maximum_fusion.8), channel_id=1, source_target_pairs={{0,8},{2,10},{4,12},{6,14},{8,0},{10,2},{12,4},{14,6},{16,24},{18,... | collective-permute-start | bytes 786440 | tf_op jit(solution)/shard_map/ppermute | solution.py:85
  84.6 14.9 %collective-permute-start.6 = (bf16[2,2,2,16,1024]{4,3,2,1,0:T(8,128)(2,1)S(1)}, bf16[2,2,2,16,1024]{4,3,2,1,0:T(8,128)(2,1)S(1)}, u32[]{:S(2)}, u32[]{:S(2)}) collective-permute-start(bf16[2,2,2,16,1024]{4,3,2,1,0:T(8,128)(2,1)S(1)} %pad_maximum_fusion.5), channel_id=1, source_target_pairs={{0,4},{2,6},{4,0},{6,2},{8,12},{10,14},{12,8},{14,10},{16,20},{18,... | collective-permute-start | bytes 786440 | tf_op jit(solution)/shard_map/ppermute | solution.py:85
  88.7 16.6 %collective-permute-start.36 = (bf16[1,2,2,2,16,1024]{5,4,3,2,1,0:T(8,128)(2,1)S(1)}, bf16[1,2,2,2,16,1024]{5,4,3,2,1,0:T(8,128)(2,1)S(1)}, u32[]{:S(2)}, u32[]{:S(2)}) collective-permute-start(bf16[1,2,2,2,16,1024]{5,4,3,2,1,0:T(8,128)(2,1)S(1)} %maximum_bitcast_fusion.17), channel_id=1, source_target_pairs={{0,16},{2,18},{4,20},{6,22},{8,24},{10,26},{12,28},{14,30},{16,0},... | collective-permute-start | bytes 786440 | tf_op jit(solution)/shard_map/ppermute | solution.py:85
  97.6 10.3 %collective-permute-start.35 = (bf16[1,2,2,2,16,1024]{5,4,3,2,1,0:T(8,128)(2,1)S(1)}, bf16[1,2,2,2,16,1024]{5,4,3,2,1,0:T(8,128)(2,1)S(1)}, u32[]{:S(2)}, u32[]{:S(2)}) collective-permute-start(bf16[1,2,2,2,16,1024]{5,4,3,2,1,0:T(8,128)(2,1)S(1)} %maximum_bitcast_fusion.16), channel_id=1, source_target_pairs={{0,8},{2,10},{4,12},{6,14},{8,0},{10,2},{12,4},{14,6},{16,24},{18,... | collective-permute-start | bytes 786440 | tf_op jit(solution)/shard_map/ppermute | solution.py:85
  97.8 10.3 %collective-permute-start.34 = (bf16[1,2,2,2,16,1024]{5,4,3,2,1,0:T(8,128)(2,1)S(1)}, bf16[1,2,2,2,16,1024]{5,4,3,2,1,0:T(8,128)(2,1)S(1)}, u32[]{:S(2)}, u32[]{:S(2)}) collective-permute-start(bf16[1,2,2,2,16,1024]{5,4,3,2,1,0:T(8,128)(2,1)S(1)} %maximum_bitcast_fusion.15), channel_id=1, source_target_pairs={{0,4},{2,6},{4,0},{6,2},{8,12},{10,14},{12,8},{14,10},{16,20},{18,... | collective-permute-start | bytes 786440 | tf_op jit(solution)/shard_map/ppermute | solution.py:85
  99.6 10.0 %collective-permute-start.33 = (bf16[1,2,2,2,16,1024]{5,4,3,2,1,0:T(8,128)(2,1)S(1)}, bf16[1,2,2,2,16,1024]{5,4,3,2,1,0:T(8,128)(2,1)S(1)}, u32[]{:S(2)}, u32[]{:S(2)}) collective-permute-start(bf16[1,2,2,2,16,1024]{5,4,3,2,1,0:T(8,128)(2,1)S(1)} %maximum_bitcast_fusion.14), channel_id=1, source_target_pairs={{0,2},{2,0},{4,6},{6,4},{8,10},{10,8},{12,14},{14,12},{16,18},{18,... | collective-permute-start | bytes 786440 | tf_op jit(solution)/shard_map/ppermute | solution.py:85
  100.6 9.0 %collective-permute-start.7 = (bf16[1,2,2,2,16,1024]{5,4,3,2,1,0:T(8,128)(2,1)S(1)}, bf16[1,2,2,2,16,1024]{5,4,3,2,1,0:T(8,128)(2,1)S(1)}, u32[]{:S(2)}, u32[]{:S(2)}) collective-permute-start(bf16[1,2,2,2,16,1024]{5,4,3,2,1,0:T(8,128)(2,1)S(1)} %maximum_bitcast_fusion.10), channel_id=1, source_target_pairs={{0,2},{2,0},{4,6},{6,4},{8,10},{10,8},{12,14},{14,12},{16,18},{18,... | collective-permute-start | bytes 786440 | tf_op jit(solution)/shard_map/ppermute | solution.py:85
  105.2 18.8 %collective-permute-start.31 = (bf16[1,2,2,2,16,1024]{5,4,3,2,1,0:T(8,128)(2,1)S(1)}, bf16[1,2,2,2,16,1024]{5,4,3,2,1,0:T(8,128)(2,1)S(1)}, u32[]{:S(2)}, u32[]{:S(2)}) collective-permute-start(bf16[1,2,2,2,16,1024]{5,4,3,2,1,0:T(8,128)(2,1)S(1)} %maximum_bitcast_fusion.13), channel_id=1, source_target_pairs={{0,16},{2,18},{4,20},{6,22},{8,24},{10,26},{12,28},{14,30},{16,0},... | collective-permute-start | bytes 786440 | tf_op jit(solution)/shard_map/ppermute | solution.py:85
  107.9 16.3 %collective-permute-start.23 = (bf16[1,2,2,2,16,1024]{5,4,3,2,1,0:T(8,128)(2,1)S(1)}, bf16[1,2,2,2,16,1024]{5,4,3,2,1,0:T(8,128)(2,1)S(1)}, u32[]{:S(2)}, u32[]{:S(2)}) collective-permute-start(bf16[1,2,2,2,16,1024]{5,4,3,2,1,0:T(8,128)(2,1)S(1)} %maximum_bitcast_fusion.12), channel_id=1, source_target_pairs={{0,8},{2,10},{4,12},{6,14},{8,0},{10,2},{12,4},{14,6},{16,24},{18,... | collective-permute-start | bytes 786440 | tf_op jit(solution)/shard_map/ppermute | solution.py:85
  108.1 16.3 %collective-permute-start.15 = (bf16[1,2,2,2,16,1024]{5,4,3,2,1,0:T(8,128)(2,1)S(1)}, bf16[1,2,2,2,16,1024]{5,4,3,2,1,0:T(8,128)(2,1)S(1)}, u32[]{:S(2)}, u32[]{:S(2)}) collective-permute-start(bf16[1,2,2,2,16,1024]{5,4,3,2,1,0:T(8,128)(2,1)S(1)} %maximum_bitcast_fusion.11), channel_id=1, source_target_pairs={{0,4},{2,6},{4,0},{6,2},{8,12},{10,14},{12,8},{14,10},{16,20},{18,... | collective-permute-start | bytes 786440 | tf_op jit(solution)/shard_map/ppermute | solution.py:85
  (22 other events, 112.5 us)

commit v14 on v13

--- a/solution.py
+++ b/solution.py
@@ -6,7 +6,7 @@
 from jax.sharding import PartitionSpec as P
 
 L = 128
-GROUP = 4
+GROUP = 8
 REACH = L + 16
 
 EPS = 1e-06

time: 156 us -> 164 us (1.051)
  waiting for transfers between devices: 41.1 us -> 50.9 us
  local copies, waits for them, and re-layouts: 15 us -> 13.3 us
    ppermute x36, waiting for transfers between devices: 35.9 us -> 46 us  [spread_blocks(): lax.ppermute(jnp.stack([v for _, v in items]), axis, [(i, i ^ mask) for i...]
    reshape x2 -> x0, local copies, waits for them, and re-layouts: 1.73 us -> none  [correlate(): corr.reshape(rounds * count, lag_count)]
    unnamed x23 -> x25, local copies, waits for them, and re-layouts: 4.15 us -> 4.17 us
  transfers between devices with their start and end apart: 45 -> 45, of which waited for: 21 -> 21; matrix products, arithmetic and copies ran while one was open for 18% -> 16% of each run, Pallas kernels for 8% -> 0%
where the time goes in v14:
time: 164 us
  starting transfers between devices  53.1 us (32%)
  waiting for transfers between devices  50.9 us (31%)
  Pallas kernels  23.4 us (14%)
  other arithmetic  18.9 us (12%)
  local copies, waits for them, and re-layouts  13.3 us (8%)
  between operations  2.67 us (2%)
    ppermute x36, waiting for transfers between devices, spread_blocks(): lax.ppermute(jnp.stack([v for _, v in items]), axis, [(i, i ^ mask) for i...  46 us
    ppermute x36, starting transfers between devices, spread_blocks(): lax.ppermute(jnp.stack([v for _, v in items]), axis, [(i, i ^ mask) for i...  43.3 us
    pallas_call x2, Pallas kernels, correlate(): pl.pallas_call(correlate_kernel, grid_spec=grid_spec, out_shape=[jax.Shap...  23.4 us
    ppermute x8, starting transfers between devices, group_sum(): got[d] = lax.ppermute(value, axis, pairs)  8.56 us
    select_n x18, other arithmetic, spread_blocks(): bufs[key] = jnp.where(holder, keeps[key], got[n])  5.66 us
    ppermute x8, waiting for transfers between devices, group_sum(): got[d] = lax.ppermute(value, axis, pairs)  4.85 us
    another operation x52, other arithmetic, spread_blocks(): jnp.stack([v for _, v in items])  4.25 us
    unnamed x25, local copies, waits for them, and re-layouts  4.17 us
  transfers between devices with their start and end apart: 45, of which 21 were waited for; matrix products, arithmetic and copies ran while one was open for 16% of the time, Pallas kernels for 0%

profile of v14, /device:TPU:0, one launch (start us, length us, event | category | flops | bytes accessed | tf_op | source)
XLA Modules:
  0.0 163.7 jit_solution(1147327555290676149)
XLA Ops:
  0.0 1.7 %slice.719 = bf16[1024,128]{1,0:T(8,128)(2,1)} slice(bf16[1024,1024]{1,0:T(8,128)(2,1)} %param.4), slice={[0:1024], [0:128]} | slice | bytes 524288 | tf_op jit(solution)/shard_map/slice | solution.py:183
  3.0 2.5 %fusion.28 = (bf16[1024,256]{1,0:T(8,128)(2,1)}, bf16[1024,256]{1,0:T(8,128)(2,1)S(1)}, bf16[1024,256]{1,0:T(8,128)(2,1)S(1)}, bf16[1024,256]{1,0:T(8,128)(2,1)S(1)}) fusion(bf16[1024,1024]{1,0:T(8,128)(2,1)} %param.4), kind=kLoop, calls=%fused_computation.302 | loop fusion | bytes 4194304 | tf_op jit(solution)/shard_map/slice | solution.py:61
  6.6 7.0 %collective-permute-start.24 = (bf16[2,2,2,2,16,1024]{5,4,3,2,1,0:T(8,128)(2,1)}, bf16[2,2,2,2,16,1024]{5,4,3,2,1,0:T(8,128)(2,1)}, u32[]{:S(2)}, u32[]{:S(2)}) collective-permute-start(bf16[2,2,2,2,16,1024]{5,4,3,2,1,0:T(8,128)(2,1)} %pad_maximum_fusion.3), channel_id=1, source_target_pairs={{0,16},{2,18},{4,20},{6,22},{8,24},{10,26},{12,28},{14,30},{16,0},... | collective-permute-start | bytes 1572872 | tf_op jit(solution)/shard_map/ppermute | solution.py:75
  14.8 1.6 collective-permute-start.16
  18.9 2.0 %copy.66 = bf16[1024,256]{0,1:T(8,128)(2,1)} copy(bf16[1024,256]{1,0:T(8,128)(2,1)} %get-tuple-element.17) | data formatting | bytes 1048576
  21.0 1.8 %fusion.29 = (bf16[1,2,2,2,16,1024]{5,4,0,1,2,3:T(8,128)(2,1)S(1)}, bf16[1,2,2,2,16,1024]{5,4,0,1,2,3:T(8,128)(2,1)S(1)}, bf16[1,2,2,2,16,1024]{5,4,0,1,2,3:T(8,128)(2,1)}) fusion(bf16[2,2,2,2,16,1024]{5,4,0,1,2,3:T(8,128)(2,1)} %bitcast.298, pred[]{:T(512)S(6)} %eq.170), kind=kLoop, calls=%fused_computation.303 | loop fusion | flops 131072 | bytes 1310721 | tf_op jit(solution)/shard_map/slice | solution.py:72
  32.6 6.2 %collective-permute-done.24 = bf16[2,2,2,2,16,1024]{5,4,3,2,1,0:T(8,128)(2,1)} collective-permute-done((bf16[2,2,2,2,16,1024]{5,4,3,2,1,0:T(8,128)(2,1)}, bf16[2,2,2,2,16,1024]{5,4,3,2,1,0:T(8,128)(2,1)}, u32[]{:S(2)}, u32[]{:S(2)}) %collective-permute-start.24) | collective-permute-done | bytes 524320 | tf_op jit(solution)/shard_map/ppermute | solution.py:75
  42.8 2.0 %collective-permute-start.9 = (bf16[2,2,2,16,1024]{4,3,2,1,0:T(8,128)(2,1)S(1)}, bf16[2,2,2,16,1024]{4,3,2,1,0:T(8,128)(2,1)S(1)}, u32[]{:S(2)}, u32[]{:S(2)}) collective-permute-start(bf16[2,2,2,16,1024]{4,3,2,1,0:T(8,128)(2,1)S(1)} %pad_maximum_fusion.7), channel_id=1, source_target_pairs={{0,8},{2,10},{4,12},{6,14},{8,0},{10,2},{12,4},{14,6},{16,24},{18,... | collective-permute-start | bytes 786440 | tf_op jit(solution)/shard_map/ppermute | solution.py:75
  49.2 5.8 %collective-permute-done.17 = bf16[2,2,2,16,1024]{4,3,2,1,0:T(8,128)(2,1)S(1)} collective-permute-done((bf16[2,2,2,16,1024]{4,3,2,1,0:T(8,128)(2,1)S(1)}, bf16[2,2,2,16,1024]{4,3,2,1,0:T(8,128)(2,1)S(1)}, u32[]{:S(2)}, u32[]{:S(2)}) %collective-permute-start.17) | collective-permute-done | bytes 262176 | tf_op jit(solution)/shard_map/ppermute | solution.py:75
  55.1 1.8 %collective-permute-start.18 = (bf16[2,2,16,1024]{3,2,1,0:T(8,128)(2,1)S(1)}, bf16[2,2,16,1024]{3,2,1,0:T(8,128)(2,1)S(1)}, u32[]{:S(2)}, u32[]{:S(2)}) collective-permute-start(bf16[2,2,16,1024]{3,2,1,0:T(8,128)(2,1)S(1)} %pad_maximum_fusion.27), channel_id=1, source_target_pairs={{0,2},{2,0},{4,6},{6,4},{8,10},{10,8},{12,14},{14,12},{16,18},{18,... | collective-permute-start | bytes 393224 | tf_op jit(solution)/shard_map/ppermute | solution.py:75
  57.3 1.8 %collective-permute-start.2 = (bf16[2,2,16,1024]{3,2,1,0:T(8,128)(2,1)S(1)}, bf16[2,2,16,1024]{3,2,1,0:T(8,128)(2,1)S(1)}, u32[]{:S(2)}, u32[]{:S(2)}) collective-permute-start(bf16[2,2,16,1024]{3,2,1,0:T(8,128)(2,1)S(1)} %pad_maximum_fusion.21), channel_id=1, source_target_pairs={{0,8},{2,10},{4,12},{6,14},{8,0},{10,2},{12,4},{14,6},{16,24},{18,... | collective-permute-start | bytes 393224 | tf_op jit(solution)/shard_map/ppermute | solution.py:75
  60.6 3.9 %collective-permute-done.10 = bf16[2,2,16,1024]{3,2,1,0:T(8,128)(2,1)S(1)} collective-permute-done((bf16[2,2,16,1024]{3,2,1,0:T(8,128)(2,1)S(1)}, bf16[2,2,16,1024]{3,2,1,0:T(8,128)(2,1)S(1)}, u32[]{:S(2)}, u32[]{:S(2)}) %collective-permute-start.10) | collective-permute-done | bytes 131104 | tf_op jit(solution)/shard_map/ppermute | solution.py:75
  66.6 2.4 %collective-permute-start.28 = (bf16[2,16,1024]{2,1,0:T(8,128)(2,1)S(1)}, bf16[2,16,1024]{2,1,0:T(8,128)(2,1)S(1)}, u32[]{:S(2)}, u32[]{:S(2)}) collective-permute-start(bf16[2,16,1024]{2,1,0:T(8,128)(2,1)S(1)} %pad_maximum_fusion.50), channel_id=1, source_target_pairs={{0,8},{2,10},{4,12},{6,14},{8,0},{10,2},{12,4},{14,6},{16,24},{18,... | collective-permute-start | bytes 196616 | tf_op jit(solution)/shard_map/ppermute | solution.py:85
  72.6 1.4 collective-permute-done.20
  74.7 2.0 %collective-permute-start.13 = (bf16[2,2,16,1024]{3,2,1,0:T(8,128)(2,1)S(1)}, bf16[2,2,16,1024]{3,2,1,0:T(8,128)(2,1)S(1)}, u32[]{:S(2)}, u32[]{:S(2)}) collective-permute-start(bf16[2,2,16,1024]{3,2,1,0:T(8,128)(2,1)S(1)} %pad_maximum_fusion.25), channel_id=1, source_target_pairs={{0,16},{2,18},{4,20},{6,22},{8,24},{10,26},{12,28},{14,30},{16,0},... | collective-permute-start | bytes 393224 | tf_op jit(solution)/shard_map/ppermute | solution.py:85
  78.0 2.5 %collective-permute-start.30 = (bf16[2,2,2,16,1024]{4,3,2,1,0:T(8,128)(2,1)S(1)}, bf16[2,2,2,16,1024]{4,3,2,1,0:T(8,128)(2,1)S(1)}, u32[]{:S(2)}, u32[]{:S(2)}) collective-permute-start(bf16[2,2,2,16,1024]{4,3,2,1,0:T(8,128)(2,1)S(1)} %pad_maximum_fusion.14), channel_id=1, source_target_pairs={{0,2},{2,0},{4,6},{6,4},{8,10},{10,8},{12,14},{14,12},{16,18},{18,... | collective-permute-start | bytes 786440 | tf_op jit(solution)/shard_map/ppermute | solution.py:85
  80.7 2.6 %collective-permute-start.22 = (bf16[2,2,2,16,1024]{4,3,2,1,0:T(8,128)(2,1)S(1)}, bf16[2,2,2,16,1024]{4,3,2,1,0:T(8,128)(2,1)S(1)}, u32[]{:S(2)}, u32[]{:S(2)}) collective-permute-start(bf16[2,2,2,16,1024]{4,3,2,1,0:T(8,128)(2,1)S(1)} %pad_maximum_fusion.11), channel_id=1, source_target_pairs={{0,16},{2,18},{4,20},{6,22},{8,24},{10,26},{12,28},{14,30},{16,0},... | collective-permute-start | bytes 786440 | tf_op jit(solution)/shard_map/ppermute | solution.py:85
  84.6 4.0 %collective-permute-start.6 = (bf16[2,2,2,16,1024]{4,3,2,1,0:T(8,128)(2,1)S(1)}, bf16[2,2,2,16,1024]{4,3,2,1,0:T(8,128)(2,1)S(1)}, u32[]{:S(2)}, u32[]{:S(2)}) collective-permute-start(bf16[2,2,2,16,1024]{4,3,2,1,0:T(8,128)(2,1)S(1)} %pad_maximum_fusion.5), channel_id=1, source_target_pairs={{0,4},{2,6},{4,0},{6,2},{8,12},{10,14},{12,8},{14,10},{16,20},{18,... | collective-permute-start | bytes 786440 | tf_op jit(solution)/shard_map/ppermute | solution.py:85
  88.6 1.6 collective-permute-start.36
  90.2 7.3 %collective-permute-done.22 = bf16[2,2,2,16,1024]{4,3,2,1,0:T(8,128)(2,1)S(1)} collective-permute-done((bf16[2,2,2,16,1024]{4,3,2,1,0:T(8,128)(2,1)S(1)}, bf16[2,2,2,16,1024]{4,3,2,1,0:T(8,128)(2,1)S(1)}, u32[]{:S(2)}, u32[]{:S(2)}) %collective-permute-start.22) | collective-permute-done | bytes 262176 | tf_op jit(solution)/shard_map/ppermute | solution.py:85
  97.8 1.7 %collective-permute-start.34 = (bf16[1,2,2,2,16,1024]{5,4,3,2,1,0:T(8,128)(2,1)S(1)}, bf16[1,2,2,2,16,1024]{5,4,3,2,1,0:T(8,128)(2,1)S(1)}, u32[]{:S(2)}, u32[]{:S(2)}) collective-permute-start(bf16[1,2,2,2,16,1024]{5,4,3,2,1,0:T(8,128)(2,1)S(1)} %maximum_bitcast_fusion.15), channel_id=1, source_target_pairs={{0,4},{2,6},{4,0},{6,2},{8,12},{10,14},{12,8},{14,10},{16,20},{18,... | collective-permute-start | bytes 786440 | tf_op jit(solution)/shard_map/ppermute | solution.py:85
  101.9 3.4 %collective-permute-done.36 = bf16[1,2,2,2,16,1024]{5,4,3,2,1,0:T(8,128)(2,1)S(1)} collective-permute-done((bf16[1,2,2,2,16,1024]{5,4,3,2,1,0:T(8,128)(2,1)S(1)}, bf16[1,2,2,2,16,1024]{5,4,3,2,1,0:T(8,128)(2,1)S(1)}, u32[]{:S(2)}, u32[]{:S(2)}) %collective-permute-start.36) | collective-permute-done | bytes 262176 | tf_op jit(solution)/shard_map/ppermute | solution.py:85
  105.4 2.6 %collective-permute-done.35 = bf16[1,2,2,2,16,1024]{5,4,3,2,1,0:T(8,128)(2,1)S(1)} collective-permute-done((bf16[1,2,2,2,16,1024]{5,4,3,2,1,0:T(8,128)(2,1)S(1)}, bf16[1,2,2,2,16,1024]{5,4,3,2,1,0:T(8,128)(2,1)S(1)}, u32[]{:S(2)}, u32[]{:S(2)}) %collective-permute-start.35) | collective-permute-done | bytes 262176 | tf_op jit(solution)/shard_map/ppermute | solution.py:85
  109.8 8.2 %collective-permute-done.31 = bf16[1,2,2,2,16,1024]{5,4,3,2,1,0:T(8,128)(2,1)S(1)} collective-permute-done((bf16[1,2,2,2,16,1024]{5,4,3,2,1,0:T(8,128)(2,1)S(1)}, bf16[1,2,2,2,16,1024]{5,4,3,2,1,0:T(8,128)(2,1)S(1)}, u32[]{:S(2)}, u32[]{:S(2)}) %collective-permute-start.31) | collective-permute-done | bytes 262176 | tf_op jit(solution)/shard_map/ppermute | solution.py:85
  118.1 2.0 %collective-permute-done.23 = bf16[1,2,2,2,16,1024]{5,4,3,2,1,0:T(8,128)(2,1)S(1)} collective-permute-done((bf16[1,2,2,2,16,1024]{5,4,3,2,1,0:T(8,128)(2,1)S(1)}, bf16[1,2,2,2,16,1024]{5,4,3,2,1,0:T(8,128)(2,1)S(1)}, u32[]{:S(2)}, u32[]{:S(2)}) %collective-permute-start.23) | collective-permute-done | bytes 262176 | tf_op jit(solution)/shard_map/ppermute | solution.py:85
  120.5 1.5 maximum_bitcast_fusion.1.blk_ref
  122.0 11.7 %shard_map.47 = (f32[2,8,1024]{2,1,0:T(8,128)}, f32[2,8,128]{2,1,0:T(8,128)}) custom-call(s32[64]{0:T(128)} %squeeze.19.meta_ref, bf16[1,1024,1024]{2,1,0:T(8,128)(2,1)} %maximum_bitcast_fusion.1.blk_ref, bf16[1024,1152]{1,0:T(8,128)(2,1)} %copy-done.3), custom_call_target="tpu_custom_call" | custom-call | flops 5435817984 | bytes 4521984 | tf_op jit(solution)/shard_map/pallas_call | solution.py:156
  133.7 1.5 maximum_bitcast_fusion.blk_ref
  135.2 11.7 %shard_map.46 = (f32[2,8,1024]{2,1,0:T(8,128)}, f32[2,8,128]{2,1,0:T(8,128)}) custom-call(s32[64]{0:T(128)} %squeeze.16.meta_ref, bf16[1,1024,1024]{2,1,0:T(8,128)(2,1)} %maximum_bitcast_fusion.blk_ref, bf16[1024,1152]{1,0:T(8,128)(2,1)} %copy-done.3), custom_call_target="tpu_custom_call" | custom-call | flops 5435817984 | bytes 4521984 | tf_op jit(solution)/shard_map/pallas_call | solution.py:156
  150.9 2.3 %collective-permute-start.40 = (f32[32]{0:T(128)S(1)}, f32[32]{0:T(128)S(1)}, u32[]{:S(2)}, u32[]{:S(2)}) collective-permute-start(f32[32]{0:T(128)S(1)} %fusion.11), channel_id=1, source_target_pairs={{0,4},{2,6},{4,0},{6,2},{8,12},{10,14},{12,8},{14,10},{16,20},{18,... | collective-permute-start | bytes 392 | tf_op jit(solution)/shard_map/ppermute | solution.py:33
  155.2 1.6 collective-permute-done.41
  157.9 3.4 %collective-permute-start.44 = (f32[32]{0:T(128)S(1)}, f32[32]{0:T(128)S(1)}, u32[]{:S(2)}, u32[]{:S(2)}) collective-permute-start(f32[32]{0:T(128)S(1)} %fusion.27), channel_id=1, source_target_pairs={{0,8},{2,10},{4,12},{6,14},{8,0},{10,2},{12,4},{14,6},{16,24},{18,... | collective-permute-start | bytes 392 | tf_op jit(solution)/shard_map/ppermute | solution.py:33
  (263 shorter events, 47.7 us)
Async XLA Ops:
  1.7 27.1 %collective-permute-start.32 = (bf16[1024,128]{1,0:T(8,128)(2,1)}, bf16[1024,128]{1,0:T(8,128)(2,1)}, u32[]{:S(2)}, u32[]{:S(2)}) collective-permute-start(bf16[1024,128]{1,0:T(8,128)(2,1)} %slice.719), channel_id=1, source_target_pairs={{2,0},{4,2},{6,4},{8,6},{10,8},{12,10},{14,12},{16,14},{18,16},{20... | collective-permute-start | bytes 786440 | tf_op jit(solution)/shard_map/ppermute | solution.py:18
  6.6 32.1 %collective-permute-start.24 = (bf16[2,2,2,2,16,1024]{5,4,3,2,1,0:T(8,128)(2,1)}, bf16[2,2,2,2,16,1024]{5,4,3,2,1,0:T(8,128)(2,1)}, u32[]{:S(2)}, u32[]{:S(2)}) collective-permute-start(bf16[2,2,2,2,16,1024]{5,4,3,2,1,0:T(8,128)(2,1)} %pad_maximum_fusion.3), channel_id=1, source_target_pairs={{0,16},{2,18},{4,20},{6,22},{8,24},{10,26},{12,28},{14,30},{16,0},... | collective-permute-start | bytes 1572872 | tf_op jit(solution)/shard_map/ppermute | solution.py:75
  14.8 25.2 %collective-permute-start.16 = (bf16[2,2,2,2,16,1024]{5,4,3,2,1,0:T(8,128)(2,1)}, bf16[2,2,2,2,16,1024]{5,4,3,2,1,0:T(8,128)(2,1)}, u32[]{:S(2)}, u32[]{:S(2)}) collective-permute-start(bf16[2,2,2,2,16,1024]{5,4,3,2,1,0:T(8,128)(2,1)} %pad_maximum_fusion.2), channel_id=1, source_target_pairs={{0,8},{2,10},{4,12},{6,14},{8,0},{10,2},{12,4},{14,6},{16,24},{18,... | collective-permute-start | bytes 1572872 | tf_op jit(solution)/shard_map/ppermute | solution.py:75
  18.3 23.3 %collective-permute-start.8 = (bf16[2,2,2,2,16,1024]{5,4,3,2,1,0:T(8,128)(2,1)}, bf16[2,2,2,2,16,1024]{5,4,3,2,1,0:T(8,128)(2,1)}, u32[]{:S(2)}, u32[]{:S(2)}) collective-permute-start(bf16[2,2,2,2,16,1024]{5,4,3,2,1,0:T(8,128)(2,1)} %pad_maximum_fusion.1), channel_id=1, source_target_pairs={{0,4},{2,6},{4,0},{6,2},{8,12},{10,14},{12,8},{14,10},{16,20},{18,... | collective-permute-start | bytes 1572872 | tf_op jit(solution)/shard_map/ppermute | solution.py:75
  23.6 21.1 %collective-permute-start = (bf16[2,2,2,2,16,1024]{5,4,0,1,2,3:T(8,128)(2,1)}, bf16[2,2,2,2,16,1024]{5,4,0,1,2,3:T(8,128)(2,1)}, u32[]{:S(2)}, u32[]{:S(2)}) collective-permute-start(bf16[2,2,2,2,16,1024]{5,4,0,1,2,3:T(8,128)(2,1)} %pad_maximum_fusion), channel_id=1, source_target_pairs={{0,2},{2,0},{4,6},{6,4},{8,10},{10,8},{12,14},{14,12},{16,18},{18,... | collective-permute-start | bytes 1572872 | tf_op jit(solution)/shard_map/ppermute | solution.py:75
  39.9 8.3 %collective-permute-start.25 = (bf16[2,2,2,16,1024]{4,3,2,1,0:T(8,128)(2,1)S(1)}, bf16[2,2,2,16,1024]{4,3,2,1,0:T(8,128)(2,1)S(1)}, u32[]{:S(2)}, u32[]{:S(2)}) collective-permute-start(bf16[2,2,2,16,1024]{4,3,2,1,0:T(8,128)(2,1)S(1)} %pad_maximum_fusion.13), channel_id=1, source_target_pairs={{0,2},{2,0},{4,6},{6,4},{8,10},{10,8},{12,14},{14,12},{16,18},{18,... | collective-permute-start | bytes 786440 | tf_op jit(solution)/shard_map/ppermute | solution.py:75
  41.2 13.9 %collective-permute-start.17 = (bf16[2,2,2,16,1024]{4,3,2,1,0:T(8,128)(2,1)S(1)}, bf16[2,2,2,16,1024]{4,3,2,1,0:T(8,128)(2,1)S(1)}, u32[]{:S(2)}, u32[]{:S(2)}) collective-permute-start(bf16[2,2,2,16,1024]{4,3,2,1,0:T(8,128)(2,1)S(1)} %pad_maximum_fusion.10), channel_id=1, source_target_pairs={{0,16},{2,18},{4,20},{6,22},{8,24},{10,26},{12,28},{14,30},{16,0},... | collective-permute-start | bytes 786440 | tf_op jit(solution)/shard_map/ppermute | solution.py:75
  42.8 14.1 %collective-permute-start.9 = (bf16[2,2,2,16,1024]{4,3,2,1,0:T(8,128)(2,1)S(1)}, bf16[2,2,2,16,1024]{4,3,2,1,0:T(8,128)(2,1)S(1)}, u32[]{:S(2)}, u32[]{:S(2)}) collective-permute-start(bf16[2,2,2,16,1024]{4,3,2,1,0:T(8,128)(2,1)S(1)} %pad_maximum_fusion.7), channel_id=1, source_target_pairs={{0,8},{2,10},{4,12},{6,14},{8,0},{10,2},{12,4},{14,6},{16,24},{18,... | collective-permute-start | bytes 786440 | tf_op jit(solution)/shard_map/ppermute | solution.py:75
  47.0 10.1 %collective-permute-start.1 = (bf16[2,2,2,16,1024]{4,3,2,1,0:T(8,128)(2,1)S(1)}, bf16[2,2,2,16,1024]{4,3,2,1,0:T(8,128)(2,1)S(1)}, u32[]{:S(2)}, u32[]{:S(2)}) collective-permute-start(bf16[2,2,2,16,1024]{4,3,2,1,0:T(8,128)(2,1)S(1)} %pad_maximum_fusion.4), channel_id=1, source_target_pairs={{0,4},{2,6},{4,0},{6,2},{8,12},{10,14},{12,8},{14,10},{16,20},{18,... | collective-permute-start | bytes 786440 | tf_op jit(solution)/shard_map/ppermute | solution.py:75
  48.3 10.7 %collective-permute-start.26 = (bf16[2,2,16,1024]{3,2,1,0:T(8,128)(2,1)S(1)}, bf16[2,2,16,1024]{3,2,1,0:T(8,128)(2,1)S(1)}, u32[]{:S(2)}, u32[]{:S(2)}) collective-permute-start(bf16[2,2,16,1024]{3,2,1,0:T(8,128)(2,1)S(1)} %pad_maximum_fusion.30), channel_id=1, source_target_pairs={{0,4},{2,6},{4,0},{6,2},{8,12},{10,14},{12,8},{14,10},{16,20},{18,... | collective-permute-start | bytes 393224 | tf_op jit(solution)/shard_map/ppermute | solution.py:75
  57.0 7.5 %collective-permute-start.10 = (bf16[2,2,16,1024]{3,2,1,0:T(8,128)(2,1)S(1)}, bf16[2,2,16,1024]{3,2,1,0:T(8,128)(2,1)S(1)}, u32[]{:S(2)}, u32[]{:S(2)}) collective-permute-start(bf16[2,2,16,1024]{3,2,1,0:T(8,128)(2,1)S(1)} %pad_maximum_fusion.24), channel_id=1, source_target_pairs={{0,16},{2,18},{4,20},{6,22},{8,24},{10,26},{12,28},{14,30},{16,0},... | collective-permute-start | bytes 393224 | tf_op jit(solution)/shard_map/ppermute | solution.py:75
  57.3 8.6 %collective-permute-start.2 = (bf16[2,2,16,1024]{3,2,1,0:T(8,128)(2,1)S(1)}, bf16[2,2,16,1024]{3,2,1,0:T(8,128)(2,1)S(1)}, u32[]{:S(2)}, u32[]{:S(2)}) collective-permute-start(bf16[2,2,16,1024]{3,2,1,0:T(8,128)(2,1)S(1)} %pad_maximum_fusion.21), channel_id=1, source_target_pairs={{0,8},{2,10},{4,12},{6,14},{8,0},{10,2},{12,4},{14,6},{16,24},{18,... | collective-permute-start | bytes 393224 | tf_op jit(solution)/shard_map/ppermute | solution.py:75
  59.1 7.4 %collective-permute-start.27 = (bf16[2,16,1024]{2,1,0:T(8,128)(2,1)S(1)}, bf16[2,16,1024]{2,1,0:T(8,128)(2,1)S(1)}, u32[]{:S(2)}, u32[]{:S(2)}) collective-permute-start(bf16[2,16,1024]{2,1,0:T(8,128)(2,1)S(1)} %pad_maximum_fusion.49), channel_id=1, source_target_pairs={{0,8},{2,10},{4,12},{6,14},{8,0},{10,2},{12,4},{14,6},{16,24},{18,... | collective-permute-start | bytes 196616 | tf_op jit(solution)/shard_map/ppermute | solution.py:75
  60.6 8.4 %collective-permute-start.19 = (bf16[2,16,1024]{2,1,0:T(8,128)(2,1)S(1)}, bf16[2,16,1024]{2,1,0:T(8,128)(2,1)S(1)}, u32[]{:S(2)}, u32[]{:S(2)}) collective-permute-start(bf16[2,16,1024]{2,1,0:T(8,128)(2,1)S(1)} %pad_maximum_fusion.45), channel_id=1, source_target_pairs={{0,4},{2,6},{4,0},{6,2},{8,12},{10,14},{12,8},{14,10},{16,20},{18,... | collective-permute-start | bytes 196616 | tf_op jit(solution)/shard_map/ppermute | solution.py:75
  65.9 5.7 %collective-permute-start.3 = (bf16[2,16,1024]{2,1,0:T(8,128)(2,1)S(1)}, bf16[2,16,1024]{2,1,0:T(8,128)(2,1)S(1)}, u32[]{:S(2)}, u32[]{:S(2)}) collective-permute-start(bf16[2,16,1024]{2,1,0:T(8,128)(2,1)S(1)} %pad_maximum_fusion.37), channel_id=1, source_target_pairs={{0,16},{2,18},{4,20},{6,22},{8,24},{10,26},{12,28},{14,30},{16,0},... | collective-permute-start | bytes 196616 | tf_op jit(solution)/shard_map/ppermute | solution.py:75
  71.6 6.1 %collective-permute-start.4 = (bf16[2,16,1024]{2,1,0:T(8,128)(2,1)S(1)}, bf16[2,16,1024]{2,1,0:T(8,128)(2,1)S(1)}, u32[]{:S(2)}, u32[]{:S(2)}) collective-permute-start(bf16[2,16,1024]{2,1,0:T(8,128)(2,1)S(1)} %pad_maximum_fusion.38), channel_id=1, source_target_pairs={{0,16},{2,18},{4,20},{6,22},{8,24},{10,26},{12,28},{14,30},{16,0},... | collective-permute-start | bytes 196616 | tf_op jit(solution)/shard_map/ppermute | solution.py:85
  72.1 5.8 %collective-permute-start.29 = (bf16[2,2,16,1024]{3,2,1,0:T(8,128)(2,1)S(1)}, bf16[2,2,16,1024]{3,2,1,0:T(8,128)(2,1)S(1)}, u32[]{:S(2)}, u32[]{:S(2)}) collective-permute-start(bf16[2,2,16,1024]{3,2,1,0:T(8,128)(2,1)S(1)} %pad_maximum_fusion.31), channel_id=1, source_target_pairs={{0,4},{2,6},{4,0},{6,2},{8,12},{10,14},{12,8},{14,10},{16,20},{18,... | collective-permute-start | bytes 393224 | tf_op jit(solution)/shard_map/ppermute | solution.py:85
  74.1 6.5 %collective-permute-start.21 = (bf16[2,2,16,1024]{3,2,1,0:T(8,128)(2,1)S(1)}, bf16[2,2,16,1024]{3,2,1,0:T(8,128)(2,1)S(1)}, u32[]{:S(2)}, u32[]{:S(2)}) collective-permute-start(bf16[2,2,16,1024]{3,2,1,0:T(8,128)(2,1)S(1)} %pad_maximum_fusion.28), channel_id=1, source_target_pairs={{0,2},{2,0},{4,6},{6,4},{8,10},{10,8},{12,14},{14,12},{16,18},{18,... | collective-permute-start | bytes 393224 | tf_op jit(solution)/shard_map/ppermute | solution.py:85
  74.7 9.1 %collective-permute-start.13 = (bf16[2,2,16,1024]{3,2,1,0:T(8,128)(2,1)S(1)}, bf16[2,2,16,1024]{3,2,1,0:T(8,128)(2,1)S(1)}, u32[]{:S(2)}, u32[]{:S(2)}) collective-permute-start(bf16[2,2,16,1024]{3,2,1,0:T(8,128)(2,1)S(1)} %pad_maximum_fusion.25), channel_id=1, source_target_pairs={{0,16},{2,18},{4,20},{6,22},{8,24},{10,26},{12,28},{14,30},{16,0},... | collective-permute-start | bytes 393224 | tf_op jit(solution)/shard_map/ppermute | solution.py:85
  77.8 6.6 %collective-permute-start.5 = (bf16[2,2,16,1024]{3,2,1,0:T(8,128)(2,1)S(1)}, bf16[2,2,16,1024]{3,2,1,0:T(8,128)(2,1)S(1)}, u32[]{:S(2)}, u32[]{:S(2)}) collective-permute-start(bf16[2,2,16,1024]{3,2,1,0:T(8,128)(2,1)S(1)} %pad_maximum_fusion.22), channel_id=1, source_target_pairs={{0,8},{2,10},{4,12},{6,14},{8,0},{10,2},{12,4},{14,6},{16,24},{18,... | collective-permute-start | bytes 393224 | tf_op jit(solution)/shard_map/ppermute | solution.py:85
  78.0 10.5 %collective-permute-start.30 = (bf16[2,2,2,16,1024]{4,3,2,1,0:T(8,128)(2,1)S(1)}, bf16[2,2,2,16,1024]{4,3,2,1,0:T(8,128)(2,1)S(1)}, u32[]{:S(2)}, u32[]{:S(2)}) collective-permute-start(bf16[2,2,2,16,1024]{4,3,2,1,0:T(8,128)(2,1)S(1)} %pad_maximum_fusion.14), channel_id=1, source_target_pairs={{0,2},{2,0},{4,6},{6,4},{8,10},{10,8},{12,14},{14,12},{16,18},{18,... | collective-permute-start | bytes 786440 | tf_op jit(solution)/shard_map/ppermute | solution.py:85
  80.7 16.9 %collective-permute-start.22 = (bf16[2,2,2,16,1024]{4,3,2,1,0:T(8,128)(2,1)S(1)}, bf16[2,2,2,16,1024]{4,3,2,1,0:T(8,128)(2,1)S(1)}, u32[]{:S(2)}, u32[]{:S(2)}) collective-permute-start(bf16[2,2,2,16,1024]{4,3,2,1,0:T(8,128)(2,1)S(1)} %pad_maximum_fusion.11), channel_id=1, source_target_pairs={{0,16},{2,18},{4,20},{6,22},{8,24},{10,26},{12,28},{14,30},{16,0},... | collective-permute-start | bytes 786440 | tf_op jit(solution)/shard_map/ppermute | solution.py:85
  83.9 13.8 %collective-permute-start.14 = (bf16[2,2,2,16,1024]{4,3,2,1,0:T(8,128)(2,1)S(1)}, bf16[2,2,2,16,1024]{4,3,2,1,0:T(8,128)(2,1)S(1)}, u32[]{:S(2)}, u32[]{:S(2)}) collective-permute-start(bf16[2,2,2,16,1024]{4,3,2,1,0:T(8,128)(2,1)S(1)} %pad_maximum_fusion.8), channel_id=1, source_target_pairs={{0,8},{2,10},{4,12},{6,14},{8,0},{10,2},{12,4},{14,6},{16,24},{18,... | collective-permute-start | bytes 786440 | tf_op jit(solution)/shard_map/ppermute | solution.py:85
  84.6 14.9 %collective-permute-start.6 = (bf16[2,2,2,16,1024]{4,3,2,1,0:T(8,128)(2,1)S(1)}, bf16[2,2,2,16,1024]{4,3,2,1,0:T(8,128)(2,1)S(1)}, u32[]{:S(2)}, u32[]{:S(2)}) collective-permute-start(bf16[2,2,2,16,1024]{4,3,2,1,0:T(8,128)(2,1)S(1)} %pad_maximum_fusion.5), channel_id=1, source_target_pairs={{0,4},{2,6},{4,0},{6,2},{8,12},{10,14},{12,8},{14,10},{16,20},{18,... | collective-permute-start | bytes 786440 | tf_op jit(solution)/shard_map/ppermute | solution.py:85
  88.6 16.6 %collective-permute-start.36 = (bf16[1,2,2,2,16,1024]{5,4,3,2,1,0:T(8,128)(2,1)S(1)}, bf16[1,2,2,2,16,1024]{5,4,3,2,1,0:T(8,128)(2,1)S(1)}, u32[]{:S(2)}, u32[]{:S(2)}) collective-permute-start(bf16[1,2,2,2,16,1024]{5,4,3,2,1,0:T(8,128)(2,1)S(1)} %maximum_bitcast_fusion.17), channel_id=1, source_target_pairs={{0,16},{2,18},{4,20},{6,22},{8,24},{10,26},{12,28},{14,30},{16,0},... | collective-permute-start | bytes 786440 | tf_op jit(solution)/shard_map/ppermute | solution.py:85
  97.6 10.3 %collective-permute-start.35 = (bf16[1,2,2,2,16,1024]{5,4,3,2,1,0:T(8,128)(2,1)S(1)}, bf16[1,2,2,2,16,1024]{5,4,3,2,1,0:T(8,128)(2,1)S(1)}, u32[]{:S(2)}, u32[]{:S(2)}) collective-permute-start(bf16[1,2,2,2,16,1024]{5,4,3,2,1,0:T(8,128)(2,1)S(1)} %maximum_bitcast_fusion.16), channel_id=1, source_target_pairs={{0,8},{2,10},{4,12},{6,14},{8,0},{10,2},{12,4},{14,6},{16,24},{18,... | collective-permute-start | bytes 786440 | tf_op jit(solution)/shard_map/ppermute | solution.py:85
  97.8 10.3 %collective-permute-start.34 = (bf16[1,2,2,2,16,1024]{5,4,3,2,1,0:T(8,128)(2,1)S(1)}, bf16[1,2,2,2,16,1024]{5,4,3,2,1,0:T(8,128)(2,1)S(1)}, u32[]{:S(2)}, u32[]{:S(2)}) collective-permute-start(bf16[1,2,2,2,16,1024]{5,4,3,2,1,0:T(8,128)(2,1)S(1)} %maximum_bitcast_fusion.15), channel_id=1, source_target_pairs={{0,4},{2,6},{4,0},{6,2},{8,12},{10,14},{12,8},{14,10},{16,20},{18,... | collective-permute-start | bytes 786440 | tf_op jit(solution)/shard_map/ppermute | solution.py:85
  99.6 10.0 %collective-permute-start.33 = (bf16[1,2,2,2,16,1024]{5,4,3,2,1,0:T(8,128)(2,1)S(1)}, bf16[1,2,2,2,16,1024]{5,4,3,2,1,0:T(8,128)(2,1)S(1)}, u32[]{:S(2)}, u32[]{:S(2)}) collective-permute-start(bf16[1,2,2,2,16,1024]{5,4,3,2,1,0:T(8,128)(2,1)S(1)} %maximum_bitcast_fusion.14), channel_id=1, source_target_pairs={{0,2},{2,0},{4,6},{6,4},{8,10},{10,8},{12,14},{14,12},{16,18},{18,... | collective-permute-start | bytes 786440 | tf_op jit(solution)/shard_map/ppermute | solution.py:85
  100.6 9.0 %collective-permute-start.7 = (bf16[1,2,2,2,16,1024]{5,4,3,2,1,0:T(8,128)(2,1)S(1)}, bf16[1,2,2,2,16,1024]{5,4,3,2,1,0:T(8,128)(2,1)S(1)}, u32[]{:S(2)}, u32[]{:S(2)}) collective-permute-start(bf16[1,2,2,2,16,1024]{5,4,3,2,1,0:T(8,128)(2,1)S(1)} %maximum_bitcast_fusion.10), channel_id=1, source_target_pairs={{0,2},{2,0},{4,6},{6,4},{8,10},{10,8},{12,14},{14,12},{16,18},{18,... | collective-permute-start | bytes 786440 | tf_op jit(solution)/shard_map/ppermute | solution.py:85
  105.2 12.7 %collective-permute-start.31 = (bf16[1,2,2,2,16,1024]{5,4,3,2,1,0:T(8,128)(2,1)S(1)}, bf16[1,2,2,2,16,1024]{5,4,3,2,1,0:T(8,128)(2,1)S(1)}, u32[]{:S(2)}, u32[]{:S(2)}) collective-permute-start(bf16[1,2,2,2,16,1024]{5,4,3,2,1,0:T(8,128)(2,1)S(1)} %maximum_bitcast_fusion.13), channel_id=1, source_target_pairs={{0,16},{2,18},{4,20},{6,22},{8,24},{10,26},{12,28},{14,30},{16,0},... | collective-permute-start | bytes 786440 | tf_op jit(solution)/shard_map/ppermute | solution.py:85
  107.9 12.2 %collective-permute-start.23 = (bf16[1,2,2,2,16,1024]{5,4,3,2,1,0:T(8,128)(2,1)S(1)}, bf16[1,2,2,2,16,1024]{5,4,3,2,1,0:T(8,128)(2,1)S(1)}, u32[]{:S(2)}, u32[]{:S(2)}) collective-permute-start(bf16[1,2,2,2,16,1024]{5,4,3,2,1,0:T(8,128)(2,1)S(1)} %maximum_bitcast_fusion.12), channel_id=1, source_target_pairs={{0,8},{2,10},{4,12},{6,14},{8,0},{10,2},{12,4},{14,6},{16,24},{18,... | collective-permute-start | bytes 786440 | tf_op jit(solution)/shard_map/ppermute | solution.py:85
  108.1 12.2 %collective-permute-start.15 = (bf16[1,2,2,2,16,1024]{5,4,3,2,1,0:T(8,128)(2,1)S(1)}, bf16[1,2,2,2,16,1024]{5,4,3,2,1,0:T(8,128)(2,1)S(1)}, u32[]{:S(2)}, u32[]{:S(2)}) collective-permute-start(bf16[1,2,2,2,16,1024]{5,4,3,2,1,0:T(8,128)(2,1)S(1)} %maximum_bitcast_fusion.11), channel_id=1, source_target_pairs={{0,4},{2,6},{4,0},{6,2},{8,12},{10,14},{12,8},{14,10},{16,20},{18,... | collective-permute-start | bytes 786440 | tf_op jit(solution)/shard_map/ppermute | solution.py:85
  (23 other events, 126.5 us)

commit v15 on v13

--- a/solution.py
+++ b/solution.py
@@ -7,7 +7,7 @@
 
 L = 128
 GROUP = 4
-REACH = L + 16
+REACH = L + 8
 
 EPS = 1e-06
 
@@ -115,7 +115,7 @@
         shift = meta_ref[4 * idx + 1]
         lower = meta_ref[4 * idx + 2]
         upper = meta_ref[4 * idx + 3]
-        rows = blk_ref[0, pl.ds(pl.multiple_of(first, 16), REACH), :]
+        rows = blk_ref[0, pl.ds(pl.multiple_of(first, 8), REACH), :]
         pick = (col == shift + (L - 1) - tap).astype(jnp.bfloat16)
         chosen = jnp.dot(pick, rows, preferred_element_type=jnp.float32)
         chosen = jnp.where((lane >= lower) & (lane < upper), chosen, 0.0)
@@ -189,7 +189,7 @@
 
     blocks = spread_blocks(signal, round_shard, "tm")
     offs = jnp.clip(offsets, 0, lag_count - L)
-    first = jnp.minimum((offs // 16) * 16, lag_count - REACH)
+    first = jnp.minimum((offs // 8) * 8, lag_count - REACH)
     base = section * chan_local
     meta = jnp.stack([first, offs - first, lower - base, upper - base], axis=-1).reshape(-1)
 

time: 156 us -> 156 us (level)
  no operation moved by 1% of the time
where the time goes in v15:
time: 156 us; the launch traced here: 155 us
  starting transfers between devices  53.1 us (34%)
  waiting for transfers between devices  41.1 us (26%)
  Pallas kernels  23.8 us (15%)
  other arithmetic  18.1 us (12%)
  local copies, waits for them, and re-layouts  15 us (10%)
  between operations  2.62 us (2%)
    ppermute x36, starting transfers between devices, spread_blocks(): lax.ppermute(jnp.stack([v for _, v in items]), axis, [(i, i ^ mask) for i...  43.3 us
    ppermute x36, waiting for transfers between devices, spread_blocks(): lax.ppermute(jnp.stack([v for _, v in items]), axis, [(i, i ^ mask) for i...  35.9 us
    pallas_call x2, Pallas kernels, correlate(): pl.pallas_call(correlate_kernel, grid_spec=grid_spec, out_shape=[jax.Shap...  23.8 us
    ppermute x8, starting transfers between devices, group_sum(): got[d] = lax.ppermute(value, axis, pairs)  8.57 us
    select_n x18, other arithmetic, spread_blocks(): bufs[key] = jnp.where(holder, keeps[key], got[n])  5.7 us
    ppermute x8, waiting for transfers between devices, group_sum(): got[d] = lax.ppermute(value, axis, pairs)  5.13 us
    another operation x52, other arithmetic, spread_blocks(): jnp.stack([v for _, v in items])  4.23 us
    unnamed x23, local copies, waits for them, and re-layouts  4.15 us
  transfers between devices with their start and end apart: 45, of which 21 were waited for; matrix products, arithmetic and copies ran while one was open for 18% of the time, Pallas kernels for 8%

profile of v15, /device:TPU:0, one launch (start us, length us, event | category | flops | bytes accessed | tf_op | source)
XLA Modules:
  0.0 155.1 jit_solution(4685931445692438105)
XLA Ops:
  0.0 1.7 %slice.719 = bf16[1024,128]{1,0:T(8,128)(2,1)} slice(bf16[1024,1024]{1,0:T(8,128)(2,1)} %param.4), slice={[0:1024], [0:128]} | slice | bytes 524288 | tf_op jit(solution)/shard_map/slice | solution.py:183
  3.0 2.5 %fusion.28 = (bf16[1024,256]{1,0:T(8,128)(2,1)}, bf16[1024,256]{1,0:T(8,128)(2,1)S(1)}, bf16[1024,256]{1,0:T(8,128)(2,1)S(1)}, bf16[1024,256]{1,0:T(8,128)(2,1)S(1)}) fusion(bf16[1024,1024]{1,0:T(8,128)(2,1)} %param.4), kind=kLoop, calls=%fused_computation.302 | loop fusion | bytes 4194304 | tf_op jit(solution)/shard_map/slice | solution.py:61
  6.6 7.0 %collective-permute-start.24 = (bf16[2,2,2,2,16,1024]{5,4,3,2,1,0:T(8,128)(2,1)}, bf16[2,2,2,2,16,1024]{5,4,3,2,1,0:T(8,128)(2,1)}, u32[]{:S(2)}, u32[]{:S(2)}) collective-permute-start(bf16[2,2,2,2,16,1024]{5,4,3,2,1,0:T(8,128)(2,1)} %pad_maximum_fusion.3), channel_id=1, source_target_pairs={{0,16},{2,18},{4,20},{6,22},{8,24},{10,26},{12,28},{14,30},{16,0},... | collective-permute-start | bytes 1572872 | tf_op jit(solution)/shard_map/ppermute | solution.py:75
  14.8 1.6 %collective-permute-start.16 = (bf16[2,2,2,2,16,1024]{5,4,3,2,1,0:T(8,128)(2,1)}, bf16[2,2,2,2,16,1024]{5,4,3,2,1,0:T(8,128)(2,1)}, u32[]{:S(2)}, u32[]{:S(2)}) collective-permute-start(bf16[2,2,2,2,16,1024]{5,4,3,2,1,0:T(8,128)(2,1)} %pad_maximum_fusion.2), channel_id=1, source_target_pairs={{0,8},{2,10},{4,12},{6,14},{8,0},{10,2},{12,4},{14,6},{16,24},{18,... | collective-permute-start | bytes 1572872 | tf_op jit(solution)/shard_map/ppermute | solution.py:75
  18.9 2.0 %copy.66 = bf16[1024,256]{0,1:T(8,128)(2,1)} copy(bf16[1024,256]{1,0:T(8,128)(2,1)} %get-tuple-element.17) | data formatting | bytes 1048576
  20.9 1.8 %fusion.29 = (bf16[1,2,2,2,16,1024]{5,4,0,1,2,3:T(8,128)(2,1)S(1)}, bf16[1,2,2,2,16,1024]{5,4,0,1,2,3:T(8,128)(2,1)S(1)}, bf16[1,2,2,2,16,1024]{5,4,0,1,2,3:T(8,128)(2,1)}) fusion(bf16[2,2,2,2,16,1024]{5,4,0,1,2,3:T(8,128)(2,1)} %bitcast.296, pred[]{:T(512)S(6)} %eq.170), kind=kLoop, calls=%fused_computation.303 | loop fusion | flops 131072 | bytes 1310721 | tf_op jit(solution)/shard_map/slice | solution.py:72
  32.4 6.3 %collective-permute-done.24 = bf16[2,2,2,2,16,1024]{5,4,3,2,1,0:T(8,128)(2,1)} collective-permute-done((bf16[2,2,2,2,16,1024]{5,4,3,2,1,0:T(8,128)(2,1)}, bf16[2,2,2,2,16,1024]{5,4,3,2,1,0:T(8,128)(2,1)}, u32[]{:S(2)}, u32[]{:S(2)}) %collective-permute-start.24) | collective-permute-done | bytes 524320 | tf_op jit(solution)/shard_map/ppermute | solution.py:75
  42.8 2.0 %collective-permute-start.9 = (bf16[2,2,2,16,1024]{4,3,2,1,0:T(8,128)(2,1)S(1)}, bf16[2,2,2,16,1024]{4,3,2,1,0:T(8,128)(2,1)S(1)}, u32[]{:S(2)}, u32[]{:S(2)}) collective-permute-start(bf16[2,2,2,16,1024]{4,3,2,1,0:T(8,128)(2,1)S(1)} %pad_maximum_fusion.7), channel_id=1, source_target_pairs={{0,8},{2,10},{4,12},{6,14},{8,0},{10,2},{12,4},{14,6},{16,24},{18,... | collective-permute-start | bytes 786440 | tf_op jit(solution)/shard_map/ppermute | solution.py:75
  49.2 5.8 %collective-permute-done.17 = bf16[2,2,2,16,1024]{4,3,2,1,0:T(8,128)(2,1)S(1)} collective-permute-done((bf16[2,2,2,16,1024]{4,3,2,1,0:T(8,128)(2,1)S(1)}, bf16[2,2,2,16,1024]{4,3,2,1,0:T(8,128)(2,1)S(1)}, u32[]{:S(2)}, u32[]{:S(2)}) %collective-permute-start.17) | collective-permute-done | bytes 262176 | tf_op jit(solution)/shard_map/ppermute | solution.py:75
  55.1 1.8 %collective-permute-start.18 = (bf16[2,2,16,1024]{3,2,1,0:T(8,128)(2,1)S(1)}, bf16[2,2,16,1024]{3,2,1,0:T(8,128)(2,1)S(1)}, u32[]{:S(2)}, u32[]{:S(2)}) collective-permute-start(bf16[2,2,16,1024]{3,2,1,0:T(8,128)(2,1)S(1)} %pad_maximum_fusion.27), channel_id=1, source_target_pairs={{0,2},{2,0},{4,6},{6,4},{8,10},{10,8},{12,14},{14,12},{16,18},{18,... | collective-permute-start | bytes 393224 | tf_op jit(solution)/shard_map/ppermute | solution.py:75
  57.3 1.8 %collective-permute-start.2 = (bf16[2,2,16,1024]{3,2,1,0:T(8,128)(2,1)S(1)}, bf16[2,2,16,1024]{3,2,1,0:T(8,128)(2,1)S(1)}, u32[]{:S(2)}, u32[]{:S(2)}) collective-permute-start(bf16[2,2,16,1024]{3,2,1,0:T(8,128)(2,1)S(1)} %pad_maximum_fusion.21), channel_id=1, source_target_pairs={{0,8},{2,10},{4,12},{6,14},{8,0},{10,2},{12,4},{14,6},{16,24},{18,... | collective-permute-start | bytes 393224 | tf_op jit(solution)/shard_map/ppermute | solution.py:75
  60.6 3.9 %collective-permute-done.10 = bf16[2,2,16,1024]{3,2,1,0:T(8,128)(2,1)S(1)} collective-permute-done((bf16[2,2,16,1024]{3,2,1,0:T(8,128)(2,1)S(1)}, bf16[2,2,16,1024]{3,2,1,0:T(8,128)(2,1)S(1)}, u32[]{:S(2)}, u32[]{:S(2)}) %collective-permute-start.10) | collective-permute-done | bytes 131104 | tf_op jit(solution)/shard_map/ppermute | solution.py:75
  66.6 2.4 %collective-permute-start.28 = (bf16[2,16,1024]{2,1,0:T(8,128)(2,1)S(1)}, bf16[2,16,1024]{2,1,0:T(8,128)(2,1)S(1)}, u32[]{:S(2)}, u32[]{:S(2)}) collective-permute-start(bf16[2,16,1024]{2,1,0:T(8,128)(2,1)S(1)} %pad_maximum_fusion.50), channel_id=1, source_target_pairs={{0,8},{2,10},{4,12},{6,14},{8,0},{10,2},{12,4},{14,6},{16,24},{18,... | collective-permute-start | bytes 196616 | tf_op jit(solution)/shard_map/ppermute | solution.py:85
  72.6 1.4 collective-permute-done.20
  74.7 2.0 %collective-permute-start.13 = (bf16[2,2,16,1024]{3,2,1,0:T(8,128)(2,1)S(1)}, bf16[2,2,16,1024]{3,2,1,0:T(8,128)(2,1)S(1)}, u32[]{:S(2)}, u32[]{:S(2)}) collective-permute-start(bf16[2,2,16,1024]{3,2,1,0:T(8,128)(2,1)S(1)} %pad_maximum_fusion.25), channel_id=1, source_target_pairs={{0,16},{2,18},{4,20},{6,22},{8,24},{10,26},{12,28},{14,30},{16,0},... | collective-permute-start | bytes 393224 | tf_op jit(solution)/shard_map/ppermute | solution.py:85
  78.0 2.5 %collective-permute-start.30 = (bf16[2,2,2,16,1024]{4,3,2,1,0:T(8,128)(2,1)S(1)}, bf16[2,2,2,16,1024]{4,3,2,1,0:T(8,128)(2,1)S(1)}, u32[]{:S(2)}, u32[]{:S(2)}) collective-permute-start(bf16[2,2,2,16,1024]{4,3,2,1,0:T(8,128)(2,1)S(1)} %pad_maximum_fusion.14), channel_id=1, source_target_pairs={{0,2},{2,0},{4,6},{6,4},{8,10},{10,8},{12,14},{14,12},{16,18},{18,... | collective-permute-start | bytes 786440 | tf_op jit(solution)/shard_map/ppermute | solution.py:85
  80.7 2.6 %collective-permute-start.22 = (bf16[2,2,2,16,1024]{4,3,2,1,0:T(8,128)(2,1)S(1)}, bf16[2,2,2,16,1024]{4,3,2,1,0:T(8,128)(2,1)S(1)}, u32[]{:S(2)}, u32[]{:S(2)}) collective-permute-start(bf16[2,2,2,16,1024]{4,3,2,1,0:T(8,128)(2,1)S(1)} %pad_maximum_fusion.11), channel_id=1, source_target_pairs={{0,16},{2,18},{4,20},{6,22},{8,24},{10,26},{12,28},{14,30},{16,0},... | collective-permute-start | bytes 786440 | tf_op jit(solution)/shard_map/ppermute | solution.py:85
  84.6 4.0 %collective-permute-start.6 = (bf16[2,2,2,16,1024]{4,3,2,1,0:T(8,128)(2,1)S(1)}, bf16[2,2,2,16,1024]{4,3,2,1,0:T(8,128)(2,1)S(1)}, u32[]{:S(2)}, u32[]{:S(2)}) collective-permute-start(bf16[2,2,2,16,1024]{4,3,2,1,0:T(8,128)(2,1)S(1)} %pad_maximum_fusion.5), channel_id=1, source_target_pairs={{0,4},{2,6},{4,0},{6,2},{8,12},{10,14},{12,8},{14,10},{16,20},{18,... | collective-permute-start | bytes 786440 | tf_op jit(solution)/shard_map/ppermute | solution.py:85
  88.7 1.6 %collective-permute-start.36 = (bf16[1,2,2,2,16,1024]{5,4,3,2,1,0:T(8,128)(2,1)S(1)}, bf16[1,2,2,2,16,1024]{5,4,3,2,1,0:T(8,128)(2,1)S(1)}, u32[]{:S(2)}, u32[]{:S(2)}) collective-permute-start(bf16[1,2,2,2,16,1024]{5,4,3,2,1,0:T(8,128)(2,1)S(1)} %maximum_bitcast_fusion.17), channel_id=1, source_target_pairs={{0,16},{2,18},{4,20},{6,22},{8,24},{10,26},{12,28},{14,30},{16,0},... | collective-permute-start | bytes 786440 | tf_op jit(solution)/shard_map/ppermute | solution.py:85
  90.3 7.3 %collective-permute-done.22 = bf16[2,2,2,16,1024]{4,3,2,1,0:T(8,128)(2,1)S(1)} collective-permute-done((bf16[2,2,2,16,1024]{4,3,2,1,0:T(8,128)(2,1)S(1)}, bf16[2,2,2,16,1024]{4,3,2,1,0:T(8,128)(2,1)S(1)}, u32[]{:S(2)}, u32[]{:S(2)}) %collective-permute-start.22) | collective-permute-done | bytes 262176 | tf_op jit(solution)/shard_map/ppermute | solution.py:85
  97.8 1.7 %collective-permute-start.34 = (bf16[1,2,2,2,16,1024]{5,4,3,2,1,0:T(8,128)(2,1)S(1)}, bf16[1,2,2,2,16,1024]{5,4,3,2,1,0:T(8,128)(2,1)S(1)}, u32[]{:S(2)}, u32[]{:S(2)}) collective-permute-start(bf16[1,2,2,2,16,1024]{5,4,3,2,1,0:T(8,128)(2,1)S(1)} %maximum_bitcast_fusion.15), channel_id=1, source_target_pairs={{0,4},{2,6},{4,0},{6,2},{8,12},{10,14},{12,8},{14,10},{16,20},{18,... | collective-permute-start | bytes 786440 | tf_op jit(solution)/shard_map/ppermute | solution.py:85
  101.9 3.3 %collective-permute-done.36 = bf16[1,2,2,2,16,1024]{5,4,3,2,1,0:T(8,128)(2,1)S(1)} collective-permute-done((bf16[1,2,2,2,16,1024]{5,4,3,2,1,0:T(8,128)(2,1)S(1)}, bf16[1,2,2,2,16,1024]{5,4,3,2,1,0:T(8,128)(2,1)S(1)}, u32[]{:S(2)}, u32[]{:S(2)}) %collective-permute-start.36) | collective-permute-done | bytes 262176 | tf_op jit(solution)/shard_map/ppermute | solution.py:85
  105.4 2.6 %collective-permute-done.35 = bf16[1,2,2,2,16,1024]{5,4,3,2,1,0:T(8,128)(2,1)S(1)} collective-permute-done((bf16[1,2,2,2,16,1024]{5,4,3,2,1,0:T(8,128)(2,1)S(1)}, bf16[1,2,2,2,16,1024]{5,4,3,2,1,0:T(8,128)(2,1)S(1)}, u32[]{:S(2)}, u32[]{:S(2)}) %collective-permute-start.35) | collective-permute-done | bytes 262176 | tf_op jit(solution)/shard_map/ppermute | solution.py:85
  108.1 1.3 collective-permute-start.15
  109.8 1.5 maximum_bitcast_fusion.1.blk_ref
  111.3 11.9 %shard_map.47 = (f32[4,4,1024]{2,1,0:T(4,128)}, f32[4,4,128]{2,1,0:T(4,128)}) custom-call(s32[64]{0:T(128)} %squeeze.19.meta_ref, bf16[1,1024,1024]{2,1,0:T(8,128)(2,1)} %maximum_bitcast_fusion.1.blk_ref, bf16[1024,1152]{1,0:T(8,128)(2,1)} %copy-done.3), custom_call_target="tpu_custom_call" | custom-call | flops 5402263552 | bytes 4521984 | tf_op jit(solution)/shard_map/pallas_call | solution.py:156
  124.7 1.5 maximum_bitcast_fusion.blk_ref
  126.2 11.9 %shard_map.46 = (f32[4,4,1024]{2,1,0:T(4,128)}, f32[4,4,128]{2,1,0:T(4,128)}) custom-call(s32[64]{0:T(128)} %squeeze.16.meta_ref, bf16[1,1024,1024]{2,1,0:T(8,128)(2,1)} %maximum_bitcast_fusion.blk_ref, bf16[1024,1152]{1,0:T(8,128)(2,1)} %copy-done.3), custom_call_target="tpu_custom_call" | custom-call | flops 5402263552 | bytes 4521984 | tf_op jit(solution)/shard_map/pallas_call | solution.py:156
  141.9 1.7 %collective-permute-start.39 = (f32[32]{0:T(128)S(1)}, f32[32]{0:T(128)S(1)}, u32[]{:S(2)}, u32[]{:S(2)}) collective-permute-start(f32[32]{0:T(128)S(1)} %fusion.11), channel_id=1, source_target_pairs={{0,6},{2,4},{4,2},{6,0},{8,14},{10,12},{12,10},{14,8},{16,22},{18,... | collective-permute-start | bytes 392 | tf_op jit(solution)/shard_map/ppermute | solution.py:33
  143.9 1.6 %collective-permute-start.41 = (f32[32]{0:T(128)S(1)}, f32[32]{0:T(128)S(1)}, u32[]{:S(2)}, u32[]{:S(2)}) collective-permute-start(f32[32]{0:T(128)S(1)} %fusion.11), channel_id=1, source_target_pairs={{0,2},{2,0},{4,6},{6,4},{8,10},{10,8},{12,14},{14,12},{16,18},{18,... | collective-permute-start | bytes 392 | tf_op jit(solution)/shard_map/ppermute | solution.py:33
  147.5 1.9 %collective-permute-start.42 = (f32[32]{0:T(128)S(1)}, f32[32]{0:T(128)S(1)}, u32[]{:S(2)}, u32[]{:S(2)}) collective-permute-start(f32[32]{0:T(128)S(1)} %fusion.27), channel_id=1, source_target_pairs={{0,24},{2,26},{4,28},{6,30},{8,16},{10,18},{12,20},{14,22},{16,8},... | collective-permute-start | bytes 392 | tf_op jit(solution)/shard_map/ppermute | solution.py:33
  149.4 1.3 collective-permute-start.43
  (263 shorter events, 48.3 us)
Async XLA Ops:
  1.7 26.9 %collective-permute-start.32 = (bf16[1024,128]{1,0:T(8,128)(2,1)}, bf16[1024,128]{1,0:T(8,128)(2,1)}, u32[]{:S(2)}, u32[]{:S(2)}) collective-permute-start(bf16[1024,128]{1,0:T(8,128)(2,1)} %slice.719), channel_id=1, source_target_pairs={{2,0},{4,2},{6,4},{8,6},{10,8},{12,10},{14,12},{16,14},{18,16},{20... | collective-permute-start | bytes 786440 | tf_op jit(solution)/shard_map/ppermute | solution.py:18
  6.6 32.1 %collective-permute-start.24 = (bf16[2,2,2,2,16,1024]{5,4,3,2,1,0:T(8,128)(2,1)}, bf16[2,2,2,2,16,1024]{5,4,3,2,1,0:T(8,128)(2,1)}, u32[]{:S(2)}, u32[]{:S(2)}) collective-permute-start(bf16[2,2,2,2,16,1024]{5,4,3,2,1,0:T(8,128)(2,1)} %pad_maximum_fusion.3), channel_id=1, source_target_pairs={{0,16},{2,18},{4,20},{6,22},{8,24},{10,26},{12,28},{14,30},{16,0},... | collective-permute-start | bytes 1572872 | tf_op jit(solution)/shard_map/ppermute | solution.py:75
  14.8 25.2 %collective-permute-start.16 = (bf16[2,2,2,2,16,1024]{5,4,3,2,1,0:T(8,128)(2,1)}, bf16[2,2,2,2,16,1024]{5,4,3,2,1,0:T(8,128)(2,1)}, u32[]{:S(2)}, u32[]{:S(2)}) collective-permute-start(bf16[2,2,2,2,16,1024]{5,4,3,2,1,0:T(8,128)(2,1)} %pad_maximum_fusion.2), channel_id=1, source_target_pairs={{0,8},{2,10},{4,12},{6,14},{8,0},{10,2},{12,4},{14,6},{16,24},{18,... | collective-permute-start | bytes 1572872 | tf_op jit(solution)/shard_map/ppermute | solution.py:75
  18.3 23.3 %collective-permute-start.8 = (bf16[2,2,2,2,16,1024]{5,4,3,2,1,0:T(8,128)(2,1)}, bf16[2,2,2,2,16,1024]{5,4,3,2,1,0:T(8,128)(2,1)}, u32[]{:S(2)}, u32[]{:S(2)}) collective-permute-start(bf16[2,2,2,2,16,1024]{5,4,3,2,1,0:T(8,128)(2,1)} %pad_maximum_fusion.1), channel_id=1, source_target_pairs={{0,4},{2,6},{4,0},{6,2},{8,12},{10,14},{12,8},{14,10},{16,20},{18,... | collective-permute-start | bytes 1572872 | tf_op jit(solution)/shard_map/ppermute | solution.py:75
  23.6 21.2 %collective-permute-start = (bf16[2,2,2,2,16,1024]{5,4,0,1,2,3:T(8,128)(2,1)}, bf16[2,2,2,2,16,1024]{5,4,0,1,2,3:T(8,128)(2,1)}, u32[]{:S(2)}, u32[]{:S(2)}) collective-permute-start(bf16[2,2,2,2,16,1024]{5,4,0,1,2,3:T(8,128)(2,1)} %pad_maximum_fusion), channel_id=1, source_target_pairs={{0,2},{2,0},{4,6},{6,4},{8,10},{10,8},{12,14},{14,12},{16,18},{18,... | collective-permute-start | bytes 1572872 | tf_op jit(solution)/shard_map/ppermute | solution.py:75
  39.9 8.3 %collective-permute-start.25 = (bf16[2,2,2,16,1024]{4,3,2,1,0:T(8,128)(2,1)S(1)}, bf16[2,2,2,16,1024]{4,3,2,1,0:T(8,128)(2,1)S(1)}, u32[]{:S(2)}, u32[]{:S(2)}) collective-permute-start(bf16[2,2,2,16,1024]{4,3,2,1,0:T(8,128)(2,1)S(1)} %pad_maximum_fusion.13), channel_id=1, source_target_pairs={{0,2},{2,0},{4,6},{6,4},{8,10},{10,8},{12,14},{14,12},{16,18},{18,... | collective-permute-start | bytes 786440 | tf_op jit(solution)/shard_map/ppermute | solution.py:75
  41.2 13.9 %collective-permute-start.17 = (bf16[2,2,2,16,1024]{4,3,2,1,0:T(8,128)(2,1)S(1)}, bf16[2,2,2,16,1024]{4,3,2,1,0:T(8,128)(2,1)S(1)}, u32[]{:S(2)}, u32[]{:S(2)}) collective-permute-start(bf16[2,2,2,16,1024]{4,3,2,1,0:T(8,128)(2,1)S(1)} %pad_maximum_fusion.10), channel_id=1, source_target_pairs={{0,16},{2,18},{4,20},{6,22},{8,24},{10,26},{12,28},{14,30},{16,0},... | collective-permute-start | bytes 786440 | tf_op jit(solution)/shard_map/ppermute | solution.py:75
  42.8 14.1 %collective-permute-start.9 = (bf16[2,2,2,16,1024]{4,3,2,1,0:T(8,128)(2,1)S(1)}, bf16[2,2,2,16,1024]{4,3,2,1,0:T(8,128)(2,1)S(1)}, u32[]{:S(2)}, u32[]{:S(2)}) collective-permute-start(bf16[2,2,2,16,1024]{4,3,2,1,0:T(8,128)(2,1)S(1)} %pad_maximum_fusion.7), channel_id=1, source_target_pairs={{0,8},{2,10},{4,12},{6,14},{8,0},{10,2},{12,4},{14,6},{16,24},{18,... | collective-permute-start | bytes 786440 | tf_op jit(solution)/shard_map/ppermute | solution.py:75
  47.0 10.1 %collective-permute-start.1 = (bf16[2,2,2,16,1024]{4,3,2,1,0:T(8,128)(2,1)S(1)}, bf16[2,2,2,16,1024]{4,3,2,1,0:T(8,128)(2,1)S(1)}, u32[]{:S(2)}, u32[]{:S(2)}) collective-permute-start(bf16[2,2,2,16,1024]{4,3,2,1,0:T(8,128)(2,1)S(1)} %pad_maximum_fusion.4), channel_id=1, source_target_pairs={{0,4},{2,6},{4,0},{6,2},{8,12},{10,14},{12,8},{14,10},{16,20},{18,... | collective-permute-start | bytes 786440 | tf_op jit(solution)/shard_map/ppermute | solution.py:75
  48.3 10.7 %collective-permute-start.26 = (bf16[2,2,16,1024]{3,2,1,0:T(8,128)(2,1)S(1)}, bf16[2,2,16,1024]{3,2,1,0:T(8,128)(2,1)S(1)}, u32[]{:S(2)}, u32[]{:S(2)}) collective-permute-start(bf16[2,2,16,1024]{3,2,1,0:T(8,128)(2,1)S(1)} %pad_maximum_fusion.30), channel_id=1, source_target_pairs={{0,4},{2,6},{4,0},{6,2},{8,12},{10,14},{12,8},{14,10},{16,20},{18,... | collective-permute-start | bytes 393224 | tf_op jit(solution)/shard_map/ppermute | solution.py:75
  57.0 7.5 %collective-permute-start.10 = (bf16[2,2,16,1024]{3,2,1,0:T(8,128)(2,1)S(1)}, bf16[2,2,16,1024]{3,2,1,0:T(8,128)(2,1)S(1)}, u32[]{:S(2)}, u32[]{:S(2)}) collective-permute-start(bf16[2,2,16,1024]{3,2,1,0:T(8,128)(2,1)S(1)} %pad_maximum_fusion.24), channel_id=1, source_target_pairs={{0,16},{2,18},{4,20},{6,22},{8,24},{10,26},{12,28},{14,30},{16,0},... | collective-permute-start | bytes 393224 | tf_op jit(solution)/shard_map/ppermute | solution.py:75
  57.3 8.6 %collective-permute-start.2 = (bf16[2,2,16,1024]{3,2,1,0:T(8,128)(2,1)S(1)}, bf16[2,2,16,1024]{3,2,1,0:T(8,128)(2,1)S(1)}, u32[]{:S(2)}, u32[]{:S(2)}) collective-permute-start(bf16[2,2,16,1024]{3,2,1,0:T(8,128)(2,1)S(1)} %pad_maximum_fusion.21), channel_id=1, source_target_pairs={{0,8},{2,10},{4,12},{6,14},{8,0},{10,2},{12,4},{14,6},{16,24},{18,... | collective-permute-start | bytes 393224 | tf_op jit(solution)/shard_map/ppermute | solution.py:75
  59.1 7.4 %collective-permute-start.27 = (bf16[2,16,1024]{2,1,0:T(8,128)(2,1)S(1)}, bf16[2,16,1024]{2,1,0:T(8,128)(2,1)S(1)}, u32[]{:S(2)}, u32[]{:S(2)}) collective-permute-start(bf16[2,16,1024]{2,1,0:T(8,128)(2,1)S(1)} %pad_maximum_fusion.49), channel_id=1, source_target_pairs={{0,8},{2,10},{4,12},{6,14},{8,0},{10,2},{12,4},{14,6},{16,24},{18,... | collective-permute-start | bytes 196616 | tf_op jit(solution)/shard_map/ppermute | solution.py:75
  60.6 8.4 %collective-permute-start.19 = (bf16[2,16,1024]{2,1,0:T(8,128)(2,1)S(1)}, bf16[2,16,1024]{2,1,0:T(8,128)(2,1)S(1)}, u32[]{:S(2)}, u32[]{:S(2)}) collective-permute-start(bf16[2,16,1024]{2,1,0:T(8,128)(2,1)S(1)} %pad_maximum_fusion.45), channel_id=1, source_target_pairs={{0,4},{2,6},{4,0},{6,2},{8,12},{10,14},{12,8},{14,10},{16,20},{18,... | collective-permute-start | bytes 196616 | tf_op jit(solution)/shard_map/ppermute | solution.py:75
  65.9 5.7 %collective-permute-start.3 = (bf16[2,16,1024]{2,1,0:T(8,128)(2,1)S(1)}, bf16[2,16,1024]{2,1,0:T(8,128)(2,1)S(1)}, u32[]{:S(2)}, u32[]{:S(2)}) collective-permute-start(bf16[2,16,1024]{2,1,0:T(8,128)(2,1)S(1)} %pad_maximum_fusion.37), channel_id=1, source_target_pairs={{0,16},{2,18},{4,20},{6,22},{8,24},{10,26},{12,28},{14,30},{16,0},... | collective-permute-start | bytes 196616 | tf_op jit(solution)/shard_map/ppermute | solution.py:75
  71.7 6.1 %collective-permute-start.4 = (bf16[2,16,1024]{2,1,0:T(8,128)(2,1)S(1)}, bf16[2,16,1024]{2,1,0:T(8,128)(2,1)S(1)}, u32[]{:S(2)}, u32[]{:S(2)}) collective-permute-start(bf16[2,16,1024]{2,1,0:T(8,128)(2,1)S(1)} %pad_maximum_fusion.38), channel_id=1, source_target_pairs={{0,16},{2,18},{4,20},{6,22},{8,24},{10,26},{12,28},{14,30},{16,0},... | collective-permute-start | bytes 196616 | tf_op jit(solution)/shard_map/ppermute | solution.py:85
  72.1 5.8 %collective-permute-start.29 = (bf16[2,2,16,1024]{3,2,1,0:T(8,128)(2,1)S(1)}, bf16[2,2,16,1024]{3,2,1,0:T(8,128)(2,1)S(1)}, u32[]{:S(2)}, u32[]{:S(2)}) collective-permute-start(bf16[2,2,16,1024]{3,2,1,0:T(8,128)(2,1)S(1)} %pad_maximum_fusion.31), channel_id=1, source_target_pairs={{0,4},{2,6},{4,0},{6,2},{8,12},{10,14},{12,8},{14,10},{16,20},{18,... | collective-permute-start | bytes 393224 | tf_op jit(solution)/shard_map/ppermute | solution.py:85
  74.1 6.5 %collective-permute-start.21 = (bf16[2,2,16,1024]{3,2,1,0:T(8,128)(2,1)S(1)}, bf16[2,2,16,1024]{3,2,1,0:T(8,128)(2,1)S(1)}, u32[]{:S(2)}, u32[]{:S(2)}) collective-permute-start(bf16[2,2,16,1024]{3,2,1,0:T(8,128)(2,1)S(1)} %pad_maximum_fusion.28), channel_id=1, source_target_pairs={{0,2},{2,0},{4,6},{6,4},{8,10},{10,8},{12,14},{14,12},{16,18},{18,... | collective-permute-start | bytes 393224 | tf_op jit(solution)/shard_map/ppermute | solution.py:85
  74.7 9.1 %collective-permute-start.13 = (bf16[2,2,16,1024]{3,2,1,0:T(8,128)(2,1)S(1)}, bf16[2,2,16,1024]{3,2,1,0:T(8,128)(2,1)S(1)}, u32[]{:S(2)}, u32[]{:S(2)}) collective-permute-start(bf16[2,2,16,1024]{3,2,1,0:T(8,128)(2,1)S(1)} %pad_maximum_fusion.25), channel_id=1, source_target_pairs={{0,16},{2,18},{4,20},{6,22},{8,24},{10,26},{12,28},{14,30},{16,0},... | collective-permute-start | bytes 393224 | tf_op jit(solution)/shard_map/ppermute | solution.py:85
  77.8 6.6 %collective-permute-start.5 = (bf16[2,2,16,1024]{3,2,1,0:T(8,128)(2,1)S(1)}, bf16[2,2,16,1024]{3,2,1,0:T(8,128)(2,1)S(1)}, u32[]{:S(2)}, u32[]{:S(2)}) collective-permute-start(bf16[2,2,16,1024]{3,2,1,0:T(8,128)(2,1)S(1)} %pad_maximum_fusion.22), channel_id=1, source_target_pairs={{0,8},{2,10},{4,12},{6,14},{8,0},{10,2},{12,4},{14,6},{16,24},{18,... | collective-permute-start | bytes 393224 | tf_op jit(solution)/shard_map/ppermute | solution.py:85
  78.0 10.6 %collective-permute-start.30 = (bf16[2,2,2,16,1024]{4,3,2,1,0:T(8,128)(2,1)S(1)}, bf16[2,2,2,16,1024]{4,3,2,1,0:T(8,128)(2,1)S(1)}, u32[]{:S(2)}, u32[]{:S(2)}) collective-permute-start(bf16[2,2,2,16,1024]{4,3,2,1,0:T(8,128)(2,1)S(1)} %pad_maximum_fusion.14), channel_id=1, source_target_pairs={{0,2},{2,0},{4,6},{6,4},{8,10},{10,8},{12,14},{14,12},{16,18},{18,... | collective-permute-start | bytes 786440 | tf_op jit(solution)/shard_map/ppermute | solution.py:85
  80.7 16.8 %collective-permute-start.22 = (bf16[2,2,2,16,1024]{4,3,2,1,0:T(8,128)(2,1)S(1)}, bf16[2,2,2,16,1024]{4,3,2,1,0:T(8,128)(2,1)S(1)}, u32[]{:S(2)}, u32[]{:S(2)}) collective-permute-start(bf16[2,2,2,16,1024]{4,3,2,1,0:T(8,128)(2,1)S(1)} %pad_maximum_fusion.11), channel_id=1, source_target_pairs={{0,16},{2,18},{4,20},{6,22},{8,24},{10,26},{12,28},{14,30},{16,0},... | collective-permute-start | bytes 786440 | tf_op jit(solution)/shard_map/ppermute | solution.py:85
  83.8 13.9 %collective-permute-start.14 = (bf16[2,2,2,16,1024]{4,3,2,1,0:T(8,128)(2,1)S(1)}, bf16[2,2,2,16,1024]{4,3,2,1,0:T(8,128)(2,1)S(1)}, u32[]{:S(2)}, u32[]{:S(2)}) collective-permute-start(bf16[2,2,2,16,1024]{4,3,2,1,0:T(8,128)(2,1)S(1)} %pad_maximum_fusion.8), channel_id=1, source_target_pairs={{0,8},{2,10},{4,12},{6,14},{8,0},{10,2},{12,4},{14,6},{16,24},{18,... | collective-permute-start | bytes 786440 | tf_op jit(solution)/shard_map/ppermute | solution.py:85
  84.6 14.9 %collective-permute-start.6 = (bf16[2,2,2,16,1024]{4,3,2,1,0:T(8,128)(2,1)S(1)}, bf16[2,2,2,16,1024]{4,3,2,1,0:T(8,128)(2,1)S(1)}, u32[]{:S(2)}, u32[]{:S(2)}) collective-permute-start(bf16[2,2,2,16,1024]{4,3,2,1,0:T(8,128)(2,1)S(1)} %pad_maximum_fusion.5), channel_id=1, source_target_pairs={{0,4},{2,6},{4,0},{6,2},{8,12},{10,14},{12,8},{14,10},{16,20},{18,... | collective-permute-start | bytes 786440 | tf_op jit(solution)/shard_map/ppermute | solution.py:85
  88.7 16.6 %collective-permute-start.36 = (bf16[1,2,2,2,16,1024]{5,4,3,2,1,0:T(8,128)(2,1)S(1)}, bf16[1,2,2,2,16,1024]{5,4,3,2,1,0:T(8,128)(2,1)S(1)}, u32[]{:S(2)}, u32[]{:S(2)}) collective-permute-start(bf16[1,2,2,2,16,1024]{5,4,3,2,1,0:T(8,128)(2,1)S(1)} %maximum_bitcast_fusion.17), channel_id=1, source_target_pairs={{0,16},{2,18},{4,20},{6,22},{8,24},{10,26},{12,28},{14,30},{16,0},... | collective-permute-start | bytes 786440 | tf_op jit(solution)/shard_map/ppermute | solution.py:85
  97.6 10.3 %collective-permute-start.35 = (bf16[1,2,2,2,16,1024]{5,4,3,2,1,0:T(8,128)(2,1)S(1)}, bf16[1,2,2,2,16,1024]{5,4,3,2,1,0:T(8,128)(2,1)S(1)}, u32[]{:S(2)}, u32[]{:S(2)}) collective-permute-start(bf16[1,2,2,2,16,1024]{5,4,3,2,1,0:T(8,128)(2,1)S(1)} %maximum_bitcast_fusion.16), channel_id=1, source_target_pairs={{0,8},{2,10},{4,12},{6,14},{8,0},{10,2},{12,4},{14,6},{16,24},{18,... | collective-permute-start | bytes 786440 | tf_op jit(solution)/shard_map/ppermute | solution.py:85
  97.8 10.3 %collective-permute-start.34 = (bf16[1,2,2,2,16,1024]{5,4,3,2,1,0:T(8,128)(2,1)S(1)}, bf16[1,2,2,2,16,1024]{5,4,3,2,1,0:T(8,128)(2,1)S(1)}, u32[]{:S(2)}, u32[]{:S(2)}) collective-permute-start(bf16[1,2,2,2,16,1024]{5,4,3,2,1,0:T(8,128)(2,1)S(1)} %maximum_bitcast_fusion.15), channel_id=1, source_target_pairs={{0,4},{2,6},{4,0},{6,2},{8,12},{10,14},{12,8},{14,10},{16,20},{18,... | collective-permute-start | bytes 786440 | tf_op jit(solution)/shard_map/ppermute | solution.py:85
  99.6 10.0 %collective-permute-start.33 = (bf16[1,2,2,2,16,1024]{5,4,3,2,1,0:T(8,128)(2,1)S(1)}, bf16[1,2,2,2,16,1024]{5,4,3,2,1,0:T(8,128)(2,1)S(1)}, u32[]{:S(2)}, u32[]{:S(2)}) collective-permute-start(bf16[1,2,2,2,16,1024]{5,4,3,2,1,0:T(8,128)(2,1)S(1)} %maximum_bitcast_fusion.14), channel_id=1, source_target_pairs={{0,2},{2,0},{4,6},{6,4},{8,10},{10,8},{12,14},{14,12},{16,18},{18,... | collective-permute-start | bytes 786440 | tf_op jit(solution)/shard_map/ppermute | solution.py:85
  100.6 9.0 %collective-permute-start.7 = (bf16[1,2,2,2,16,1024]{5,4,3,2,1,0:T(8,128)(2,1)S(1)}, bf16[1,2,2,2,16,1024]{5,4,3,2,1,0:T(8,128)(2,1)S(1)}, u32[]{:S(2)}, u32[]{:S(2)}) collective-permute-start(bf16[1,2,2,2,16,1024]{5,4,3,2,1,0:T(8,128)(2,1)S(1)} %maximum_bitcast_fusion.10), channel_id=1, source_target_pairs={{0,2},{2,0},{4,6},{6,4},{8,10},{10,8},{12,14},{14,12},{16,18},{18,... | collective-permute-start | bytes 786440 | tf_op jit(solution)/shard_map/ppermute | solution.py:85
  105.2 18.8 %collective-permute-start.31 = (bf16[1,2,2,2,16,1024]{5,4,3,2,1,0:T(8,128)(2,1)S(1)}, bf16[1,2,2,2,16,1024]{5,4,3,2,1,0:T(8,128)(2,1)S(1)}, u32[]{:S(2)}, u32[]{:S(2)}) collective-permute-start(bf16[1,2,2,2,16,1024]{5,4,3,2,1,0:T(8,128)(2,1)S(1)} %maximum_bitcast_fusion.13), channel_id=1, source_target_pairs={{0,16},{2,18},{4,20},{6,22},{8,24},{10,26},{12,28},{14,30},{16,0},... | collective-permute-start | bytes 786440 | tf_op jit(solution)/shard_map/ppermute | solution.py:85
  107.9 16.3 %collective-permute-start.23 = (bf16[1,2,2,2,16,1024]{5,4,3,2,1,0:T(8,128)(2,1)S(1)}, bf16[1,2,2,2,16,1024]{5,4,3,2,1,0:T(8,128)(2,1)S(1)}, u32[]{:S(2)}, u32[]{:S(2)}) collective-permute-start(bf16[1,2,2,2,16,1024]{5,4,3,2,1,0:T(8,128)(2,1)S(1)} %maximum_bitcast_fusion.12), channel_id=1, source_target_pairs={{0,8},{2,10},{4,12},{6,14},{8,0},{10,2},{12,4},{14,6},{16,24},{18,... | collective-permute-start | bytes 786440 | tf_op jit(solution)/shard_map/ppermute | solution.py:85
  108.1 16.3 %collective-permute-start.15 = (bf16[1,2,2,2,16,1024]{5,4,3,2,1,0:T(8,128)(2,1)S(1)}, bf16[1,2,2,2,16,1024]{5,4,3,2,1,0:T(8,128)(2,1)S(1)}, u32[]{:S(2)}, u32[]{:S(2)}) collective-permute-start(bf16[1,2,2,2,16,1024]{5,4,3,2,1,0:T(8,128)(2,1)S(1)} %maximum_bitcast_fusion.11), channel_id=1, source_target_pairs={{0,4},{2,6},{4,0},{6,2},{8,12},{10,14},{12,8},{14,10},{16,20},{18,... | collective-permute-start | bytes 786440 | tf_op jit(solution)/shard_map/ppermute | solution.py:85
  (22 other events, 112.6 us)

commit v16 on v14

--- a/solution.py
+++ b/solution.py
@@ -6,7 +6,7 @@
 from jax.sharding import PartitionSpec as P
 
 L = 128
-GROUP = 8
+GROUP = 2
 REACH = L + 16
 
 EPS = 1e-06

time: 164 us -> 158 us (0.963)
  waiting for transfers between devices: 50.9 us -> 41.1 us
  Pallas kernels: 23.4 us -> 26 us
  local copies, waits for them, and re-layouts: 13.3 us -> 15 us
    ppermute x36, waiting for transfers between devices: 46 us -> 35.9 us  [spread_blocks(): lax.ppermute(jnp.stack([v for _, v in items]), axis, [(i, i ^ mask) for i...]
    pallas_call x2, Pallas kernels: 23.4 us -> 26 us  [correlate(): pl.pallas_call(correlate_kernel, grid_spec=grid_spec, out_shape=[jax.Shap...]
    reshape x0 -> x2, local copies, waits for them, and re-layouts: none -> 1.77 us  [correlate(): corr.reshape(rounds * count, lag_count)]
    unnamed x25 -> x23, local copies, waits for them, and re-layouts: 4.17 us -> 4.15 us
  transfers between devices with their start and end apart: 45 -> 45, of which waited for: 21 -> 21; matrix products, arithmetic and copies ran while one was open for 16% -> 18% of each run, Pallas kernels for 0% -> 8%
where the time goes in v16:
time: 158 us; the launch traced here: 157 us
  starting transfers between devices  53.1 us (34%)
  waiting for transfers between devices  41.1 us (26%)
  Pallas kernels  26 us (16%)
  other arithmetic  18.1 us (11%)
  local copies, waits for them, and re-layouts  15 us (9%)
  between operations  2.62 us (2%)
    ppermute x36, starting transfers between devices, spread_blocks(): lax.ppermute(jnp.stack([v for _, v in items]), axis, [(i, i ^ mask) for i...  43.3 us
    ppermute x36, waiting for transfers between devices, spread_blocks(): lax.ppermute(jnp.stack([v for _, v in items]), axis, [(i, i ^ mask) for i...  35.9 us
    pallas_call x2, Pallas kernels, correlate(): pl.pallas_call(correlate_kernel, grid_spec=grid_spec, out_shape=[jax.Shap...  26 us
    ppermute x8, starting transfers between devices, group_sum(): got[d] = lax.ppermute(value, axis, pairs)  8.57 us
    select_n x18, other arithmetic, spread_blocks(): bufs[key] = jnp.where(holder, keeps[key], got[n])  5.7 us
    ppermute x8, waiting for transfers between devices, group_sum(): got[d] = lax.ppermute(value, axis, pairs)  5.14 us
    another operation x52, other arithmetic, spread_blocks(): jnp.stack([v for _, v in items])  4.23 us
    unnamed x23, local copies, waits for them, and re-layouts  4.15 us
  transfers between devices with their start and end apart: 45, of which 21 were waited for; matrix products, arithmetic and copies ran while one was open for 18% of the time, Pallas kernels for 8%

profile of v16, /device:TPU:0, one launch (start us, length us, event | category | flops | bytes accessed | tf_op | source)
XLA Modules:
  0.0 157.4 jit_solution(16474144827129213395)
XLA Ops:
  0.0 1.7 %slice.719 = bf16[1024,128]{1,0:T(8,128)(2,1)} slice(bf16[1024,1024]{1,0:T(8,128)(2,1)} %param.4), slice={[0:1024], [0:128]} | slice | bytes 524288 | tf_op jit(solution)/shard_map/slice | solution.py:183
  3.0 2.5 %fusion.28 = (bf16[1024,256]{1,0:T(8,128)(2,1)}, bf16[1024,256]{1,0:T(8,128)(2,1)S(1)}, bf16[1024,256]{1,0:T(8,128)(2,1)S(1)}, bf16[1024,256]{1,0:T(8,128)(2,1)S(1)}) fusion(bf16[1024,1024]{1,0:T(8,128)(2,1)} %param.4), kind=kLoop, calls=%fused_computation.302 | loop fusion | bytes 4194304 | tf_op jit(solution)/shard_map/slice | solution.py:61
  6.6 7.0 %collective-permute-start.24 = (bf16[2,2,2,2,16,1024]{5,4,3,2,1,0:T(8,128)(2,1)}, bf16[2,2,2,2,16,1024]{5,4,3,2,1,0:T(8,128)(2,1)}, u32[]{:S(2)}, u32[]{:S(2)}) collective-permute-start(bf16[2,2,2,2,16,1024]{5,4,3,2,1,0:T(8,128)(2,1)} %pad_maximum_fusion.3), channel_id=1, source_target_pairs={{0,16},{2,18},{4,20},{6,22},{8,24},{10,26},{12,28},{14,30},{16,0},... | collective-permute-start | bytes 1572872 | tf_op jit(solution)/shard_map/ppermute | solution.py:75
  14.8 1.6 %collective-permute-start.16 = (bf16[2,2,2,2,16,1024]{5,4,3,2,1,0:T(8,128)(2,1)}, bf16[2,2,2,2,16,1024]{5,4,3,2,1,0:T(8,128)(2,1)}, u32[]{:S(2)}, u32[]{:S(2)}) collective-permute-start(bf16[2,2,2,2,16,1024]{5,4,3,2,1,0:T(8,128)(2,1)} %pad_maximum_fusion.2), channel_id=1, source_target_pairs={{0,8},{2,10},{4,12},{6,14},{8,0},{10,2},{12,4},{14,6},{16,24},{18,... | collective-permute-start | bytes 1572872 | tf_op jit(solution)/shard_map/ppermute | solution.py:75
  18.9 2.0 %copy.66 = bf16[1024,256]{0,1:T(8,128)(2,1)} copy(bf16[1024,256]{1,0:T(8,128)(2,1)} %get-tuple-element.17) | data formatting | bytes 1048576
  20.9 1.8 %fusion.29 = (bf16[1,2,2,2,16,1024]{5,4,0,1,2,3:T(8,128)(2,1)S(1)}, bf16[1,2,2,2,16,1024]{5,4,0,1,2,3:T(8,128)(2,1)S(1)}, bf16[1,2,2,2,16,1024]{5,4,0,1,2,3:T(8,128)(2,1)}) fusion(bf16[2,2,2,2,16,1024]{5,4,0,1,2,3:T(8,128)(2,1)} %bitcast.296, pred[]{:T(512)S(6)} %eq.170), kind=kLoop, calls=%fused_computation.303 | loop fusion | flops 131072 | bytes 1310721 | tf_op jit(solution)/shard_map/slice | solution.py:72
  32.4 6.3 %collective-permute-done.24 = bf16[2,2,2,2,16,1024]{5,4,3,2,1,0:T(8,128)(2,1)} collective-permute-done((bf16[2,2,2,2,16,1024]{5,4,3,2,1,0:T(8,128)(2,1)}, bf16[2,2,2,2,16,1024]{5,4,3,2,1,0:T(8,128)(2,1)}, u32[]{:S(2)}, u32[]{:S(2)}) %collective-permute-start.24) | collective-permute-done | bytes 524320 | tf_op jit(solution)/shard_map/ppermute | solution.py:75
  42.8 2.0 %collective-permute-start.9 = (bf16[2,2,2,16,1024]{4,3,2,1,0:T(8,128)(2,1)S(1)}, bf16[2,2,2,16,1024]{4,3,2,1,0:T(8,128)(2,1)S(1)}, u32[]{:S(2)}, u32[]{:S(2)}) collective-permute-start(bf16[2,2,2,16,1024]{4,3,2,1,0:T(8,128)(2,1)S(1)} %pad_maximum_fusion.7), channel_id=1, source_target_pairs={{0,8},{2,10},{4,12},{6,14},{8,0},{10,2},{12,4},{14,6},{16,24},{18,... | collective-permute-start | bytes 786440 | tf_op jit(solution)/shard_map/ppermute | solution.py:75
  49.2 5.8 %collective-permute-done.17 = bf16[2,2,2,16,1024]{4,3,2,1,0:T(8,128)(2,1)S(1)} collective-permute-done((bf16[2,2,2,16,1024]{4,3,2,1,0:T(8,128)(2,1)S(1)}, bf16[2,2,2,16,1024]{4,3,2,1,0:T(8,128)(2,1)S(1)}, u32[]{:S(2)}, u32[]{:S(2)}) %collective-permute-start.17) | collective-permute-done | bytes 262176 | tf_op jit(solution)/shard_map/ppermute | solution.py:75
  55.1 1.8 %collective-permute-start.18 = (bf16[2,2,16,1024]{3,2,1,0:T(8,128)(2,1)S(1)}, bf16[2,2,16,1024]{3,2,1,0:T(8,128)(2,1)S(1)}, u32[]{:S(2)}, u32[]{:S(2)}) collective-permute-start(bf16[2,2,16,1024]{3,2,1,0:T(8,128)(2,1)S(1)} %pad_maximum_fusion.27), channel_id=1, source_target_pairs={{0,2},{2,0},{4,6},{6,4},{8,10},{10,8},{12,14},{14,12},{16,18},{18,... | collective-permute-start | bytes 393224 | tf_op jit(solution)/shard_map/ppermute | solution.py:75
  57.3 1.8 %collective-permute-start.2 = (bf16[2,2,16,1024]{3,2,1,0:T(8,128)(2,1)S(1)}, bf16[2,2,16,1024]{3,2,1,0:T(8,128)(2,1)S(1)}, u32[]{:S(2)}, u32[]{:S(2)}) collective-permute-start(bf16[2,2,16,1024]{3,2,1,0:T(8,128)(2,1)S(1)} %pad_maximum_fusion.21), channel_id=1, source_target_pairs={{0,8},{2,10},{4,12},{6,14},{8,0},{10,2},{12,4},{14,6},{16,24},{18,... | collective-permute-start | bytes 393224 | tf_op jit(solution)/shard_map/ppermute | solution.py:75
  60.6 3.9 %collective-permute-done.10 = bf16[2,2,16,1024]{3,2,1,0:T(8,128)(2,1)S(1)} collective-permute-done((bf16[2,2,16,1024]{3,2,1,0:T(8,128)(2,1)S(1)}, bf16[2,2,16,1024]{3,2,1,0:T(8,128)(2,1)S(1)}, u32[]{:S(2)}, u32[]{:S(2)}) %collective-permute-start.10) | collective-permute-done | bytes 131104 | tf_op jit(solution)/shard_map/ppermute | solution.py:75
  66.6 2.4 %collective-permute-start.28 = (bf16[2,16,1024]{2,1,0:T(8,128)(2,1)S(1)}, bf16[2,16,1024]{2,1,0:T(8,128)(2,1)S(1)}, u32[]{:S(2)}, u32[]{:S(2)}) collective-permute-start(bf16[2,16,1024]{2,1,0:T(8,128)(2,1)S(1)} %pad_maximum_fusion.50), channel_id=1, source_target_pairs={{0,8},{2,10},{4,12},{6,14},{8,0},{10,2},{12,4},{14,6},{16,24},{18,... | collective-permute-start | bytes 196616 | tf_op jit(solution)/shard_map/ppermute | solution.py:85
  72.6 1.4 collective-permute-done.20
  74.7 2.0 %collective-permute-start.13 = (bf16[2,2,16,1024]{3,2,1,0:T(8,128)(2,1)S(1)}, bf16[2,2,16,1024]{3,2,1,0:T(8,128)(2,1)S(1)}, u32[]{:S(2)}, u32[]{:S(2)}) collective-permute-start(bf16[2,2,16,1024]{3,2,1,0:T(8,128)(2,1)S(1)} %pad_maximum_fusion.25), channel_id=1, source_target_pairs={{0,16},{2,18},{4,20},{6,22},{8,24},{10,26},{12,28},{14,30},{16,0},... | collective-permute-start | bytes 393224 | tf_op jit(solution)/shard_map/ppermute | solution.py:85
  78.0 2.5 %collective-permute-start.30 = (bf16[2,2,2,16,1024]{4,3,2,1,0:T(8,128)(2,1)S(1)}, bf16[2,2,2,16,1024]{4,3,2,1,0:T(8,128)(2,1)S(1)}, u32[]{:S(2)}, u32[]{:S(2)}) collective-permute-start(bf16[2,2,2,16,1024]{4,3,2,1,0:T(8,128)(2,1)S(1)} %pad_maximum_fusion.14), channel_id=1, source_target_pairs={{0,2},{2,0},{4,6},{6,4},{8,10},{10,8},{12,14},{14,12},{16,18},{18,... | collective-permute-start | bytes 786440 | tf_op jit(solution)/shard_map/ppermute | solution.py:85
  80.7 2.6 %collective-permute-start.22 = (bf16[2,2,2,16,1024]{4,3,2,1,0:T(8,128)(2,1)S(1)}, bf16[2,2,2,16,1024]{4,3,2,1,0:T(8,128)(2,1)S(1)}, u32[]{:S(2)}, u32[]{:S(2)}) collective-permute-start(bf16[2,2,2,16,1024]{4,3,2,1,0:T(8,128)(2,1)S(1)} %pad_maximum_fusion.11), channel_id=1, source_target_pairs={{0,16},{2,18},{4,20},{6,22},{8,24},{10,26},{12,28},{14,30},{16,0},... | collective-permute-start | bytes 786440 | tf_op jit(solution)/shard_map/ppermute | solution.py:85
  84.6 4.0 %collective-permute-start.6 = (bf16[2,2,2,16,1024]{4,3,2,1,0:T(8,128)(2,1)S(1)}, bf16[2,2,2,16,1024]{4,3,2,1,0:T(8,128)(2,1)S(1)}, u32[]{:S(2)}, u32[]{:S(2)}) collective-permute-start(bf16[2,2,2,16,1024]{4,3,2,1,0:T(8,128)(2,1)S(1)} %pad_maximum_fusion.5), channel_id=1, source_target_pairs={{0,4},{2,6},{4,0},{6,2},{8,12},{10,14},{12,8},{14,10},{16,20},{18,... | collective-permute-start | bytes 786440 | tf_op jit(solution)/shard_map/ppermute | solution.py:85
  88.7 1.6 %collective-permute-start.36 = (bf16[1,2,2,2,16,1024]{5,4,3,2,1,0:T(8,128)(2,1)S(1)}, bf16[1,2,2,2,16,1024]{5,4,3,2,1,0:T(8,128)(2,1)S(1)}, u32[]{:S(2)}, u32[]{:S(2)}) collective-permute-start(bf16[1,2,2,2,16,1024]{5,4,3,2,1,0:T(8,128)(2,1)S(1)} %maximum_bitcast_fusion.17), channel_id=1, source_target_pairs={{0,16},{2,18},{4,20},{6,22},{8,24},{10,26},{12,28},{14,30},{16,0},... | collective-permute-start | bytes 786440 | tf_op jit(solution)/shard_map/ppermute | solution.py:85
  90.3 7.3 %collective-permute-done.22 = bf16[2,2,2,16,1024]{4,3,2,1,0:T(8,128)(2,1)S(1)} collective-permute-done((bf16[2,2,2,16,1024]{4,3,2,1,0:T(8,128)(2,1)S(1)}, bf16[2,2,2,16,1024]{4,3,2,1,0:T(8,128)(2,1)S(1)}, u32[]{:S(2)}, u32[]{:S(2)}) %collective-permute-start.22) | collective-permute-done | bytes 262176 | tf_op jit(solution)/shard_map/ppermute | solution.py:85
  97.8 1.7 %collective-permute-start.34 = (bf16[1,2,2,2,16,1024]{5,4,3,2,1,0:T(8,128)(2,1)S(1)}, bf16[1,2,2,2,16,1024]{5,4,3,2,1,0:T(8,128)(2,1)S(1)}, u32[]{:S(2)}, u32[]{:S(2)}) collective-permute-start(bf16[1,2,2,2,16,1024]{5,4,3,2,1,0:T(8,128)(2,1)S(1)} %maximum_bitcast_fusion.15), channel_id=1, source_target_pairs={{0,4},{2,6},{4,0},{6,2},{8,12},{10,14},{12,8},{14,10},{16,20},{18,... | collective-permute-start | bytes 786440 | tf_op jit(solution)/shard_map/ppermute | solution.py:85
  101.9 3.3 %collective-permute-done.36 = bf16[1,2,2,2,16,1024]{5,4,3,2,1,0:T(8,128)(2,1)S(1)} collective-permute-done((bf16[1,2,2,2,16,1024]{5,4,3,2,1,0:T(8,128)(2,1)S(1)}, bf16[1,2,2,2,16,1024]{5,4,3,2,1,0:T(8,128)(2,1)S(1)}, u32[]{:S(2)}, u32[]{:S(2)}) %collective-permute-start.36) | collective-permute-done | bytes 262176 | tf_op jit(solution)/shard_map/ppermute | solution.py:85
  105.4 2.6 %collective-permute-done.35 = bf16[1,2,2,2,16,1024]{5,4,3,2,1,0:T(8,128)(2,1)S(1)} collective-permute-done((bf16[1,2,2,2,16,1024]{5,4,3,2,1,0:T(8,128)(2,1)S(1)}, bf16[1,2,2,2,16,1024]{5,4,3,2,1,0:T(8,128)(2,1)S(1)}, u32[]{:S(2)}, u32[]{:S(2)}) %collective-permute-start.35) | collective-permute-done | bytes 262176 | tf_op jit(solution)/shard_map/ppermute | solution.py:85
  108.1 1.3 collective-permute-start.15
  109.8 1.5 maximum_bitcast_fusion.1.blk_ref
  111.3 13.0 %shard_map.47 = (f32[8,2,1024]{2,1,0:T(2,128)}, f32[8,2,128]{2,1,0:T(2,128)}) custom-call(s32[64]{0:T(128)} %squeeze.19.meta_ref, bf16[1,1024,1024]{2,1,0:T(8,128)(2,1)} %maximum_bitcast_fusion.1.blk_ref, bf16[1024,1152]{1,0:T(8,128)(2,1)} %copy-done.3), custom_call_target="tpu_custom_call" | custom-call | flops 5435817984 | bytes 4521984 | tf_op jit(solution)/shard_map/pallas_call | solution.py:156
  125.8 1.5 maximum_bitcast_fusion.blk_ref
  127.3 13.0 %shard_map.46 = (f32[8,2,1024]{2,1,0:T(2,128)}, f32[8,2,128]{2,1,0:T(2,128)}) custom-call(s32[64]{0:T(128)} %squeeze.16.meta_ref, bf16[1,1024,1024]{2,1,0:T(8,128)(2,1)} %maximum_bitcast_fusion.blk_ref, bf16[1024,1152]{1,0:T(8,128)(2,1)} %copy-done.3), custom_call_target="tpu_custom_call" | custom-call | flops 5435817984 | bytes 4521984 | tf_op jit(solution)/shard_map/pallas_call | solution.py:156
  144.2 1.7 %collective-permute-start.39 = (f32[32]{0:T(128)S(1)}, f32[32]{0:T(128)S(1)}, u32[]{:S(2)}, u32[]{:S(2)}) collective-permute-start(f32[32]{0:T(128)S(1)} %fusion.11), channel_id=1, source_target_pairs={{0,6},{2,4},{4,2},{6,0},{8,14},{10,12},{12,10},{14,8},{16,22},{18,... | collective-permute-start | bytes 392 | tf_op jit(solution)/shard_map/ppermute | solution.py:33
  146.2 1.6 collective-permute-start.41
  149.7 1.9 %collective-permute-start.42 = (f32[32]{0:T(128)S(1)}, f32[32]{0:T(128)S(1)}, u32[]{:S(2)}, u32[]{:S(2)}) collective-permute-start(f32[32]{0:T(128)S(1)} %fusion.27), channel_id=1, source_target_pairs={{0,24},{2,26},{4,28},{6,30},{8,16},{10,18},{12,20},{14,22},{16,8},... | collective-permute-start | bytes 392 | tf_op jit(solution)/shard_map/ppermute | solution.py:33
  151.7 1.3 collective-permute-start.43
  (263 shorter events, 48.3 us)
Async XLA Ops:
  1.7 26.9 %collective-permute-start.32 = (bf16[1024,128]{1,0:T(8,128)(2,1)}, bf16[1024,128]{1,0:T(8,128)(2,1)}, u32[]{:S(2)}, u32[]{:S(2)}) collective-permute-start(bf16[1024,128]{1,0:T(8,128)(2,1)} %slice.719), channel_id=1, source_target_pairs={{2,0},{4,2},{6,4},{8,6},{10,8},{12,10},{14,12},{16,14},{18,16},{20... | collective-permute-start | bytes 786440 | tf_op jit(solution)/shard_map/ppermute | solution.py:18
  6.6 32.1 %collective-permute-start.24 = (bf16[2,2,2,2,16,1024]{5,4,3,2,1,0:T(8,128)(2,1)}, bf16[2,2,2,2,16,1024]{5,4,3,2,1,0:T(8,128)(2,1)}, u32[]{:S(2)}, u32[]{:S(2)}) collective-permute-start(bf16[2,2,2,2,16,1024]{5,4,3,2,1,0:T(8,128)(2,1)} %pad_maximum_fusion.3), channel_id=1, source_target_pairs={{0,16},{2,18},{4,20},{6,22},{8,24},{10,26},{12,28},{14,30},{16,0},... | collective-permute-start | bytes 1572872 | tf_op jit(solution)/shard_map/ppermute | solution.py:75
  14.8 25.2 %collective-permute-start.16 = (bf16[2,2,2,2,16,1024]{5,4,3,2,1,0:T(8,128)(2,1)}, bf16[2,2,2,2,16,1024]{5,4,3,2,1,0:T(8,128)(2,1)}, u32[]{:S(2)}, u32[]{:S(2)}) collective-permute-start(bf16[2,2,2,2,16,1024]{5,4,3,2,1,0:T(8,128)(2,1)} %pad_maximum_fusion.2), channel_id=1, source_target_pairs={{0,8},{2,10},{4,12},{6,14},{8,0},{10,2},{12,4},{14,6},{16,24},{18,... | collective-permute-start | bytes 1572872 | tf_op jit(solution)/shard_map/ppermute | solution.py:75
  18.3 23.3 %collective-permute-start.8 = (bf16[2,2,2,2,16,1024]{5,4,3,2,1,0:T(8,128)(2,1)}, bf16[2,2,2,2,16,1024]{5,4,3,2,1,0:T(8,128)(2,1)}, u32[]{:S(2)}, u32[]{:S(2)}) collective-permute-start(bf16[2,2,2,2,16,1024]{5,4,3,2,1,0:T(8,128)(2,1)} %pad_maximum_fusion.1), channel_id=1, source_target_pairs={{0,4},{2,6},{4,0},{6,2},{8,12},{10,14},{12,8},{14,10},{16,20},{18,... | collective-permute-start | bytes 1572872 | tf_op jit(solution)/shard_map/ppermute | solution.py:75
  23.6 21.2 %collective-permute-start = (bf16[2,2,2,2,16,1024]{5,4,0,1,2,3:T(8,128)(2,1)}, bf16[2,2,2,2,16,1024]{5,4,0,1,2,3:T(8,128)(2,1)}, u32[]{:S(2)}, u32[]{:S(2)}) collective-permute-start(bf16[2,2,2,2,16,1024]{5,4,0,1,2,3:T(8,128)(2,1)} %pad_maximum_fusion), channel_id=1, source_target_pairs={{0,2},{2,0},{4,6},{6,4},{8,10},{10,8},{12,14},{14,12},{16,18},{18,... | collective-permute-start | bytes 1572872 | tf_op jit(solution)/shard_map/ppermute | solution.py:75
  39.9 8.3 %collective-permute-start.25 = (bf16[2,2,2,16,1024]{4,3,2,1,0:T(8,128)(2,1)S(1)}, bf16[2,2,2,16,1024]{4,3,2,1,0:T(8,128)(2,1)S(1)}, u32[]{:S(2)}, u32[]{:S(2)}) collective-permute-start(bf16[2,2,2,16,1024]{4,3,2,1,0:T(8,128)(2,1)S(1)} %pad_maximum_fusion.13), channel_id=1, source_target_pairs={{0,2},{2,0},{4,6},{6,4},{8,10},{10,8},{12,14},{14,12},{16,18},{18,... | collective-permute-start | bytes 786440 | tf_op jit(solution)/shard_map/ppermute | solution.py:75
  41.2 13.9 %collective-permute-start.17 = (bf16[2,2,2,16,1024]{4,3,2,1,0:T(8,128)(2,1)S(1)}, bf16[2,2,2,16,1024]{4,3,2,1,0:T(8,128)(2,1)S(1)}, u32[]{:S(2)}, u32[]{:S(2)}) collective-permute-start(bf16[2,2,2,16,1024]{4,3,2,1,0:T(8,128)(2,1)S(1)} %pad_maximum_fusion.10), channel_id=1, source_target_pairs={{0,16},{2,18},{4,20},{6,22},{8,24},{10,26},{12,28},{14,30},{16,0},... | collective-permute-start | bytes 786440 | tf_op jit(solution)/shard_map/ppermute | solution.py:75
  42.8 14.1 %collective-permute-start.9 = (bf16[2,2,2,16,1024]{4,3,2,1,0:T(8,128)(2,1)S(1)}, bf16[2,2,2,16,1024]{4,3,2,1,0:T(8,128)(2,1)S(1)}, u32[]{:S(2)}, u32[]{:S(2)}) collective-permute-start(bf16[2,2,2,16,1024]{4,3,2,1,0:T(8,128)(2,1)S(1)} %pad_maximum_fusion.7), channel_id=1, source_target_pairs={{0,8},{2,10},{4,12},{6,14},{8,0},{10,2},{12,4},{14,6},{16,24},{18,... | collective-permute-start | bytes 786440 | tf_op jit(solution)/shard_map/ppermute | solution.py:75
  47.0 10.1 %collective-permute-start.1 = (bf16[2,2,2,16,1024]{4,3,2,1,0:T(8,128)(2,1)S(1)}, bf16[2,2,2,16,1024]{4,3,2,1,0:T(8,128)(2,1)S(1)}, u32[]{:S(2)}, u32[]{:S(2)}) collective-permute-start(bf16[2,2,2,16,1024]{4,3,2,1,0:T(8,128)(2,1)S(1)} %pad_maximum_fusion.4), channel_id=1, source_target_pairs={{0,4},{2,6},{4,0},{6,2},{8,12},{10,14},{12,8},{14,10},{16,20},{18,... | collective-permute-start | bytes 786440 | tf_op jit(solution)/shard_map/ppermute | solution.py:75
  48.3 10.7 %collective-permute-start.26 = (bf16[2,2,16,1024]{3,2,1,0:T(8,128)(2,1)S(1)}, bf16[2,2,16,1024]{3,2,1,0:T(8,128)(2,1)S(1)}, u32[]{:S(2)}, u32[]{:S(2)}) collective-permute-start(bf16[2,2,16,1024]{3,2,1,0:T(8,128)(2,1)S(1)} %pad_maximum_fusion.30), channel_id=1, source_target_pairs={{0,4},{2,6},{4,0},{6,2},{8,12},{10,14},{12,8},{14,10},{16,20},{18,... | collective-permute-start | bytes 393224 | tf_op jit(solution)/shard_map/ppermute | solution.py:75
  57.0 7.5 %collective-permute-start.10 = (bf16[2,2,16,1024]{3,2,1,0:T(8,128)(2,1)S(1)}, bf16[2,2,16,1024]{3,2,1,0:T(8,128)(2,1)S(1)}, u32[]{:S(2)}, u32[]{:S(2)}) collective-permute-start(bf16[2,2,16,1024]{3,2,1,0:T(8,128)(2,1)S(1)} %pad_maximum_fusion.24), channel_id=1, source_target_pairs={{0,16},{2,18},{4,20},{6,22},{8,24},{10,26},{12,28},{14,30},{16,0},... | collective-permute-start | bytes 393224 | tf_op jit(solution)/shard_map/ppermute | solution.py:75
  57.3 8.6 %collective-permute-start.2 = (bf16[2,2,16,1024]{3,2,1,0:T(8,128)(2,1)S(1)}, bf16[2,2,16,1024]{3,2,1,0:T(8,128)(2,1)S(1)}, u32[]{:S(2)}, u32[]{:S(2)}) collective-permute-start(bf16[2,2,16,1024]{3,2,1,0:T(8,128)(2,1)S(1)} %pad_maximum_fusion.21), channel_id=1, source_target_pairs={{0,8},{2,10},{4,12},{6,14},{8,0},{10,2},{12,4},{14,6},{16,24},{18,... | collective-permute-start | bytes 393224 | tf_op jit(solution)/shard_map/ppermute | solution.py:75
  59.1 7.4 %collective-permute-start.27 = (bf16[2,16,1024]{2,1,0:T(8,128)(2,1)S(1)}, bf16[2,16,1024]{2,1,0:T(8,128)(2,1)S(1)}, u32[]{:S(2)}, u32[]{:S(2)}) collective-permute-start(bf16[2,16,1024]{2,1,0:T(8,128)(2,1)S(1)} %pad_maximum_fusion.49), channel_id=1, source_target_pairs={{0,8},{2,10},{4,12},{6,14},{8,0},{10,2},{12,4},{14,6},{16,24},{18,... | collective-permute-start | bytes 196616 | tf_op jit(solution)/shard_map/ppermute | solution.py:75
  60.6 8.4 %collective-permute-start.19 = (bf16[2,16,1024]{2,1,0:T(8,128)(2,1)S(1)}, bf16[2,16,1024]{2,1,0:T(8,128)(2,1)S(1)}, u32[]{:S(2)}, u32[]{:S(2)}) collective-permute-start(bf16[2,16,1024]{2,1,0:T(8,128)(2,1)S(1)} %pad_maximum_fusion.45), channel_id=1, source_target_pairs={{0,4},{2,6},{4,0},{6,2},{8,12},{10,14},{12,8},{14,10},{16,20},{18,... | collective-permute-start | bytes 196616 | tf_op jit(solution)/shard_map/ppermute | solution.py:75
  65.9 5.7 %collective-permute-start.3 = (bf16[2,16,1024]{2,1,0:T(8,128)(2,1)S(1)}, bf16[2,16,1024]{2,1,0:T(8,128)(2,1)S(1)}, u32[]{:S(2)}, u32[]{:S(2)}) collective-permute-start(bf16[2,16,1024]{2,1,0:T(8,128)(2,1)S(1)} %pad_maximum_fusion.37), channel_id=1, source_target_pairs={{0,16},{2,18},{4,20},{6,22},{8,24},{10,26},{12,28},{14,30},{16,0},... | collective-permute-start | bytes 196616 | tf_op jit(solution)/shard_map/ppermute | solution.py:75
  71.7 6.1 %collective-permute-start.4 = (bf16[2,16,1024]{2,1,0:T(8,128)(2,1)S(1)}, bf16[2,16,1024]{2,1,0:T(8,128)(2,1)S(1)}, u32[]{:S(2)}, u32[]{:S(2)}) collective-permute-start(bf16[2,16,1024]{2,1,0:T(8,128)(2,1)S(1)} %pad_maximum_fusion.38), channel_id=1, source_target_pairs={{0,16},{2,18},{4,20},{6,22},{8,24},{10,26},{12,28},{14,30},{16,0},... | collective-permute-start | bytes 196616 | tf_op jit(solution)/shard_map/ppermute | solution.py:85
  72.1 5.8 %collective-permute-start.29 = (bf16[2,2,16,1024]{3,2,1,0:T(8,128)(2,1)S(1)}, bf16[2,2,16,1024]{3,2,1,0:T(8,128)(2,1)S(1)}, u32[]{:S(2)}, u32[]{:S(2)}) collective-permute-start(bf16[2,2,16,1024]{3,2,1,0:T(8,128)(2,1)S(1)} %pad_maximum_fusion.31), channel_id=1, source_target_pairs={{0,4},{2,6},{4,0},{6,2},{8,12},{10,14},{12,8},{14,10},{16,20},{18,... | collective-permute-start | bytes 393224 | tf_op jit(solution)/shard_map/ppermute | solution.py:85
  74.1 6.5 %collective-permute-start.21 = (bf16[2,2,16,1024]{3,2,1,0:T(8,128)(2,1)S(1)}, bf16[2,2,16,1024]{3,2,1,0:T(8,128)(2,1)S(1)}, u32[]{:S(2)}, u32[]{:S(2)}) collective-permute-start(bf16[2,2,16,1024]{3,2,1,0:T(8,128)(2,1)S(1)} %pad_maximum_fusion.28), channel_id=1, source_target_pairs={{0,2},{2,0},{4,6},{6,4},{8,10},{10,8},{12,14},{14,12},{16,18},{18,... | collective-permute-start | bytes 393224 | tf_op jit(solution)/shard_map/ppermute | solution.py:85
  74.7 9.1 %collective-permute-start.13 = (bf16[2,2,16,1024]{3,2,1,0:T(8,128)(2,1)S(1)}, bf16[2,2,16,1024]{3,2,1,0:T(8,128)(2,1)S(1)}, u32[]{:S(2)}, u32[]{:S(2)}) collective-permute-start(bf16[2,2,16,1024]{3,2,1,0:T(8,128)(2,1)S(1)} %pad_maximum_fusion.25), channel_id=1, source_target_pairs={{0,16},{2,18},{4,20},{6,22},{8,24},{10,26},{12,28},{14,30},{16,0},... | collective-permute-start | bytes 393224 | tf_op jit(solution)/shard_map/ppermute | solution.py:85
  77.8 6.6 %collective-permute-start.5 = (bf16[2,2,16,1024]{3,2,1,0:T(8,128)(2,1)S(1)}, bf16[2,2,16,1024]{3,2,1,0:T(8,128)(2,1)S(1)}, u32[]{:S(2)}, u32[]{:S(2)}) collective-permute-start(bf16[2,2,16,1024]{3,2,1,0:T(8,128)(2,1)S(1)} %pad_maximum_fusion.22), channel_id=1, source_target_pairs={{0,8},{2,10},{4,12},{6,14},{8,0},{10,2},{12,4},{14,6},{16,24},{18,... | collective-permute-start | bytes 393224 | tf_op jit(solution)/shard_map/ppermute | solution.py:85
  78.0 10.6 %collective-permute-start.30 = (bf16[2,2,2,16,1024]{4,3,2,1,0:T(8,128)(2,1)S(1)}, bf16[2,2,2,16,1024]{4,3,2,1,0:T(8,128)(2,1)S(1)}, u32[]{:S(2)}, u32[]{:S(2)}) collective-permute-start(bf16[2,2,2,16,1024]{4,3,2,1,0:T(8,128)(2,1)S(1)} %pad_maximum_fusion.14), channel_id=1, source_target_pairs={{0,2},{2,0},{4,6},{6,4},{8,10},{10,8},{12,14},{14,12},{16,18},{18,... | collective-permute-start | bytes 786440 | tf_op jit(solution)/shard_map/ppermute | solution.py:85
  80.7 16.8 %collective-permute-start.22 = (bf16[2,2,2,16,1024]{4,3,2,1,0:T(8,128)(2,1)S(1)}, bf16[2,2,2,16,1024]{4,3,2,1,0:T(8,128)(2,1)S(1)}, u32[]{:S(2)}, u32[]{:S(2)}) collective-permute-start(bf16[2,2,2,16,1024]{4,3,2,1,0:T(8,128)(2,1)S(1)} %pad_maximum_fusion.11), channel_id=1, source_target_pairs={{0,16},{2,18},{4,20},{6,22},{8,24},{10,26},{12,28},{14,30},{16,0},... | collective-permute-start | bytes 786440 | tf_op jit(solution)/shard_map/ppermute | solution.py:85
  83.8 13.9 %collective-permute-start.14 = (bf16[2,2,2,16,1024]{4,3,2,1,0:T(8,128)(2,1)S(1)}, bf16[2,2,2,16,1024]{4,3,2,1,0:T(8,128)(2,1)S(1)}, u32[]{:S(2)}, u32[]{:S(2)}) collective-permute-start(bf16[2,2,2,16,1024]{4,3,2,1,0:T(8,128)(2,1)S(1)} %pad_maximum_fusion.8), channel_id=1, source_target_pairs={{0,8},{2,10},{4,12},{6,14},{8,0},{10,2},{12,4},{14,6},{16,24},{18,... | collective-permute-start | bytes 786440 | tf_op jit(solution)/shard_map/ppermute | solution.py:85
  84.6 14.9 %collective-permute-start.6 = (bf16[2,2,2,16,1024]{4,3,2,1,0:T(8,128)(2,1)S(1)}, bf16[2,2,2,16,1024]{4,3,2,1,0:T(8,128)(2,1)S(1)}, u32[]{:S(2)}, u32[]{:S(2)}) collective-permute-start(bf16[2,2,2,16,1024]{4,3,2,1,0:T(8,128)(2,1)S(1)} %pad_maximum_fusion.5), channel_id=1, source_target_pairs={{0,4},{2,6},{4,0},{6,2},{8,12},{10,14},{12,8},{14,10},{16,20},{18,... | collective-permute-start | bytes 786440 | tf_op jit(solution)/shard_map/ppermute | solution.py:85
  88.7 16.6 %collective-permute-start.36 = (bf16[1,2,2,2,16,1024]{5,4,3,2,1,0:T(8,128)(2,1)S(1)}, bf16[1,2,2,2,16,1024]{5,4,3,2,1,0:T(8,128)(2,1)S(1)}, u32[]{:S(2)}, u32[]{:S(2)}) collective-permute-start(bf16[1,2,2,2,16,1024]{5,4,3,2,1,0:T(8,128)(2,1)S(1)} %maximum_bitcast_fusion.17), channel_id=1, source_target_pairs={{0,16},{2,18},{4,20},{6,22},{8,24},{10,26},{12,28},{14,30},{16,0},... | collective-permute-start | bytes 786440 | tf_op jit(solution)/shard_map/ppermute | solution.py:85
  97.6 10.3 %collective-permute-start.35 = (bf16[1,2,2,2,16,1024]{5,4,3,2,1,0:T(8,128)(2,1)S(1)}, bf16[1,2,2,2,16,1024]{5,4,3,2,1,0:T(8,128)(2,1)S(1)}, u32[]{:S(2)}, u32[]{:S(2)}) collective-permute-start(bf16[1,2,2,2,16,1024]{5,4,3,2,1,0:T(8,128)(2,1)S(1)} %maximum_bitcast_fusion.16), channel_id=1, source_target_pairs={{0,8},{2,10},{4,12},{6,14},{8,0},{10,2},{12,4},{14,6},{16,24},{18,... | collective-permute-start | bytes 786440 | tf_op jit(solution)/shard_map/ppermute | solution.py:85
  97.8 10.3 %collective-permute-start.34 = (bf16[1,2,2,2,16,1024]{5,4,3,2,1,0:T(8,128)(2,1)S(1)}, bf16[1,2,2,2,16,1024]{5,4,3,2,1,0:T(8,128)(2,1)S(1)}, u32[]{:S(2)}, u32[]{:S(2)}) collective-permute-start(bf16[1,2,2,2,16,1024]{5,4,3,2,1,0:T(8,128)(2,1)S(1)} %maximum_bitcast_fusion.15), channel_id=1, source_target_pairs={{0,4},{2,6},{4,0},{6,2},{8,12},{10,14},{12,8},{14,10},{16,20},{18,... | collective-permute-start | bytes 786440 | tf_op jit(solution)/shard_map/ppermute | solution.py:85
  99.6 10.0 %collective-permute-start.33 = (bf16[1,2,2,2,16,1024]{5,4,3,2,1,0:T(8,128)(2,1)S(1)}, bf16[1,2,2,2,16,1024]{5,4,3,2,1,0:T(8,128)(2,1)S(1)}, u32[]{:S(2)}, u32[]{:S(2)}) collective-permute-start(bf16[1,2,2,2,16,1024]{5,4,3,2,1,0:T(8,128)(2,1)S(1)} %maximum_bitcast_fusion.14), channel_id=1, source_target_pairs={{0,2},{2,0},{4,6},{6,4},{8,10},{10,8},{12,14},{14,12},{16,18},{18,... | collective-permute-start | bytes 786440 | tf_op jit(solution)/shard_map/ppermute | solution.py:85
  100.6 9.0 %collective-permute-start.7 = (bf16[1,2,2,2,16,1024]{5,4,3,2,1,0:T(8,128)(2,1)S(1)}, bf16[1,2,2,2,16,1024]{5,4,3,2,1,0:T(8,128)(2,1)S(1)}, u32[]{:S(2)}, u32[]{:S(2)}) collective-permute-start(bf16[1,2,2,2,16,1024]{5,4,3,2,1,0:T(8,128)(2,1)S(1)} %maximum_bitcast_fusion.10), channel_id=1, source_target_pairs={{0,2},{2,0},{4,6},{6,4},{8,10},{10,8},{12,14},{14,12},{16,18},{18,... | collective-permute-start | bytes 786440 | tf_op jit(solution)/shard_map/ppermute | solution.py:85
  105.2 20.0 %collective-permute-start.31 = (bf16[1,2,2,2,16,1024]{5,4,3,2,1,0:T(8,128)(2,1)S(1)}, bf16[1,2,2,2,16,1024]{5,4,3,2,1,0:T(8,128)(2,1)S(1)}, u32[]{:S(2)}, u32[]{:S(2)}) collective-permute-start(bf16[1,2,2,2,16,1024]{5,4,3,2,1,0:T(8,128)(2,1)S(1)} %maximum_bitcast_fusion.13), channel_id=1, source_target_pairs={{0,16},{2,18},{4,20},{6,22},{8,24},{10,26},{12,28},{14,30},{16,0},... | collective-permute-start | bytes 786440 | tf_op jit(solution)/shard_map/ppermute | solution.py:85
  107.9 17.4 %collective-permute-start.23 = (bf16[1,2,2,2,16,1024]{5,4,3,2,1,0:T(8,128)(2,1)S(1)}, bf16[1,2,2,2,16,1024]{5,4,3,2,1,0:T(8,128)(2,1)S(1)}, u32[]{:S(2)}, u32[]{:S(2)}) collective-permute-start(bf16[1,2,2,2,16,1024]{5,4,3,2,1,0:T(8,128)(2,1)S(1)} %maximum_bitcast_fusion.12), channel_id=1, source_target_pairs={{0,8},{2,10},{4,12},{6,14},{8,0},{10,2},{12,4},{14,6},{16,24},{18,... | collective-permute-start | bytes 786440 | tf_op jit(solution)/shard_map/ppermute | solution.py:85
  108.1 17.4 %collective-permute-start.15 = (bf16[1,2,2,2,16,1024]{5,4,3,2,1,0:T(8,128)(2,1)S(1)}, bf16[1,2,2,2,16,1024]{5,4,3,2,1,0:T(8,128)(2,1)S(1)}, u32[]{:S(2)}, u32[]{:S(2)}) collective-permute-start(bf16[1,2,2,2,16,1024]{5,4,3,2,1,0:T(8,128)(2,1)S(1)} %maximum_bitcast_fusion.11), channel_id=1, source_target_pairs={{0,4},{2,6},{4,0},{6,2},{8,12},{10,14},{12,8},{14,10},{16,20},{18,... | collective-permute-start | bytes 786440 | tf_op jit(solution)/shard_map/ppermute | solution.py:85
  (22 other events, 113.7 us)

commit v17 on v13

--- a/solution.py
+++ b/solution.py
@@ -42,7 +42,7 @@
     return value
 
 
-def spread_blocks(block, roots, axis):
+def spread_blocks(block, roots, axis, later=None):
     size = lax.axis_size(axis)
     place = lax.axis_index(axis)
     nbits = size.bit_length() - 1
@@ -53,7 +53,7 @@
         own = place == roots
         flipped = jnp.transpose(block)
         masked = jnp.where(own[:, None, None], flipped[None], jnp.zeros_like(flipped)[None])
-        return lax.psum(masked, axis)
+        return lax.psum(masked, axis), later
     piece = rows // (parts * size)
     orders = [[1 << ((p + s) % nbits) for s in range(nbits)] for p in range(parts)]
     bufs = {}
@@ -77,6 +77,10 @@
                 held = sum(orders[key[0]][:s])
                 holder = ((place ^ roots[key[1]]) & (size - 1 - held)) == 0
                 bufs[key] = jnp.where(holder, keeps[key], got[n])
+        if s == 0:
+            keys = sorted(bufs)
+            vals, later = lax.optimization_barrier(([bufs[k] for k in keys], later))
+            bufs = dict(zip(keys, vals))
     for s in reversed(range(nbits)):
         sends = {}
         for (p, r), buf in bufs.items():
@@ -96,7 +100,7 @@
             inverse = [perm.index(k) for k in range(nbits)] + [nbits, nbits + 1]
             segs.append(jnp.transpose(bufs[p, r], inverse).reshape(piece * size, chans))
         out.append(jnp.concatenate(segs, axis=0))
-    return jnp.stack(out)
+    return jnp.stack(out), later
 
 
 def correlate_kernel(meta_ref, blk_ref, ext_ref, corr_ref, power_ref):
@@ -187,7 +191,7 @@
     upper = chan_range[:, :, 1]
     inside = (channel >= lower[:, :, None]) & (channel < upper[:, :, None])
 
-    blocks = spread_blocks(signal, round_shard, "tm")
+    blocks, extended = spread_blocks(signal, round_shard, "tm", extended)
     offs = jnp.clip(offsets, 0, lag_count - L)
     first = jnp.minimum((offs // 16) * 16, lag_count - REACH)
     base = section * chan_local

time: 156 us -> 165 us (1.058)
  waiting for transfers between devices: 41.1 us -> 46.3 us
  starting transfers between devices: 53.1 us -> 57.9 us
  local copies, waits for them, and re-layouts: 15 us -> 12.3 us
    ppermute x1, waiting for transfers between devices: 0.01 us -> 11.6 us  [from_behind(): return lax.ppermute(value, axis, pairs)]
    ppermute x36, waiting for transfers between devices: 35.9 us -> 28.7 us  [spread_blocks(): lax.ppermute(jnp.stack([v for _, v in items]), axis, [(i, i ^ mask) for i...]
    ppermute x36, starting transfers between devices: 43.3 us -> 48 us  [spread_blocks(): lax.ppermute(jnp.stack([v for _, v in items]), axis, [(i, i ^ mask) for i...]
    unnamed x23 -> x22, local copies, waits for them, and re-layouts: 4.15 us -> 3.49 us
  transfers between devices with their start and end apart: 45 -> 45, of which waited for: 21 -> 18; matrix products, arithmetic and copies ran while one was open for 18% -> 14% of each run, Pallas kernels for 8% -> 7%
where the time goes in v17:
time: 165 us; the launch traced here: 164 us
  starting transfers between devices  57.9 us (35%)
  waiting for transfers between devices  46.3 us (28%)
  Pallas kernels  23.8 us (14%)
  other arithmetic  19.7 us (12%)
  local copies, waits for them, and re-layouts  12.3 us (7%)
  between operations  2.65 us (2%)
    ppermute x36, starting transfers between devices, spread_blocks(): lax.ppermute(jnp.stack([v for _, v in items]), axis, [(i, i ^ mask) for i...  48 us
    ppermute x36, waiting for transfers between devices, spread_blocks(): lax.ppermute(jnp.stack([v for _, v in items]), axis, [(i, i ^ mask) for i...  28.7 us
    pallas_call x2, Pallas kernels, correlate(): pl.pallas_call(correlate_kernel, grid_spec=grid_spec, out_shape=[jax.Shap...  23.8 us
    ppermute x1, waiting for transfers between devices, from_behind(): return lax.ppermute(value, axis, pairs)  11.6 us
    ppermute x8, starting transfers between devices, group_sum(): got[d] = lax.ppermute(value, axis, pairs)  8.61 us
    select_n x18, other arithmetic, spread_blocks(): bufs[key] = jnp.where(holder, keeps[key], got[n])  6.19 us
    ppermute x8, waiting for transfers between devices, group_sum(): got[d] = lax.ppermute(value, axis, pairs)  5.98 us
    another operation x52, other arithmetic, spread_blocks(): jnp.stack([v for _, v in items])  4.23 us
  transfers between devices with their start and end apart: 45, of which 18 were waited for; matrix products, arithmetic and copies ran while one was open for 14% of the time, Pallas kernels for 7%

profile of v17, /device:TPU:0, one launch (start us, length us, event | category | flops | bytes accessed | tf_op | source)
XLA Modules:
  0.0 164.0 jit_solution(392290092558753180)
XLA Ops:
  0.0 2.5 %fusion.35 = (bf16[1024,256]{1,0:T(8,128)(2,1)S(1)}, bf16[1024,256]{1,0:T(8,128)(2,1)S(1)}, bf16[1024,256]{1,0:T(8,128)(2,1)S(1)}, bf16[1024,256]{1,0:T(8,128)(2,1)}) fusion(bf16[1024,1024]{1,0:T(8,128)(2,1)} %param.4), kind=kLoop, calls=%fused_computation.309 | loop fusion | bytes 4194304 | tf_op jit(solution)/shard_map/slice | solution.py:61
  3.6 4.0 %collective-permute-start.3 = (bf16[2,2,2,2,16,1024]{5,4,3,2,1,0:T(8,128)(2,1)}, bf16[2,2,2,2,16,1024]{5,4,3,2,1,0:T(8,128)(2,1)}, u32[]{:S(2)}, u32[]{:S(2)}) collective-permute-start(bf16[2,2,2,2,16,1024]{5,4,3,2,1,0:T(8,128)(2,1)} %pad_maximum_fusion.4), channel_id=1, source_target_pairs={{0,16},{2,18},{4,20},{6,22},{8,24},{10,26},{12,28},{14,30},{16,0},... | collective-permute-start | bytes 1572872 | tf_op jit(solution)/shard_map/ppermute | solution.py:75
  8.8 1.6 collective-permute-start.2
  13.9 2.0 %copy.66 = bf16[1024,256]{0,1:T(8,128)(2,1)} copy(bf16[1024,256]{1,0:T(8,128)(2,1)} %get-tuple-element.38) | data formatting | bytes 1048576
  15.9 1.8 %fusion.36 = (bf16[1,2,2,2,16,1024]{5,4,0,1,2,3:T(8,128)(2,1)S(1)}, bf16[1,2,2,2,16,1024]{5,4,0,1,2,3:T(8,128)(2,1)S(1)}, bf16[1,2,2,2,16,1024]{5,4,0,1,2,3:T(8,128)(2,1)}) fusion(bf16[2,2,2,2,16,1024]{5,4,0,1,2,3:T(8,128)(2,1)} %bitcast.280, pred[]{:T(512)S(6)} %eq.170), kind=kLoop, calls=%fused_computation.310 | loop fusion | flops 131072 | bytes 1310721 | tf_op jit(solution)/shard_map/slice | solution.py:72
  25.7 11.6 %collective-permute-done.4 = bf16[1024,128]{1,0:T(8,128)(2,1)} collective-permute-done((bf16[1024,128]{1,0:T(8,128)(2,1)}, bf16[1024,128]{1,0:T(8,128)(2,1)}, u32[]{:S(2)}, u32[]{:S(2)}) %collective-permute-start.4) | collective-permute-done | bytes 262176 | tf_op jit(solution)/shard_map/ppermute | solution.py:18
  38.5 1.6 fusion.5
  46.2 2.9 %collective-permute-start.26 = (bf16[2,2,2,16,1024]{4,3,2,1,0:T(8,128)(2,1)S(1)}, bf16[2,2,2,16,1024]{4,3,2,1,0:T(8,128)(2,1)S(1)}, u32[]{:S(2)}, u32[]{:S(2)}) collective-permute-start(bf16[2,2,2,16,1024]{4,3,2,1,0:T(8,128)(2,1)S(1)} %pad_maximum_fusion.14), channel_id=1, source_target_pairs={{0,2},{2,0},{4,6},{6,4},{8,10},{10,8},{12,14},{14,12},{16,18},{18,... | collective-permute-start | bytes 786440 | tf_op jit(solution)/shard_map/ppermute | solution.py:75
  51.5 2.1 %collective-permute-start.6 = (bf16[2,2,16,1024]{3,2,1,0:T(8,128)(2,1)S(1)}, bf16[2,2,16,1024]{3,2,1,0:T(8,128)(2,1)S(1)}, u32[]{:S(2)}, u32[]{:S(2)}) collective-permute-start(bf16[2,2,16,1024]{3,2,1,0:T(8,128)(2,1)S(1)} %pad_maximum_fusion.22), channel_id=1, source_target_pairs={{0,8},{2,10},{4,12},{6,14},{8,0},{10,2},{12,4},{14,6},{16,24},{18,... | collective-permute-start | bytes 393224 | tf_op jit(solution)/shard_map/ppermute | solution.py:75
  53.6 4.2 %collective-permute-done.12 = bf16[2,2,2,16,1024]{4,3,2,1,0:T(8,128)(2,1)S(1)} collective-permute-done((bf16[2,2,2,16,1024]{4,3,2,1,0:T(8,128)(2,1)S(1)}, bf16[2,2,2,16,1024]{4,3,2,1,0:T(8,128)(2,1)S(1)}, u32[]{:S(2)}, u32[]{:S(2)}) %collective-permute-start.12) | collective-permute-done | bytes 262176 | tf_op jit(solution)/shard_map/ppermute | solution.py:75
  58.0 3.5 %collective-permute-done.19 = bf16[2,2,2,16,1024]{4,3,2,1,0:T(8,128)(2,1)S(1)} collective-permute-done((bf16[2,2,2,16,1024]{4,3,2,1,0:T(8,128)(2,1)S(1)}, bf16[2,2,2,16,1024]{4,3,2,1,0:T(8,128)(2,1)S(1)}, u32[]{:S(2)}, u32[]{:S(2)}) %collective-permute-start.19) | collective-permute-done | bytes 262176 | tf_op jit(solution)/shard_map/ppermute | solution.py:75
  62.6 3.0 %collective-permute-start.27 = (bf16[2,2,16,1024]{3,2,1,0:T(8,128)(2,1)S(1)}, bf16[2,2,16,1024]{3,2,1,0:T(8,128)(2,1)S(1)}, u32[]{:S(2)}, u32[]{:S(2)}) collective-permute-start(bf16[2,2,16,1024]{3,2,1,0:T(8,128)(2,1)S(1)} %pad_maximum_fusion.31), channel_id=1, source_target_pairs={{0,4},{2,6},{4,0},{6,2},{8,12},{10,14},{12,8},{14,10},{16,20},{18,... | collective-permute-start | bytes 393224 | tf_op jit(solution)/shard_map/ppermute | solution.py:75
  66.1 3.6 %collective-permute-start.14 = (bf16[2,16,1024]{2,1,0:T(8,128)(2,1)S(1)}, bf16[2,16,1024]{2,1,0:T(8,128)(2,1)S(1)}, u32[]{:S(2)}, u32[]{:S(2)}) collective-permute-start(bf16[2,16,1024]{2,1,0:T(8,128)(2,1)S(1)} %pad_maximum_fusion.42), channel_id=1, source_target_pairs={{0,2},{2,0},{4,6},{6,4},{8,10},{10,8},{12,14},{14,12},{16,18},{18,... | collective-permute-start | bytes 196616 | tf_op jit(solution)/shard_map/ppermute | solution.py:75
  72.4 1.7 %collective-permute-start.15 = (bf16[2,16,1024]{2,1,0:T(8,128)(2,1)S(1)}, bf16[2,16,1024]{2,1,0:T(8,128)(2,1)S(1)}, u32[]{:S(2)}, u32[]{:S(2)}) collective-permute-start(bf16[2,16,1024]{2,1,0:T(8,128)(2,1)S(1)} %pad_maximum_fusion.43), channel_id=1, source_target_pairs={{0,2},{2,0},{4,6},{6,4},{8,10},{10,8},{12,14},{14,12},{16,18},{18,... | collective-permute-start | bytes 196616 | tf_op jit(solution)/shard_map/ppermute | solution.py:89
  74.9 1.8 %collective-permute-done.28 = bf16[2,16,1024]{2,1,0:T(8,128)(2,1)S(1)} collective-permute-done((bf16[2,16,1024]{2,1,0:T(8,128)(2,1)S(1)}, bf16[2,16,1024]{2,1,0:T(8,128)(2,1)S(1)}, u32[]{:S(2)}, u32[]{:S(2)}) %collective-permute-start.28) | collective-permute-done | bytes 65568 | tf_op jit(solution)/shard_map/ppermute | solution.py:75
  76.8 2.2 %collective-permute-done.8 = bf16[2,16,1024]{2,1,0:T(8,128)(2,1)S(1)} collective-permute-done((bf16[2,16,1024]{2,1,0:T(8,128)(2,1)S(1)}, bf16[2,16,1024]{2,1,0:T(8,128)(2,1)S(1)}, u32[]{:S(2)}, u32[]{:S(2)}) %collective-permute-start.8) | collective-permute-done | bytes 65568 | tf_op jit(solution)/shard_map/ppermute | solution.py:89
  79.3 2.3 %collective-permute-start.16 = (bf16[2,2,16,1024]{3,2,1,0:T(8,128)(2,1)S(1)}, bf16[2,2,16,1024]{3,2,1,0:T(8,128)(2,1)S(1)}, u32[]{:S(2)}, u32[]{:S(2)}) collective-permute-start(bf16[2,2,16,1024]{3,2,1,0:T(8,128)(2,1)S(1)} %pad_maximum_fusion.26), channel_id=1, source_target_pairs={{0,16},{2,18},{4,20},{6,22},{8,24},{10,26},{12,28},{14,30},{16,0},... | collective-permute-start | bytes 393224 | tf_op jit(solution)/shard_map/ppermute | solution.py:89
  81.8 2.1 %collective-permute-start.30 = (bf16[2,2,16,1024]{3,2,1,0:T(8,128)(2,1)S(1)}, bf16[2,2,16,1024]{3,2,1,0:T(8,128)(2,1)S(1)}, u32[]{:S(2)}, u32[]{:S(2)}) collective-permute-start(bf16[2,2,16,1024]{3,2,1,0:T(8,128)(2,1)S(1)} %pad_maximum_fusion.32), channel_id=1, source_target_pairs={{0,4},{2,6},{4,0},{6,2},{8,12},{10,14},{12,8},{14,10},{16,20},{18,... | collective-permute-start | bytes 393224 | tf_op jit(solution)/shard_map/ppermute | solution.py:89
  83.9 4.8 %collective-permute-done.9 = bf16[2,2,16,1024]{3,2,1,0:T(8,128)(2,1)S(1)} collective-permute-done((bf16[2,2,16,1024]{3,2,1,0:T(8,128)(2,1)S(1)}, bf16[2,2,16,1024]{3,2,1,0:T(8,128)(2,1)S(1)}, u32[]{:S(2)}, u32[]{:S(2)}) %collective-permute-start.9) | collective-permute-done | bytes 131104 | tf_op jit(solution)/shard_map/ppermute | solution.py:89
  88.8 2.0 %collective-permute-start.10 = (bf16[2,2,2,16,1024]{4,3,2,1,0:T(8,128)(2,1)S(1)}, bf16[2,2,2,16,1024]{4,3,2,1,0:T(8,128)(2,1)S(1)}, u32[]{:S(2)}, u32[]{:S(2)}) collective-permute-start(bf16[2,2,2,16,1024]{4,3,2,1,0:T(8,128)(2,1)S(1)} %pad_maximum_fusion.6), channel_id=1, source_target_pairs={{0,4},{2,6},{4,0},{6,2},{8,12},{10,14},{12,8},{14,10},{16,20},{18,... | collective-permute-start | bytes 786440 | tf_op jit(solution)/shard_map/ppermute | solution.py:89
  91.2 2.7 %collective-permute-start.24 = (bf16[2,2,2,16,1024]{4,3,2,1,0:T(8,128)(2,1)S(1)}, bf16[2,2,2,16,1024]{4,3,2,1,0:T(8,128)(2,1)S(1)}, u32[]{:S(2)}, u32[]{:S(2)}) collective-permute-start(bf16[2,2,2,16,1024]{4,3,2,1,0:T(8,128)(2,1)S(1)} %pad_maximum_fusion.12), channel_id=1, source_target_pairs={{0,16},{2,18},{4,20},{6,22},{8,24},{10,26},{12,28},{14,30},{16,0},... | collective-permute-start | bytes 786440 | tf_op jit(solution)/shard_map/ppermute | solution.py:89
  94.2 3.9 %collective-permute-done.10 = bf16[2,2,2,16,1024]{4,3,2,1,0:T(8,128)(2,1)S(1)} collective-permute-done((bf16[2,2,2,16,1024]{4,3,2,1,0:T(8,128)(2,1)S(1)}, bf16[2,2,2,16,1024]{4,3,2,1,0:T(8,128)(2,1)S(1)}, u32[]{:S(2)}, u32[]{:S(2)}) %collective-permute-start.10) | collective-permute-done | bytes 262176 | tf_op jit(solution)/shard_map/ppermute | solution.py:89
  100.3 4.7 %collective-permute-done.17 = bf16[2,2,2,16,1024]{4,3,2,1,0:T(8,128)(2,1)S(1)} collective-permute-done((bf16[2,2,2,16,1024]{4,3,2,1,0:T(8,128)(2,1)S(1)}, bf16[2,2,2,16,1024]{4,3,2,1,0:T(8,128)(2,1)S(1)}, u32[]{:S(2)}, u32[]{:S(2)}) %collective-permute-start.17) | collective-permute-done | bytes 262176 | tf_op jit(solution)/shard_map/ppermute | solution.py:89
  105.1 1.8 %collective-permute-start.18 = (bf16[1,2,2,2,16,1024]{5,4,3,2,1,0:T(8,128)(2,1)S(1)}, bf16[1,2,2,2,16,1024]{5,4,3,2,1,0:T(8,128)(2,1)S(1)}, u32[]{:S(2)}, u32[]{:S(2)}) collective-permute-start(bf16[1,2,2,2,16,1024]{5,4,3,2,1,0:T(8,128)(2,1)S(1)} %maximum_bitcast_fusion.11), channel_id=1, source_target_pairs={{0,4},{2,6},{4,0},{6,2},{8,12},{10,14},{12,8},{14,10},{16,20},{18,... | collective-permute-start | bytes 786440 | tf_op jit(solution)/shard_map/ppermute | solution.py:89
  107.3 2.7 %collective-permute-start.32 = (bf16[1,2,2,2,16,1024]{5,4,3,2,1,0:T(8,128)(2,1)S(1)}, bf16[1,2,2,2,16,1024]{5,4,3,2,1,0:T(8,128)(2,1)S(1)}, u32[]{:S(2)}, u32[]{:S(2)}) collective-permute-start(bf16[1,2,2,2,16,1024]{5,4,3,2,1,0:T(8,128)(2,1)S(1)} %maximum_bitcast_fusion.13), channel_id=1, source_target_pairs={{0,16},{2,18},{4,20},{6,22},{8,24},{10,26},{12,28},{14,30},{16,0},... | collective-permute-start | bytes 786440 | tf_op jit(solution)/shard_map/ppermute | solution.py:89
  110.1 1.7 %collective-permute-start.34 = (bf16[1,2,2,2,16,1024]{5,4,3,2,1,0:T(8,128)(2,1)S(1)}, bf16[1,2,2,2,16,1024]{5,4,3,2,1,0:T(8,128)(2,1)S(1)}, u32[]{:S(2)}, u32[]{:S(2)}) collective-permute-start(bf16[1,2,2,2,16,1024]{5,4,3,2,1,0:T(8,128)(2,1)S(1)} %maximum_bitcast_fusion.15), channel_id=1, source_target_pairs={{0,4},{2,6},{4,0},{6,2},{8,12},{10,14},{12,8},{14,10},{16,20},{18,... | collective-permute-start | bytes 786440 | tf_op jit(solution)/shard_map/ppermute | solution.py:89
  112.0 2.7 %collective-permute-start.36 = (bf16[1,2,2,2,16,1024]{5,4,3,2,1,0:T(8,128)(2,1)S(1)}, bf16[1,2,2,2,16,1024]{5,4,3,2,1,0:T(8,128)(2,1)S(1)}, u32[]{:S(2)}, u32[]{:S(2)}) collective-permute-start(bf16[1,2,2,2,16,1024]{5,4,3,2,1,0:T(8,128)(2,1)S(1)} %maximum_bitcast_fusion.17), channel_id=1, source_target_pairs={{0,16},{2,18},{4,20},{6,22},{8,24},{10,26},{12,28},{14,30},{16,0},... | collective-permute-start | bytes 786440 | tf_op jit(solution)/shard_map/ppermute | solution.py:89
  119.5 11.9 %shard_map.46 = (f32[4,4,1024]{2,1,0:T(4,128)}, f32[4,4,128]{2,1,0:T(4,128)}) custom-call(s32[64]{0:T(128)} %squeeze.16.meta_ref, bf16[1,1024,1024]{2,1,0:T(8,128)(2,1)} %maximum_bitcast_fusion.blk_ref, bf16[1024,1152]{1,0:T(8,128)(2,1)} %copy-done.3), custom_call_target="tpu_custom_call" | custom-call | flops 5435817984 | bytes 4521984 | tf_op jit(solution)/shard_map/pallas_call | solution.py:160
  134.4 11.9 %shard_map.47 = (f32[4,4,1024]{2,1,0:T(4,128)}, f32[4,4,128]{2,1,0:T(4,128)}) custom-call(s32[64]{0:T(128)} %squeeze.19.meta_ref, bf16[1,1024,1024]{2,1,0:T(8,128)(2,1)} %maximum_bitcast_fusion.1.blk_ref, bf16[1024,1152]{1,0:T(8,128)(2,1)} %copy-done.3), custom_call_target="tpu_custom_call" | custom-call | flops 5435817984 | bytes 4521984 | tf_op jit(solution)/shard_map/pallas_call | solution.py:160
  150.0 2.6 %collective-permute-start.39 = (f32[32]{0:T(128)S(1)}, f32[32]{0:T(128)S(1)}, u32[]{:S(2)}, u32[]{:S(2)}) collective-permute-start(f32[32]{0:T(128)S(1)} %fusion.18), channel_id=1, source_target_pairs={{0,6},{2,4},{4,2},{6,0},{8,14},{10,12},{12,10},{14,8},{16,22},{18,... | collective-permute-start | bytes 392 | tf_op jit(solution)/shard_map/ppermute | solution.py:33
  154.5 1.6 collective-permute-done.40
  158.7 2.9 %collective-permute-start.44 = (f32[32]{0:T(128)S(1)}, f32[32]{0:T(128)S(1)}, u32[]{:S(2)}, u32[]{:S(2)}) collective-permute-start(f32[32]{0:T(128)S(1)} %fusion.34), channel_id=1, source_target_pairs={{0,8},{2,10},{4,12},{6,14},{8,0},{10,2},{12,4},{14,6},{16,24},{18,... | collective-permute-start | bytes 392 | tf_op jit(solution)/shard_map/ppermute | solution.py:33
  (261 shorter events, 49.1 us)
Async XLA Ops:
  3.6 34.9 %collective-permute-start.3 = (bf16[2,2,2,2,16,1024]{5,4,3,2,1,0:T(8,128)(2,1)}, bf16[2,2,2,2,16,1024]{5,4,3,2,1,0:T(8,128)(2,1)}, u32[]{:S(2)}, u32[]{:S(2)}) collective-permute-start(bf16[2,2,2,2,16,1024]{5,4,3,2,1,0:T(8,128)(2,1)} %pad_maximum_fusion.4), channel_id=1, source_target_pairs={{0,16},{2,18},{4,20},{6,22},{8,24},{10,26},{12,28},{14,30},{16,0},... | collective-permute-start | bytes 1572872 | tf_op jit(solution)/shard_map/ppermute | solution.py:75
  8.8 31.3 %collective-permute-start.2 = (bf16[2,2,2,2,16,1024]{5,4,3,2,1,0:T(8,128)(2,1)}, bf16[2,2,2,2,16,1024]{5,4,3,2,1,0:T(8,128)(2,1)}, u32[]{:S(2)}, u32[]{:S(2)}) collective-permute-start(bf16[2,2,2,2,16,1024]{5,4,3,2,1,0:T(8,128)(2,1)} %pad_maximum_fusion.3), channel_id=1, source_target_pairs={{0,8},{2,10},{4,12},{6,14},{8,0},{10,2},{12,4},{14,6},{16,24},{18,... | collective-permute-start | bytes 1572872 | tf_op jit(solution)/shard_map/ppermute | solution.py:75
  12.3 28.9 %collective-permute-start.1 = (bf16[2,2,2,2,16,1024]{5,4,3,2,1,0:T(8,128)(2,1)}, bf16[2,2,2,2,16,1024]{5,4,3,2,1,0:T(8,128)(2,1)}, u32[]{:S(2)}, u32[]{:S(2)}) collective-permute-start(bf16[2,2,2,2,16,1024]{5,4,3,2,1,0:T(8,128)(2,1)} %pad_maximum_fusion.2), channel_id=1, source_target_pairs={{0,4},{2,6},{4,0},{6,2},{8,12},{10,14},{12,8},{14,10},{16,20},{18,... | collective-permute-start | bytes 1572872 | tf_op jit(solution)/shard_map/ppermute | solution.py:75
  18.6 23.8 %collective-permute-start = (bf16[2,2,2,2,16,1024]{5,4,0,1,2,3:T(8,128)(2,1)}, bf16[2,2,2,2,16,1024]{5,4,0,1,2,3:T(8,128)(2,1)}, u32[]{:S(2)}, u32[]{:S(2)}) collective-permute-start(bf16[2,2,2,2,16,1024]{5,4,0,1,2,3:T(8,128)(2,1)} %pad_maximum_fusion.1), channel_id=1, source_target_pairs={{0,2},{2,0},{4,6},{6,4},{8,10},{10,8},{12,14},{14,12},{16,18},{18,... | collective-permute-start | bytes 1572872 | tf_op jit(solution)/shard_map/ppermute | solution.py:75
  20.8 16.5 %collective-permute-start.4 = (bf16[1024,128]{1,0:T(8,128)(2,1)}, bf16[1024,128]{1,0:T(8,128)(2,1)}, u32[]{:S(2)}, u32[]{:S(2)}) collective-permute-start(bf16[1024,128]{1,0:T(8,128)(2,1)} %slice.611), channel_id=1, source_target_pairs={{2,0},{4,2},{6,4},{8,6},{10,8},{12,10},{14,12},{16,14},{18,16},{20... | collective-permute-start | bytes 786440 | tf_op jit(solution)/shard_map/ppermute | solution.py:18
  44.6 6.8 %collective-permute-start.5 = (bf16[2,2,2,16,1024]{4,3,2,1,0:T(8,128)(2,1)S(1)}, bf16[2,2,2,16,1024]{4,3,2,1,0:T(8,128)(2,1)S(1)}, u32[]{:S(2)}, u32[]{:S(2)}) collective-permute-start(bf16[2,2,2,16,1024]{4,3,2,1,0:T(8,128)(2,1)S(1)} %pad_maximum_fusion.5), channel_id=1, source_target_pairs={{0,4},{2,6},{4,0},{6,2},{8,12},{10,14},{12,8},{14,10},{16,20},{18,... | collective-permute-start | bytes 786440 | tf_op jit(solution)/shard_map/ppermute | solution.py:75
  45.2 12.5 %collective-permute-start.12 = (bf16[2,2,2,16,1024]{4,3,2,1,0:T(8,128)(2,1)S(1)}, bf16[2,2,2,16,1024]{4,3,2,1,0:T(8,128)(2,1)S(1)}, u32[]{:S(2)}, u32[]{:S(2)}) collective-permute-start(bf16[2,2,2,16,1024]{4,3,2,1,0:T(8,128)(2,1)S(1)} %pad_maximum_fusion.8), channel_id=1, source_target_pairs={{0,8},{2,10},{4,12},{6,14},{8,0},{10,2},{12,4},{14,6},{16,24},{18,... | collective-permute-start | bytes 786440 | tf_op jit(solution)/shard_map/ppermute | solution.py:75
  45.8 15.6 %collective-permute-start.19 = (bf16[2,2,2,16,1024]{4,3,2,1,0:T(8,128)(2,1)S(1)}, bf16[2,2,2,16,1024]{4,3,2,1,0:T(8,128)(2,1)S(1)}, u32[]{:S(2)}, u32[]{:S(2)}) collective-permute-start(bf16[2,2,2,16,1024]{4,3,2,1,0:T(8,128)(2,1)S(1)} %pad_maximum_fusion.11), channel_id=1, source_target_pairs={{0,16},{2,18},{4,20},{6,22},{8,24},{10,26},{12,28},{14,30},{16,0},... | collective-permute-start | bytes 786440 | tf_op jit(solution)/shard_map/ppermute | solution.py:75
  46.2 16.3 %collective-permute-start.26 = (bf16[2,2,2,16,1024]{4,3,2,1,0:T(8,128)(2,1)S(1)}, bf16[2,2,2,16,1024]{4,3,2,1,0:T(8,128)(2,1)S(1)}, u32[]{:S(2)}, u32[]{:S(2)}) collective-permute-start(bf16[2,2,2,16,1024]{4,3,2,1,0:T(8,128)(2,1)S(1)} %pad_maximum_fusion.14), channel_id=1, source_target_pairs={{0,2},{2,0},{4,6},{6,4},{8,10},{10,8},{12,14},{14,12},{16,18},{18,... | collective-permute-start | bytes 786440 | tf_op jit(solution)/shard_map/ppermute | solution.py:75
  51.5 14.1 %collective-permute-start.6 = (bf16[2,2,16,1024]{3,2,1,0:T(8,128)(2,1)S(1)}, bf16[2,2,16,1024]{3,2,1,0:T(8,128)(2,1)S(1)}, u32[]{:S(2)}, u32[]{:S(2)}) collective-permute-start(bf16[2,2,16,1024]{3,2,1,0:T(8,128)(2,1)S(1)} %pad_maximum_fusion.22), channel_id=1, source_target_pairs={{0,8},{2,10},{4,12},{6,14},{8,0},{10,2},{12,4},{14,6},{16,24},{18,... | collective-permute-start | bytes 393224 | tf_op jit(solution)/shard_map/ppermute | solution.py:75
  57.9 8.2 %collective-permute-start.13 = (bf16[2,2,16,1024]{3,2,1,0:T(8,128)(2,1)S(1)}, bf16[2,2,16,1024]{3,2,1,0:T(8,128)(2,1)S(1)}, u32[]{:S(2)}, u32[]{:S(2)}) collective-permute-start(bf16[2,2,16,1024]{3,2,1,0:T(8,128)(2,1)S(1)} %pad_maximum_fusion.25), channel_id=1, source_target_pairs={{0,16},{2,18},{4,20},{6,22},{8,24},{10,26},{12,28},{14,30},{16,0},... | collective-permute-start | bytes 393224 | tf_op jit(solution)/shard_map/ppermute | solution.py:75
  61.5 8.2 %collective-permute-start.20 = (bf16[2,2,16,1024]{3,2,1,0:T(8,128)(2,1)S(1)}, bf16[2,2,16,1024]{3,2,1,0:T(8,128)(2,1)S(1)}, u32[]{:S(2)}, u32[]{:S(2)}) collective-permute-start(bf16[2,2,16,1024]{3,2,1,0:T(8,128)(2,1)S(1)} %pad_maximum_fusion.28), channel_id=1, source_target_pairs={{0,2},{2,0},{4,6},{6,4},{8,10},{10,8},{12,14},{14,12},{16,18},{18,... | collective-permute-start | bytes 393224 | tf_op jit(solution)/shard_map/ppermute | solution.py:75
  62.6 7.9 %collective-permute-start.27 = (bf16[2,2,16,1024]{3,2,1,0:T(8,128)(2,1)S(1)}, bf16[2,2,16,1024]{3,2,1,0:T(8,128)(2,1)S(1)}, u32[]{:S(2)}, u32[]{:S(2)}) collective-permute-start(bf16[2,2,16,1024]{3,2,1,0:T(8,128)(2,1)S(1)} %pad_maximum_fusion.31), channel_id=1, source_target_pairs={{0,4},{2,6},{4,0},{6,2},{8,12},{10,14},{12,8},{14,10},{16,20},{18,... | collective-permute-start | bytes 393224 | tf_op jit(solution)/shard_map/ppermute | solution.py:75
  71.4 7.7 %collective-permute-start.8 = (bf16[2,16,1024]{2,1,0:T(8,128)(2,1)S(1)}, bf16[2,16,1024]{2,1,0:T(8,128)(2,1)S(1)}, u32[]{:S(2)}, u32[]{:S(2)}) collective-permute-start(bf16[2,16,1024]{2,1,0:T(8,128)(2,1)S(1)} %pad_maximum_fusion.39), channel_id=1, source_target_pairs={{0,16},{2,18},{4,20},{6,22},{8,24},{10,26},{12,28},{14,30},{16,0},... | collective-permute-start | bytes 196616 | tf_op jit(solution)/shard_map/ppermute | solution.py:89
  72.4 6.8 %collective-permute-start.15 = (bf16[2,16,1024]{2,1,0:T(8,128)(2,1)S(1)}, bf16[2,16,1024]{2,1,0:T(8,128)(2,1)S(1)}, u32[]{:S(2)}, u32[]{:S(2)}) collective-permute-start(bf16[2,16,1024]{2,1,0:T(8,128)(2,1)S(1)} %pad_maximum_fusion.43), channel_id=1, source_target_pairs={{0,2},{2,0},{4,6},{6,4},{8,10},{10,8},{12,14},{14,12},{16,18},{18,... | collective-permute-start | bytes 196616 | tf_op jit(solution)/shard_map/ppermute | solution.py:89
  74.2 7.4 %collective-permute-start.22 = (bf16[2,16,1024]{2,1,0:T(8,128)(2,1)S(1)}, bf16[2,16,1024]{2,1,0:T(8,128)(2,1)S(1)}, u32[]{:S(2)}, u32[]{:S(2)}) collective-permute-start(bf16[2,16,1024]{2,1,0:T(8,128)(2,1)S(1)} %pad_maximum_fusion.47), channel_id=1, source_target_pairs={{0,4},{2,6},{4,0},{6,2},{8,12},{10,14},{12,8},{14,10},{16,20},{18,... | collective-permute-start | bytes 196616 | tf_op jit(solution)/shard_map/ppermute | solution.py:89
  79.1 9.6 %collective-permute-start.9 = (bf16[2,2,16,1024]{3,2,1,0:T(8,128)(2,1)S(1)}, bf16[2,2,16,1024]{3,2,1,0:T(8,128)(2,1)S(1)}, u32[]{:S(2)}, u32[]{:S(2)}) collective-permute-start(bf16[2,2,16,1024]{3,2,1,0:T(8,128)(2,1)S(1)} %pad_maximum_fusion.23), channel_id=1, source_target_pairs={{0,8},{2,10},{4,12},{6,14},{8,0},{10,2},{12,4},{14,6},{16,24},{18,... | collective-permute-start | bytes 393224 | tf_op jit(solution)/shard_map/ppermute | solution.py:89
  79.3 11.6 %collective-permute-start.16 = (bf16[2,2,16,1024]{3,2,1,0:T(8,128)(2,1)S(1)}, bf16[2,2,16,1024]{3,2,1,0:T(8,128)(2,1)S(1)}, u32[]{:S(2)}, u32[]{:S(2)}) collective-permute-start(bf16[2,2,16,1024]{3,2,1,0:T(8,128)(2,1)S(1)} %pad_maximum_fusion.26), channel_id=1, source_target_pairs={{0,16},{2,18},{4,20},{6,22},{8,24},{10,26},{12,28},{14,30},{16,0},... | collective-permute-start | bytes 393224 | tf_op jit(solution)/shard_map/ppermute | solution.py:89
  81.6 9.4 %collective-permute-start.23 = (bf16[2,2,16,1024]{3,2,1,0:T(8,128)(2,1)S(1)}, bf16[2,2,16,1024]{3,2,1,0:T(8,128)(2,1)S(1)}, u32[]{:S(2)}, u32[]{:S(2)}) collective-permute-start(bf16[2,2,16,1024]{3,2,1,0:T(8,128)(2,1)S(1)} %pad_maximum_fusion.29), channel_id=1, source_target_pairs={{0,2},{2,0},{4,6},{6,4},{8,10},{10,8},{12,14},{14,12},{16,18},{18,... | collective-permute-start | bytes 393224 | tf_op jit(solution)/shard_map/ppermute | solution.py:89
  81.8 12.1 %collective-permute-start.30 = (bf16[2,2,16,1024]{3,2,1,0:T(8,128)(2,1)S(1)}, bf16[2,2,16,1024]{3,2,1,0:T(8,128)(2,1)S(1)}, u32[]{:S(2)}, u32[]{:S(2)}) collective-permute-start(bf16[2,2,16,1024]{3,2,1,0:T(8,128)(2,1)S(1)} %pad_maximum_fusion.32), channel_id=1, source_target_pairs={{0,4},{2,6},{4,0},{6,2},{8,12},{10,14},{12,8},{14,10},{16,20},{18,... | collective-permute-start | bytes 393224 | tf_op jit(solution)/shard_map/ppermute | solution.py:89
  88.8 9.2 %collective-permute-start.10 = (bf16[2,2,2,16,1024]{4,3,2,1,0:T(8,128)(2,1)S(1)}, bf16[2,2,2,16,1024]{4,3,2,1,0:T(8,128)(2,1)S(1)}, u32[]{:S(2)}, u32[]{:S(2)}) collective-permute-start(bf16[2,2,2,16,1024]{4,3,2,1,0:T(8,128)(2,1)S(1)} %pad_maximum_fusion.6), channel_id=1, source_target_pairs={{0,4},{2,6},{4,0},{6,2},{8,12},{10,14},{12,8},{14,10},{16,20},{18,... | collective-permute-start | bytes 786440 | tf_op jit(solution)/shard_map/ppermute | solution.py:89
  91.0 14.1 %collective-permute-start.17 = (bf16[2,2,2,16,1024]{4,3,2,1,0:T(8,128)(2,1)S(1)}, bf16[2,2,2,16,1024]{4,3,2,1,0:T(8,128)(2,1)S(1)}, u32[]{:S(2)}, u32[]{:S(2)}) collective-permute-start(bf16[2,2,2,16,1024]{4,3,2,1,0:T(8,128)(2,1)S(1)} %pad_maximum_fusion.9), channel_id=1, source_target_pairs={{0,8},{2,10},{4,12},{6,14},{8,0},{10,2},{12,4},{14,6},{16,24},{18,... | collective-permute-start | bytes 786440 | tf_op jit(solution)/shard_map/ppermute | solution.py:89
  91.2 15.9 %collective-permute-start.24 = (bf16[2,2,2,16,1024]{4,3,2,1,0:T(8,128)(2,1)S(1)}, bf16[2,2,2,16,1024]{4,3,2,1,0:T(8,128)(2,1)S(1)}, u32[]{:S(2)}, u32[]{:S(2)}) collective-permute-start(bf16[2,2,2,16,1024]{4,3,2,1,0:T(8,128)(2,1)S(1)} %pad_maximum_fusion.12), channel_id=1, source_target_pairs={{0,16},{2,18},{4,20},{6,22},{8,24},{10,26},{12,28},{14,30},{16,0},... | collective-permute-start | bytes 786440 | tf_op jit(solution)/shard_map/ppermute | solution.py:89
  94.0 13.2 %collective-permute-start.31 = (bf16[2,2,2,16,1024]{4,3,2,1,0:T(8,128)(2,1)S(1)}, bf16[2,2,2,16,1024]{4,3,2,1,0:T(8,128)(2,1)S(1)}, u32[]{:S(2)}, u32[]{:S(2)}) collective-permute-start(bf16[2,2,2,16,1024]{4,3,2,1,0:T(8,128)(2,1)S(1)} %pad_maximum_fusion.15), channel_id=1, source_target_pairs={{0,2},{2,0},{4,6},{6,4},{8,10},{10,8},{12,14},{14,12},{16,18},{18,... | collective-permute-start | bytes 786440 | tf_op jit(solution)/shard_map/ppermute | solution.py:89
  98.1 11.9 %collective-permute-start.11 = (bf16[1,2,2,2,16,1024]{5,4,3,2,1,0:T(8,128)(2,1)S(1)}, bf16[1,2,2,2,16,1024]{5,4,3,2,1,0:T(8,128)(2,1)S(1)}, u32[]{:S(2)}, u32[]{:S(2)}) collective-permute-start(bf16[1,2,2,2,16,1024]{5,4,3,2,1,0:T(8,128)(2,1)S(1)} %maximum_bitcast_fusion.10), channel_id=1, source_target_pairs={{0,2},{2,0},{4,6},{6,4},{8,10},{10,8},{12,14},{14,12},{16,18},{18,... | collective-permute-start | bytes 786440 | tf_op jit(solution)/shard_map/ppermute | solution.py:89
  99.3 12.5 %collective-permute-start.33 = (bf16[1,2,2,2,16,1024]{5,4,3,2,1,0:T(8,128)(2,1)S(1)}, bf16[1,2,2,2,16,1024]{5,4,3,2,1,0:T(8,128)(2,1)S(1)}, u32[]{:S(2)}, u32[]{:S(2)}) collective-permute-start(bf16[1,2,2,2,16,1024]{5,4,3,2,1,0:T(8,128)(2,1)S(1)} %maximum_bitcast_fusion.14), channel_id=1, source_target_pairs={{0,2},{2,0},{4,6},{6,4},{8,10},{10,8},{12,14},{14,12},{16,18},{18,... | collective-permute-start | bytes 786440 | tf_op jit(solution)/shard_map/ppermute | solution.py:89
  105.1 6.9 %collective-permute-start.18 = (bf16[1,2,2,2,16,1024]{5,4,3,2,1,0:T(8,128)(2,1)S(1)}, bf16[1,2,2,2,16,1024]{5,4,3,2,1,0:T(8,128)(2,1)S(1)}, u32[]{:S(2)}, u32[]{:S(2)}) collective-permute-start(bf16[1,2,2,2,16,1024]{5,4,3,2,1,0:T(8,128)(2,1)S(1)} %maximum_bitcast_fusion.11), channel_id=1, source_target_pairs={{0,4},{2,6},{4,0},{6,2},{8,12},{10,14},{12,8},{14,10},{16,20},{18,... | collective-permute-start | bytes 786440 | tf_op jit(solution)/shard_map/ppermute | solution.py:89
  107.1 9.2 %collective-permute-start.25 = (bf16[1,2,2,2,16,1024]{5,4,3,2,1,0:T(8,128)(2,1)S(1)}, bf16[1,2,2,2,16,1024]{5,4,3,2,1,0:T(8,128)(2,1)S(1)}, u32[]{:S(2)}, u32[]{:S(2)}) collective-permute-start(bf16[1,2,2,2,16,1024]{5,4,3,2,1,0:T(8,128)(2,1)S(1)} %maximum_bitcast_fusion.12), channel_id=1, source_target_pairs={{0,8},{2,10},{4,12},{6,14},{8,0},{10,2},{12,4},{14,6},{16,24},{18,... | collective-permute-start | bytes 786440 | tf_op jit(solution)/shard_map/ppermute | solution.py:89
  107.3 10.5 %collective-permute-start.32 = (bf16[1,2,2,2,16,1024]{5,4,3,2,1,0:T(8,128)(2,1)S(1)}, bf16[1,2,2,2,16,1024]{5,4,3,2,1,0:T(8,128)(2,1)S(1)}, u32[]{:S(2)}, u32[]{:S(2)}) collective-permute-start(bf16[1,2,2,2,16,1024]{5,4,3,2,1,0:T(8,128)(2,1)S(1)} %maximum_bitcast_fusion.13), channel_id=1, source_target_pairs={{0,16},{2,18},{4,20},{6,22},{8,24},{10,26},{12,28},{14,30},{16,0},... | collective-permute-start | bytes 786440 | tf_op jit(solution)/shard_map/ppermute | solution.py:89
  110.1 22.3 %collective-permute-start.34 = (bf16[1,2,2,2,16,1024]{5,4,3,2,1,0:T(8,128)(2,1)S(1)}, bf16[1,2,2,2,16,1024]{5,4,3,2,1,0:T(8,128)(2,1)S(1)}, u32[]{:S(2)}, u32[]{:S(2)}) collective-permute-start(bf16[1,2,2,2,16,1024]{5,4,3,2,1,0:T(8,128)(2,1)S(1)} %maximum_bitcast_fusion.15), channel_id=1, source_target_pairs={{0,4},{2,6},{4,0},{6,2},{8,12},{10,14},{12,8},{14,10},{16,20},{18,... | collective-permute-start | bytes 786440 | tf_op jit(solution)/shard_map/ppermute | solution.py:89
  111.8 20.7 %collective-permute-start.35 = (bf16[1,2,2,2,16,1024]{5,4,3,2,1,0:T(8,128)(2,1)S(1)}, bf16[1,2,2,2,16,1024]{5,4,3,2,1,0:T(8,128)(2,1)S(1)}, u32[]{:S(2)}, u32[]{:S(2)}) collective-permute-start(bf16[1,2,2,2,16,1024]{5,4,3,2,1,0:T(8,128)(2,1)S(1)} %maximum_bitcast_fusion.16), channel_id=1, source_target_pairs={{0,8},{2,10},{4,12},{6,14},{8,0},{10,2},{12,4},{14,6},{16,24},{18,... | collective-permute-start | bytes 786440 | tf_op jit(solution)/shard_map/ppermute | solution.py:89
  112.0 20.7 %collective-permute-start.36 = (bf16[1,2,2,2,16,1024]{5,4,3,2,1,0:T(8,128)(2,1)S(1)}, bf16[1,2,2,2,16,1024]{5,4,3,2,1,0:T(8,128)(2,1)S(1)}, u32[]{:S(2)}, u32[]{:S(2)}) collective-permute-start(bf16[1,2,2,2,16,1024]{5,4,3,2,1,0:T(8,128)(2,1)S(1)} %maximum_bitcast_fusion.17), channel_id=1, source_target_pairs={{0,16},{2,18},{4,20},{6,22},{8,24},{10,26},{12,28},{14,30},{16,0},... | collective-permute-start | bytes 786440 | tf_op jit(solution)/shard_map/ppermute | solution.py:89
  (22 other events, 128.6 us)
